TPU v7x, 128 devices: a whole 4x4x4 slice. The times are simulated.
128 devices in a mesh: gx: 16 (over x, z_lo, core), gy: 8 (over z_hi, y).
Axes of the slice: x: 4, y: 4, z: 4 (z_hi: 2, z_lo: 2; z = z_hi * 2 + z_lo), core: 2. Of those that a mesh axis runs over, the one named last changes fastest.
Arguments:
- points_rhs: float32 [16, 2097152], P(None, ('gx', 'gy')), may hold values from -6 to 6
- morton_order: int32 [2097152], P(('gx', 'gy')), may hold values from 0 to 16383, as said below
- band_offsets: int32 [8192], P(('gx', 'gy')), may hold values from -16 to 16, as said below
- leaf_basis: bfloat16 [8192, 32, 256], P(('gx', 'gy')), may hold values from -0.375 to 0.375
- band_blocks: bfloat16 [8192, 2, 256, 256], P(('gx', 'gy')), may hold values from -0.375 to 0.375
- translations: float32 [128, 7, 8, 2, 32, 32], P(('gx', 'gy'))
- out_basis: bfloat16 [8192, 32, 256], P(('gx', 'gy')), may hold values from -1 to 1
Outputs:
- transformed: float32 [16, 2097152], P(None, ('gx', 'gy'))
Inputs may be any that keep to these rules, and one draw needn't show every extreme that they name: `morton_order`: for every node k, entries 16384 * k to 16384 * (k + 1) - 1 hold each of 0 to 16383 exactly once. `band_offsets`: never zero; the first leaf of every node has offset -16 and the last leaf of every node has offset 16.
All inputs are finite; a program needn't handle non-finite values.
Results may differ from a plain program's by a relative error of at most 0.0033.
Values may be sent and summed in bfloat16 or wider, within the bound.
No kernel may reach another device: no remote copies, remote signals or barrier semaphores. Data moves between devices by JAX's collectives and lax.ppermute only.
A program may use at most 128 MiB of HBM per device.

v0:
```python
import jax
import jax.numpy as jnp
from jax import lax
from jax.sharding import PartitionSpec as P

HW = 16


def from_partner(x, axis, distance):
    return lax.ppermute(x, axis, [(i, i ^ 1 << distance) for i in range(lax.axis_size(axis))])


def extended(x, sides, width):
    for axis, dim in sides:
        count, length = (lax.axis_size(axis), x.shape[dim])
        up = [(i, (i + 1) % count) for i in range(count - 1)]
        down = [(j, i) for i, j in up]
        last = lax.slice_in_dim(x, length - width, length, axis=dim)
        initial = lax.slice_in_dim(x, 0, width, axis=dim)
        before = lax.ppermute(last, axis, up)
        after = lax.ppermute(initial, axis, down)
        x = jnp.concatenate([before, x, after], axis=dim)
    return x


def translate(level_weights, own_coeffs, other_coeffs):
    first = jnp.einsum(
        "gab,bgm->agm",
        level_weights[:, 0],
        own_coeffs,
        precision=lax.Precision.HIGHEST,
        preferred_element_type=jnp.float32,
    )
    second = jnp.einsum(
        "gab,bgm->agm",
        level_weights[:, 1],
        other_coeffs,
        precision=lax.Precision.HIGHEST,
        preferred_element_type=jnp.float32,
    )
    return first + second


def local(points_rhs, morton_order, band_offsets, leaf_basis, band_blocks, translations, out_basis):
    rhs_count, point_count = points_rhs.shape
    leaf_count, rank_size, leaf_size = leaf_basis.shape
    group_total = translations.shape[2]
    total_cols = leaf_count * rhs_count
    group_width = total_cols // group_total
    ordered = points_rhs[:, morton_order].astype(jnp.bfloat16)
    leaves = ordered.reshape(rhs_count, leaf_count, leaf_size)
    coeffs = jnp.einsum(
        "lrp,slp->rls", leaf_basis, leaves, preferred_element_type=jnp.float32
    ).reshape(rank_size, total_cols)
    weights = translations[0]
    low_bits = lax.axis_size("gy").bit_length() - 1
    high_bits = lax.axis_size("gx").bit_length() - 1
    coeffs = coeffs.reshape(rank_size, group_total, group_width)
    for level_bit in range(low_bits):
        partner = from_partner(coeffs, "gy", level_bit)
        coeffs = translate(weights[level_bit], coeffs, partner)
    for level_bit in range(high_bits):
        partner = from_partner(coeffs, "gx", level_bit)
        coeffs = translate(weights[low_bits + level_bit], coeffs, partner)
    coeffs = coeffs.reshape(rank_size, total_cols)
    coeff_bf = coeffs.astype(jnp.bfloat16).reshape(rank_size, leaf_count, rhs_count)
    far_term = jnp.einsum("lrp,rls->slp", out_basis, coeff_bf, preferred_element_type=jnp.float32)
    padded = extended(ordered, ((("gx", "gy"), 1),), HW * leaf_size)
    blocks_all = padded.reshape(rhs_count, leaf_count + 2 * HW, leaf_size)
    block_index = jnp.arange(leaf_count, dtype=jnp.int32) + HW + band_offsets
    picked = jnp.take(blocks_all, block_index, axis=1)
    own_term = jnp.einsum(
        "lpq,slq->slp", band_blocks[:, 0], leaves, preferred_element_type=jnp.float32
    )
    partner_term = jnp.einsum(
        "lpq,slq->slp", band_blocks[:, 1], picked, preferred_element_type=jnp.float32
    )
    return (far_term + own_term + partner_term).reshape(rhs_count, point_count)


def solution(mesh):
    return jax.shard_map(
        local,
        mesh=mesh,
        in_specs=(
            P(None, ("gx", "gy")),
            P(("gx", "gy")),
            P(("gx", "gy")),
            P(("gx", "gy"), None, None),
            P(("gx", "gy"), None, None, None),
            P(("gx", "gy"), None, None, None, None, None),
            P(("gx", "gy"), None, None),
        ),
        out_specs=P(None, ("gx", "gy")),
        check_vma=False,
    )
```

profile of v0, /device:TPU:0, one launch (start us, length us, event | category | flops | bytes accessed | tf_op | source)
XLA Modules:
  0.0 143.6 jit_solution(17379679716495308189)
XLA Ops:
  0.0 4.7 %copy.58 = bf16[16,16384]{0,1:T(8,128)(2,1)} copy(f32[16,16384]{1,0:T(8,128)} %param.7) | data formatting | bytes 1572864 | tf_op args[0]
  4.8 57.7 %gather_fusion = bf16[16384,16]{1,0:T(8,128)(2,1)} fusion(bf16[16,16384]{0,1:T(8,128)(2,1)} %copy.58, s32[16384]{0:T(1024)S(1)} %fusion.27), kind=kCustom, calls=%fused_computation | custom fusion | bytes 1114112 | tf_op jit(solution)/shard_map/gather | solution.py:50
  62.4 1.7 %fusion.29 = (bf16[16,4096]{0,1:T(8,128)(2,1)S(1)}, bf16[16,4096]{0,1:T(8,128)(2,1)S(1)}) fusion(bf16[16,16384]{0,1:T(8,128)(2,1)} %bitcast.124), kind=kLoop, calls=%fused_computation.66 | loop fusion | bytes 524288 | tf_op jit(solution)/shard_map/slice | solution.py:18
  65.1 1.3 collective-permute-start.8
  67.4 5.2 %collective-permute-start.7 = (bf16[16,4096]{1,0:T(8,128)(2,1)}, bf16[16,4096]{1,0:T(8,128)(2,1)}, u32[]{:S(2)}, u32[]{:S(2)}) collective-permute-start(bf16[16,4096]{1,0:T(8,128)(2,1)} %copy.72), channel_id=1, source_target_pairs={{0,1},{1,2},{2,3},{3,4},{4,5},{5,6},{6,7},{7,8},{8,9},{9,10},{10,1... | collective-permute-start | bytes 393224 | tf_op jit(solution)/shard_map/ppermute | solution.py:20
  72.6 3.7 %fusion.31 = f32[64,16,32]{2,1,0:T(8,128)S(1)} fusion(bf16[16,64,256]{0,2,1:T(8,128)(2,1)} %bitcast.125, bf16[64,32,256]{2,1,0:T(8,128)(2,1)} %param.10), kind=kOutput, calls=%fused_computation.68 | convolution fusion | flops 16777216 | bytes 1703936 | tf_op jit(solution)/shard_map/lrp,slp->rls/dot_general | solution.py:52
  78.2 6.9 %fusion.2 = f32[64,16,256]{2,1,0:T(8,128)S(1)} fusion(bf16[16,64,256]{0,2,1:T(8,128)(2,1)} %bitcast.126, bf16[64,2,256,256]{3,2,1,0:T(8,128)(2,1)} %param.11), kind=kOutput, calls=%fused_computation.4 | convolution fusion | flops 134217728 | bytes 13631488 | tf_op jit(solution)/shard_map/lpq,slq->slp/dot_general | solution.py:72
  86.1 1.6 %fusion.26 = f32[8,128,32]{1,2,0:T(8,128)} fusion(f32[32,8,128]{0,2,1:T(8,128)S(1)} %bitcast.129, f32[8,2,32,32]{3,2,0,1:T(8,128)S(1)} %bitcast.145), kind=kOutput, calls=%fused_computation.60 | convolution fusion | flops 12582912 | bytes 786432 | tf_op jit(solution)/shard_map/gab,bgm->agm/dot_general | solution.py:27
  87.7 3.5 %copy.74 = bf16[16,16384]{1,0:T(8,128)(2,1)S(1)} copy(bf16[16,16384]{0,1:T(8,128)(2,1)} %bitcast.127) | data formatting | bytes 1048576 | tf_op jit(solution)/shard_map/convert_element_type | solution.py:50
  91.2 1.7 %copy.106 = f32[1,1,8,2,32,32]{5,4,2,3,1,0:T(8,128)} copy(f32[1,1,8,2,32,32]{5,4,3,2,1,0:T(8,128)} %get-tuple-element.14) | data formatting | bytes 131072
  92.9 1.7 %copy.105 = f32[1,1,8,2,32,32]{5,4,2,3,1,0:T(8,128)} copy(f32[1,1,8,2,32,32]{5,4,3,2,1,0:T(8,128)} %get-tuple-element.13) | data formatting | bytes 131072
  94.6 1.7 %copy.104 = f32[1,1,8,2,32,32]{5,4,2,3,1,0:T(8,128)} copy(f32[1,1,8,2,32,32]{5,4,3,2,1,0:T(8,128)} %get-tuple-element.12) | data formatting | bytes 131072
  98.8 1.2 fusion.13
  100.0 6.6 %collective-permute-start.1 = (f32[32,8,128]{2,0,1:T(8,128)S(1)}, f32[32,8,128]{2,0,1:T(8,128)}, u32[]{:S(2)}, u32[]{:S(2)}) collective-permute-start(f32[32,8,128]{2,0,1:T(8,128)S(1)} %fusion.13), channel_id=1, source_target_pairs={{0,2},{1,3},{2,0},{3,1},{4,6},{5,7},{6,4},{7,5},{8,10},{9,11},{10,... | collective-permute-start | bytes 393224 | tf_op jit(solution)/shard_map/ppermute | solution.py:10
  106.6 1.4 gather_fusion.1
  108.0 5.9 %fusion = f32[64,16,256]{2,1,0:T(8,128)S(1)} fusion(bf16[64,2,256,256]{3,2,1,0:T(8,128)(2,1)} %param.11, bf16[64,16,256]{2,1,0:T(8,128)(2,1)} %gather_fusion.1, pred[64]{0:T(512)(128)(4,1)S(1)} %get-tuple-element.5), kind=kOutput, calls=%fused_computation.2 | convolution fusion | flops 134479872 | bytes 9961536 | tf_op jit(solution)/shard_map/lpq,slq->slp/dot_general | solution.py:75
  115.4 3.7 %collective-permute-start.2 = (f32[32,8,128]{2,0,1:T(8,128)S(1)}, f32[32,8,128]{2,0,1:T(8,128)S(1)}, u32[]{:S(2)}, u32[]{:S(2)}) collective-permute-start(f32[32,8,128]{2,0,1:T(8,128)S(1)} %fusion.12), channel_id=1, source_target_pairs={{0,4},{1,5},{2,6},{3,7},{4,0},{5,1},{6,2},{7,3},{8,12},{9,13},{10,... | collective-permute-start | bytes 393224 | tf_op jit(solution)/shard_map/ppermute | solution.py:10
  119.3 2.7 %collective-permute-done.2 = f32[32,8,128]{2,0,1:T(8,128)S(1)} collective-permute-done((f32[32,8,128]{2,0,1:T(8,128)S(1)}, f32[32,8,128]{2,0,1:T(8,128)S(1)}, u32[]{:S(2)}, u32[]{:S(2)}) %collective-permute-start.2) | collective-permute-done | bytes 131104 | tf_op jit(solution)/shard_map/ppermute | solution.py:10
  123.9 1.9 %collective-permute-start.4 = (f32[32,8,128]{2,0,1:T(8,128)S(1)}, f32[32,8,128]{2,0,1:T(8,128)S(1)}, u32[]{:S(2)}, u32[]{:S(2)}) collective-permute-start(f32[32,8,128]{2,0,1:T(8,128)S(1)} %fusion.10), channel_id=1, source_target_pairs={{0,16},{8,24},{16,0},{24,8},{32,48},{40,56},{48,32},{56,40},{64,80... | collective-permute-start | bytes 393224 | tf_op jit(solution)/shard_map/ppermute | solution.py:10
  126.1 3.5 %collective-permute-done.4 = f32[32,8,128]{2,0,1:T(8,128)S(1)} collective-permute-done((f32[32,8,128]{2,0,1:T(8,128)S(1)}, f32[32,8,128]{2,0,1:T(8,128)S(1)}, u32[]{:S(2)}, u32[]{:S(2)}) %collective-permute-start.4) | collective-permute-done | bytes 131104 | tf_op jit(solution)/shard_map/ppermute | solution.py:10
  129.9 1.6 %collective-permute-start.5 = (f32[32,8,128]{2,0,1:T(8,128)S(1)}, f32[32,8,128]{2,0,1:T(8,128)S(1)}, u32[]{:S(2)}, u32[]{:S(2)}) collective-permute-start(f32[32,8,128]{2,0,1:T(8,128)S(1)} %fusion.9), channel_id=1, source_target_pairs={{0,32},{8,40},{16,48},{24,56},{32,0},{40,8},{48,16},{56,24},{64,96... | collective-permute-start | bytes 393224 | tf_op jit(solution)/shard_map/ppermute | solution.py:10
  131.8 3.2 %collective-permute-done.5 = f32[32,8,128]{2,0,1:T(8,128)S(1)} collective-permute-done((f32[32,8,128]{2,0,1:T(8,128)S(1)}, f32[32,8,128]{2,0,1:T(8,128)S(1)}, u32[]{:S(2)}, u32[]{:S(2)}) %collective-permute-start.5) | collective-permute-done | bytes 131104 | tf_op jit(solution)/shard_map/ppermute | solution.py:10
  135.2 3.1 %collective-permute-start.6 = (f32[32,8,128]{2,0,1:T(8,128)S(1)}, f32[32,8,128]{2,0,1:T(8,128)S(1)}, u32[]{:S(2)}, u32[]{:S(2)}) collective-permute-start(f32[32,8,128]{2,0,1:T(8,128)S(1)} %fusion.8), channel_id=1, source_target_pairs={{0,64},{8,72},{16,80},{24,88},{32,96},{40,104},{48,112},{56,120},{... | collective-permute-start | bytes 393224 | tf_op jit(solution)/shard_map/ppermute | solution.py:10
  138.6 3.2 %collective-permute-done.6 = f32[32,8,128]{2,0,1:T(8,128)S(1)} collective-permute-done((f32[32,8,128]{2,0,1:T(8,128)S(1)}, f32[32,8,128]{2,0,1:T(8,128)S(1)}, u32[]{:S(2)}, u32[]{:S(2)}) %collective-permute-start.6) | collective-permute-done | bytes 131104 | tf_op jit(solution)/shard_map/ppermute | solution.py:10
  (59 shorter events, 14.0 us)
Async XLA Ops:
  0.0 142.2 %copy-start = (bf16[64,32,256]{2,1,0:T(8,128)(2,1)S(1)}, bf16[64,32,256]{2,1,0:T(8,128)(2,1)}, u32[]{:S(2)}) copy-start(bf16[64,32,256]{2,1,0:T(8,128)(2,1)} %param.13) | copy-start | bytes 3145732
  0.0 4.7 %copy-start.10 = (s32[16384]{0:T(1024)S(1)}, s32[16384]{0:T(1024)}, u32[]{:S(2)}) copy-start(s32[16384]{0:T(1024)} %param.8) | copy-start | bytes 196612
  65.1 32.6 %collective-permute-start.8 = (bf16[16,4096]{1,0:T(8,128)(2,1)}, bf16[16,4096]{1,0:T(8,128)(2,1)S(1)}, u32[]{:S(2)}, u32[]{:S(2)}) collective-permute-start(bf16[16,4096]{1,0:T(8,128)(2,1)} %copy.73), channel_id=1, source_target_pairs={{1,0},{2,1},{3,2},{4,3},{5,4},{6,5},{7,6},{8,7},{9,8},{10,9},{11,1... | collective-permute-start | bytes 393224 | tf_op jit(solution)/shard_map/ppermute | solution.py:21
  67.4 30.4 %collective-permute-start.7 = (bf16[16,4096]{1,0:T(8,128)(2,1)}, bf16[16,4096]{1,0:T(8,128)(2,1)}, u32[]{:S(2)}, u32[]{:S(2)}) collective-permute-start(bf16[16,4096]{1,0:T(8,128)(2,1)} %copy.72), channel_id=1, source_target_pairs={{0,1},{1,2},{2,3},{3,4},{4,5},{5,6},{6,7},{7,8},{8,9},{9,10},{10,1... | collective-permute-start | bytes 393224 | tf_op jit(solution)/shard_map/ppermute | solution.py:20
  77.1 8.0 %copy-start.1 = (f32[1,7,8,2,32,32]{5,4,3,2,1,0:T(8,128)S(1)}, f32[1,7,8,2,32,32]{5,4,3,2,1,0:T(8,128)}, u32[]{:S(2)}) copy-start(f32[1,7,8,2,32,32]{5,4,3,2,1,0:T(8,128)} %param.12) | copy-start | bytes 1376260
  77.1 21.7 %collective-permute-start = (f32[32,8,128]{2,0,1:T(8,128)}, f32[32,8,128]{2,0,1:T(8,128)}, u32[]{:S(2)}, u32[]{:S(2)}) collective-permute-start(f32[32,8,128]{2,0,1:T(8,128)} %copy.62), channel_id=1, source_target_pairs={{0,1},{1,0},{2,3},{3,2},{4,5},{5,4},{6,7},{7,6},{8,9},{9,8},{10,11... | collective-permute-start | bytes 393224 | tf_op jit(solution)/shard_map/ppermute | solution.py:10
  85.1 2.6 %copy-start.11 = (s32[64]{0:T(128)S(1)}, s32[64]{0:T(128)}, u32[]{:S(2)}) copy-start(s32[64]{0:T(128)} %param.9) | copy-start | bytes 772
  86.1 1.6 %copy-start.7 = (f32[1,1,8,2,32,32]{5,4,2,3,1,0:T(8,128)}, f32[1,1,8,2,32,32]{5,4,2,3,1,0:T(8,128)S(1)}, u32[]{:S(2)}) copy-start(f32[1,1,8,2,32,32]{5,4,2,3,1,0:T(8,128)S(1)} %copy.107) | copy-start | bytes 196612
  91.2 7.6 %copy-start.8 = (f32[1,1,8,2,32,32]{5,4,2,3,1,0:T(8,128)S(1)}, f32[1,1,8,2,32,32]{5,4,2,3,1,0:T(8,128)}, u32[]{:S(2)}) copy-start(f32[1,1,8,2,32,32]{5,4,2,3,1,0:T(8,128)} %copy-done.7) | copy-start | bytes 196612
  91.2 7.6 %copy-start.9 = (f32[8,128,32]{1,2,0:T(8,128)S(1)}, f32[8,128,32]{1,2,0:T(8,128)}, u32[]{:S(2)}) copy-start(f32[8,128,32]{1,2,0:T(8,128)} %fusion.26) | copy-start | bytes 393220
  100.0 14.2 %collective-permute-start.1 = (f32[32,8,128]{2,0,1:T(8,128)S(1)}, f32[32,8,128]{2,0,1:T(8,128)}, u32[]{:S(2)}, u32[]{:S(2)}) collective-permute-start(f32[32,8,128]{2,0,1:T(8,128)S(1)} %fusion.13), channel_id=1, source_target_pairs={{0,2},{1,3},{2,0},{3,1},{4,6},{5,7},{6,4},{7,5},{8,10},{9,11},{10,... | collective-permute-start | bytes 393224 | tf_op jit(solution)/shard_map/ppermute | solution.py:10
  108.0 6.0 %copy-start.6 = (f32[1,1,8,2,32,32]{5,4,2,3,1,0:T(8,128)S(1)}, f32[1,1,8,2,32,32]{5,4,2,3,1,0:T(8,128)}, u32[]{:S(2)}) copy-start(f32[1,1,8,2,32,32]{5,4,2,3,1,0:T(8,128)} %copy.106) | copy-start | bytes 196612
  108.0 11.1 %copy-start.5 = (f32[1,1,8,2,32,32]{5,4,2,3,1,0:T(8,128)S(1)}, f32[1,1,8,2,32,32]{5,4,2,3,1,0:T(8,128)}, u32[]{:S(2)}) copy-start(f32[1,1,8,2,32,32]{5,4,2,3,1,0:T(8,128)} %copy.105) | copy-start | bytes 196612
  108.0 14.4 %copy-start.4 = (f32[1,1,8,2,32,32]{5,4,2,3,1,0:T(8,128)S(1)}, f32[1,1,8,2,32,32]{5,4,2,3,1,0:T(8,128)}, u32[]{:S(2)}) copy-start(f32[1,1,8,2,32,32]{5,4,2,3,1,0:T(8,128)} %copy.104) | copy-start | bytes 196612
  108.0 17.9 %copy-start.3 = (f32[1,1,8,2,32,32]{5,4,2,3,1,0:T(8,128)S(1)}, f32[1,1,8,2,32,32]{5,4,2,3,1,0:T(8,128)}, u32[]{:S(2)}) copy-start(f32[1,1,8,2,32,32]{5,4,2,3,1,0:T(8,128)} %copy.103) | copy-start | bytes 196612
  108.0 23.5 %copy-start.2 = (f32[1,1,8,2,32,32]{5,4,2,3,1,0:T(8,128)S(1)}, f32[1,1,8,2,32,32]{5,4,2,3,1,0:T(8,128)}, u32[]{:S(2)}) copy-start(f32[1,1,8,2,32,32]{5,4,2,3,1,0:T(8,128)} %copy.102) | copy-start | bytes 196612
  115.4 6.6 %collective-permute-start.2 = (f32[32,8,128]{2,0,1:T(8,128)S(1)}, f32[32,8,128]{2,0,1:T(8,128)S(1)}, u32[]{:S(2)}, u32[]{:S(2)}) collective-permute-start(f32[32,8,128]{2,0,1:T(8,128)S(1)} %fusion.12), channel_id=1, source_target_pairs={{0,4},{1,5},{2,6},{3,7},{4,0},{5,1},{6,2},{7,3},{8,12},{9,13},{10,... | collective-permute-start | bytes 393224 | tf_op jit(solution)/shard_map/ppermute | solution.py:10
  122.2 1.4 collective-permute-start.3
  123.9 5.7 %collective-permute-start.4 = (f32[32,8,128]{2,0,1:T(8,128)S(1)}, f32[32,8,128]{2,0,1:T(8,128)S(1)}, u32[]{:S(2)}, u32[]{:S(2)}) collective-permute-start(f32[32,8,128]{2,0,1:T(8,128)S(1)} %fusion.10), channel_id=1, source_target_pairs={{0,16},{8,24},{16,0},{24,8},{32,48},{40,56},{48,32},{56,40},{64,80... | collective-permute-start | bytes 393224 | tf_op jit(solution)/shard_map/ppermute | solution.py:10
  129.9 5.0 %collective-permute-start.5 = (f32[32,8,128]{2,0,1:T(8,128)S(1)}, f32[32,8,128]{2,0,1:T(8,128)S(1)}, u32[]{:S(2)}, u32[]{:S(2)}) collective-permute-start(f32[32,8,128]{2,0,1:T(8,128)S(1)} %fusion.9), channel_id=1, source_target_pairs={{0,32},{8,40},{16,48},{24,56},{32,0},{40,8},{48,16},{56,24},{64,96... | collective-permute-start | bytes 393224 | tf_op jit(solution)/shard_map/ppermute | solution.py:10
  135.2 6.6 %collective-permute-start.6 = (f32[32,8,128]{2,0,1:T(8,128)S(1)}, f32[32,8,128]{2,0,1:T(8,128)S(1)}, u32[]{:S(2)}, u32[]{:S(2)}) collective-permute-start(f32[32,8,128]{2,0,1:T(8,128)S(1)} %fusion.8), channel_id=1, source_target_pairs={{0,64},{8,72},{16,80},{24,88},{32,96},{40,104},{48,112},{56,120},{... | collective-permute-start | bytes 393224 | tf_op jit(solution)/shard_map/ppermute | solution.py:10
where the time goes:
time: 144 us
  local copies, waits for them, and re-layouts  80.6 us (56%)
  starting transfers between devices  24.5 us (17%)
  matrix products  23.6 us (16%)
  waiting for transfers between devices  13.7 us (10%)
    gather x1, local copies, waits for them, and re-layouts, local(): ordered = points_rhs[:, morton_order].astype(jnp.bfloat16)  57.7 us
    ppermute x7, starting transfers between devices, from_partner(): lax.ppermute(x, axis, [(i, i ^ 1 << distance) for i in range(lax.axis_siz...  18 us
    ppermute x7, waiting for transfers between devices, from_partner(): lax.ppermute(x, axis, [(i, i ^ 1 << distance) for i in range(lax.axis_siz...  13.7 us
    unnamed x32, local copies, waits for them, and re-layouts  11.3 us
    dot_general x1, matrix products, local(): jnp.einsum('lpq,slq->slp', band_blocks[:, 0], leaves, preferred_element_t...  6.93 us
    dot_general x1, matrix products, local(): jnp.einsum('lpq,slq->slp', band_blocks[:, 1], picked, preferred_element_t...  5.94 us
    ppermute x1, starting transfers between devices, extended(): before = lax.ppermute(last, axis, up)  5.19 us
    dot_general x1, matrix products, local(): jnp.einsum('lrp,slp->rls', leaf_basis, leaves, preferred_element_type=jnp...  3.71 us
  transfers between devices with their start and end apart: 9, of which 5 were waited for; matrix products, arithmetic and copies ran while one was open for 24% of the time, Pallas kernels for 0%

commit v1 on v0

--- a/solution.py
+++ b/solution.py
@@ -1,9 +1,37 @@
 import jax
 import jax.numpy as jnp
 from jax import lax
+from jax.experimental import pallas as pl
+from jax.experimental.pallas import tpu as pltpu
 from jax.sharding import PartitionSpec as P
 
 HW = 16
+
+
+ROWS = 32
+
+
+def gather_kernel(idx_ref, x_ref, o_ref):
+    def body(i, carry):
+        base = pl.multiple_of(i * ROWS, ROWS)
+        for g in range(ROWS // 8):
+            rows = [x_ref[pl.ds(idx_ref[base + g * 8 + u], 1), :] for u in range(8)]
+            o_ref[pl.ds(pl.multiple_of(base + g * 8, 8), 8), :] = jnp.concatenate(rows, axis=0)
+        return carry
+
+    lax.fori_loop(0, o_ref.shape[0] // ROWS, body, 0)
+
+
+def row_gather(rows, index):
+    count, width = rows.shape
+    return pl.pallas_call(
+        gather_kernel,
+        out_shape=jax.ShapeDtypeStruct((count, width), rows.dtype),
+        in_specs=[pl.BlockSpec(memory_space=pltpu.SMEM), pl.BlockSpec(memory_space=pltpu.VMEM)],
+        out_specs=pl.BlockSpec(memory_space=pltpu.VMEM),
+        compiler_params=pltpu.CompilerParams(vmem_limit_bytes=40 * 1024 * 1024),
+        cost_estimate=pl.CostEstimate(flops=0, transcendentals=0, bytes_accessed=2 * count * width * 4),
+    )(index, rows)
 
 
 def from_partner(x, axis, distance):
@@ -47,7 +75,7 @@
     group_total = translations.shape[2]
     total_cols = leaf_count * rhs_count
     group_width = total_cols // group_total
-    ordered = points_rhs[:, morton_order].astype(jnp.bfloat16)
+    ordered = row_gather(points_rhs.T, morton_order).T.astype(jnp.bfloat16)
     leaves = ordered.reshape(rhs_count, leaf_count, leaf_size)
     coeffs = jnp.einsum(
         "lrp,slp->rls", leaf_basis, leaves, preferred_element_type=jnp.float32

time: 144 us -> 114 us (0.79)
  local copies, waits for them, and re-layouts: 80.6 us -> 29.3 us
  Pallas kernels: 0 us -> 19 us
  other arithmetic: 0.99 us -> 5.11 us
  matrix products: 23.6 us -> 21.1 us
    gather x1 -> x0, local copies, waits for them, and re-layouts: 57.7 us -> none  [local(): ordered = points_rhs[:, morton_order].astype(jnp.bfloat16)]
    pallas_call x0 -> x1, Pallas kernels: none -> 19 us  [row_gather(): pl.pallas_call(gather_kernel, out_shape=jax.ShapeDtypeStruct((count, widt...]
    unnamed x32 -> x40, local copies, waits for them, and re-layouts: 11.3 us -> 19.2 us
    convert_element_type x0 -> x2, other arithmetic: none -> 4.14 us  [local(): ordered = row_gather(points_rhs.T, morton_order).T.astype(jnp.bfloat16)]
    dot_general x1, matrix products: 3.71 us -> 1.22 us  [local(): jnp.einsum('lrp,slp->rls', leaf_basis, leaves, preferred_element_type=jnp...]
    slice x2, local copies, waits for them, and re-layouts: 2.65 us -> 1.11 us  [extended(): last = lax.slice_in_dim(x, length - width, length, axis=dim)]
  transfers between devices with their start and end apart: 9 -> 9, of which waited for: 5 -> 5; matrix products, arithmetic and copies ran while one was open for 24% -> 32% of each run, Pallas kernels for 0% -> 0%
where the time goes in v1:
time: 114 us; the launch traced here: 113 us
  local copies, waits for them, and re-layouts  29.3 us (26%)
  starting transfers between devices  24.6 us (22%)
  matrix products  21.1 us (19%)
  Pallas kernels  19 us (17%)
  waiting for transfers between devices  13.7 us (12%)
  other arithmetic  5.11 us (4%)
    unnamed x40, local copies, waits for them, and re-layouts  19.2 us
    pallas_call x1, Pallas kernels, row_gather(): pl.pallas_call(gather_kernel, out_shape=jax.ShapeDtypeStruct((count, widt...  19 us
    ppermute x7, starting transfers between devices, from_partner(): lax.ppermute(x, axis, [(i, i ^ 1 << distance) for i in range(lax.axis_siz...  18 us
    ppermute x7, waiting for transfers between devices, from_partner(): lax.ppermute(x, axis, [(i, i ^ 1 << distance) for i in range(lax.axis_siz...  13.7 us
    dot_general x1, matrix products, local(): jnp.einsum('lpq,slq->slp', band_blocks[:, 0], leaves, preferred_element_t...  6.93 us
    dot_general x1, matrix products, local(): jnp.einsum('lpq,slq->slp', band_blocks[:, 1], picked, preferred_element_t...  5.94 us
    ppermute x1, starting transfers between devices, extended(): before = lax.ppermute(last, axis, up)  5.32 us
    convert_element_type x2, other arithmetic, local(): ordered = row_gather(points_rhs.T, morton_order).T.astype(jnp.bfloat16)  4.14 us
  transfers between devices with their start and end apart: 9, of which 5 were waited for; matrix products, arithmetic and copies ran while one was open for 32% of the time, Pallas kernels for 0%

profile of v1, /device:TPU:0, one launch (start us, length us, event | category | flops | bytes accessed | tf_op | source)
XLA Modules:
  0.0 113.1 jit_solution(10794859116197931687)
XLA Ops:
  0.0 6.1 %copy.58 = f32[16,16384]{0,1:T(8,128)} copy(f32[16,16384]{1,0:T(8,128)} %param.7) | data formatting | bytes 2097152 | tf_op args[0]
  6.1 19.0 %shard_map.73 = f32[16384,16]{1,0:T(8,128)S(1)} custom-call(s32[16384]{0:T(1024)S(1)} %copy-done.2, f32[16384,16]{1,0:T(8,128)} %bitcast.128), custom_call_target="tpu_custom_call" | custom-call | bytes 2097152 | tf_op jit(solution)/shard_map/pallas_call | solution.py:27
  25.6 2.8 %copy-done.1 = f32[16384,16]{1,0:T(8,128)} copy-done((f32[16384,16]{1,0:T(8,128)}, f32[16384,16]{1,0:T(8,128)S(1)}, u32[]{:S(2)}) %copy-start.1) | copy-done | bytes 1048600
  28.5 1.8 %copy-done.4 = bf16[16,16384]{0,1:T(8,128)(2,1)} copy-done((bf16[16,16384]{0,1:T(8,128)(2,1)}, bf16[16,16384]{0,1:T(8,128)(2,1)S(1)}, u32[]{:S(2)}) %copy-start.4) | copy-done | bytes 524312
  33.6 5.3 %collective-permute-start.7 = (bf16[16,4096]{1,0:T(8,128)(2,1)}, bf16[16,4096]{1,0:T(8,128)(2,1)}, u32[]{:S(2)}, u32[]{:S(2)}) collective-permute-start(bf16[16,4096]{1,0:T(8,128)(2,1)} %copy.72), channel_id=1, source_target_pairs={{0,1},{1,2},{2,3},{3,4},{4,5},{5,6},{6,7},{7,8},{8,9},{9,10},{10,1... | collective-permute-start | bytes 393224 | tf_op jit(solution)/shard_map/ppermute | solution.py:48
  38.9 3.7 %convert_element_type.16 = bf16[16384,16]{1,0:T(8,128)(2,1)S(1)} convert(f32[16384,16]{1,0:T(8,128)} %copy-done.1) | non-fusion elementwise | flops 262144 | bytes 1572864 | tf_op jit(solution)/shard_map/convert_element_type | solution.py:78
  42.6 1.9 %copy-done.3 = bf16[16384,16]{1,0:T(8,128)(2,1)} copy-done((bf16[16384,16]{1,0:T(8,128)(2,1)}, bf16[16384,16]{1,0:T(8,128)(2,1)S(1)}, u32[]{:S(2)}) %copy-start.3) | copy-done | bytes 524312
  47.7 6.9 %fusion.2 = f32[64,16,256]{2,1,0:T(8,128)S(1)} fusion(bf16[16,64,256]{0,2,1:T(8,128)(2,1)} %bitcast.127, bf16[64,2,256,256]{3,2,1,0:T(8,128)(2,1)} %param.11), kind=kOutput, calls=%fused_computation.3 | convolution fusion | flops 134217728 | bytes 13631488 | tf_op jit(solution)/shard_map/lpq,slq->slp/dot_general | solution.py:100
  55.7 1.6 %fusion.26 = f32[8,128,32]{1,2,0:T(8,128)} fusion(f32[32,8,128]{0,2,1:T(8,128)S(1)} %bitcast.130, f32[8,2,32,32]{3,2,0,1:T(8,128)S(1)} %bitcast.146), kind=kOutput, calls=%fused_computation.58 | convolution fusion | flops 12582912 | bytes 786432 | tf_op jit(solution)/shard_map/gab,bgm->agm/dot_general | solution.py:55
  57.3 3.5 %copy.74 = bf16[16,16384]{1,0:T(8,128)(2,1)S(1)} copy(bf16[16,16384]{0,1:T(8,128)(2,1)} %copy-done.4) | data formatting | bytes 1048576 | tf_op jit(solution)/shard_map/convert_element_type | solution.py:78
  60.8 1.7 %copy.106 = f32[1,1,8,2,32,32]{5,4,2,3,1,0:T(8,128)} copy(f32[1,1,8,2,32,32]{5,4,3,2,1,0:T(8,128)} %get-tuple-element.14) | data formatting | bytes 131072
  62.5 1.7 %copy.105 = f32[1,1,8,2,32,32]{5,4,2,3,1,0:T(8,128)} copy(f32[1,1,8,2,32,32]{5,4,3,2,1,0:T(8,128)} %get-tuple-element.13) | data formatting | bytes 131072
  64.1 1.7 %copy.104 = f32[1,1,8,2,32,32]{5,4,2,3,1,0:T(8,128)} copy(f32[1,1,8,2,32,32]{5,4,3,2,1,0:T(8,128)} %get-tuple-element.12) | data formatting | bytes 131072
  69.5 6.6 %collective-permute-start.1 = (f32[32,8,128]{2,0,1:T(8,128)S(1)}, f32[32,8,128]{2,0,1:T(8,128)}, u32[]{:S(2)}, u32[]{:S(2)}) collective-permute-start(f32[32,8,128]{2,0,1:T(8,128)S(1)} %fusion.13), channel_id=1, source_target_pairs={{0,2},{1,3},{2,0},{3,1},{4,6},{5,7},{6,4},{7,5},{8,10},{9,11},{10,... | collective-permute-start | bytes 393224 | tf_op jit(solution)/shard_map/ppermute | solution.py:38
  76.1 1.4 %gather_fusion = bf16[64,16,256]{2,1,0:T(8,128)(2,1)} fusion(bf16[16,96,256]{2,0,1:T(8,128)(2,1)S(1)} %bitcast.132, s32[1024]{0:T(1024)S(1)} %pad_clamp_fusion), kind=kCustom, calls=%fused_computation | custom fusion | bytes 1048832 | tf_op jit(solution)/shard_map/jit(_take)/gather | solution.py:99
  77.5 5.9 %fusion = f32[64,16,256]{2,1,0:T(8,128)S(1)} fusion(bf16[64,2,256,256]{3,2,1,0:T(8,128)(2,1)} %param.11, bf16[64,16,256]{2,1,0:T(8,128)(2,1)} %gather_fusion, pred[64]{0:T(512)(128)(4,1)S(1)} %get-tuple-element.5), kind=kOutput, calls=%fused_computation.1 | convolution fusion | flops 134479872 | bytes 9961536 | tf_op jit(solution)/shard_map/lpq,slq->slp/dot_general | solution.py:103
  84.9 3.7 %collective-permute-start.2 = (f32[32,8,128]{2,0,1:T(8,128)S(1)}, f32[32,8,128]{2,0,1:T(8,128)S(1)}, u32[]{:S(2)}, u32[]{:S(2)}) collective-permute-start(f32[32,8,128]{2,0,1:T(8,128)S(1)} %fusion.12), channel_id=1, source_target_pairs={{0,4},{1,5},{2,6},{3,7},{4,0},{5,1},{6,2},{7,3},{8,12},{9,13},{10,... | collective-permute-start | bytes 393224 | tf_op jit(solution)/shard_map/ppermute | solution.py:38
  88.8 2.7 %collective-permute-done.2 = f32[32,8,128]{2,0,1:T(8,128)S(1)} collective-permute-done((f32[32,8,128]{2,0,1:T(8,128)S(1)}, f32[32,8,128]{2,0,1:T(8,128)S(1)}, u32[]{:S(2)}, u32[]{:S(2)}) %collective-permute-start.2) | collective-permute-done | bytes 131104 | tf_op jit(solution)/shard_map/ppermute | solution.py:38
  93.5 1.9 %collective-permute-start.4 = (f32[32,8,128]{2,0,1:T(8,128)S(1)}, f32[32,8,128]{2,0,1:T(8,128)S(1)}, u32[]{:S(2)}, u32[]{:S(2)}) collective-permute-start(f32[32,8,128]{2,0,1:T(8,128)S(1)} %fusion.10), channel_id=1, source_target_pairs={{0,16},{8,24},{16,0},{24,8},{32,48},{40,56},{48,32},{56,40},{64,80... | collective-permute-start | bytes 393224 | tf_op jit(solution)/shard_map/ppermute | solution.py:38
  95.7 3.5 %collective-permute-done.4 = f32[32,8,128]{2,0,1:T(8,128)S(1)} collective-permute-done((f32[32,8,128]{2,0,1:T(8,128)S(1)}, f32[32,8,128]{2,0,1:T(8,128)S(1)}, u32[]{:S(2)}, u32[]{:S(2)}) %collective-permute-start.4) | collective-permute-done | bytes 131104 | tf_op jit(solution)/shard_map/ppermute | solution.py:38
  99.5 1.6 %collective-permute-start.5 = (f32[32,8,128]{2,0,1:T(8,128)S(1)}, f32[32,8,128]{2,0,1:T(8,128)S(1)}, u32[]{:S(2)}, u32[]{:S(2)}) collective-permute-start(f32[32,8,128]{2,0,1:T(8,128)S(1)} %fusion.9), channel_id=1, source_target_pairs={{0,32},{8,40},{16,48},{24,56},{32,0},{40,8},{48,16},{56,24},{64,96... | collective-permute-start | bytes 393224 | tf_op jit(solution)/shard_map/ppermute | solution.py:38
  101.3 3.2 %collective-permute-done.5 = f32[32,8,128]{2,0,1:T(8,128)S(1)} collective-permute-done((f32[32,8,128]{2,0,1:T(8,128)S(1)}, f32[32,8,128]{2,0,1:T(8,128)S(1)}, u32[]{:S(2)}, u32[]{:S(2)}) %collective-permute-start.5) | collective-permute-done | bytes 131104 | tf_op jit(solution)/shard_map/ppermute | solution.py:38
  104.8 3.1 %collective-permute-start.6 = (f32[32,8,128]{2,0,1:T(8,128)S(1)}, f32[32,8,128]{2,0,1:T(8,128)S(1)}, u32[]{:S(2)}, u32[]{:S(2)}) collective-permute-start(f32[32,8,128]{2,0,1:T(8,128)S(1)} %fusion.8), channel_id=1, source_target_pairs={{0,64},{8,72},{16,80},{24,88},{32,96},{40,104},{48,112},{56,120},{... | collective-permute-start | bytes 393224 | tf_op jit(solution)/shard_map/ppermute | solution.py:38
  108.1 3.2 %collective-permute-done.6 = f32[32,8,128]{2,0,1:T(8,128)S(1)} collective-permute-done((f32[32,8,128]{2,0,1:T(8,128)S(1)}, f32[32,8,128]{2,0,1:T(8,128)S(1)}, u32[]{:S(2)}, u32[]{:S(2)}) %collective-permute-start.6) | collective-permute-done | bytes 131104 | tf_op jit(solution)/shard_map/ppermute | solution.py:38
  (68 shorter events, 18.2 us)
Async XLA Ops:
  0.0 111.8 %copy-start = (bf16[64,32,256]{2,1,0:T(8,128)(2,1)S(1)}, bf16[64,32,256]{2,1,0:T(8,128)(2,1)}, u32[]{:S(2)}) copy-start(bf16[64,32,256]{2,1,0:T(8,128)(2,1)} %param.13) | copy-start | bytes 3145732
  0.0 6.1 %copy-start.2 = (s32[16384]{0:T(1024)S(1)}, s32[16384]{0:T(1024)}, u32[]{:S(2)}) copy-start(s32[16384]{0:T(1024)} %idx_ref.1) | copy-start | bytes 196612
  25.1 3.3 %copy-start.1 = (f32[16384,16]{1,0:T(8,128)}, f32[16384,16]{1,0:T(8,128)S(1)}, u32[]{:S(2)}) copy-start(f32[16384,16]{1,0:T(8,128)S(1)} %shard_map.73) | copy-start | bytes 3145732
  28.4 2.0 %copy-start.4 = (bf16[16,16384]{0,1:T(8,128)(2,1)}, bf16[16,16384]{0,1:T(8,128)(2,1)S(1)}, u32[]{:S(2)}) copy-start(bf16[16,16384]{0,1:T(8,128)(2,1)S(1)} %convert_bitcast_fusion) | copy-start | bytes 1572868
  31.4 35.9 %collective-permute-start.8 = (bf16[16,4096]{1,0:T(8,128)(2,1)}, bf16[16,4096]{1,0:T(8,128)(2,1)S(1)}, u32[]{:S(2)}, u32[]{:S(2)}) collective-permute-start(bf16[16,4096]{1,0:T(8,128)(2,1)} %copy.73), channel_id=1, source_target_pairs={{1,0},{2,1},{3,2},{4,3},{5,4},{6,5},{7,6},{8,7},{9,8},{10,9},{11,1... | collective-permute-start | bytes 393224 | tf_op jit(solution)/shard_map/ppermute | solution.py:49
  33.6 11.0 %copy-start.13 = (bf16[64,32,256]{2,1,0:T(8,128)(2,1)S(1)}, bf16[64,32,256]{2,1,0:T(8,128)(2,1)}, u32[]{:S(2)}) copy-start(bf16[64,32,256]{2,1,0:T(8,128)(2,1)} %param.10) | copy-start | bytes 3145732
  33.6 33.7 %collective-permute-start.7 = (bf16[16,4096]{1,0:T(8,128)(2,1)}, bf16[16,4096]{1,0:T(8,128)(2,1)}, u32[]{:S(2)}, u32[]{:S(2)}) collective-permute-start(bf16[16,4096]{1,0:T(8,128)(2,1)} %copy.72), channel_id=1, source_target_pairs={{0,1},{1,2},{2,3},{3,4},{4,5},{5,6},{6,7},{7,8},{8,9},{9,10},{10,1... | collective-permute-start | bytes 393224 | tf_op jit(solution)/shard_map/ppermute | solution.py:48
  42.6 2.0 %copy-start.3 = (bf16[16384,16]{1,0:T(8,128)(2,1)}, bf16[16384,16]{1,0:T(8,128)(2,1)S(1)}, u32[]{:S(2)}) copy-start(bf16[16384,16]{1,0:T(8,128)(2,1)S(1)} %convert_element_type.16) | copy-start | bytes 1572868
  46.6 8.0 %copy-start.5 = (f32[1,7,8,2,32,32]{5,4,3,2,1,0:T(8,128)S(1)}, f32[1,7,8,2,32,32]{5,4,3,2,1,0:T(8,128)}, u32[]{:S(2)}) copy-start(f32[1,7,8,2,32,32]{5,4,3,2,1,0:T(8,128)} %param.12) | copy-start | bytes 1376260
  46.6 21.7 %collective-permute-start = (f32[32,8,128]{2,0,1:T(8,128)}, f32[32,8,128]{2,0,1:T(8,128)}, u32[]{:S(2)}, u32[]{:S(2)}) collective-permute-start(f32[32,8,128]{2,0,1:T(8,128)} %copy.62), channel_id=1, source_target_pairs={{0,1},{1,0},{2,3},{3,2},{4,5},{5,4},{6,7},{7,6},{8,9},{9,8},{10,11... | collective-permute-start | bytes 393224 | tf_op jit(solution)/shard_map/ppermute | solution.py:38
  54.6 2.6 %copy-start.15 = (s32[64]{0:T(128)S(1)}, s32[64]{0:T(128)}, u32[]{:S(2)}) copy-start(s32[64]{0:T(128)} %param.9) | copy-start | bytes 772
  60.7 7.6 %copy-start.12 = (f32[1,1,8,2,32,32]{5,4,2,3,1,0:T(8,128)S(1)}, f32[1,1,8,2,32,32]{5,4,2,3,1,0:T(8,128)}, u32[]{:S(2)}) copy-start(f32[1,1,8,2,32,32]{5,4,2,3,1,0:T(8,128)} %copy-done.11) | copy-start | bytes 196612
  60.7 7.6 %copy-start.14 = (f32[8,128,32]{1,2,0:T(8,128)S(1)}, f32[8,128,32]{1,2,0:T(8,128)}, u32[]{:S(2)}) copy-start(f32[8,128,32]{1,2,0:T(8,128)} %fusion.26) | copy-start | bytes 393220
  69.5 14.2 %collective-permute-start.1 = (f32[32,8,128]{2,0,1:T(8,128)S(1)}, f32[32,8,128]{2,0,1:T(8,128)}, u32[]{:S(2)}, u32[]{:S(2)}) collective-permute-start(f32[32,8,128]{2,0,1:T(8,128)S(1)} %fusion.13), channel_id=1, source_target_pairs={{0,2},{1,3},{2,0},{3,1},{4,6},{5,7},{6,4},{7,5},{8,10},{9,11},{10,... | collective-permute-start | bytes 393224 | tf_op jit(solution)/shard_map/ppermute | solution.py:38
  77.5 6.0 %copy-start.10 = (f32[1,1,8,2,32,32]{5,4,2,3,1,0:T(8,128)S(1)}, f32[1,1,8,2,32,32]{5,4,2,3,1,0:T(8,128)}, u32[]{:S(2)}) copy-start(f32[1,1,8,2,32,32]{5,4,2,3,1,0:T(8,128)} %copy.106) | copy-start | bytes 196612
  77.5 11.1 %copy-start.9 = (f32[1,1,8,2,32,32]{5,4,2,3,1,0:T(8,128)S(1)}, f32[1,1,8,2,32,32]{5,4,2,3,1,0:T(8,128)}, u32[]{:S(2)}) copy-start(f32[1,1,8,2,32,32]{5,4,2,3,1,0:T(8,128)} %copy.105) | copy-start | bytes 196612
  77.5 14.4 %copy-start.8 = (f32[1,1,8,2,32,32]{5,4,2,3,1,0:T(8,128)S(1)}, f32[1,1,8,2,32,32]{5,4,2,3,1,0:T(8,128)}, u32[]{:S(2)}) copy-start(f32[1,1,8,2,32,32]{5,4,2,3,1,0:T(8,128)} %copy.104) | copy-start | bytes 196612
  77.5 17.9 %copy-start.7 = (f32[1,1,8,2,32,32]{5,4,2,3,1,0:T(8,128)S(1)}, f32[1,1,8,2,32,32]{5,4,2,3,1,0:T(8,128)}, u32[]{:S(2)}) copy-start(f32[1,1,8,2,32,32]{5,4,2,3,1,0:T(8,128)} %copy.103) | copy-start | bytes 196612
  77.5 23.5 %copy-start.6 = (f32[1,1,8,2,32,32]{5,4,2,3,1,0:T(8,128)S(1)}, f32[1,1,8,2,32,32]{5,4,2,3,1,0:T(8,128)}, u32[]{:S(2)}) copy-start(f32[1,1,8,2,32,32]{5,4,2,3,1,0:T(8,128)} %copy.102) | copy-start | bytes 196612
  84.9 6.6 %collective-permute-start.2 = (f32[32,8,128]{2,0,1:T(8,128)S(1)}, f32[32,8,128]{2,0,1:T(8,128)S(1)}, u32[]{:S(2)}, u32[]{:S(2)}) collective-permute-start(f32[32,8,128]{2,0,1:T(8,128)S(1)} %fusion.12), channel_id=1, source_target_pairs={{0,4},{1,5},{2,6},{3,7},{4,0},{5,1},{6,2},{7,3},{8,12},{9,13},{10,... | collective-permute-start | bytes 393224 | tf_op jit(solution)/shard_map/ppermute | solution.py:38
  91.8 1.4 %collective-permute-start.3 = (f32[32,8,128]{2,0,1:T(8,128)S(1)}, f32[32,8,128]{2,0,1:T(8,128)S(1)}, u32[]{:S(2)}, u32[]{:S(2)}) collective-permute-start(f32[32,8,128]{2,0,1:T(8,128)S(1)} %fusion.11), channel_id=1, source_target_pairs={{0,8},{8,0},{16,24},{24,16},{32,40},{40,32},{48,56},{56,48},{64,72... | collective-permute-start | bytes 393224 | tf_op jit(solution)/shard_map/ppermute | solution.py:38
  93.5 5.7 %collective-permute-start.4 = (f32[32,8,128]{2,0,1:T(8,128)S(1)}, f32[32,8,128]{2,0,1:T(8,128)S(1)}, u32[]{:S(2)}, u32[]{:S(2)}) collective-permute-start(f32[32,8,128]{2,0,1:T(8,128)S(1)} %fusion.10), channel_id=1, source_target_pairs={{0,16},{8,24},{16,0},{24,8},{32,48},{40,56},{48,32},{56,40},{64,80... | collective-permute-start | bytes 393224 | tf_op jit(solution)/shard_map/ppermute | solution.py:38
  99.5 5.0 %collective-permute-start.5 = (f32[32,8,128]{2,0,1:T(8,128)S(1)}, f32[32,8,128]{2,0,1:T(8,128)S(1)}, u32[]{:S(2)}, u32[]{:S(2)}) collective-permute-start(f32[32,8,128]{2,0,1:T(8,128)S(1)} %fusion.9), channel_id=1, source_target_pairs={{0,32},{8,40},{16,48},{24,56},{32,0},{40,8},{48,16},{56,24},{64,96... | collective-permute-start | bytes 393224 | tf_op jit(solution)/shard_map/ppermute | solution.py:38
  104.8 6.6 %collective-permute-start.6 = (f32[32,8,128]{2,0,1:T(8,128)S(1)}, f32[32,8,128]{2,0,1:T(8,128)S(1)}, u32[]{:S(2)}, u32[]{:S(2)}) collective-permute-start(f32[32,8,128]{2,0,1:T(8,128)S(1)} %fusion.8), channel_id=1, source_target_pairs={{0,64},{8,72},{16,80},{24,88},{32,96},{40,104},{48,112},{56,120},{... | collective-permute-start | bytes 393224 | tf_op jit(solution)/shard_map/ppermute | solution.py:38
  (1 other events, 1.6 us)

commit v2 on v1

--- a/solution.py
+++ b/solution.py
@@ -69,6 +69,44 @@
     return first + second
 
 
+NODE_AXES = ("gx", "gy")
+
+
+def node_partner(x, mask):
+    count = lax.axis_size(NODE_AXES)
+    return lax.ppermute(x, NODE_AXES, [(i, i ^ mask) for i in range(count)])
+
+
+def chain(left, right):
+    return jnp.einsum(
+        "gab,gbc->gac", left, right, precision=lax.Precision.HIGHEST, preferred_element_type=jnp.float32
+    )
+
+
+def apply(matrix, values):
+    return jnp.einsum(
+        "gab,bgm->agm", matrix, values, precision=lax.Precision.HIGHEST, preferred_element_type=jnp.float32
+    )
+
+
+def two_levels(weights, first, coeffs):
+    near, far = 1 << first, 1 << (first + 1)
+    lower, upper = weights[first], weights[first + 1]
+    lower_far = node_partner(lower, far)
+    terms = (
+        (chain(upper[:, 0], lower[:, 0]), 0),
+        (chain(upper[:, 0], lower[:, 1]), near),
+        (chain(upper[:, 1], lower_far[:, 0]), far),
+        (chain(upper[:, 1], lower_far[:, 1]), near | far),
+    )
+    total = None
+    for matrix, mask in terms:
+        values = coeffs if mask == 0 else node_partner(coeffs, mask)
+        term = apply(matrix, values)
+        total = term if total is None else total + term
+    return total
+
+
 def local(points_rhs, morton_order, band_offsets, leaf_basis, band_blocks, translations, out_basis):
     rhs_count, point_count = points_rhs.shape
     leaf_count, rank_size, leaf_size = leaf_basis.shape
@@ -81,15 +119,13 @@
         "lrp,slp->rls", leaf_basis, leaves, preferred_element_type=jnp.float32
     ).reshape(rank_size, total_cols)
     weights = translations[0]
-    low_bits = lax.axis_size("gy").bit_length() - 1
-    high_bits = lax.axis_size("gx").bit_length() - 1
+    level_count = weights.shape[0]
     coeffs = coeffs.reshape(rank_size, group_total, group_width)
-    for level_bit in range(low_bits):
-        partner = from_partner(coeffs, "gy", level_bit)
-        coeffs = translate(weights[level_bit], coeffs, partner)
-    for level_bit in range(high_bits):
-        partner = from_partner(coeffs, "gx", level_bit)
-        coeffs = translate(weights[low_bits + level_bit], coeffs, partner)
+    for first in range(0, level_count - 1, 2):
+        coeffs = two_levels(weights, first, coeffs)
+    if level_count % 2:
+        partner = node_partner(coeffs, 1 << (level_count - 1))
+        coeffs = translate(weights[level_count - 1], coeffs, partner)
     coeffs = coeffs.reshape(rank_size, total_cols)
     coeff_bf = coeffs.astype(jnp.bfloat16).reshape(rank_size, leaf_count, rhs_count)
     far_term = jnp.einsum("lrp,rls->slp", out_basis, coeff_bf, preferred_element_type=jnp.float32)

time: 114 us -> 132 us (1.16)
  matrix products: 21.1 us -> 42 us
  waiting for transfers between devices: 13.7 us -> 9.27 us
  starting transfers between devices: 24.6 us -> 26.4 us
    dot_general x0 -> x24, matrix products: none -> 27 us  [the longest x12 16.3 us: chain(): jnp.einsum('gab,gbc->gac', left, right, precision=lax.Precision.HIGHEST,...]
    ppermute x7 -> x13, waiting for transfers between devices: 13.7 us -> 9.27 us  [node_partner(): return lax.ppermute(x, NODE_AXES, [(i, i ^ mask) for i in range(count)])]
    dot_general x7 -> x1, matrix products: 3.57 us -> 0.26 us  [translate(): jnp.einsum('gab,bgm->agm', level_weights[:, 1], other_coeffs, precision=l...]
    dot_general x7 -> x1, matrix products: 3.11 us -> 0.25 us  [translate(): jnp.einsum('gab,bgm->agm', level_weights[:, 0], own_coeffs, precision=lax...]
    unnamed x40 -> x70, local copies, waits for them, and re-layouts: 19.2 us -> 16.7 us
    ppermute x7 -> x13, starting transfers between devices: 18 us -> 20.5 us  [node_partner(): return lax.ppermute(x, NODE_AXES, [(i, i ^ mask) for i in range(count)])]
  transfers between devices with their start and end apart: 9 -> 15, of which waited for: 5 -> 2; matrix products, arithmetic and copies ran while one was open for 32% -> 43% of each run, Pallas kernels for 0% -> 0%
where the time goes in v2:
time: 132 us; the launch traced here: 131 us
  matrix products  42 us (32%)
  local copies, waits for them, and re-layouts  30.1 us (23%)
  starting transfers between devices  26.4 us (20%)
  Pallas kernels  19 us (14%)
  waiting for transfers between devices  9.27 us (7%)
  other arithmetic  4.21 us (3%)
    ppermute x13, starting transfers between devices, node_partner(): return lax.ppermute(x, NODE_AXES, [(i, i ^ mask) for i in range(count)])  20.5 us
    pallas_call x1, Pallas kernels, row_gather(): pl.pallas_call(gather_kernel, out_shape=jax.ShapeDtypeStruct((count, widt...  19 us
    unnamed x70, local copies, waits for them, and re-layouts  16.7 us
    dot_general x12, matrix products, chain(): jnp.einsum('gab,gbc->gac', left, right, precision=lax.Precision.HIGHEST,...  16.3 us
    dot_general x12, matrix products, apply(): jnp.einsum('gab,bgm->agm', matrix, values, precision=lax.Precision.HIGHES...  10.7 us
    ppermute x13, waiting for transfers between devices, node_partner(): return lax.ppermute(x, NODE_AXES, [(i, i ^ mask) for i in range(count)])  9.27 us
    dot_general x1, matrix products, local(): jnp.einsum('lpq,slq->slp', band_blocks[:, 0], leaves, preferred_element_t...  7.02 us
    dot_general x1, matrix products, local(): jnp.einsum('lpq,slq->slp', band_blocks[:, 1], picked, preferred_element_t...  5.94 us
  transfers between devices with their start and end apart: 15, of which 2 were waited for; matrix products, arithmetic and copies ran while one was open for 43% of the time, Pallas kernels for 0%

profile of v2, /device:TPU:0, one launch (start us, length us, event | category | flops | bytes accessed | tf_op | source)
XLA Modules:
  0.0 131.5 jit_solution(8571520755161145655)
XLA Ops:
  0.0 6.1 %copy.52 = f32[16,16384]{0,1:T(8,128)} copy(f32[16,16384]{1,0:T(8,128)} %param.7) | data formatting | bytes 2097152 | tf_op args[0]
  6.1 19.0 %shard_map.73 = f32[16384,16]{1,0:T(8,128)S(1)} custom-call(s32[16384]{0:T(1024)S(1)} %copy-done.2, f32[16384,16]{1,0:T(8,128)} %bitcast.158), custom_call_target="tpu_custom_call" | custom-call | bytes 2097152 | tf_op jit(solution)/shard_map/pallas_call | solution.py:27
  25.6 2.8 %copy-done.1 = f32[16384,16]{1,0:T(8,128)} copy-done((f32[16384,16]{1,0:T(8,128)}, f32[16384,16]{1,0:T(8,128)S(1)}, u32[]{:S(2)}) %copy-start.1) | copy-done | bytes 1048600
  28.4 2.1 %copy-done.3 = bf16[16384,16]{1,0:T(8,128)(2,1)} copy-done((bf16[16384,16]{1,0:T(8,128)(2,1)}, bf16[16384,16]{1,0:T(8,128)(2,1)S(1)}, u32[]{:S(2)}) %copy-start.3) | copy-done | bytes 524312
  32.6 3.1 %collective-permute-start.3 = (f32[32,8,128]{2,0,1:T(8,128)}, f32[32,8,128]{2,0,1:T(8,128)}, u32[]{:S(2)}, u32[]{:S(2)}) collective-permute-start(f32[32,8,128]{2,0,1:T(8,128)} %copy.57), channel_id=1, source_target_pairs={{0,3},{1,2},{2,1},{3,0},{4,7},{5,6},{6,5},{7,4},{8,11},{9,10},{10,... | collective-permute-start | bytes 393224 | tf_op jit(solution)/shard_map/ppermute | solution.py:77
  39.1 2.1 %collective-permute-start.2 = (f32[8,2,32,32]{3,2,0,1:T(8,128)}, f32[8,2,32,32]{3,2,0,1:T(8,128)}, u32[]{:S(2)}, u32[]{:S(2)}) collective-permute-start(f32[8,2,32,32]{3,2,0,1:T(8,128)} %bitcast.154), channel_id=1, source_target_pairs={{0,2},{1,3},{2,0},{3,1},{4,6},{5,7},{6,4},{7,5},{8,10},{9,11},{10,... | collective-permute-start | bytes 196616 | tf_op jit(solution)/shard_map/ppermute | solution.py:77
  41.9 3.7 %convert_bitcast_fusion = bf16[16,16384]{0,1:T(8,128)(2,1)S(1)} fusion(f32[16384,16]{1,0:T(8,128)} %copy-done.1), kind=kLoop, calls=%fused_computation.84 | loop fusion | flops 262144 | bytes 1572864 | tf_op jit(solution)/shard_map/convert_element_type | solution.py:116
  45.6 2.0 %copy-done.4 = bf16[16,16384]{0,1:T(8,128)(2,1)} copy-done((bf16[16,16384]{0,1:T(8,128)(2,1)}, bf16[16,16384]{0,1:T(8,128)(2,1)S(1)}, u32[]{:S(2)}) %copy-start.4) | copy-done | bytes 524312
  48.6 4.5 %copy.70 = bf16[16,16384]{1,0:T(8,128)(2,1)} copy(bf16[16,16384]{0,1:T(8,128)(2,1)} %copy-done.4) | data formatting | bytes 1048576 | tf_op jit(solution)/shard_map/convert_element_type | solution.py:116
  54.2 1.9 %fusion.32 = f32[8,32,32]{2,1,0:T(8,128)} fusion(f32[8,2,32,32]{3,2,0,1:T(8,128)} %bitcast.154, f32[8,2,32,32]{3,2,0,1:T(8,128)S(1)} %bitcast.170), kind=kOutput, calls=%fused_computation.69 | convolution fusion | flops 3145728 | bytes 294912 | tf_op jit(solution)/shard_map/gab,gbc->gac/dot_general | solution.py:81
  57.9 1.9 %fusion.28 = f32[8,32,32]{2,1,0:T(8,128)} fusion(f32[8,2,32,32]{3,2,0,1:T(8,128)} %bitcast.152, f32[8,2,32,32]{3,2,0,1:T(8,128)S(1)} %bitcast.166), kind=kOutput, calls=%fused_computation.59 | convolution fusion | flops 3145728 | bytes 294912 | tf_op jit(solution)/shard_map/gab,gbc->gac/dot_general | solution.py:81
  59.8 1.8 %fusion.27 = f32[8,32,32]{2,1,0:T(8,128)} fusion(f32[8,2,32,32]{3,2,0,1:T(8,128)} %bitcast.152, f32[8,2,32,32]{3,2,0,1:T(8,128)S(1)} %bitcast.167), kind=kOutput, calls=%fused_computation.57 | convolution fusion | flops 3145728 | bytes 294912 | tf_op jit(solution)/shard_map/gab,gbc->gac/dot_general | solution.py:81
  63.3 2.2 %copy.69 = bf16[16,4096]{1,0:T(8,128)(2,1)} copy(bf16[16,4096]{0,1:T(8,128)(2,1)} %get-tuple-element.8) | data formatting | bytes 262144 | tf_op jit(solution)/shard_map/slice | solution.py:47
  66.6 7.0 %fusion.2 = f32[64,16,256]{2,1,0:T(8,128)S(1)} fusion(bf16[16,64,256]{0,2,1:T(8,128)(2,1)} %bitcast.157, bf16[64,2,256,256]{3,2,1,0:T(8,128)(2,1)} %param.11), kind=kOutput, calls=%fused_computation.3 | convolution fusion | flops 134217728 | bytes 13631488 | tf_op jit(solution)/shard_map/lpq,slq->slp/dot_general | solution.py:136
  80.5 1.8 %fusion.25 = f32[8,32,32]{2,1,0:T(8,128)} fusion(f32[8,2,32,32]{3,2,0,1:T(8,128)} %collective-permute-done.6, f32[8,2,32,32]{3,2,0,1:T(8,128)S(1)} %bitcast.168), kind=kOutput, calls=%fused_computation.52 | convolution fusion | flops 3145728 | bytes 294912 | tf_op jit(solution)/shard_map/gab,gbc->gac/dot_general | solution.py:81
  82.3 1.8 %fusion.26 = f32[8,32,32]{2,1,0:T(8,128)} fusion(f32[8,2,32,32]{3,2,0,1:T(8,128)} %collective-permute-done.6, f32[8,2,32,32]{3,2,0,1:T(8,128)S(1)} %bitcast.169), kind=kOutput, calls=%fused_computation.54 | convolution fusion | flops 3145728 | bytes 294912 | tf_op jit(solution)/shard_map/gab,gbc->gac/dot_general | solution.py:81
  84.2 4.5 %collective-permute-start.13 = (bf16[16,4096]{1,0:T(8,128)(2,1)S(1)}, bf16[16,4096]{1,0:T(8,128)(2,1)S(1)}, u32[]{:S(2)}, u32[]{:S(2)}) collective-permute-start(bf16[16,4096]{1,0:T(8,128)(2,1)S(1)} %copy-done.28), channel_id=1, source_target_pairs={{0,1},{1,2},{2,3},{3,4},{4,5},{5,6},{6,7},{7,8},{8,9},{9,10},{10,1... | collective-permute-start | bytes 393224 | tf_op jit(solution)/shard_map/ppermute | solution.py:48
  94.7 3.3 %collective-permute-start.7 = (f32[32,8,128]{2,0,1:T(8,128)}, f32[32,8,128]{2,0,1:T(8,128)}, u32[]{:S(2)}, u32[]{:S(2)}) collective-permute-start(f32[32,8,128]{2,0,1:T(8,128)} %fusion.13), channel_id=1, source_target_pairs={{0,12},{1,13},{2,14},{3,15},{4,8},{5,9},{6,10},{7,11},{8,4},{9,5},... | collective-permute-start | bytes 393224 | tf_op jit(solution)/shard_map/ppermute | solution.py:77
  98.0 2.3 %collective-permute-start.4 = (f32[32,8,128]{2,0,1:T(8,128)}, f32[32,8,128]{2,0,1:T(8,128)}, u32[]{:S(2)}, u32[]{:S(2)}) collective-permute-start(f32[32,8,128]{2,0,1:T(8,128)} %fusion.13), channel_id=1, source_target_pairs={{0,4},{1,5},{2,6},{3,7},{4,0},{5,1},{6,2},{7,3},{8,12},{9,13},{10,... | collective-permute-start | bytes 393224 | tf_op jit(solution)/shard_map/ppermute | solution.py:77
  101.9 5.9 %fusion = f32[64,16,256]{2,1,0:T(8,128)S(1)} fusion(bf16[64,2,256,256]{3,2,1,0:T(8,128)(2,1)} %param.11, bf16[64,16,256]{2,1,0:T(8,128)(2,1)} %gather_fusion, pred[64]{0:T(512)(128)(4,1)S(1)} %get-tuple-element.5), kind=kOutput, calls=%fused_computation.1 | convolution fusion | flops 134479872 | bytes 9961536 | tf_op jit(solution)/shard_map/lpq,slq->slp/dot_general | solution.py:139
  113.6 2.0 %collective-permute-start.8 = (f32[32,8,128]{2,0,1:T(8,128)S(1)}, f32[32,8,128]{2,0,1:T(8,128)S(1)}, u32[]{:S(2)}, u32[]{:S(2)}) collective-permute-start(f32[32,8,128]{2,0,1:T(8,128)S(1)} %fusion.11), channel_id=1, source_target_pairs={{0,16},{1,17},{2,18},{3,19},{4,20},{5,21},{6,22},{7,23},{8,24},{9,... | collective-permute-start | bytes 393224 | tf_op jit(solution)/shard_map/ppermute | solution.py:77
  116.4 5.7 %collective-permute-done.8 = f32[32,8,128]{2,0,1:T(8,128)S(1)} collective-permute-done((f32[32,8,128]{2,0,1:T(8,128)S(1)}, f32[32,8,128]{2,0,1:T(8,128)S(1)}, u32[]{:S(2)}, u32[]{:S(2)}) %collective-permute-start.8) | collective-permute-done | bytes 131104 | tf_op jit(solution)/shard_map/ppermute | solution.py:77
  122.9 3.0 %collective-permute-start.12 = (f32[32,8,128]{2,0,1:T(8,128)S(1)}, f32[32,8,128]{2,0,1:T(8,128)S(1)}, u32[]{:S(2)}, u32[]{:S(2)}) collective-permute-start(f32[32,8,128]{2,0,1:T(8,128)S(1)} %fusion.9), channel_id=1, source_target_pairs={{0,64},{1,65},{2,66},{3,67},{4,68},{5,69},{6,70},{7,71},{8,72},{9,... | collective-permute-start | bytes 393224 | tf_op jit(solution)/shard_map/ppermute | solution.py:77
  126.1 3.6 %collective-permute-done.12 = f32[32,8,128]{2,0,1:T(8,128)S(1)} collective-permute-done((f32[32,8,128]{2,0,1:T(8,128)S(1)}, f32[32,8,128]{2,0,1:T(8,128)S(1)}, u32[]{:S(2)}, u32[]{:S(2)}) %collective-permute-start.12) | collective-permute-done | bytes 131104 | tf_op jit(solution)/shard_map/ppermute | solution.py:77
  (122 shorter events, 36.8 us)
Async XLA Ops:
  0.0 130.1 %copy-start = (bf16[64,32,256]{2,1,0:T(8,128)(2,1)S(1)}, bf16[64,32,256]{2,1,0:T(8,128)(2,1)}, u32[]{:S(2)}) copy-start(bf16[64,32,256]{2,1,0:T(8,128)(2,1)} %param.13) | copy-start | bytes 3145732
  32.6 59.1 %collective-permute-start.3 = (f32[32,8,128]{2,0,1:T(8,128)}, f32[32,8,128]{2,0,1:T(8,128)}, u32[]{:S(2)}, u32[]{:S(2)}) collective-permute-start(f32[32,8,128]{2,0,1:T(8,128)} %copy.57), channel_id=1, source_target_pairs={{0,3},{1,2},{2,1},{3,0},{4,7},{5,6},{6,5},{7,4},{8,11},{9,10},{10,... | collective-permute-start | bytes 393224 | tf_op jit(solution)/shard_map/ppermute | solution.py:77
  35.7 54.9 %collective-permute-start = (f32[32,8,128]{2,0,1:T(8,128)}, f32[32,8,128]{2,0,1:T(8,128)}, u32[]{:S(2)}, u32[]{:S(2)}) collective-permute-start(f32[32,8,128]{2,0,1:T(8,128)} %copy.57), channel_id=1, source_target_pairs={{0,1},{1,0},{2,3},{3,2},{4,5},{5,4},{6,7},{7,6},{8,9},{9,8},{10,11... | collective-permute-start | bytes 393224 | tf_op jit(solution)/shard_map/ppermute | solution.py:77
  35.8 57.1 %collective-permute-start.1 = (f32[32,8,128]{2,0,1:T(8,128)}, f32[32,8,128]{2,0,1:T(8,128)}, u32[]{:S(2)}, u32[]{:S(2)}) collective-permute-start(f32[32,8,128]{2,0,1:T(8,128)} %copy.57), channel_id=1, source_target_pairs={{0,2},{1,3},{2,0},{3,1},{4,6},{5,7},{6,4},{7,5},{8,10},{9,11},{10,... | collective-permute-start | bytes 393224 | tf_op jit(solution)/shard_map/ppermute | solution.py:77
  39.1 36.2 %collective-permute-start.2 = (f32[8,2,32,32]{3,2,0,1:T(8,128)}, f32[8,2,32,32]{3,2,0,1:T(8,128)}, u32[]{:S(2)}, u32[]{:S(2)}) collective-permute-start(f32[8,2,32,32]{3,2,0,1:T(8,128)} %bitcast.154), channel_id=1, source_target_pairs={{0,2},{1,3},{2,0},{3,1},{4,6},{5,7},{6,4},{7,5},{8,10},{9,11},{10,... | collective-permute-start | bytes 196616 | tf_op jit(solution)/shard_map/ppermute | solution.py:77
  41.9 37.3 %collective-permute-start.6 = (f32[8,2,32,32]{3,2,0,1:T(8,128)}, f32[8,2,32,32]{3,2,0,1:T(8,128)}, u32[]{:S(2)}, u32[]{:S(2)}) collective-permute-start(f32[8,2,32,32]{3,2,0,1:T(8,128)} %bitcast.152), channel_id=1, source_target_pairs={{0,8},{1,9},{2,10},{3,11},{4,12},{5,13},{6,14},{7,15},{8,0},{9,1},... | collective-permute-start | bytes 196616 | tf_op jit(solution)/shard_map/ppermute | solution.py:77
  66.5 14.0 %copy-start.6 = (f32[1,1,8,2,32,32]{5,4,2,3,1,0:T(8,128)S(1)}, f32[1,1,8,2,32,32]{5,4,2,3,1,0:T(8,128)}, u32[]{:S(2)}) copy-start(f32[1,1,8,2,32,32]{5,4,2,3,1,0:T(8,128)} %copy-done.5) | copy-start | bytes 196612
  66.5 17.6 %copy-start.28 = (bf16[16,4096]{1,0:T(8,128)(2,1)S(1)}, bf16[16,4096]{1,0:T(8,128)(2,1)}, u32[]{:S(2)}) copy-start(bf16[16,4096]{1,0:T(8,128)(2,1)} %copy.68) | copy-start | bytes 393220
  66.6 24.0 %copy-start.26 = (f32[8,32,32]{2,1,0:T(8,128)S(1)}, f32[8,32,32]{2,1,0:T(8,128)}, u32[]{:S(2)}) copy-start(f32[8,32,32]{2,1,0:T(8,128)} %fusion.31) | copy-start | bytes 98308
  73.6 26.7 %copy-start.9 = (bf16[16,16384]{1,0:T(8,128)(2,1)S(1)}, bf16[16,16384]{1,0:T(8,128)(2,1)}, u32[]{:S(2)}) copy-start(bf16[16,16384]{1,0:T(8,128)(2,1)} %copy.70) | copy-start | bytes 1572868
  75.3 8.9 %collective-permute-start.10 = (f32[8,2,32,32]{3,2,0,1:T(8,128)S(1)}, f32[8,2,32,32]{3,2,0,1:T(8,128)S(1)}, u32[]{:S(2)}, u32[]{:S(2)}) collective-permute-start(f32[8,2,32,32]{3,2,0,1:T(8,128)S(1)} %bitcast.180), channel_id=1, source_target_pairs={{0,32},{1,33},{2,34},{3,35},{4,36},{5,37},{6,38},{7,39},{8,40},{9,... | collective-permute-start | bytes 196616 | tf_op jit(solution)/shard_map/ppermute | solution.py:77
  79.2 21.1 %collective-permute-start.14 = (bf16[16,4096]{1,0:T(8,128)(2,1)S(1)}, bf16[16,4096]{1,0:T(8,128)(2,1)S(1)}, u32[]{:S(2)}, u32[]{:S(2)}) collective-permute-start(bf16[16,4096]{1,0:T(8,128)(2,1)S(1)} %copy-done.29), channel_id=1, source_target_pairs={{1,0},{2,1},{3,2},{4,3},{5,4},{6,5},{7,6},{8,7},{9,8},{10,9},{11,1... | collective-permute-start | bytes 393224 | tf_op jit(solution)/shard_map/ppermute | solution.py:49
  84.2 16.1 %collective-permute-start.13 = (bf16[16,4096]{1,0:T(8,128)(2,1)S(1)}, bf16[16,4096]{1,0:T(8,128)(2,1)S(1)}, u32[]{:S(2)}, u32[]{:S(2)}) collective-permute-start(bf16[16,4096]{1,0:T(8,128)(2,1)S(1)} %copy-done.28), channel_id=1, source_target_pairs={{0,1},{1,2},{2,3},{3,4},{4,5},{5,6},{6,7},{7,8},{8,9},{9,10},{10,1... | collective-permute-start | bytes 393224 | tf_op jit(solution)/shard_map/ppermute | solution.py:48
  94.7 15.5 %collective-permute-start.7 = (f32[32,8,128]{2,0,1:T(8,128)}, f32[32,8,128]{2,0,1:T(8,128)}, u32[]{:S(2)}, u32[]{:S(2)}) collective-permute-start(f32[32,8,128]{2,0,1:T(8,128)} %fusion.13), channel_id=1, source_target_pairs={{0,12},{1,13},{2,14},{3,15},{4,8},{5,9},{6,10},{7,11},{8,4},{9,5},... | collective-permute-start | bytes 393224 | tf_op jit(solution)/shard_map/ppermute | solution.py:77
  98.0 11.0 %collective-permute-start.4 = (f32[32,8,128]{2,0,1:T(8,128)}, f32[32,8,128]{2,0,1:T(8,128)}, u32[]{:S(2)}, u32[]{:S(2)}) collective-permute-start(f32[32,8,128]{2,0,1:T(8,128)} %fusion.13), channel_id=1, source_target_pairs={{0,4},{1,5},{2,6},{3,7},{4,0},{5,1},{6,2},{7,3},{8,12},{9,13},{10,... | collective-permute-start | bytes 393224 | tf_op jit(solution)/shard_map/ppermute | solution.py:77
  100.3 11.1 %collective-permute-start.5 = (f32[32,8,128]{2,0,1:T(8,128)}, f32[32,8,128]{2,0,1:T(8,128)}, u32[]{:S(2)}, u32[]{:S(2)}) collective-permute-start(f32[32,8,128]{2,0,1:T(8,128)} %fusion.13), channel_id=1, source_target_pairs={{0,8},{1,9},{2,10},{3,11},{4,12},{5,13},{6,14},{7,15},{8,0},{9,1},... | collective-permute-start | bytes 393224 | tf_op jit(solution)/shard_map/ppermute | solution.py:77
  101.8 20.2 %copy-start.24 = (f32[8,32,32]{2,1,0:T(8,128)S(1)}, f32[8,32,32]{2,1,0:T(8,128)}, u32[]{:S(2)}) copy-start(f32[8,32,32]{2,1,0:T(8,128)} %fusion.23) | copy-start | bytes 98308
  101.9 20.5 %copy-start.21 = (f32[8,32,32]{2,1,0:T(8,128)S(1)}, f32[8,32,32]{2,1,0:T(8,128)}, u32[]{:S(2)}) copy-start(f32[8,32,32]{2,1,0:T(8,128)} %fusion.21) | copy-start | bytes 98308
  101.9 20.7 %copy-start.20 = (f32[8,32,32]{2,1,0:T(8,128)S(1)}, f32[8,32,32]{2,1,0:T(8,128)}, u32[]{:S(2)}) copy-start(f32[8,32,32]{2,1,0:T(8,128)} %fusion.22) | copy-start | bytes 98308
  101.9 24.0 %copy-start.15 = (f32[1,1,8,2,32,32]{5,4,2,3,1,0:T(8,128)S(1)}, f32[1,1,8,2,32,32]{5,4,2,3,1,0:T(8,128)}, u32[]{:S(2)}) copy-start(f32[1,1,8,2,32,32]{5,4,2,3,1,0:T(8,128)} %copy.97) | copy-start | bytes 196612
  112.5 9.8 %collective-permute-start.11 = (f32[32,8,128]{2,0,1:T(8,128)S(1)}, f32[32,8,128]{2,0,1:T(8,128)S(1)}, u32[]{:S(2)}, u32[]{:S(2)}) collective-permute-start(f32[32,8,128]{2,0,1:T(8,128)S(1)} %fusion.11), channel_id=1, source_target_pairs={{0,48},{1,49},{2,50},{3,51},{4,52},{5,53},{6,54},{7,55},{8,56},{9,... | collective-permute-start | bytes 393224 | tf_op jit(solution)/shard_map/ppermute | solution.py:77
  113.6 8.4 %collective-permute-start.8 = (f32[32,8,128]{2,0,1:T(8,128)S(1)}, f32[32,8,128]{2,0,1:T(8,128)S(1)}, u32[]{:S(2)}, u32[]{:S(2)}) collective-permute-start(f32[32,8,128]{2,0,1:T(8,128)S(1)} %fusion.11), channel_id=1, source_target_pairs={{0,16},{1,17},{2,18},{3,19},{4,20},{5,21},{6,22},{7,23},{8,24},{9,... | collective-permute-start | bytes 393224 | tf_op jit(solution)/shard_map/ppermute | solution.py:77
  115.6 7.0 %collective-permute-start.9 = (f32[32,8,128]{2,0,1:T(8,128)S(1)}, f32[32,8,128]{2,0,1:T(8,128)S(1)}, u32[]{:S(2)}, u32[]{:S(2)}) collective-permute-start(f32[32,8,128]{2,0,1:T(8,128)S(1)} %fusion.11), channel_id=1, source_target_pairs={{0,32},{1,33},{2,34},{3,35},{4,36},{5,37},{6,38},{7,39},{8,40},{9,... | collective-permute-start | bytes 393224 | tf_op jit(solution)/shard_map/ppermute | solution.py:77
  122.9 6.8 %collective-permute-start.12 = (f32[32,8,128]{2,0,1:T(8,128)S(1)}, f32[32,8,128]{2,0,1:T(8,128)S(1)}, u32[]{:S(2)}, u32[]{:S(2)}) collective-permute-start(f32[32,8,128]{2,0,1:T(8,128)S(1)} %fusion.9), channel_id=1, source_target_pairs={{0,64},{1,65},{2,66},{3,67},{4,68},{5,69},{6,70},{7,71},{8,72},{9,... | collective-permute-start | bytes 393224 | tf_op jit(solution)/shard_map/ppermute | solution.py:77
  (22 other events, 163.5 us)

commit v3 on v1

--- a/solution.py
+++ b/solution.py
@@ -69,6 +69,12 @@
     return first + second
 
 
+def near_piece(own_blocks, own_leaves, other_blocks, other_leaves):
+    own = jnp.einsum("lpq,slq->slp", own_blocks, own_leaves, preferred_element_type=jnp.float32)
+    other = jnp.einsum("lpq,slq->slp", other_blocks, other_leaves, preferred_element_type=jnp.float32)
+    return own + other
+
+
 def local(points_rhs, morton_order, band_offsets, leaf_basis, band_blocks, translations, out_basis):
     rhs_count, point_count = points_rhs.shape
     leaf_count, rank_size, leaf_size = leaf_basis.shape
@@ -77,33 +83,37 @@
     group_width = total_cols // group_total
     ordered = row_gather(points_rhs.T, morton_order).T.astype(jnp.bfloat16)
     leaves = ordered.reshape(rhs_count, leaf_count, leaf_size)
+    padded = extended(ordered, ((("gx", "gy"), 1),), HW * leaf_size)
     coeffs = jnp.einsum(
         "lrp,slp->rls", leaf_basis, leaves, preferred_element_type=jnp.float32
     ).reshape(rank_size, total_cols)
     weights = translations[0]
     low_bits = lax.axis_size("gy").bit_length() - 1
     high_bits = lax.axis_size("gx").bit_length() - 1
+    levels = [("gy", bit, bit) for bit in range(low_bits)]
+    levels += [("gx", bit, low_bits + bit) for bit in range(high_bits)]
+    pieces = len(levels)
+    bounds = [leaf_count * k // pieces for k in range(pieces + 1)]
+    blocks_all = padded.reshape(rhs_count, leaf_count + 2 * HW, leaf_size)
+    block_index = jnp.arange(leaf_count, dtype=jnp.int32) + HW + band_offsets
     coeffs = coeffs.reshape(rank_size, group_total, group_width)
-    for level_bit in range(low_bits):
-        partner = from_partner(coeffs, "gy", level_bit)
-        coeffs = translate(weights[level_bit], coeffs, partner)
-    for level_bit in range(high_bits):
-        partner = from_partner(coeffs, "gx", level_bit)
-        coeffs = translate(weights[low_bits + level_bit], coeffs, partner)
+    near_parts = []
+    for piece, (axis, bit, level) in enumerate(levels):
+        low, high = bounds[piece], bounds[piece + 1]
+        coeffs, piece_leaves, piece_index = lax.optimization_barrier(
+            (coeffs, leaves[:, low:high], block_index[low:high])
+        )
+        partner = from_partner(coeffs, axis, bit)
+        picked = jnp.take(blocks_all, piece_index, axis=1)
+        near_parts.append(
+            near_piece(band_blocks[low:high, 0], piece_leaves, band_blocks[low:high, 1], picked)
+        )
+        coeffs = translate(weights[level], coeffs, partner)
     coeffs = coeffs.reshape(rank_size, total_cols)
     coeff_bf = coeffs.astype(jnp.bfloat16).reshape(rank_size, leaf_count, rhs_count)
     far_term = jnp.einsum("lrp,rls->slp", out_basis, coeff_bf, preferred_element_type=jnp.float32)
-    padded = extended(ordered, ((("gx", "gy"), 1),), HW * leaf_size)
-    blocks_all = padded.reshape(rhs_count, leaf_count + 2 * HW, leaf_size)
-    block_index = jnp.arange(leaf_count, dtype=jnp.int32) + HW + band_offsets
-    picked = jnp.take(blocks_all, block_index, axis=1)
-    own_term = jnp.einsum(
-        "lpq,slq->slp", band_blocks[:, 0], leaves, preferred_element_type=jnp.float32
-    )
-    partner_term = jnp.einsum(
-        "lpq,slq->slp", band_blocks[:, 1], picked, preferred_element_type=jnp.float32
-    )
-    return (far_term + own_term + partner_term).reshape(rhs_count, point_count)
+    near_term = jnp.concatenate(near_parts, axis=1)
+    return (far_term + near_term).reshape(rhs_count, point_count)
 
 
 def solution(mesh):

time: 114 us -> 144 us (1.26)
  local copies, waits for them, and re-layouts: 29.3 us -> 49.7 us
  matrix products: 21.1 us -> 37.7 us
  waiting for transfers between devices: 13.7 us -> 3.83 us
  other arithmetic: 5.11 us -> 8.15 us
    dot_general x2 -> x14, matrix products: 12.9 us -> 24.6 us  [the longest x7 12.5 us: near_piece(): jnp.einsum('lpq,slq->slp', own_blocks, own_leaves, preferred_element_type...]
    optimization_barrier x0 -> x8, local copies, waits for them, and re-layouts: none -> 9.92 us  [local(): lax.optimization_barrier((coeffs, leaves[:, low:high], block_index[low:hi...]
    ppermute x7, waiting for transfers between devices: 13.7 us -> 3.83 us  [from_partner(): lax.ppermute(x, axis, [(i, i ^ 1 << distance) for i in range(lax.axis_siz...]
    slice x1 -> x5, local copies, waits for them, and re-layouts: 1 us -> 6.32 us  [the longest x1 2.6 us: local(): coeffs = translate(weights[level], coeffs, partner)]
    gather x1 -> x7, local copies, waits for them, and re-layouts: 1.39 us -> 3.98 us  [local(): picked = jnp.take(blocks_all, piece_index, axis=1)]
    dot_general x7, matrix products: 3.11 us -> 5.66 us  [translate(): jnp.einsum('gab,bgm->agm', level_weights[:, 0], own_coeffs, precision=lax...]
    unnamed x40 -> x50, local copies, waits for them, and re-layouts: 19.2 us -> 21.6 us
    dot_general x7, matrix products: 3.57 us -> 5.93 us  [translate(): jnp.einsum('gab,bgm->agm', level_weights[:, 1], other_coeffs, precision=l...]
  transfers between devices with their start and end apart: 9 -> 9, of which waited for: 5 -> 1; matrix products, arithmetic and copies ran while one was open for 32% -> 49% of each run, Pallas kernels for 0% -> 0%
where the time goes in v3:
time: 144 us; the launch traced here: 143 us
  local copies, waits for them, and re-layouts  49.7 us (35%)
  matrix products  37.7 us (26%)
  starting transfers between devices  23.7 us (16%)
  Pallas kernels  19 us (13%)
  other arithmetic  8.15 us (6%)
  waiting for transfers between devices  3.83 us (3%)
    unnamed x50, local copies, waits for them, and re-layouts  21.6 us
    pallas_call x1, Pallas kernels, row_gather(): pl.pallas_call(gather_kernel, out_shape=jax.ShapeDtypeStruct((count, widt...  19 us
    ppermute x7, starting transfers between devices, from_partner(): lax.ppermute(x, axis, [(i, i ^ 1 << distance) for i in range(lax.axis_siz...  17.2 us
    dot_general x7, matrix products, near_piece(): jnp.einsum('lpq,slq->slp', own_blocks, own_leaves, preferred_element_type...  12.5 us
    dot_general x7, matrix products, near_piece(): jnp.einsum('lpq,slq->slp', other_blocks, other_leaves, preferred_element_...  12.1 us
    optimization_barrier x8, local copies, waits for them, and re-layouts, local(): lax.optimization_barrier((coeffs, leaves[:, low:high], block_index[low:hi...  9.92 us
    dot_general x7, matrix products, translate(): jnp.einsum('gab,bgm->agm', level_weights[:, 1], other_coeffs, precision=l...  5.93 us
    dot_general x7, matrix products, translate(): jnp.einsum('gab,bgm->agm', level_weights[:, 0], own_coeffs, precision=lax...  5.66 us
  transfers between devices with their start and end apart: 9, of which 1 were waited for; matrix products, arithmetic and copies ran while one was open for 49% of the time, Pallas kernels for 0%

profile of v3, /device:TPU:0, one launch (start us, length us, event | category | flops | bytes accessed | tf_op | source)
XLA Modules:
  0.0 142.5 jit_solution(7726489761524742223)
XLA Ops:
  0.0 6.1 %copy.118 = f32[16,16384]{0,1:T(8,128)} copy(f32[16,16384]{1,0:T(8,128)} %param.9) | data formatting | bytes 2097152 | tf_op args[0]
  6.1 19.0 %shard_map.73 = f32[16384,16]{1,0:T(8,128)S(1)} custom-call(s32[16384]{0:T(1024)S(1)} %copy-done.2, f32[16384,16]{1,0:T(8,128)} %bitcast.288), custom_call_target="tpu_custom_call" | custom-call | bytes 2097152 | tf_op jit(solution)/shard_map/pallas_call | solution.py:27
  25.6 2.8 %copy-done.1 = f32[16384,16]{1,0:T(8,128)} copy-done((f32[16384,16]{1,0:T(8,128)}, f32[16384,16]{1,0:T(8,128)S(1)}, u32[]{:S(2)}) %copy-start.1) | copy-done | bytes 1048600
  28.6 1.9 %copy-done.4 = bf16[16,16384]{0,1:T(8,128)(2,1)} copy-done((bf16[16,16384]{0,1:T(8,128)(2,1)}, bf16[16,16384]{0,1:T(8,128)(2,1)S(1)}, u32[]{:S(2)}) %copy-start.4) | copy-done | bytes 524312
  33.7 5.2 %collective-permute-start.7 = (bf16[16,4096]{1,0:T(8,128)(2,1)}, bf16[16,4096]{1,0:T(8,128)(2,1)}, u32[]{:S(2)}, u32[]{:S(2)}) collective-permute-start(bf16[16,4096]{1,0:T(8,128)(2,1)} %copy.138), channel_id=1, source_target_pairs={{0,1},{1,2},{2,3},{3,4},{4,5},{5,6},{6,7},{7,8},{8,9},{9,10},{10,1... | collective-permute-start | bytes 393224 | tf_op jit(solution)/shard_map/ppermute | solution.py:48
  38.9 3.7 %convert_element_type.16 = bf16[16384,16]{1,0:T(8,128)(2,1)S(1)} convert(f32[16384,16]{1,0:T(8,128)} %copy-done.1) | non-fusion elementwise | flops 262144 | bytes 1572864 | tf_op jit(solution)/shard_map/convert_element_type | solution.py:84
  45.8 1.9 %copy.164 = bf16[16,9,256]{2,0,1:T(8,128)(2,1)} copy(bf16[16,9,256]{0,2,1:T(8,128)(2,1)} %get-tuple-element.53) | data formatting | bytes 147456 | tf_op jit(solution)/shard_map/optimization_barrier | solution.py:103
  50.1 2.6 %fusion.159 = (f32[1,1,8,2,32,32]{5,4,3,2,1,0:T(8,128)}, f32[1,1,8,2,32,32]{5,4,3,2,1,0:T(8,128)}, f32[1,1,8,2,32,32]{5,4,3,2,1,0:T(8,128)}, f32[1,1,8,2,32,32]{...) fusion(f32[1,7,8,2,32,32]{5,4,3,2,1,0:T(8,128)} %param.14), kind=kLoop, calls=%fused_computation.177 | loop fusion | bytes 917504 | tf_op jit(solution)/shard_map/slice | solution.py:111
  54.4 4.5 %copy.140 = bf16[16,16384]{1,0:T(8,128)(2,1)} copy(bf16[16,16384]{0,1:T(8,128)(2,1)} %copy-done.4) | data formatting | bytes 1048576 | tf_op jit(solution)/shard_map/convert_element_type | solution.py:84
  60.6 1.9 %copy.166 = bf16[16,9,256]{2,0,1:T(8,128)(2,1)} copy(bf16[16,9,256]{0,2,1:T(8,128)(2,1)} %get-tuple-element.52) | data formatting | bytes 147456 | tf_op jit(solution)/shard_map/optimization_barrier | solution.py:103
  64.2 1.9 %copy.168 = bf16[16,9,256]{2,0,1:T(8,128)(2,1)} copy(bf16[16,9,256]{0,2,1:T(8,128)(2,1)} %get-tuple-element.51) | data formatting | bytes 147456 | tf_op jit(solution)/shard_map/optimization_barrier | solution.py:103
  80.3 6.6 %collective-permute-start.1 = (f32[32,8,128]{2,0,1:T(8,128)S(1)}, f32[32,8,128]{2,0,1:T(8,128)}, u32[]{:S(2)}, u32[]{:S(2)}) collective-permute-start(f32[32,8,128]{2,0,1:T(8,128)S(1)} %fusion.112), channel_id=1, source_target_pairs={{0,2},{1,3},{2,0},{3,1},{4,6},{5,7},{6,4},{7,5},{8,10},{9,11},{10,... | collective-permute-start | bytes 393224 | tf_op jit(solution)/shard_map/ppermute | solution.py:38
  90.7 1.8 %fusion.59 = f32[16,64,256]{2,0,1:T(8,128)S(1)} fusion(f32[9,16,256]{2,1,0:T(8,128)S(1)} %fusion.28, bf16[16,9,256]{2,0,1:T(8,128)(2,1)} %copy.164, bf16[64,2,256,256]{3,2,1,0:T(8,128)(2,1)} %param.13), kind=kOutput, calls=%fused_computation.57 | convolution fusion | flops 18911232 | bytes 1548288 | tf_op jit(solution)/shard_map/lpq,slq->slp/dot_general | solution.py:73
  93.1 1.9 %fusion.111 = f32[32,8,128]{2,0,1:T(8,128)} fusion(f32[8,128,32]{1,2,0:T(8,128)} %fusion.120, f32[32,8,128]{2,0,1:T(8,128)} %collective-permute-done.1, f32[8,2,32,32]{3,2,0,1:T(8,128)} %bitcast.309), kind=kOutput, calls=%fused_computation.83 | convolution fusion | flops 12615680 | bytes 524288 | tf_op jit(solution)/shard_map/gab,bgm->agm/dot_general | solution.py:62
  96.2 3.7 %collective-permute-start.2 = (f32[32,8,128]{2,0,1:T(8,128)}, f32[32,8,128]{2,0,1:T(8,128)S(1)}, u32[]{:S(2)}, u32[]{:S(2)}) collective-permute-start(f32[32,8,128]{2,0,1:T(8,128)} %fusion.111), channel_id=1, source_target_pairs={{0,4},{1,5},{2,6},{3,7},{4,0},{5,1},{6,2},{7,3},{8,12},{9,13},{10,... | collective-permute-start | bytes 393224 | tf_op jit(solution)/shard_map/ppermute | solution.py:38
  103.3 1.8 %fusion.68 = f32[16,64,256]{2,0,1:T(8,128)S(1)} fusion(f32[16,64,256]{2,0,1:T(8,128)S(1)} %fusion.59, f32[9,16,256]{2,1,0:T(8,128)S(1)} %fusion.24, bf16[16,9,256]{2,0,1:T(8,128)(2,1)} %copy.166, bf16[64,2,256,256]{3,2,1,0:T(8,128)(2,1)} %param.13), kind=kOutput, calls=%fused_computation.60 | convolution fusion | flops 18911232 | bytes 1548288 | tf_op jit(solution)/shard_map/lpq,slq->slp/dot_general | solution.py:73
  105.1 1.8 %fusion.77 = f32[16,64,256]{2,0,1:T(8,128)S(1)} fusion(f32[16,64,256]{2,0,1:T(8,128)S(1)} %fusion.68, f32[9,16,256]{2,1,0:T(8,128)S(1)} %fusion.20, bf16[16,9,256]{2,0,1:T(8,128)(2,1)} %copy.168, bf16[64,2,256,256]{3,2,1,0:T(8,128)(2,1)} %param.13), kind=kOutput, calls=%fused_computation.63 | convolution fusion | flops 18911232 | bytes 1548288 | tf_op jit(solution)/shard_map/lpq,slq->slp/dot_general | solution.py:73
  110.2 1.8 %fusion.109 = f32[32,8,128]{2,0,1:T(8,128)} fusion(f32[8,128,32]{1,2,0:T(8,128)S(1)} %fusion.118, f32[32,8,128]{2,0,1:T(8,128)S(1)} %collective-permute-done.3, f32[8,2,32,32]{3,2,0,1:T(8,128)} %bitcast.306), kind=kOutput, calls=%fused_computation.79 | convolution fusion | flops 12615680 | bytes 524288 | tf_op jit(solution)/shard_map/gab,bgm->agm/dot_general | solution.py:62
  119.1 1.8 %fusion.86 = f32[16,64,256]{2,0,1:T(8,128)S(1)} fusion(f32[16,64,256]{2,0,1:T(8,128)S(1)} %fusion.77, f32[9,16,256]{2,1,0:T(8,128)S(1)} %fusion.16, bf16[16,9,256]{2,0,1:T(8,128)(2,1)} %copy.170, bf16[64,2,256,256]{3,2,1,0:T(8,128)(2,1)} %param.13), kind=kOutput, calls=%fused_computation.66 | convolution fusion | flops 18911232 | bytes 1548288 | tf_op jit(solution)/shard_map/lpq,slq->slp/dot_general | solution.py:73
  125.0 3.8 %collective-permute-done.5 = f32[32,8,128]{2,0,1:T(8,128)S(1)} collective-permute-done((f32[32,8,128]{2,0,1:T(8,128)S(1)}, f32[32,8,128]{2,0,1:T(8,128)S(1)}, u32[]{:S(2)}, u32[]{:S(2)}) %collective-permute-start.5) | collective-permute-done | bytes 131104 | tf_op jit(solution)/shard_map/ppermute | solution.py:38
  130.3 3.1 %collective-permute-start.6 = (f32[32,8,128]{2,0,1:T(8,128)S(1)}, f32[32,8,128]{2,0,1:T(8,128)S(1)}, u32[]{:S(2)}, u32[]{:S(2)}) collective-permute-start(f32[32,8,128]{2,0,1:T(8,128)S(1)} %fusion.107), channel_id=1, source_target_pairs={{0,64},{8,72},{16,80},{24,88},{32,96},{40,104},{48,112},{56,120},{... | collective-permute-start | bytes 393224 | tf_op jit(solution)/shard_map/ppermute | solution.py:38
  135.1 1.8 %fusion.2 = f32[10,16,256]{2,1,0:T(8,128)S(1)} fusion(bf16[64,2,256,256]{3,2,1,0:T(8,128)(2,1)} %param.13, bf16[10,16,256]{2,1,0:T(8,128)(2,1)S(1)} %gather_fusion, pred[10]{0:T(512)(128)(4,1)S(1)} %compare_and_fusion.6), kind=kOutput, calls=%fused_computation.10 | convolution fusion | flops 21012480 | bytes 1556490 | tf_op jit(solution)/shard_map/lpq,slq->slp/dot_general | solution.py:74
  136.9 1.8 %fusion.104 = f32[16,64,256]{2,0,1:T(8,128)S(1)} fusion(f32[16,64,256]{2,0,1:T(8,128)S(1)} %fusion.95, f32[9,16,256]{2,1,0:T(8,128)S(1)} %fusion.8, bf16[16,9,256]{2,0,1:T(8,128)(2,1)} %copy.174, bf16[64,2,256,256]{3,2,1,0:T(8,128)(2,1)} %param.13), kind=kOutput, calls=%fused_computation.72 | convolution fusion | flops 18911232 | bytes 1548288 | tf_op jit(solution)/shard_map/lpq,slq->slp/dot_general | solution.py:73
  138.6 1.8 %fusion.50 = f32[16,64,256]{2,0,1:T(8,128)S(1)} fusion(f32[16,64,256]{2,0,1:T(8,128)S(1)} %fusion.104, f32[10,16,256]{2,1,0:T(8,128)S(1)} %fusion.2, bf16[16,10,256]{2,0,1:T(8,128)(2,1)} %copy.176, bf16[64,2,256,256]{3,2,1,0:T(8,128)(2,1)} %param.13), kind=kOutput, calls=%fused_computation.54 | convolution fusion | flops 21012480 | bytes 1720320 | tf_op jit(solution)/shard_map/lpq,slq->slp/dot_general | solution.py:73
  (124 shorter events, 57.1 us)
Async XLA Ops:
  0.0 141.2 %copy-start = (bf16[64,32,256]{2,1,0:T(8,128)(2,1)S(1)}, bf16[64,32,256]{2,1,0:T(8,128)(2,1)}, u32[]{:S(2)}) copy-start(bf16[64,32,256]{2,1,0:T(8,128)(2,1)} %param.15) | copy-start | bytes 3145732
  0.0 6.1 %copy-start.2 = (s32[16384]{0:T(1024)S(1)}, s32[16384]{0:T(1024)}, u32[]{:S(2)}) copy-start(s32[16384]{0:T(1024)} %idx_ref.1) | copy-start | bytes 196612
  31.4 46.6 %collective-permute-start.8 = (bf16[16,4096]{1,0:T(8,128)(2,1)}, bf16[16,4096]{1,0:T(8,128)(2,1)}, u32[]{:S(2)}, u32[]{:S(2)}) collective-permute-start(bf16[16,4096]{1,0:T(8,128)(2,1)} %copy.139), channel_id=1, source_target_pairs={{1,0},{2,1},{3,2},{4,3},{5,4},{6,5},{7,6},{8,7},{9,8},{10,9},{11,1... | collective-permute-start | bytes 393224 | tf_op jit(solution)/shard_map/ppermute | solution.py:49
  33.7 44.4 %collective-permute-start.7 = (bf16[16,4096]{1,0:T(8,128)(2,1)}, bf16[16,4096]{1,0:T(8,128)(2,1)}, u32[]{:S(2)}, u32[]{:S(2)}) collective-permute-start(bf16[16,4096]{1,0:T(8,128)(2,1)} %copy.138), channel_id=1, source_target_pairs={{0,1},{1,2},{2,3},{3,4},{4,5},{5,6},{6,7},{7,8},{8,9},{9,10},{10,1... | collective-permute-start | bytes 393224 | tf_op jit(solution)/shard_map/ppermute | solution.py:48
  49.1 30.0 %collective-permute-start = (f32[32,8,128]{2,0,1:T(8,128)}, f32[32,8,128]{2,0,1:T(8,128)}, u32[]{:S(2)}, u32[]{:S(2)}) collective-permute-start(f32[32,8,128]{2,0,1:T(8,128)} %copy.123), channel_id=1, source_target_pairs={{0,1},{1,0},{2,3},{3,2},{4,5},{5,4},{6,7},{7,6},{8,9},{9,8},{10,11... | collective-permute-start | bytes 393224 | tf_op jit(solution)/shard_map/ppermute | solution.py:38
  68.6 9.4 %copy-start.5 = (bf16[16,16384]{1,0:T(8,128)(2,1)S(1)}, bf16[16,16384]{1,0:T(8,128)(2,1)}, u32[]{:S(2)}) copy-start(bf16[16,16384]{1,0:T(8,128)(2,1)} %copy.140) | copy-start | bytes 1572868
  71.2 7.9 %copy-start.13 = (f32[1,1,8,2,32,32]{5,4,2,3,1,0:T(8,128)S(1)}, f32[1,1,8,2,32,32]{5,4,2,3,1,0:T(8,128)}, u32[]{:S(2)}) copy-start(f32[1,1,8,2,32,32]{5,4,2,3,1,0:T(8,128)} %copy-done.12) | copy-start | bytes 196612
  71.2 15.7 %copy-start.11 = (f32[1,1,8,2,32,32]{5,4,2,3,1,0:T(8,128)S(1)}, f32[1,1,8,2,32,32]{5,4,2,3,1,0:T(8,128)}, u32[]{:S(2)}) copy-start(f32[1,1,8,2,32,32]{5,4,2,3,1,0:T(8,128)} %copy.208) | copy-start | bytes 196612
  73.8 5.4 %copy-start.16 = (f32[8,128,32]{1,2,0:T(8,128)S(1)}, f32[8,128,32]{1,2,0:T(8,128)}, u32[]{:S(2)}) copy-start(f32[8,128,32]{1,2,0:T(8,128)} %fusion.121) | copy-start | bytes 393220
  80.3 12.8 %collective-permute-start.1 = (f32[32,8,128]{2,0,1:T(8,128)S(1)}, f32[32,8,128]{2,0,1:T(8,128)}, u32[]{:S(2)}, u32[]{:S(2)}) collective-permute-start(f32[32,8,128]{2,0,1:T(8,128)S(1)} %fusion.112), channel_id=1, source_target_pairs={{0,2},{1,3},{2,0},{3,1},{4,6},{5,7},{6,4},{7,5},{8,10},{9,11},{10,... | collective-permute-start | bytes 393224 | tf_op jit(solution)/shard_map/ppermute | solution.py:38
  90.7 16.2 %copy-start.10 = (f32[1,1,8,2,32,32]{5,4,2,3,1,0:T(8,128)S(1)}, f32[1,1,8,2,32,32]{5,4,2,3,1,0:T(8,128)}, u32[]{:S(2)}) copy-start(f32[1,1,8,2,32,32]{5,4,2,3,1,0:T(8,128)} %copy.207) | copy-start | bytes 196612
  96.2 11.9 %collective-permute-start.2 = (f32[32,8,128]{2,0,1:T(8,128)}, f32[32,8,128]{2,0,1:T(8,128)S(1)}, u32[]{:S(2)}, u32[]{:S(2)}) collective-permute-start(f32[32,8,128]{2,0,1:T(8,128)} %fusion.111), channel_id=1, source_target_pairs={{0,4},{1,5},{2,6},{3,7},{4,0},{5,1},{6,2},{7,3},{8,12},{9,13},{10,... | collective-permute-start | bytes 393224 | tf_op jit(solution)/shard_map/ppermute | solution.py:38
  106.9 15.7 %copy-start.8 = (f32[1,1,8,2,32,32]{5,4,2,3,1,0:T(8,128)S(1)}, f32[1,1,8,2,32,32]{5,4,2,3,1,0:T(8,128)}, u32[]{:S(2)}) copy-start(f32[1,1,8,2,32,32]{5,4,2,3,1,0:T(8,128)} %copy.205) | copy-start | bytes 196612
  108.4 16.4 %copy-start.7 = (f32[1,1,8,2,32,32]{5,4,2,3,1,0:T(8,128)S(1)}, f32[1,1,8,2,32,32]{5,4,2,3,1,0:T(8,128)}, u32[]{:S(2)}) copy-start(f32[1,1,8,2,32,32]{5,4,2,3,1,0:T(8,128)} %copy.204) | copy-start | bytes 196612
  108.4 1.9 %collective-permute-start.3 = (f32[32,8,128]{2,0,1:T(8,128)S(1)}, f32[32,8,128]{2,0,1:T(8,128)S(1)}, u32[]{:S(2)}, u32[]{:S(2)}) collective-permute-start(f32[32,8,128]{2,0,1:T(8,128)S(1)} %fusion.110), channel_id=1, source_target_pairs={{0,8},{8,0},{16,24},{24,16},{32,40},{40,32},{48,56},{56,48},{64,72... | collective-permute-start | bytes 393224 | tf_op jit(solution)/shard_map/ppermute | solution.py:38
  114.4 6.4 %copy-start.17 = (bf16[16,9,256]{2,0,1:T(8,128)(2,1)S(1)}, bf16[16,9,256]{2,0,1:T(8,128)(2,1)}, u32[]{:S(2)}) copy-start(bf16[16,9,256]{2,0,1:T(8,128)(2,1)} %copy.172) | copy-start | bytes 221188
  114.5 8.1 %copy-start.15 = (f32[32,8,128]{2,0,1:T(8,128)S(1)}, f32[32,8,128]{2,0,1:T(8,128)}, u32[]{:S(2)}) copy-start(f32[32,8,128]{2,0,1:T(8,128)} %fusion.109) | copy-start | bytes 393220
  114.5 8.4 %copy-start.9 = (f32[1,1,8,2,32,32]{5,4,2,3,1,0:T(8,128)S(1)}, f32[1,1,8,2,32,32]{5,4,2,3,1,0:T(8,128)}, u32[]{:S(2)}) copy-start(f32[1,1,8,2,32,32]{5,4,2,3,1,0:T(8,128)} %copy.205) | copy-start | bytes 196612
  114.5 10.5 %copy-start.18 = (s32[9]{0:T(128)S(1)}, s32[9]{0:T(128)}, u32[]{:S(2)}) copy-start(s32[9]{0:T(128)} %get-tuple-element.45) | copy-start | bytes 112
  114.5 14.6 %copy-start.20 = (s32[10]{0:T(128)S(1)}, s32[10]{0:T(128)}, u32[]{:S(2)}) copy-start(s32[10]{0:T(128)} %slice.191) | copy-start | bytes 124
  114.5 8.4 %collective-permute-start.4 = (f32[32,8,128]{2,0,1:T(8,128)}, f32[32,8,128]{2,0,1:T(8,128)S(1)}, u32[]{:S(2)}, u32[]{:S(2)}) collective-permute-start(f32[32,8,128]{2,0,1:T(8,128)} %fusion.109), channel_id=1, source_target_pairs={{0,16},{8,24},{16,0},{24,8},{32,48},{40,56},{48,32},{56,40},{64,80... | collective-permute-start | bytes 393224 | tf_op jit(solution)/shard_map/ppermute | solution.py:38
  122.9 17.6 %copy-start.6 = (f32[1,1,8,2,32,32]{5,4,2,3,1,0:T(8,128)S(1)}, f32[1,1,8,2,32,32]{5,4,2,3,1,0:T(8,128)}, u32[]{:S(2)}) copy-start(f32[1,1,8,2,32,32]{5,4,2,3,1,0:T(8,128)} %copy.203) | copy-start | bytes 196612
  123.1 5.7 %collective-permute-start.5 = (f32[32,8,128]{2,0,1:T(8,128)S(1)}, f32[32,8,128]{2,0,1:T(8,128)S(1)}, u32[]{:S(2)}, u32[]{:S(2)}) collective-permute-start(f32[32,8,128]{2,0,1:T(8,128)S(1)} %fusion.108), channel_id=1, source_target_pairs={{0,32},{8,40},{16,48},{24,56},{32,0},{40,8},{48,16},{56,24},{64,96... | collective-permute-start | bytes 393224 | tf_op jit(solution)/shard_map/ppermute | solution.py:38
  130.3 10.5 %collective-permute-start.6 = (f32[32,8,128]{2,0,1:T(8,128)S(1)}, f32[32,8,128]{2,0,1:T(8,128)S(1)}, u32[]{:S(2)}, u32[]{:S(2)}) collective-permute-start(f32[32,8,128]{2,0,1:T(8,128)S(1)} %fusion.107), channel_id=1, source_target_pairs={{0,64},{8,72},{16,80},{24,88},{32,96},{40,104},{48,112},{56,120},{... | collective-permute-start | bytes 393224 | tf_op jit(solution)/shard_map/ppermute | solution.py:38
  (6 other events, 15.2 us)

commit v4 on v0

--- a/solution.py
+++ b/solution.py
@@ -1,9 +1,46 @@
 import jax
 import jax.numpy as jnp
 from jax import lax
+from jax.experimental import pallas as pl
+from jax.experimental.pallas import tpu as pltpu
 from jax.sharding import PartitionSpec as P
 
 HW = 16
+
+
+CHUNK = 128
+
+
+def gather_kernel(idx_ref, x_ref, o_ref, xt_ref):
+    count = o_ref.shape[1]
+
+    def spread(c, carry):
+        col = pl.multiple_of(c * CHUNK, CHUNK)
+        xt_ref[pl.ds(col, CHUNK), :] = x_ref[:, pl.ds(col, CHUNK)].T
+        return carry
+
+    lax.fori_loop(0, count // CHUNK, spread, 0)
+
+    def body(c, carry):
+        col = pl.multiple_of(c * CHUNK, CHUNK)
+        rows = [xt_ref[pl.ds(idx_ref[col + u], 1), :] for u in range(CHUNK)]
+        o_ref[:, pl.ds(col, CHUNK)] = jnp.concatenate(rows, axis=0).T.astype(o_ref.dtype)
+        return carry
+
+    lax.fori_loop(0, count // CHUNK, body, 0)
+
+
+def gather_points(points, index):
+    width, count = points.shape
+    return pl.pallas_call(
+        gather_kernel,
+        out_shape=jax.ShapeDtypeStruct((width, count), jnp.bfloat16),
+        in_specs=[pl.BlockSpec(memory_space=pltpu.SMEM), pl.BlockSpec(memory_space=pltpu.VMEM)],
+        out_specs=pl.BlockSpec(memory_space=pltpu.VMEM),
+        scratch_shapes=[pltpu.VMEM((count, width), jnp.float32)],
+        compiler_params=pltpu.CompilerParams(vmem_limit_bytes=40 * 1024 * 1024),
+        cost_estimate=pl.CostEstimate(flops=0, transcendentals=0, bytes_accessed=count * width * 6),
+    )(index, points)
 
 
 def from_partner(x, axis, distance):
@@ -47,7 +84,7 @@
     group_total = translations.shape[2]
     total_cols = leaf_count * rhs_count
     group_width = total_cols // group_total
-    ordered = points_rhs[:, morton_order].astype(jnp.bfloat16)
+    ordered = gather_points(points_rhs, morton_order)
     leaves = ordered.reshape(rhs_count, leaf_count, leaf_size)
     coeffs = jnp.einsum(
         "lrp,slp->rls", leaf_basis, leaves, preferred_element_type=jnp.float32

time: 144 us -> 103 us (0.72)
  local copies, waits for them, and re-layouts: 80.6 us -> 10.3 us
  Pallas kernels: 0 us -> 32.6 us
  matrix products: 23.6 us -> 26.8 us
  starting transfers between devices: 24.5 us -> 21.3 us
  waiting for transfers between devices: 13.7 us -> 10.9 us
    gather x1 -> x0, local copies, waits for them, and re-layouts: 57.7 us -> none  [local(): ordered = points_rhs[:, morton_order].astype(jnp.bfloat16)]
    pallas_call x0 -> x1, Pallas kernels: none -> 32.6 us  [gather_points(): pl.pallas_call(gather_kernel, out_shape=jax.ShapeDtypeStruct((width, coun...]
    unnamed x32 -> x15, local copies, waits for them, and re-layouts: 11.3 us -> 5.83 us
    dot_general x7, matrix products: 3.12 us -> 6.97 us  [translate(): jnp.einsum('gab,bgm->agm', level_weights[:, 0], own_coeffs, precision=lax...]
    convert_element_type x1 -> x0, local copies, waits for them, and re-layouts: 3.46 us -> none  [local(): ordered = points_rhs[:, morton_order].astype(jnp.bfloat16)]
    ppermute x1, starting transfers between devices: 5.19 us -> 2.25 us  [extended(): before = lax.ppermute(last, axis, up)]
    ppermute x7, waiting for transfers between devices: 13.7 us -> 10.9 us  [from_partner(): lax.ppermute(x, axis, [(i, i ^ 1 << distance) for i in range(lax.axis_siz...]
    dot_general x7, matrix products: 3.57 us -> 6.37 us  [translate(): jnp.einsum('gab,bgm->agm', level_weights[:, 1], other_coeffs, precision=l...]
  transfers between devices with their start and end apart: 9 -> 9, of which waited for: 5 -> 5; matrix products, arithmetic and copies ran while one was open for 24% -> 25% of each run, Pallas kernels for 0% -> 0%
where the time goes in v4:
time: 103 us; the launch traced here: 102 us
  Pallas kernels  32.6 us (32%)
  matrix products  26.8 us (26%)
  starting transfers between devices  21.3 us (21%)
  waiting for transfers between devices  10.9 us (11%)
  local copies, waits for them, and re-layouts  10.3 us (10%)
    pallas_call x1, Pallas kernels, gather_points(): pl.pallas_call(gather_kernel, out_shape=jax.ShapeDtypeStruct((width, coun...  32.6 us
    ppermute x7, starting transfers between devices, from_partner(): lax.ppermute(x, axis, [(i, i ^ 1 << distance) for i in range(lax.axis_siz...  17.8 us
    ppermute x7, waiting for transfers between devices, from_partner(): lax.ppermute(x, axis, [(i, i ^ 1 << distance) for i in range(lax.axis_siz...  10.9 us
    dot_general x7, matrix products, translate(): jnp.einsum('gab,bgm->agm', level_weights[:, 0], own_coeffs, precision=lax...  6.97 us
    dot_general x7, matrix products, translate(): jnp.einsum('gab,bgm->agm', level_weights[:, 1], other_coeffs, precision=l...  6.37 us
    dot_general x1, matrix products, local(): jnp.einsum('lpq,slq->slp', band_blocks[:, 1], picked, preferred_element_t...  5.86 us
    unnamed x15, local copies, waits for them, and re-layouts  5.83 us
    dot_general x1, matrix products, local(): jnp.einsum('lpq,slq->slp', band_blocks[:, 0], leaves, preferred_element_t...  5.69 us
  transfers between devices with their start and end apart: 9, of which 5 were waited for; matrix products, arithmetic and copies ran while one was open for 25% of the time, Pallas kernels for 0%

profile of v4, /device:TPU:0, one launch (start us, length us, event | category | flops | bytes accessed | tf_op | source)
XLA Modules:
  0.0 102.2 jit_solution(9703191879341447524)
XLA Ops:
  0.0 1.3 %copy-done.1 = f32[16,16384]{1,0:T(8,128)S(1)} copy-done((f32[16,16384]{1,0:T(8,128)S(1)}, f32[16,16384]{1,0:T(8,128)}, u32[]{:S(2)}) %copy-start.1) | copy-done | bytes 1048600
  2.2 32.6 %shard_map.73 = bf16[16,16384]{1,0:T(8,128)(2,1)S(1)} custom-call(s32[16384]{0:T(1024)S(1)} %copy-done.2, f32[16,16384]{1,0:T(8,128)S(1)} %copy-done.1), custom_call_target="tpu_custom_call" | custom-call | bytes 1572864 | tf_op jit(solution)/shard_map/pallas_call | solution.py:35
  34.8 1.6 %fusion.17 = f32[64,16,32]{2,1,0:T(8,128)S(1)} fusion(bf16[64,32,256]{2,1,0:T(8,128)(2,1)} %param.10, bf16[2,64,8,256]{3,2,1,0:T(8,128)(2,1)S(1)} %bitcast.125), kind=kOutput, calls=%fused_computation.28 | convolution fusion | flops 16777216 | bytes 1703936 | tf_op jit(solution)/shard_map/lrp,slp->rls/dot_general | solution.py:89
  36.5 1.8 %collective-permute-start = (f32[32,8,128]{2,0,1:T(8,128)S(1)}, f32[32,8,128]{2,0,1:T(8,128)S(1)}, u32[]{:S(2)}, u32[]{:S(2)}) collective-permute-start(f32[32,8,128]{2,0,1:T(8,128)S(1)} %copy.24), channel_id=1, source_target_pairs={{0,1},{1,0},{2,3},{3,2},{4,5},{5,4},{6,7},{7,6},{8,9},{9,8},{10,11... | collective-permute-start | bytes 393224 | tf_op jit(solution)/shard_map/ppermute | solution.py:47
  38.3 2.2 %collective-permute-start.7 = (bf16[16,4096]{1,0:T(8,128)(2,1)S(1)}, bf16[16,4096]{1,0:T(8,128)(2,1)S(1)}, u32[]{:S(2)}, u32[]{:S(2)}) collective-permute-start(bf16[16,4096]{1,0:T(8,128)(2,1)S(1)} %get-tuple-element.14), channel_id=1, source_target_pairs={{0,1},{1,2},{2,3},{3,4},{4,5},{5,6},{6,7},{7,8},{8,9},{9,10},{10,1... | collective-permute-start | bytes 393224 | tf_op jit(solution)/shard_map/ppermute | solution.py:57
  40.6 1.3 %collective-permute-start.8 = (bf16[16,4096]{1,0:T(8,128)(2,1)S(1)}, bf16[16,4096]{1,0:T(8,128)(2,1)S(1)}, u32[]{:S(2)}, u32[]{:S(2)}) collective-permute-start(bf16[16,4096]{1,0:T(8,128)(2,1)S(1)} %get-tuple-element.15), channel_id=1, source_target_pairs={{1,0},{2,1},{3,2},{4,3},{5,4},{6,5},{7,6},{8,7},{9,8},{10,9},{11,1... | collective-permute-start | bytes 393224 | tf_op jit(solution)/shard_map/ppermute | solution.py:58
  41.9 1.6 %fusion.33 = (f32[1,1,8,2,32,32]{5,4,3,2,1,0:T(8,128)S(1)}, f32[1,1,8,2,32,32]{5,4,3,2,1,0:T(8,128)S(1)}, f32[1,1,8,2,32,32]{5,4,3,2,1,0:T(8,128)S(1)}, f32[1,1,...) fusion(f32[1,7,8,2,32,32]{5,4,3,2,1,0:T(8,128)} %param.12), kind=kLoop, calls=%fused_computation.68 | loop fusion | bytes 917504 | tf_op jit(solution)/shard_map/slice | solution.py:101
  44.5 5.7 %fusion.2 = f32[64,16,256]{2,1,0:T(8,128)S(1)} fusion(bf16[64,2,256,256]{3,2,1,0:T(8,128)(2,1)} %param.11, bf16[2,64,8,256]{3,2,1,0:T(8,128)(2,1)S(1)} %bitcast.126), kind=kOutput, calls=%fused_computation.3 | convolution fusion | flops 134217728 | bytes 9961472 | tf_op jit(solution)/shard_map/lpq,slq->slp/dot_general | solution.py:109
  54.1 5.3 %collective-permute-start.1 = (f32[32,8,128]{2,0,1:T(8,128)S(1)}, f32[32,8,128]{2,0,1:T(8,128)}, u32[]{:S(2)}, u32[]{:S(2)}) collective-permute-start(f32[32,8,128]{2,0,1:T(8,128)S(1)} %fusion.13), channel_id=1, source_target_pairs={{0,2},{1,3},{2,0},{3,1},{4,6},{5,7},{6,4},{7,5},{8,10},{9,11},{10,... | collective-permute-start | bytes 393224 | tf_op jit(solution)/shard_map/ppermute | solution.py:47
  59.5 1.4 %gather_fusion = bf16[64,16,256]{2,1,0:T(8,128)(2,1)} fusion(bf16[16,96,256]{2,0,1:T(8,128)(2,1)S(1)} %bitcast.130, s32[1024]{0:T(1024)S(1)} %pad_clamp_fusion), kind=kCustom, calls=%fused_computation | custom fusion | bytes 1048832 | tf_op jit(solution)/shard_map/jit(_take)/gather | solution.py:108
  60.9 5.9 %fusion = f32[64,16,256]{2,1,0:T(8,128)S(1)} fusion(bf16[64,2,256,256]{3,2,1,0:T(8,128)(2,1)} %param.11, bf16[64,16,256]{2,1,0:T(8,128)(2,1)} %gather_fusion, pred[64]{0:T(512)(128)(4,1)S(1)} %get-tuple-element.5), kind=kOutput, calls=%fused_computation.1 | convolution fusion | flops 134479872 | bytes 9961536 | tf_op jit(solution)/shard_map/lpq,slq->slp/dot_general | solution.py:112
  66.8 1.2 %fusion.30 = f32[8,128,32]{1,2,0:T(8,128)S(1)} fusion(f32[32,8,128]{2,0,1:T(8,128)S(1)} %fusion.13, f32[8,2,32,32]{3,2,0,1:T(8,128)} %bitcast.142), kind=kOutput, calls=%fused_computation.60 | convolution fusion | flops 12582912 | bytes 393216 | tf_op jit(solution)/shard_map/gab,bgm->agm/dot_general | solution.py:64
  68.0 1.2 %fusion.12 = f32[32,8,128]{2,0,1:T(8,128)S(1)} fusion(f32[8,128,32]{1,2,0:T(8,128)S(1)} %fusion.30, f32[32,8,128]{2,0,1:T(8,128)} %collective-permute-done.1, f32[8,2,32,32]{3,2,0,1:T(8,128)} %bitcast.143), kind=kOutput, calls=%fused_computation.20 | convolution fusion | flops 12615680 | bytes 524288 | tf_op jit(solution)/shard_map/gab,bgm->agm/dot_general | solution.py:71
  69.2 4.7 %collective-permute-start.2 = (f32[32,8,128]{2,0,1:T(8,128)S(1)}, f32[32,8,128]{2,0,1:T(8,128)S(1)}, u32[]{:S(2)}, u32[]{:S(2)}) collective-permute-start(f32[32,8,128]{2,0,1:T(8,128)S(1)} %fusion.12), channel_id=1, source_target_pairs={{0,4},{1,5},{2,6},{3,7},{4,0},{5,1},{6,2},{7,3},{8,12},{9,13},{10,... | collective-permute-start | bytes 393224 | tf_op jit(solution)/shard_map/ppermute | solution.py:47
  75.1 1.8 %collective-permute-done.2 = f32[32,8,128]{2,0,1:T(8,128)S(1)} collective-permute-done((f32[32,8,128]{2,0,1:T(8,128)S(1)}, f32[32,8,128]{2,0,1:T(8,128)S(1)}, u32[]{:S(2)}, u32[]{:S(2)}) %collective-permute-start.2) | collective-permute-done | bytes 131104 | tf_op jit(solution)/shard_map/ppermute | solution.py:47
  76.9 1.2 %fusion.11 = f32[32,8,128]{2,0,1:T(8,128)S(1)} fusion(f32[8,128,32]{1,2,0:T(8,128)S(1)} %fusion.29, f32[32,8,128]{2,0,1:T(8,128)S(1)} %collective-permute-done.2, f32[8,2,32,32]{3,2,0,1:T(8,128)} %bitcast.141), kind=kOutput, calls=%fused_computation.18 | convolution fusion | flops 12615680 | bytes 524288 | tf_op jit(solution)/shard_map/gab,bgm->agm/dot_general | solution.py:71
  78.2 1.2 %fusion.28 = f32[8,128,32]{1,2,0:T(8,128)S(1)} fusion(f32[32,8,128]{2,0,1:T(8,128)S(1)} %fusion.11, f32[8,2,32,32]{3,2,0,1:T(8,128)} %bitcast.138), kind=kOutput, calls=%fused_computation.54 | convolution fusion | flops 12582912 | bytes 393216 | tf_op jit(solution)/shard_map/gab,bgm->agm/dot_general | solution.py:64
  79.5 1.2 %fusion.10 = f32[32,8,128]{2,0,1:T(8,128)S(1)} fusion(f32[8,128,32]{1,2,0:T(8,128)S(1)} %fusion.28, f32[32,8,128]{2,0,1:T(8,128)S(1)} %collective-permute-done.3, f32[8,2,32,32]{3,2,0,1:T(8,128)} %bitcast.139), kind=kOutput, calls=%fused_computation.16 | convolution fusion | flops 12615680 | bytes 524288 | tf_op jit(solution)/shard_map/gab,bgm->agm/dot_general | solution.py:71
  80.7 1.3 %collective-permute-start.4 = (f32[32,8,128]{2,0,1:T(8,128)S(1)}, f32[32,8,128]{2,0,1:T(8,128)S(1)}, u32[]{:S(2)}, u32[]{:S(2)}) collective-permute-start(f32[32,8,128]{2,0,1:T(8,128)S(1)} %fusion.10), channel_id=1, source_target_pairs={{0,16},{8,24},{16,0},{24,8},{32,48},{40,56},{48,32},{56,40},{64,80... | collective-permute-start | bytes 393224 | tf_op jit(solution)/shard_map/ppermute | solution.py:47
  83.1 3.4 %collective-permute-done.4 = f32[32,8,128]{2,0,1:T(8,128)S(1)} collective-permute-done((f32[32,8,128]{2,0,1:T(8,128)S(1)}, f32[32,8,128]{2,0,1:T(8,128)S(1)}, u32[]{:S(2)}, u32[]{:S(2)}) %collective-permute-start.4) | collective-permute-done | bytes 131104 | tf_op jit(solution)/shard_map/ppermute | solution.py:47
  87.7 1.6 %collective-permute-start.5 = (f32[32,8,128]{2,0,1:T(8,128)S(1)}, f32[32,8,128]{2,0,1:T(8,128)S(1)}, u32[]{:S(2)}, u32[]{:S(2)}) collective-permute-start(f32[32,8,128]{2,0,1:T(8,128)S(1)} %fusion.9), channel_id=1, source_target_pairs={{0,32},{8,40},{16,48},{24,56},{32,0},{40,8},{48,16},{56,24},{64,96... | collective-permute-start | bytes 393224 | tf_op jit(solution)/shard_map/ppermute | solution.py:47
  90.4 2.3 %collective-permute-done.5 = f32[32,8,128]{2,0,1:T(8,128)S(1)} collective-permute-done((f32[32,8,128]{2,0,1:T(8,128)S(1)}, f32[32,8,128]{2,0,1:T(8,128)S(1)}, u32[]{:S(2)}, u32[]{:S(2)}) %collective-permute-start.5) | collective-permute-done | bytes 131104 | tf_op jit(solution)/shard_map/ppermute | solution.py:47
  93.9 3.1 %collective-permute-start.6 = (f32[32,8,128]{2,0,1:T(8,128)S(1)}, f32[32,8,128]{2,0,1:T(8,128)S(1)}, u32[]{:S(2)}, u32[]{:S(2)}) collective-permute-start(f32[32,8,128]{2,0,1:T(8,128)S(1)} %fusion.8), channel_id=1, source_target_pairs={{0,64},{8,72},{16,80},{24,88},{32,96},{40,104},{48,112},{56,120},{... | collective-permute-start | bytes 393224 | tf_op jit(solution)/shard_map/ppermute | solution.py:47
  97.3 3.2 %collective-permute-done.6 = f32[32,8,128]{2,0,1:T(8,128)S(1)} collective-permute-done((f32[32,8,128]{2,0,1:T(8,128)S(1)}, f32[32,8,128]{2,0,1:T(8,128)S(1)}, u32[]{:S(2)}, u32[]{:S(2)}) %collective-permute-start.6) | collective-permute-done | bytes 131104 | tf_op jit(solution)/shard_map/ppermute | solution.py:47
  (38 shorter events, 14.1 us)
Async XLA Ops:
  0.0 100.9 %copy-start = (bf16[64,32,256]{2,1,0:T(8,128)(2,1)S(1)}, bf16[64,32,256]{2,1,0:T(8,128)(2,1)}, u32[]{:S(2)}) copy-start(bf16[64,32,256]{2,1,0:T(8,128)(2,1)} %param.13) | copy-start | bytes 3145732
  0.0 1.3 %copy-start.1 = (f32[16,16384]{1,0:T(8,128)S(1)}, f32[16,16384]{1,0:T(8,128)}, u32[]{:S(2)}) copy-start(f32[16,16384]{1,0:T(8,128)} %x_ref.1) | copy-start | bytes 3145732
  1.3 0.8 copy-start.2
  36.4 13.8 %copy-start.3 = (s32[64]{0:T(128)S(1)}, s32[64]{0:T(128)}, u32[]{:S(2)}) copy-start(s32[64]{0:T(128)} %param.9) | copy-start | bytes 772
  36.5 17.3 %collective-permute-start = (f32[32,8,128]{2,0,1:T(8,128)S(1)}, f32[32,8,128]{2,0,1:T(8,128)S(1)}, u32[]{:S(2)}, u32[]{:S(2)}) collective-permute-start(f32[32,8,128]{2,0,1:T(8,128)S(1)} %copy.24), channel_id=1, source_target_pairs={{0,1},{1,0},{2,3},{3,2},{4,5},{5,4},{6,7},{7,6},{8,9},{9,8},{10,11... | collective-permute-start | bytes 393224 | tf_op jit(solution)/shard_map/ppermute | solution.py:47
  38.3 21.1 %collective-permute-start.7 = (bf16[16,4096]{1,0:T(8,128)(2,1)S(1)}, bf16[16,4096]{1,0:T(8,128)(2,1)S(1)}, u32[]{:S(2)}, u32[]{:S(2)}) collective-permute-start(bf16[16,4096]{1,0:T(8,128)(2,1)S(1)} %get-tuple-element.14), channel_id=1, source_target_pairs={{0,1},{1,2},{2,3},{3,4},{4,5},{5,6},{6,7},{7,8},{8,9},{9,10},{10,1... | collective-permute-start | bytes 393224 | tf_op jit(solution)/shard_map/ppermute | solution.py:57
  40.6 18.8 %collective-permute-start.8 = (bf16[16,4096]{1,0:T(8,128)(2,1)S(1)}, bf16[16,4096]{1,0:T(8,128)(2,1)S(1)}, u32[]{:S(2)}, u32[]{:S(2)}) collective-permute-start(bf16[16,4096]{1,0:T(8,128)(2,1)S(1)} %get-tuple-element.15), channel_id=1, source_target_pairs={{1,0},{2,1},{3,2},{4,3},{5,4},{6,5},{7,6},{8,7},{9,8},{10,9},{11,1... | collective-permute-start | bytes 393224 | tf_op jit(solution)/shard_map/ppermute | solution.py:58
  54.1 13.8 %collective-permute-start.1 = (f32[32,8,128]{2,0,1:T(8,128)S(1)}, f32[32,8,128]{2,0,1:T(8,128)}, u32[]{:S(2)}, u32[]{:S(2)}) collective-permute-start(f32[32,8,128]{2,0,1:T(8,128)S(1)} %fusion.13), channel_id=1, source_target_pairs={{0,2},{1,3},{2,0},{3,1},{4,6},{5,7},{6,4},{7,5},{8,10},{9,11},{10,... | collective-permute-start | bytes 393224 | tf_op jit(solution)/shard_map/ppermute | solution.py:47
  69.2 7.7 %collective-permute-start.2 = (f32[32,8,128]{2,0,1:T(8,128)S(1)}, f32[32,8,128]{2,0,1:T(8,128)S(1)}, u32[]{:S(2)}, u32[]{:S(2)}) collective-permute-start(f32[32,8,128]{2,0,1:T(8,128)S(1)} %fusion.12), channel_id=1, source_target_pairs={{0,4},{1,5},{2,6},{3,7},{4,0},{5,1},{6,2},{7,3},{8,12},{9,13},{10,... | collective-permute-start | bytes 393224 | tf_op jit(solution)/shard_map/ppermute | solution.py:47
  78.1 1.4 %collective-permute-start.3 = (f32[32,8,128]{2,0,1:T(8,128)S(1)}, f32[32,8,128]{2,0,1:T(8,128)S(1)}, u32[]{:S(2)}, u32[]{:S(2)}) collective-permute-start(f32[32,8,128]{2,0,1:T(8,128)S(1)} %fusion.11), channel_id=1, source_target_pairs={{0,8},{8,0},{16,24},{24,16},{32,40},{40,32},{48,56},{56,48},{64,72... | collective-permute-start | bytes 393224 | tf_op jit(solution)/shard_map/ppermute | solution.py:47
  80.7 5.8 %collective-permute-start.4 = (f32[32,8,128]{2,0,1:T(8,128)S(1)}, f32[32,8,128]{2,0,1:T(8,128)S(1)}, u32[]{:S(2)}, u32[]{:S(2)}) collective-permute-start(f32[32,8,128]{2,0,1:T(8,128)S(1)} %fusion.10), channel_id=1, source_target_pairs={{0,16},{8,24},{16,0},{24,8},{32,48},{40,56},{48,32},{56,40},{64,80... | collective-permute-start | bytes 393224 | tf_op jit(solution)/shard_map/ppermute | solution.py:47
  87.7 5.0 %collective-permute-start.5 = (f32[32,8,128]{2,0,1:T(8,128)S(1)}, f32[32,8,128]{2,0,1:T(8,128)S(1)}, u32[]{:S(2)}, u32[]{:S(2)}) collective-permute-start(f32[32,8,128]{2,0,1:T(8,128)S(1)} %fusion.9), channel_id=1, source_target_pairs={{0,32},{8,40},{16,48},{24,56},{32,0},{40,8},{48,16},{56,24},{64,96... | collective-permute-start | bytes 393224 | tf_op jit(solution)/shard_map/ppermute | solution.py:47
  93.9 6.6 %collective-permute-start.6 = (f32[32,8,128]{2,0,1:T(8,128)S(1)}, f32[32,8,128]{2,0,1:T(8,128)S(1)}, u32[]{:S(2)}, u32[]{:S(2)}) collective-permute-start(f32[32,8,128]{2,0,1:T(8,128)S(1)} %fusion.8), channel_id=1, source_target_pairs={{0,64},{8,72},{16,80},{24,88},{32,96},{40,104},{48,112},{56,120},{... | collective-permute-start | bytes 393224 | tf_op jit(solution)/shard_map/ppermute | solution.py:47

commit v5 on v4

--- a/solution.py
+++ b/solution.py
@@ -65,14 +65,14 @@
         "gab,bgm->agm",
         level_weights[:, 0],
         own_coeffs,
-        precision=lax.Precision.HIGHEST,
+        precision=lax.Precision.HIGH,
         preferred_element_type=jnp.float32,
     )
     second = jnp.einsum(
         "gab,bgm->agm",
         level_weights[:, 1],
         other_coeffs,
-        precision=lax.Precision.HIGHEST,
+        precision=lax.Precision.HIGH,
         preferred_element_type=jnp.float32,
     )
     return first + second

time: 103 us -> 102 us (level)
  matrix products: 26.8 us -> 25.6 us
  transfers between devices with their start and end apart: 9 -> 9, of which waited for: 5 -> 5; matrix products, arithmetic and copies ran while one was open for 25% -> 24% of each run, Pallas kernels for 0% -> 0%
where the time goes in v5:
time: 102 us; the launch traced here: 101 us
  Pallas kernels  32.6 us (32%)
  matrix products  25.6 us (25%)
  starting transfers between devices  21.3 us (21%)
  waiting for transfers between devices  11.1 us (11%)
  local copies, waits for them, and re-layouts  10.3 us (10%)
    pallas_call x1, Pallas kernels, gather_points(): pl.pallas_call(gather_kernel, out_shape=jax.ShapeDtypeStruct((width, coun...  32.6 us
    ppermute x7, starting transfers between devices, from_partner(): lax.ppermute(x, axis, [(i, i ^ 1 << distance) for i in range(lax.axis_siz...  17.8 us
    ppermute x7, waiting for transfers between devices, from_partner(): lax.ppermute(x, axis, [(i, i ^ 1 << distance) for i in range(lax.axis_siz...  11.1 us
    dot_general x7, matrix products, translate(): jnp.einsum('gab,bgm->agm', level_weights[:, 0], own_coeffs, precision=lax...  6.2 us
    dot_general x7, matrix products, translate(): jnp.einsum('gab,bgm->agm', level_weights[:, 1], other_coeffs, precision=l...  5.94 us
    dot_general x1, matrix products, local(): jnp.einsum('lpq,slq->slp', band_blocks[:, 1], picked, preferred_element_t...  5.86 us
    unnamed x15, local copies, waits for them, and re-layouts  5.83 us
    dot_general x1, matrix products, local(): jnp.einsum('lpq,slq->slp', band_blocks[:, 0], leaves, preferred_element_t...  5.69 us
  transfers between devices with their start and end apart: 9, of which 5 were waited for; matrix products, arithmetic and copies ran while one was open for 24% of the time, Pallas kernels for 0%

profile of v5, /device:TPU:0, one launch (start us, length us, event | category | flops | bytes accessed | tf_op | source)
XLA Modules:
  0.0 101.3 jit_solution(18393188116042042211)
XLA Ops:
  0.0 1.3 %copy-done.1 = f32[16,16384]{1,0:T(8,128)S(1)} copy-done((f32[16,16384]{1,0:T(8,128)S(1)}, f32[16,16384]{1,0:T(8,128)}, u32[]{:S(2)}) %copy-start.1) | copy-done | bytes 1048600
  2.2 32.6 %shard_map.73 = bf16[16,16384]{1,0:T(8,128)(2,1)S(1)} custom-call(s32[16384]{0:T(1024)S(1)} %copy-done.2, f32[16,16384]{1,0:T(8,128)S(1)} %copy-done.1), custom_call_target="tpu_custom_call" | custom-call | bytes 1572864 | tf_op jit(solution)/shard_map/pallas_call | solution.py:35
  34.8 1.6 %fusion.17 = f32[64,16,32]{2,1,0:T(8,128)S(1)} fusion(bf16[64,32,256]{2,1,0:T(8,128)(2,1)} %param.10, bf16[2,64,8,256]{3,2,1,0:T(8,128)(2,1)S(1)} %bitcast.125), kind=kOutput, calls=%fused_computation.28 | convolution fusion | flops 16777216 | bytes 1703936 | tf_op jit(solution)/shard_map/lrp,slp->rls/dot_general | solution.py:89
  36.5 1.8 %collective-permute-start = (f32[32,8,128]{2,0,1:T(8,128)S(1)}, f32[32,8,128]{2,0,1:T(8,128)S(1)}, u32[]{:S(2)}, u32[]{:S(2)}) collective-permute-start(f32[32,8,128]{2,0,1:T(8,128)S(1)} %copy.24), channel_id=1, source_target_pairs={{0,1},{1,0},{2,3},{3,2},{4,5},{5,4},{6,7},{7,6},{8,9},{9,8},{10,11... | collective-permute-start | bytes 393224 | tf_op jit(solution)/shard_map/ppermute | solution.py:47
  38.3 2.2 %collective-permute-start.7 = (bf16[16,4096]{1,0:T(8,128)(2,1)S(1)}, bf16[16,4096]{1,0:T(8,128)(2,1)S(1)}, u32[]{:S(2)}, u32[]{:S(2)}) collective-permute-start(bf16[16,4096]{1,0:T(8,128)(2,1)S(1)} %get-tuple-element.14), channel_id=1, source_target_pairs={{0,1},{1,2},{2,3},{3,4},{4,5},{5,6},{6,7},{7,8},{8,9},{9,10},{10,1... | collective-permute-start | bytes 393224 | tf_op jit(solution)/shard_map/ppermute | solution.py:57
  40.6 1.3 %collective-permute-start.8 = (bf16[16,4096]{1,0:T(8,128)(2,1)S(1)}, bf16[16,4096]{1,0:T(8,128)(2,1)S(1)}, u32[]{:S(2)}, u32[]{:S(2)}) collective-permute-start(bf16[16,4096]{1,0:T(8,128)(2,1)S(1)} %get-tuple-element.15), channel_id=1, source_target_pairs={{1,0},{2,1},{3,2},{4,3},{5,4},{6,5},{7,6},{8,7},{9,8},{10,9},{11,1... | collective-permute-start | bytes 393224 | tf_op jit(solution)/shard_map/ppermute | solution.py:58
  41.9 1.6 %fusion.33 = (f32[1,1,8,2,32,32]{5,4,3,2,1,0:T(8,128)S(1)}, f32[1,1,8,2,32,32]{5,4,3,2,1,0:T(8,128)S(1)}, f32[1,1,8,2,32,32]{5,4,3,2,1,0:T(8,128)S(1)}, f32[1,1,...) fusion(f32[1,7,8,2,32,32]{5,4,3,2,1,0:T(8,128)} %param.12), kind=kLoop, calls=%fused_computation.68 | loop fusion | bytes 917504 | tf_op jit(solution)/shard_map/slice | solution.py:101
  44.1 5.7 %fusion.2 = f32[64,16,256]{2,1,0:T(8,128)S(1)} fusion(bf16[64,2,256,256]{3,2,1,0:T(8,128)(2,1)} %param.11, bf16[2,64,8,256]{3,2,1,0:T(8,128)(2,1)S(1)} %bitcast.126), kind=kOutput, calls=%fused_computation.3 | convolution fusion | flops 134217728 | bytes 9961472 | tf_op jit(solution)/shard_map/lpq,slq->slp/dot_general | solution.py:109
  53.7 5.3 %collective-permute-start.1 = (f32[32,8,128]{2,0,1:T(8,128)S(1)}, f32[32,8,128]{2,0,1:T(8,128)}, u32[]{:S(2)}, u32[]{:S(2)}) collective-permute-start(f32[32,8,128]{2,0,1:T(8,128)S(1)} %fusion.13), channel_id=1, source_target_pairs={{0,2},{1,3},{2,0},{3,1},{4,6},{5,7},{6,4},{7,5},{8,10},{9,11},{10,... | collective-permute-start | bytes 393224 | tf_op jit(solution)/shard_map/ppermute | solution.py:47
  59.1 1.4 %gather_fusion = bf16[64,16,256]{2,1,0:T(8,128)(2,1)} fusion(bf16[16,96,256]{2,0,1:T(8,128)(2,1)S(1)} %bitcast.130, s32[1024]{0:T(1024)S(1)} %pad_clamp_fusion), kind=kCustom, calls=%fused_computation | custom fusion | bytes 1048832 | tf_op jit(solution)/shard_map/jit(_take)/gather | solution.py:108
  60.5 5.9 %fusion = f32[64,16,256]{2,1,0:T(8,128)S(1)} fusion(bf16[64,2,256,256]{3,2,1,0:T(8,128)(2,1)} %param.11, bf16[64,16,256]{2,1,0:T(8,128)(2,1)} %gather_fusion, pred[64]{0:T(512)(128)(4,1)S(1)} %get-tuple-element.5), kind=kOutput, calls=%fused_computation.1 | convolution fusion | flops 134479872 | bytes 9961536 | tf_op jit(solution)/shard_map/lpq,slq->slp/dot_general | solution.py:112
  66.3 1.1 %fusion.30 = f32[8,128,32]{1,2,0:T(8,128)S(1)} fusion(f32[32,8,128]{2,0,1:T(8,128)S(1)} %fusion.13, f32[8,2,32,32]{3,2,0,1:T(8,128)} %bitcast.142), kind=kOutput, calls=%fused_computation.60 | convolution fusion | flops 6291456 | bytes 393216 | tf_op jit(solution)/shard_map/gab,bgm->agm/dot_general | solution.py:64
  67.5 1.2 %fusion.12 = f32[32,8,128]{2,0,1:T(8,128)S(1)} fusion(f32[8,128,32]{1,2,0:T(8,128)S(1)} %fusion.30, f32[32,8,128]{2,0,1:T(8,128)} %collective-permute-done.1, f32[8,2,32,32]{3,2,0,1:T(8,128)} %bitcast.143), kind=kOutput, calls=%fused_computation.20 | convolution fusion | flops 6324224 | bytes 524288 | tf_op jit(solution)/shard_map/gab,bgm->agm/dot_general | solution.py:71
  68.6 4.7 %collective-permute-start.2 = (f32[32,8,128]{2,0,1:T(8,128)S(1)}, f32[32,8,128]{2,0,1:T(8,128)S(1)}, u32[]{:S(2)}, u32[]{:S(2)}) collective-permute-start(f32[32,8,128]{2,0,1:T(8,128)S(1)} %fusion.12), channel_id=1, source_target_pairs={{0,4},{1,5},{2,6},{3,7},{4,0},{5,1},{6,2},{7,3},{8,12},{9,13},{10,... | collective-permute-start | bytes 393224 | tf_op jit(solution)/shard_map/ppermute | solution.py:47
  74.4 1.9 %collective-permute-done.2 = f32[32,8,128]{2,0,1:T(8,128)S(1)} collective-permute-done((f32[32,8,128]{2,0,1:T(8,128)S(1)}, f32[32,8,128]{2,0,1:T(8,128)S(1)}, u32[]{:S(2)}, u32[]{:S(2)}) %collective-permute-start.2) | collective-permute-done | bytes 131104 | tf_op jit(solution)/shard_map/ppermute | solution.py:47
  77.5 1.1 %fusion.28 = f32[8,128,32]{1,2,0:T(8,128)S(1)} fusion(f32[32,8,128]{2,0,1:T(8,128)S(1)} %fusion.11, f32[8,2,32,32]{3,2,0,1:T(8,128)} %bitcast.138), kind=kOutput, calls=%fused_computation.54 | convolution fusion | flops 6291456 | bytes 393216 | tf_op jit(solution)/shard_map/gab,bgm->agm/dot_general | solution.py:64
  78.9 1.1 %fusion.10 = f32[32,8,128]{2,0,1:T(8,128)S(1)} fusion(f32[8,128,32]{1,2,0:T(8,128)S(1)} %fusion.28, f32[32,8,128]{2,0,1:T(8,128)S(1)} %collective-permute-done.3, f32[8,2,32,32]{3,2,0,1:T(8,128)} %bitcast.139), kind=kOutput, calls=%fused_computation.16 | convolution fusion | flops 6324224 | bytes 524288 | tf_op jit(solution)/shard_map/gab,bgm->agm/dot_general | solution.py:71
  80.0 1.3 %collective-permute-start.4 = (f32[32,8,128]{2,0,1:T(8,128)S(1)}, f32[32,8,128]{2,0,1:T(8,128)S(1)}, u32[]{:S(2)}, u32[]{:S(2)}) collective-permute-start(f32[32,8,128]{2,0,1:T(8,128)S(1)} %fusion.10), channel_id=1, source_target_pairs={{0,16},{8,24},{16,0},{24,8},{32,48},{40,56},{48,32},{56,40},{64,80... | collective-permute-start | bytes 393224 | tf_op jit(solution)/shard_map/ppermute | solution.py:47
  82.4 3.4 %collective-permute-done.4 = f32[32,8,128]{2,0,1:T(8,128)S(1)} collective-permute-done((f32[32,8,128]{2,0,1:T(8,128)S(1)}, f32[32,8,128]{2,0,1:T(8,128)S(1)}, u32[]{:S(2)}, u32[]{:S(2)}) %collective-permute-start.4) | collective-permute-done | bytes 131104 | tf_op jit(solution)/shard_map/ppermute | solution.py:47
  85.7 1.1 %fusion.9 = f32[32,8,128]{2,0,1:T(8,128)S(1)} fusion(f32[8,128,32]{1,2,0:T(8,128)S(1)} %fusion.27, f32[32,8,128]{2,0,1:T(8,128)S(1)} %collective-permute-done.4, f32[8,2,32,32]{3,2,0,1:T(8,128)} %bitcast.137), kind=kOutput, calls=%fused_computation.14 | convolution fusion | flops 6324224 | bytes 524288 | tf_op jit(solution)/shard_map/gab,bgm->agm/dot_general | solution.py:71
  86.8 1.6 %collective-permute-start.5 = (f32[32,8,128]{2,0,1:T(8,128)S(1)}, f32[32,8,128]{2,0,1:T(8,128)S(1)}, u32[]{:S(2)}, u32[]{:S(2)}) collective-permute-start(f32[32,8,128]{2,0,1:T(8,128)S(1)} %fusion.9), channel_id=1, source_target_pairs={{0,32},{8,40},{16,48},{24,56},{32,0},{40,8},{48,16},{56,24},{64,96... | collective-permute-start | bytes 393224 | tf_op jit(solution)/shard_map/ppermute | solution.py:47
  89.5 2.4 %collective-permute-done.5 = f32[32,8,128]{2,0,1:T(8,128)S(1)} collective-permute-done((f32[32,8,128]{2,0,1:T(8,128)S(1)}, f32[32,8,128]{2,0,1:T(8,128)S(1)}, u32[]{:S(2)}, u32[]{:S(2)}) %collective-permute-start.5) | collective-permute-done | bytes 131104 | tf_op jit(solution)/shard_map/ppermute | solution.py:47
  93.0 3.1 %collective-permute-start.6 = (f32[32,8,128]{2,0,1:T(8,128)S(1)}, f32[32,8,128]{2,0,1:T(8,128)S(1)}, u32[]{:S(2)}, u32[]{:S(2)}) collective-permute-start(f32[32,8,128]{2,0,1:T(8,128)S(1)} %fusion.8), channel_id=1, source_target_pairs={{0,64},{8,72},{16,80},{24,88},{32,96},{40,104},{48,112},{56,120},{... | collective-permute-start | bytes 393224 | tf_op jit(solution)/shard_map/ppermute | solution.py:47
  96.3 3.2 %collective-permute-done.6 = f32[32,8,128]{2,0,1:T(8,128)S(1)} collective-permute-done((f32[32,8,128]{2,0,1:T(8,128)S(1)}, f32[32,8,128]{2,0,1:T(8,128)S(1)}, u32[]{:S(2)}, u32[]{:S(2)}) %collective-permute-start.6) | collective-permute-done | bytes 131104 | tf_op jit(solution)/shard_map/ppermute | solution.py:47
  (38 shorter events, 13.3 us)
Async XLA Ops:
  0.0 99.9 %copy-start = (bf16[64,32,256]{2,1,0:T(8,128)(2,1)S(1)}, bf16[64,32,256]{2,1,0:T(8,128)(2,1)}, u32[]{:S(2)}) copy-start(bf16[64,32,256]{2,1,0:T(8,128)(2,1)} %param.13) | copy-start | bytes 3145732
  0.0 1.3 %copy-start.1 = (f32[16,16384]{1,0:T(8,128)S(1)}, f32[16,16384]{1,0:T(8,128)}, u32[]{:S(2)}) copy-start(f32[16,16384]{1,0:T(8,128)} %x_ref.1) | copy-start | bytes 3145732
  1.3 0.8 copy-start.2
  36.4 13.4 %copy-start.3 = (s32[64]{0:T(128)S(1)}, s32[64]{0:T(128)}, u32[]{:S(2)}) copy-start(s32[64]{0:T(128)} %param.9) | copy-start | bytes 772
  36.5 16.9 %collective-permute-start = (f32[32,8,128]{2,0,1:T(8,128)S(1)}, f32[32,8,128]{2,0,1:T(8,128)S(1)}, u32[]{:S(2)}, u32[]{:S(2)}) collective-permute-start(f32[32,8,128]{2,0,1:T(8,128)S(1)} %copy.24), channel_id=1, source_target_pairs={{0,1},{1,0},{2,3},{3,2},{4,5},{5,4},{6,7},{7,6},{8,9},{9,8},{10,11... | collective-permute-start | bytes 393224 | tf_op jit(solution)/shard_map/ppermute | solution.py:47
  38.3 20.6 %collective-permute-start.7 = (bf16[16,4096]{1,0:T(8,128)(2,1)S(1)}, bf16[16,4096]{1,0:T(8,128)(2,1)S(1)}, u32[]{:S(2)}, u32[]{:S(2)}) collective-permute-start(bf16[16,4096]{1,0:T(8,128)(2,1)S(1)} %get-tuple-element.14), channel_id=1, source_target_pairs={{0,1},{1,2},{2,3},{3,4},{4,5},{5,6},{6,7},{7,8},{8,9},{9,10},{10,1... | collective-permute-start | bytes 393224 | tf_op jit(solution)/shard_map/ppermute | solution.py:57
  40.6 18.4 %collective-permute-start.8 = (bf16[16,4096]{1,0:T(8,128)(2,1)S(1)}, bf16[16,4096]{1,0:T(8,128)(2,1)S(1)}, u32[]{:S(2)}, u32[]{:S(2)}) collective-permute-start(bf16[16,4096]{1,0:T(8,128)(2,1)S(1)} %get-tuple-element.15), channel_id=1, source_target_pairs={{1,0},{2,1},{3,2},{4,3},{5,4},{6,5},{7,6},{8,7},{9,8},{10,9},{11,1... | collective-permute-start | bytes 393224 | tf_op jit(solution)/shard_map/ppermute | solution.py:58
  53.7 13.8 %collective-permute-start.1 = (f32[32,8,128]{2,0,1:T(8,128)S(1)}, f32[32,8,128]{2,0,1:T(8,128)}, u32[]{:S(2)}, u32[]{:S(2)}) collective-permute-start(f32[32,8,128]{2,0,1:T(8,128)S(1)} %fusion.13), channel_id=1, source_target_pairs={{0,2},{1,3},{2,0},{3,1},{4,6},{5,7},{6,4},{7,5},{8,10},{9,11},{10,... | collective-permute-start | bytes 393224 | tf_op jit(solution)/shard_map/ppermute | solution.py:47
  68.6 7.7 %collective-permute-start.2 = (f32[32,8,128]{2,0,1:T(8,128)S(1)}, f32[32,8,128]{2,0,1:T(8,128)S(1)}, u32[]{:S(2)}, u32[]{:S(2)}) collective-permute-start(f32[32,8,128]{2,0,1:T(8,128)S(1)} %fusion.12), channel_id=1, source_target_pairs={{0,4},{1,5},{2,6},{3,7},{4,0},{5,1},{6,2},{7,3},{8,12},{9,13},{10,... | collective-permute-start | bytes 393224 | tf_op jit(solution)/shard_map/ppermute | solution.py:47
  77.4 1.4 %collective-permute-start.3 = (f32[32,8,128]{2,0,1:T(8,128)S(1)}, f32[32,8,128]{2,0,1:T(8,128)S(1)}, u32[]{:S(2)}, u32[]{:S(2)}) collective-permute-start(f32[32,8,128]{2,0,1:T(8,128)S(1)} %fusion.11), channel_id=1, source_target_pairs={{0,8},{8,0},{16,24},{24,16},{32,40},{40,32},{48,56},{56,48},{64,72... | collective-permute-start | bytes 393224 | tf_op jit(solution)/shard_map/ppermute | solution.py:47
  80.0 5.8 %collective-permute-start.4 = (f32[32,8,128]{2,0,1:T(8,128)S(1)}, f32[32,8,128]{2,0,1:T(8,128)S(1)}, u32[]{:S(2)}, u32[]{:S(2)}) collective-permute-start(f32[32,8,128]{2,0,1:T(8,128)S(1)} %fusion.10), channel_id=1, source_target_pairs={{0,16},{8,24},{16,0},{24,8},{32,48},{40,56},{48,32},{56,40},{64,80... | collective-permute-start | bytes 393224 | tf_op jit(solution)/shard_map/ppermute | solution.py:47
  86.8 5.0 %collective-permute-start.5 = (f32[32,8,128]{2,0,1:T(8,128)S(1)}, f32[32,8,128]{2,0,1:T(8,128)S(1)}, u32[]{:S(2)}, u32[]{:S(2)}) collective-permute-start(f32[32,8,128]{2,0,1:T(8,128)S(1)} %fusion.9), channel_id=1, source_target_pairs={{0,32},{8,40},{16,48},{24,56},{32,0},{40,8},{48,16},{56,24},{64,96... | collective-permute-start | bytes 393224 | tf_op jit(solution)/shard_map/ppermute | solution.py:47
  93.0 6.6 %collective-permute-start.6 = (f32[32,8,128]{2,0,1:T(8,128)S(1)}, f32[32,8,128]{2,0,1:T(8,128)S(1)}, u32[]{:S(2)}, u32[]{:S(2)}) collective-permute-start(f32[32,8,128]{2,0,1:T(8,128)S(1)} %fusion.8), channel_id=1, source_target_pairs={{0,64},{8,72},{16,80},{24,88},{32,96},{40,104},{48,112},{56,120},{... | collective-permute-start | bytes 393224 | tf_op jit(solution)/shard_map/ppermute | solution.py:47

commit v6 on v4

--- a/solution.py
+++ b/solution.py
@@ -60,17 +60,22 @@
     return x
 
 
+def block_diagonal(blocks):
+    groups, rank, _ = blocks.shape
+    eye = jnp.eye(groups, dtype=blocks.dtype)
+    spread = eye[:, None, :, None] * blocks[:, :, None, :]
+    return spread.reshape(groups * rank, groups * rank)
+
+
 def translate(level_weights, own_coeffs, other_coeffs):
-    first = jnp.einsum(
-        "gab,bgm->agm",
-        level_weights[:, 0],
+    first = jnp.dot(
+        block_diagonal(level_weights[:, 0]),
         own_coeffs,
         precision=lax.Precision.HIGHEST,
         preferred_element_type=jnp.float32,
     )
-    second = jnp.einsum(
-        "gab,bgm->agm",
-        level_weights[:, 1],
+    second = jnp.dot(
+        block_diagonal(level_weights[:, 1]),
         other_coeffs,
         precision=lax.Precision.HIGHEST,
         preferred_element_type=jnp.float32,
@@ -92,13 +97,15 @@
     weights = translations[0]
     low_bits = lax.axis_size("gy").bit_length() - 1
     high_bits = lax.axis_size("gx").bit_length() - 1
-    coeffs = coeffs.reshape(rank_size, group_total, group_width)
+    coeffs = coeffs.reshape(rank_size, group_total, group_width).transpose(1, 0, 2)
+    coeffs = coeffs.reshape(group_total * rank_size, group_width)
     for level_bit in range(low_bits):
         partner = from_partner(coeffs, "gy", level_bit)
         coeffs = translate(weights[level_bit], coeffs, partner)
     for level_bit in range(high_bits):
         partner = from_partner(coeffs, "gx", level_bit)
         coeffs = translate(weights[low_bits + level_bit], coeffs, partner)
+    coeffs = coeffs.reshape(group_total, rank_size, group_width).transpose(1, 0, 2)
     coeffs = coeffs.reshape(rank_size, total_cols)
     coeff_bf = coeffs.astype(jnp.bfloat16).reshape(rank_size, leaf_count, rhs_count)
     far_term = jnp.einsum("lrp,rls->slp", out_basis, coeff_bf, preferred_element_type=jnp.float32)

time: 103 us -> 133 us (1.29)
  local copies, waits for them, and re-layouts: 10.3 us -> 35.5 us
  other arithmetic: 0.08 us -> 5.12 us
  matrix products: 26.8 us -> 22.7 us
  waiting for transfers between devices: 10.9 us -> 13.7 us
    mul x0 -> x18, local copies, waits for them, and re-layouts: none -> 28.9 us  [block_diagonal(): spread = eye[:, None, :, None] * blocks[:, :, None, :]]
    dot_general x14, matrix products: 13.3 us -> 7.08 us  [the longest x7 4.45 us: translate(): jnp.dot(block_diagonal(level_weights[:, 1]), other_coeffs, precision=lax....]
    mul x0 -> x1, other arithmetic: none -> 5.03 us  [block_diagonal(): spread = eye[:, None, :, None] * blocks[:, :, None, :]]
    unnamed x15 -> x32, local copies, waits for them, and re-layouts: 5.83 us -> 2.21 us
    ppermute x7, waiting for transfers between devices: 10.9 us -> 13.7 us  [from_partner(): lax.ppermute(x, axis, [(i, i ^ 1 << distance) for i in range(lax.axis_siz...]
    slice x1 -> x0, local copies, waits for them, and re-layouts: 1.63 us -> none  [local(): coeffs = translate(weights[low_bits + level_bit], coeffs, partner)]
    squeeze x0 -> x1, local copies, waits for them, and re-layouts: none -> 1.63 us  [local(): coeffs = translate(weights[level_bit], coeffs, partner)]
  transfers between devices with their start and end apart: 9 -> 9, of which waited for: 5 -> 5; matrix products, arithmetic and copies ran while one was open for 25% -> 41% of each run, Pallas kernels for 0% -> 0%
where the time goes in v6:
time: 133 us; the launch traced here: 132 us
  local copies, waits for them, and re-layouts  35.5 us (27%)
  Pallas kernels  32.6 us (25%)
  matrix products  22.7 us (17%)
  starting transfers between devices  21.5 us (16%)
  waiting for transfers between devices  13.7 us (10%)
  other arithmetic  5.12 us (4%)
    pallas_call x1, Pallas kernels, gather_points(): pl.pallas_call(gather_kernel, out_shape=jax.ShapeDtypeStruct((width, coun...  32.6 us
    mul x18, local copies, waits for them, and re-layouts, block_diagonal(): spread = eye[:, None, :, None] * blocks[:, :, None, :]  28.9 us
    ppermute x7, starting transfers between devices, from_partner(): lax.ppermute(x, axis, [(i, i ^ 1 << distance) for i in range(lax.axis_siz...  17.9 us
    ppermute x7, waiting for transfers between devices, from_partner(): lax.ppermute(x, axis, [(i, i ^ 1 << distance) for i in range(lax.axis_siz...  13.7 us
    dot_general x1, matrix products, local(): jnp.einsum('lpq,slq->slp', band_blocks[:, 1], picked, preferred_element_t...  6.82 us
    dot_general x1, matrix products, local(): jnp.einsum('lpq,slq->slp', band_blocks[:, 0], leaves, preferred_element_t...  5.67 us
    mul x1, other arithmetic, block_diagonal(): spread = eye[:, None, :, None] * blocks[:, :, None, :]  5.03 us
    dot_general x7, matrix products, translate(): jnp.dot(block_diagonal(level_weights[:, 1]), other_coeffs, precision=lax....  4.45 us
  transfers between devices with their start and end apart: 9, of which 5 were waited for; matrix products, arithmetic and copies ran while one was open for 41% of the time, Pallas kernels for 0%

profile of v6, /device:TPU:0, one launch (start us, length us, event | category | flops | bytes accessed | tf_op | source)
XLA Modules:
  0.0 131.5 jit_solution(18057301648390971151)
XLA Ops:
  2.2 32.6 %shard_map.73 = bf16[16,16384]{1,0:T(8,128)(2,1)S(1)} custom-call(s32[16384]{0:T(1024)S(1)} %copy-done.2, f32[16,16384]{1,0:T(8,128)S(1)} %copy-done.1), custom_call_target="tpu_custom_call" | custom-call | bytes 1572864 | tf_op jit(solution)/shard_map/pallas_call | solution.py:35
  39.0 2.2 %collective-permute-start.7 = (bf16[16,4096]{1,0:T(8,128)(2,1)}, bf16[16,4096]{1,0:T(8,128)(2,1)S(1)}, u32[]{:S(2)}, u32[]{:S(2)}) collective-permute-start(bf16[16,4096]{1,0:T(8,128)(2,1)} %get-tuple-element.14), channel_id=1, source_target_pairs={{0,1},{1,2},{2,3},{3,4},{4,5},{5,6},{6,7},{7,8},{8,9},{9,10},{10,1... | collective-permute-start | bytes 393224 | tf_op jit(solution)/shard_map/ppermute | solution.py:57
  44.4 5.0 %broadcast_multiply_fusion = (f32[8,32,8,32]{3,2,1,0:T(8,128)}, f32[8,32,8,32]{3,2,1,0:T(8,128)}, f32[8,32,8,32]{3,2,1,0:T(8,128)}, f32[8,32,8,32]{3,2,1,0:T(8,1...) fusion(f32[8,32,32]{2,1,0:T(8,128)S(1)} %get-tuple-element.16, ...), kind=kLoop, calls=%fused_computation.25 | loop fusion | flops 917504 | bytes 4129024 | tf_op jit(solution)/shard_map/mul | solution.py:66
  50.1 5.7 %fusion.2 = f32[64,16,256]{2,1,0:T(8,128)S(1)} fusion(bf16[64,2,256,256]{3,2,1,0:T(8,128)(2,1)} %param.11, bf16[2,64,8,256]{3,2,1,0:T(8,128)(2,1)S(1)} %bitcast.139), kind=kOutput, calls=%fused_computation.3 | convolution fusion | flops 134217728 | bytes 9961472 | tf_op jit(solution)/shard_map/lpq,slq->slp/dot_general | solution.py:116
  57.4 2.2 %mul.296 = f32[256,256]{1,0:T(8,128)} reshape(f32[8,32,8,32]{3,2,1,0:T(8,128)} %get-tuple-element.35) | data formatting | bytes 524288 | tf_op jit(solution)/shard_map/mul | solution.py:66
  59.6 2.2 %mul.308 = f32[256,256]{1,0:T(8,128)} reshape(f32[8,32,8,32]{3,2,1,0:T(8,128)} %get-tuple-element.38) | data formatting | bytes 524288 | tf_op jit(solution)/shard_map/mul | solution.py:66
  61.9 2.2 %mul.292 = f32[256,256]{1,0:T(8,128)} reshape(f32[8,32,8,32]{3,2,1,0:T(8,128)} %get-tuple-element.34) | data formatting | bytes 524288 | tf_op jit(solution)/shard_map/mul | solution.py:66
  64.1 2.2 %mul.312 = f32[256,256]{1,0:T(8,128)} reshape(f32[8,32,8,32]{3,2,1,0:T(8,128)} %get-tuple-element.39) | data formatting | bytes 524288 | tf_op jit(solution)/shard_map/mul | solution.py:66
  66.3 2.3 %mul.288 = f32[256,256]{1,0:T(8,128)} reshape(f32[8,32,8,32]{3,2,1,0:T(8,128)} %get-tuple-element.33) | data formatting | bytes 524288 | tf_op jit(solution)/shard_map/mul | solution.py:66
  68.6 2.3 %mul.316 = f32[256,256]{1,0:T(8,128)} reshape(f32[8,32,8,32]{3,2,1,0:T(8,128)} %get-tuple-element.40) | data formatting | bytes 524288 | tf_op jit(solution)/shard_map/mul | solution.py:66
  70.9 2.2 %mul.284 = f32[256,256]{1,0:T(8,128)} reshape(f32[8,32,8,32]{3,2,1,0:T(8,128)} %get-tuple-element.32) | data formatting | bytes 524288 | tf_op jit(solution)/shard_map/mul | solution.py:66
  73.1 2.2 %mul.320 = f32[256,256]{1,0:T(8,128)} reshape(f32[8,32,8,32]{3,2,1,0:T(8,128)} %get-tuple-element.41) | data formatting | bytes 524288 | tf_op jit(solution)/shard_map/mul | solution.py:66
  75.4 2.2 %mul.280 = f32[256,256]{1,0:T(8,128)} reshape(f32[8,32,8,32]{3,2,1,0:T(8,128)} %get-tuple-element.31) | data formatting | bytes 524288 | tf_op jit(solution)/shard_map/mul | solution.py:66
  77.6 2.2 %mul.324 = f32[256,256]{1,0:T(8,128)} reshape(f32[8,32,8,32]{3,2,1,0:T(8,128)} %get-tuple-element.42) | data formatting | bytes 524288 | tf_op jit(solution)/shard_map/mul | solution.py:66
  79.8 2.2 %mul.276 = f32[256,256]{1,0:T(8,128)} reshape(f32[8,32,8,32]{3,2,1,0:T(8,128)} %get-tuple-element.43) | data formatting | bytes 524288 | tf_op jit(solution)/shard_map/mul | solution.py:66
  82.1 2.2 %mul.328 = f32[256,256]{1,0:T(8,128)} reshape(f32[8,32,8,32]{3,2,1,0:T(8,128)} %get-tuple-element.30) | data formatting | bytes 524288 | tf_op jit(solution)/shard_map/mul | solution.py:66
  85.6 5.3 %collective-permute-start.1 = (f32[256,128]{1,0:T(8,128)S(1)}, f32[256,128]{1,0:T(8,128)}, u32[]{:S(2)}, u32[]{:S(2)}) collective-permute-start(f32[256,128]{1,0:T(8,128)S(1)} %convolution_add_fusion.7), channel_id=1, source_target_pairs={{0,2},{1,3},{2,0},{3,1},{4,6},{5,7},{6,4},{7,5},{8,10},{9,11},{10,... | collective-permute-start | bytes 393224 | tf_op jit(solution)/shard_map/ppermute | solution.py:47
  91.7 6.8 %fusion = f32[64,16,256]{2,1,0:T(8,128)} fusion(bf16[64,2,256,256]{3,2,1,0:T(8,128)(2,1)} %param.11, bf16[64,16,256]{2,1,0:T(8,128)(2,1)S(1)} %gather_fusion, pred[64]{0:T(512)(128)(4,1)S(1)} %get-tuple-element.5), kind=kOutput, calls=%fused_computation.1 | convolution fusion | flops 134479872 | bytes 9961536 | tf_op jit(solution)/shard_map/lpq,slq->slp/dot_general | solution.py:119
  100.3 4.9 %collective-permute-start.2 = (f32[256,128]{1,0:T(8,128)S(1)}, f32[256,128]{1,0:T(8,128)S(1)}, u32[]{:S(2)}, u32[]{:S(2)}) collective-permute-start(f32[256,128]{1,0:T(8,128)S(1)} %convolution_add_fusion.6), channel_id=1, source_target_pairs={{0,4},{1,5},{2,6},{3,7},{4,0},{5,1},{6,2},{7,3},{8,12},{9,13},{10,... | collective-permute-start | bytes 393224 | tf_op jit(solution)/shard_map/ppermute | solution.py:47
  105.5 2.6 %collective-permute-done.2 = f32[256,128]{1,0:T(8,128)S(1)} collective-permute-done((f32[256,128]{1,0:T(8,128)S(1)}, f32[256,128]{1,0:T(8,128)S(1)}, u32[]{:S(2)}, u32[]{:S(2)}) %collective-permute-start.2) | collective-permute-done | bytes 131104 | tf_op jit(solution)/shard_map/ppermute | solution.py:47
  112.0 4.0 %collective-permute-done.4 = f32[256,128]{1,0:T(8,128)S(1)} collective-permute-done((f32[256,128]{1,0:T(8,128)S(1)}, f32[256,128]{1,0:T(8,128)S(1)}, u32[]{:S(2)}, u32[]{:S(2)}) %collective-permute-start.4) | collective-permute-done | bytes 131104 | tf_op jit(solution)/shard_map/ppermute | solution.py:47
  118.3 3.1 %collective-permute-done.5 = f32[256,128]{1,0:T(8,128)S(1)} collective-permute-done((f32[256,128]{1,0:T(8,128)S(1)}, f32[256,128]{1,0:T(8,128)S(1)}, u32[]{:S(2)}, u32[]{:S(2)}) %collective-permute-start.5) | collective-permute-done | bytes 131104 | tf_op jit(solution)/shard_map/ppermute | solution.py:47
  121.8 3.1 %collective-permute-start.6 = (f32[256,128]{1,0:T(8,128)S(1)}, f32[256,128]{1,0:T(8,128)S(1)}, u32[]{:S(2)}, u32[]{:S(2)}) collective-permute-start(f32[256,128]{1,0:T(8,128)S(1)} %convolution_add_fusion.2), channel_id=1, source_target_pairs={{0,64},{8,72},{16,80},{24,88},{32,96},{40,104},{48,112},{56,120},{... | collective-permute-start | bytes 393224 | tf_op jit(solution)/shard_map/ppermute | solution.py:47
  125.3 3.1 %collective-permute-done.6 = f32[256,128]{1,0:T(8,128)S(1)} collective-permute-done((f32[256,128]{1,0:T(8,128)S(1)}, f32[256,128]{1,0:T(8,128)S(1)}, u32[]{:S(2)}, u32[]{:S(2)}) %collective-permute-start.6) | collective-permute-done | bytes 131104 | tf_op jit(solution)/shard_map/ppermute | solution.py:47
  (75 shorter events, 25.8 us)
Async XLA Ops:
  0.0 128.9 %copy-start = (bf16[64,32,256]{2,1,0:T(8,128)(2,1)S(1)}, bf16[64,32,256]{2,1,0:T(8,128)(2,1)}, u32[]{:S(2)}) copy-start(bf16[64,32,256]{2,1,0:T(8,128)(2,1)} %param.13) | copy-start | bytes 3145732
  0.0 1.3 copy-start.1
  36.5 47.8 %collective-permute-start = (f32[256,128]{1,0:T(8,128)S(1)}, f32[256,128]{1,0:T(8,128)}, u32[]{:S(2)}, u32[]{:S(2)}) collective-permute-start(f32[256,128]{1,0:T(8,128)S(1)} %bitcast.144), channel_id=1, source_target_pairs={{0,1},{1,0},{2,3},{3,2},{4,5},{5,4},{6,7},{7,6},{8,9},{9,8},{10,11... | collective-permute-start | bytes 393224 | tf_op jit(solution)/shard_map/ppermute | solution.py:47
  39.0 51.9 %collective-permute-start.7 = (bf16[16,4096]{1,0:T(8,128)(2,1)}, bf16[16,4096]{1,0:T(8,128)(2,1)S(1)}, u32[]{:S(2)}, u32[]{:S(2)}) collective-permute-start(bf16[16,4096]{1,0:T(8,128)(2,1)} %get-tuple-element.14), channel_id=1, source_target_pairs={{0,1},{1,2},{2,3},{3,4},{4,5},{5,6},{6,7},{7,8},{8,9},{9,10},{10,1... | collective-permute-start | bytes 393224 | tf_op jit(solution)/shard_map/ppermute | solution.py:57
  41.3 49.6 %collective-permute-start.8 = (bf16[16,4096]{1,0:T(8,128)(2,1)}, bf16[16,4096]{1,0:T(8,128)(2,1)S(1)}, u32[]{:S(2)}, u32[]{:S(2)}) collective-permute-start(bf16[16,4096]{1,0:T(8,128)(2,1)} %get-tuple-element.15), channel_id=1, source_target_pairs={{1,0},{2,1},{3,2},{4,3},{5,4},{6,5},{7,6},{8,7},{9,8},{10,9},{11,1... | collective-permute-start | bytes 393224 | tf_op jit(solution)/shard_map/ppermute | solution.py:58
  49.4 6.4 %copy-start.15 = (s32[64]{0:T(128)S(1)}, s32[64]{0:T(128)}, u32[]{:S(2)}) copy-start(s32[64]{0:T(128)} %param.9) | copy-start | bytes 772
  85.6 13.3 %collective-permute-start.1 = (f32[256,128]{1,0:T(8,128)S(1)}, f32[256,128]{1,0:T(8,128)}, u32[]{:S(2)}, u32[]{:S(2)}) collective-permute-start(f32[256,128]{1,0:T(8,128)S(1)} %convolution_add_fusion.7), channel_id=1, source_target_pairs={{0,2},{1,3},{2,0},{3,1},{4,6},{5,7},{6,4},{7,5},{8,10},{9,11},{10,... | collective-permute-start | bytes 393224 | tf_op jit(solution)/shard_map/ppermute | solution.py:47
  91.6 6.9 %copy-start.14 = (f32[256,256]{1,0:T(8,128)S(1)}, f32[256,256]{1,0:T(8,128)}, u32[]{:S(2)}) copy-start(f32[256,256]{1,0:T(8,128)} %mul.296) | copy-start | bytes 786436
  91.6 7.3 %copy-start.13 = (f32[256,256]{1,0:T(8,128)S(1)}, f32[256,256]{1,0:T(8,128)}, u32[]{:S(2)}) copy-start(f32[256,256]{1,0:T(8,128)} %mul.308) | copy-start | bytes 786436
  91.6 13.5 %copy-start.12 = (f32[256,256]{1,0:T(8,128)S(1)}, f32[256,256]{1,0:T(8,128)}, u32[]{:S(2)}) copy-start(f32[256,256]{1,0:T(8,128)} %mul.292) | copy-start | bytes 786436
  91.7 16.5 %copy-start.11 = (f32[256,256]{1,0:T(8,128)S(1)}, f32[256,256]{1,0:T(8,128)}, u32[]{:S(2)}) copy-start(f32[256,256]{1,0:T(8,128)} %mul.312) | copy-start | bytes 786436
  91.7 17.0 %copy-start.10 = (f32[256,256]{1,0:T(8,128)S(1)}, f32[256,256]{1,0:T(8,128)}, u32[]{:S(2)}) copy-start(f32[256,256]{1,0:T(8,128)} %mul.288) | copy-start | bytes 786436
  91.7 18.3 %copy-start.9 = (f32[256,256]{1,0:T(8,128)S(1)}, f32[256,256]{1,0:T(8,128)}, u32[]{:S(2)}) copy-start(f32[256,256]{1,0:T(8,128)} %mul.316) | copy-start | bytes 786436
  91.7 20.0 %copy-start.8 = (f32[256,256]{1,0:T(8,128)S(1)}, f32[256,256]{1,0:T(8,128)}, u32[]{:S(2)}) copy-start(f32[256,256]{1,0:T(8,128)} %mul.284) | copy-start | bytes 786436
  91.7 24.3 %copy-start.7 = (f32[256,256]{1,0:T(8,128)S(1)}, f32[256,256]{1,0:T(8,128)}, u32[]{:S(2)}) copy-start(f32[256,256]{1,0:T(8,128)} %mul.320) | copy-start | bytes 786436
  91.7 26.2 %copy-start.6 = (f32[256,256]{1,0:T(8,128)S(1)}, f32[256,256]{1,0:T(8,128)}, u32[]{:S(2)}) copy-start(f32[256,256]{1,0:T(8,128)} %mul.280) | copy-start | bytes 786436
  91.7 29.7 %copy-start.5 = (f32[256,256]{1,0:T(8,128)S(1)}, f32[256,256]{1,0:T(8,128)}, u32[]{:S(2)}) copy-start(f32[256,256]{1,0:T(8,128)} %mul.324) | copy-start | bytes 786436
  91.7 33.2 %copy-start.4 = (f32[256,256]{1,0:T(8,128)S(1)}, f32[256,256]{1,0:T(8,128)}, u32[]{:S(2)}) copy-start(f32[256,256]{1,0:T(8,128)} %mul.276) | copy-start | bytes 786436
  91.7 36.6 %copy-start.3 = (f32[256,256]{1,0:T(8,128)S(1)}, f32[256,256]{1,0:T(8,128)}, u32[]{:S(2)}) copy-start(f32[256,256]{1,0:T(8,128)} %mul.328) | copy-start | bytes 786436
  100.3 7.9 %collective-permute-start.2 = (f32[256,128]{1,0:T(8,128)S(1)}, f32[256,128]{1,0:T(8,128)S(1)}, u32[]{:S(2)}, u32[]{:S(2)}) collective-permute-start(f32[256,128]{1,0:T(8,128)S(1)} %convolution_add_fusion.6), channel_id=1, source_target_pairs={{0,4},{1,5},{2,6},{3,7},{4,0},{5,1},{6,2},{7,3},{8,12},{9,13},{10,... | collective-permute-start | bytes 393224 | tf_op jit(solution)/shard_map/ppermute | solution.py:47
  108.5 1.4 %collective-permute-start.3 = (f32[256,128]{1,0:T(8,128)S(1)}, f32[256,128]{1,0:T(8,128)S(1)}, u32[]{:S(2)}, u32[]{:S(2)}) collective-permute-start(f32[256,128]{1,0:T(8,128)S(1)} %convolution_add_fusion.5), channel_id=1, source_target_pairs={{0,8},{8,0},{16,24},{24,16},{32,40},{40,32},{48,56},{56,48},{64,72... | collective-permute-start | bytes 393224 | tf_op jit(solution)/shard_map/ppermute | solution.py:47
  110.4 5.6 %collective-permute-start.4 = (f32[256,128]{1,0:T(8,128)S(1)}, f32[256,128]{1,0:T(8,128)S(1)}, u32[]{:S(2)}, u32[]{:S(2)}) collective-permute-start(f32[256,128]{1,0:T(8,128)S(1)} %convolution_add_fusion.4), channel_id=1, source_target_pairs={{0,16},{8,24},{16,0},{24,8},{32,48},{40,56},{48,32},{56,40},{64,80... | collective-permute-start | bytes 393224 | tf_op jit(solution)/shard_map/ppermute | solution.py:47
  116.4 5.0 %collective-permute-start.5 = (f32[256,128]{1,0:T(8,128)S(1)}, f32[256,128]{1,0:T(8,128)S(1)}, u32[]{:S(2)}, u32[]{:S(2)}) collective-permute-start(f32[256,128]{1,0:T(8,128)S(1)} %convolution_add_fusion.3), channel_id=1, source_target_pairs={{0,32},{8,40},{16,48},{24,56},{32,0},{40,8},{48,16},{56,24},{64,96... | collective-permute-start | bytes 393224 | tf_op jit(solution)/shard_map/ppermute | solution.py:47
  121.8 6.6 %collective-permute-start.6 = (f32[256,128]{1,0:T(8,128)S(1)}, f32[256,128]{1,0:T(8,128)S(1)}, u32[]{:S(2)}, u32[]{:S(2)}) collective-permute-start(f32[256,128]{1,0:T(8,128)S(1)} %convolution_add_fusion.2), channel_id=1, source_target_pairs={{0,64},{8,72},{16,80},{24,88},{32,96},{40,104},{48,112},{56,120},{... | collective-permute-start | bytes 393224 | tf_op jit(solution)/shard_map/ppermute | solution.py:47
  (1 other events, 0.8 us)

commit v7 on v6

--- a/solution.py
+++ b/solution.py
@@ -60,22 +60,26 @@
     return x
 
 
-def block_diagonal(blocks):
-    groups, rank, _ = blocks.shape
-    eye = jnp.eye(groups, dtype=blocks.dtype)
-    spread = eye[:, None, :, None] * blocks[:, :, None, :]
-    return spread.reshape(groups * rank, groups * rank)
+def block_diagonals(weights):
+    levels, groups, terms, rank, _ = weights.shape
+    width = groups * rank
+    shape = (groups, rank, width)
+    target = lax.broadcasted_iota(jnp.int32, shape, 0) * rank + lax.broadcasted_iota(jnp.int32, shape, 1)
+    spread = (lax.broadcasted_iota(jnp.int32, shape, 2) == target).astype(weights.dtype)
+    return jnp.einsum(
+        "lgtab,gbc->ltgac", weights, spread, precision=lax.Precision.HIGHEST, preferred_element_type=jnp.float32
+    ).reshape(levels, terms, width, width)
 
 
-def translate(level_weights, own_coeffs, other_coeffs):
+def translate(level_matrices, own_coeffs, other_coeffs):
     first = jnp.dot(
-        block_diagonal(level_weights[:, 0]),
+        level_matrices[0],
         own_coeffs,
         precision=lax.Precision.HIGHEST,
         preferred_element_type=jnp.float32,
     )
     second = jnp.dot(
-        block_diagonal(level_weights[:, 1]),
+        level_matrices[1],
         other_coeffs,
         precision=lax.Precision.HIGHEST,
         preferred_element_type=jnp.float32,
@@ -94,7 +98,7 @@
     coeffs = jnp.einsum(
         "lrp,slp->rls", leaf_basis, leaves, preferred_element_type=jnp.float32
     ).reshape(rank_size, total_cols)
-    weights = translations[0]
+    weights = block_diagonals(translations[0])
     low_bits = lax.axis_size("gy").bit_length() - 1
     high_bits = lax.axis_size("gx").bit_length() - 1
     coeffs = coeffs.reshape(rank_size, group_total, group_width).transpose(1, 0, 2)

time: 133 us -> 100 us (0.75)
  local copies, waits for them, and re-layouts: 35.5 us -> 8.01 us
  other arithmetic: 5.12 us -> 0.08 us
    mul x18 -> x0, local copies, waits for them, and re-layouts: 28.9 us -> none  [block_diagonal(): spread = eye[:, None, :, None] * blocks[:, :, None, :]]
    mul x1, other arithmetic: 5.03 us -> 0.01 us  [block_diagonals(): lax.broadcasted_iota(jnp.int32, shape, 0) * rank]
    slice x0 -> x1, local copies, waits for them, and re-layouts: none -> 1.66 us  [translate(): level_matrices[1]]
    squeeze x1 -> x0, local copies, waits for them, and re-layouts: 1.63 us -> none  [local(): coeffs = translate(weights[level_bit], coeffs, partner)]
    dot_general x14 -> x15, matrix products: 7.08 us -> 7.91 us  [the longest x7 3.58 us: translate(): jnp.dot(level_matrices[1], other_coeffs, precision=lax.Precision.HIGHEST,...]
  transfers between devices with their start and end apart: 9 -> 9, of which waited for: 5 -> 5; matrix products, arithmetic and copies ran while one was open for 41% -> 22% of each run, Pallas kernels for 0% -> 0%
where the time goes in v7:
time: 100 us; the launch traced here: 99.8 us
  Pallas kernels  32.6 us (33%)
  matrix products  23.8 us (24%)
  starting transfers between devices  21.3 us (21%)
  waiting for transfers between devices  13.7 us (14%)
  local copies, waits for them, and re-layouts  8.01 us (8%)
    pallas_call x1, Pallas kernels, gather_points(): pl.pallas_call(gather_kernel, out_shape=jax.ShapeDtypeStruct((width, coun...  32.6 us
    ppermute x7, starting transfers between devices, from_partner(): lax.ppermute(x, axis, [(i, i ^ 1 << distance) for i in range(lax.axis_siz...  17.8 us
    ppermute x7, waiting for transfers between devices, from_partner(): lax.ppermute(x, axis, [(i, i ^ 1 << distance) for i in range(lax.axis_siz...  13.7 us
    dot_general x1, matrix products, local(): jnp.einsum('lpq,slq->slp', band_blocks[:, 1], picked, preferred_element_t...  6.78 us
    dot_general x1, matrix products, local(): jnp.einsum('lpq,slq->slp', band_blocks[:, 0], leaves, preferred_element_t...  5.67 us
    dot_general x7, matrix products, translate(): jnp.dot(level_matrices[1], other_coeffs, precision=lax.Precision.HIGHEST,...  3.58 us
    dot_general x7, matrix products, translate(): jnp.dot(level_matrices[0], own_coeffs, precision=lax.Precision.HIGHEST, p...  2.63 us
    unnamed x32, local copies, waits for them, and re-layouts  2.26 us
  transfers between devices with their start and end apart: 9, of which 5 were waited for; matrix products, arithmetic and copies ran while one was open for 22% of the time, Pallas kernels for 0%

profile of v7, /device:TPU:0, one launch (start us, length us, event | category | flops | bytes accessed | tf_op | source)
XLA Modules:
  0.0 99.8 jit_solution(3743104217286235644)
XLA Ops:
  0.0 1.4 %copy-done.1 = f32[16,16384]{1,0:T(8,128)S(1)} copy-done((f32[16,16384]{1,0:T(8,128)S(1)}, f32[16,16384]{1,0:T(8,128)}, u32[]{:S(2)}) %copy-start.1) | copy-done | bytes 1048600
  2.2 32.6 %shard_map.73 = bf16[16,16384]{1,0:T(8,128)(2,1)S(1)} custom-call(s32[16384]{0:T(1024)S(1)} %copy-done.2, f32[16,16384]{1,0:T(8,128)S(1)} %copy-done.1), custom_call_target="tpu_custom_call" | custom-call | bytes 1572864 | tf_op jit(solution)/shard_map/pallas_call | solution.py:35
  34.8 1.6 %fusion.11 = f32[64,16,32]{2,1,0:T(8,128)S(1)} fusion(bf16[64,32,256]{2,1,0:T(8,128)(2,1)} %param.10, bf16[2,64,8,256]{3,2,1,0:T(8,128)(2,1)S(1)} %bitcast.93), kind=kOutput, calls=%fused_computation.23 | convolution fusion | flops 16777216 | bytes 1703936 | tf_op jit(solution)/shard_map/lrp,slp->rls/dot_general | solution.py:98
  36.6 1.8 %collective-permute-start = (f32[256,128]{1,0:T(8,128)S(1)}, f32[256,128]{1,0:T(8,128)S(1)}, u32[]{:S(2)}, u32[]{:S(2)}) collective-permute-start(f32[256,128]{1,0:T(8,128)S(1)} %bitcast.113), channel_id=1, source_target_pairs={{0,1},{1,0},{2,3},{3,2},{4,5},{5,4},{6,7},{7,6},{8,9},{9,8},{10,11... | collective-permute-start | bytes 393224 | tf_op jit(solution)/shard_map/ppermute | solution.py:47
  38.4 2.2 %collective-permute-start.7 = (bf16[16,4096]{1,0:T(8,128)(2,1)S(1)}, bf16[16,4096]{1,0:T(8,128)(2,1)S(1)}, u32[]{:S(2)}, u32[]{:S(2)}) collective-permute-start(bf16[16,4096]{1,0:T(8,128)(2,1)S(1)} %get-tuple-element.21), channel_id=1, source_target_pairs={{0,1},{1,2},{2,3},{3,4},{4,5},{5,6},{6,7},{7,8},{8,9},{9,10},{10,1... | collective-permute-start | bytes 393224 | tf_op jit(solution)/shard_map/ppermute | solution.py:57
  40.6 1.3 %collective-permute-start.8 = (bf16[16,4096]{1,0:T(8,128)(2,1)S(1)}, bf16[16,4096]{1,0:T(8,128)(2,1)S(1)}, u32[]{:S(2)}, u32[]{:S(2)}) collective-permute-start(bf16[16,4096]{1,0:T(8,128)(2,1)S(1)} %get-tuple-element.22), channel_id=1, source_target_pairs={{1,0},{2,1},{3,2},{4,3},{5,4},{6,5},{7,6},{8,7},{9,8},{10,9},{11,1... | collective-permute-start | bytes 393224 | tf_op jit(solution)/shard_map/ppermute | solution.py:58
  41.9 1.7 %convolution_bitcast_fusion = f32[7,2,8,32,256]{4,3,1,0,2:T(8,128)S(1)} fusion(s32[8]{0:T(128)S(1)} %iota_multiply_fusion, f32[1,7,8,2,32,32]{5,4,3,2,1,0:T(8,128)S(1)} %copy-done), kind=kOutput, calls=%fused_computation.7 | convolution fusion | flops 352452608 | bytes 4128800 | tf_op jit(solution)/shard_map/lgtab,gbc->ltgac/dot_general | solution.py:69
  43.7 1.7 %fusion.23 = (f32[1,1,8,32,256]{4,3,1,0,2:T(8,128)}, f32[1,1,8,32,256]{4,3,1,0,2:T(8,128)}, f32[1,1,8,32,256]{4,3,1,0,2:T(8,128)}, f32[1,1,8,32,256]{4,3,1,0,2:T...) fusion(f32[7,2,8,32,256]{4,3,1,0,2:T(8,128)S(1)} %convolution_b, ...), kind=kLoop, calls=%fused_computation.39 | loop fusion | bytes 7340032 | tf_op jit(solution)/shard_map/slice | solution.py:82
  45.7 5.7 %fusion.2 = f32[64,16,256]{2,1,0:T(8,128)S(1)} fusion(bf16[64,2,256,256]{3,2,1,0:T(8,128)(2,1)} %param.11, bf16[2,64,8,256]{3,2,1,0:T(8,128)(2,1)S(1)} %bitcast.94), kind=kOutput, calls=%fused_computation.3 | convolution fusion | flops 134217728 | bytes 9961472 | tf_op jit(solution)/shard_map/lpq,slq->slp/dot_general | solution.py:120
  51.8 5.3 %collective-permute-start.1 = (f32[256,128]{1,0:T(8,128)S(1)}, f32[256,128]{1,0:T(8,128)}, u32[]{:S(2)}, u32[]{:S(2)}) collective-permute-start(f32[256,128]{1,0:T(8,128)S(1)} %convolution_add_fusion.7), channel_id=1, source_target_pairs={{0,2},{1,3},{2,0},{3,1},{4,6},{5,7},{6,4},{7,5},{8,10},{9,11},{10,... | collective-permute-start | bytes 393224 | tf_op jit(solution)/shard_map/ppermute | solution.py:47
  58.1 1.7 %gather_fusion = bf16[64,16,256]{2,1,0:T(8,128)(2,1)S(1)} fusion(bf16[16,96,256]{2,0,1:T(8,128)(2,1)} %bitcast.96, s32[1024]{0:T(1024)S(1)} %pad_clamp_fusion), kind=kCustom, calls=%fused_computation | custom fusion | bytes 1048832 | tf_op jit(solution)/shard_map/jit(_take)/gather | solution.py:119
  59.9 6.8 %fusion = f32[64,16,256]{2,1,0:T(8,128)} fusion(bf16[64,2,256,256]{3,2,1,0:T(8,128)(2,1)} %param.11, bf16[64,16,256]{2,1,0:T(8,128)(2,1)S(1)} %gather_fusion, pred[64]{0:T(512)(128)(4,1)S(1)} %get-tuple-element.5), kind=kOutput, calls=%fused_computation.1 | convolution fusion | flops 134479872 | bytes 9961536 | tf_op jit(solution)/shard_map/lpq,slq->slp/dot_general | solution.py:123
  67.1 1.3 %convolution_add_fusion.6 = f32[256,128]{1,0:T(8,128)S(1)} fusion(f32[256,128]{1,0:T(8,128)S(1)} %fusion.26, f32[256,256]{1,0:T(8,128)S(1)} %bitcast.109, f32[256,128]{1,0:T(8,128)} %collective-permute-done.1), kind=kOutput, calls=%fused_computation.17 | convolution fusion | flops 100696064 | bytes 655360 | tf_op jit(solution)/shard_map/dot_general | solution.py:81
  68.5 4.7 %collective-permute-start.2 = (f32[256,128]{1,0:T(8,128)S(1)}, f32[256,128]{1,0:T(8,128)S(1)}, u32[]{:S(2)}, u32[]{:S(2)}) collective-permute-start(f32[256,128]{1,0:T(8,128)S(1)} %convolution_add_fusion.6), channel_id=1, source_target_pairs={{0,4},{1,5},{2,6},{3,7},{4,0},{5,1},{6,2},{7,3},{8,12},{9,13},{10,... | collective-permute-start | bytes 393224 | tf_op jit(solution)/shard_map/ppermute | solution.py:47
  73.5 2.6 %collective-permute-done.2 = f32[256,128]{1,0:T(8,128)S(1)} collective-permute-done((f32[256,128]{1,0:T(8,128)S(1)}, f32[256,128]{1,0:T(8,128)S(1)}, u32[]{:S(2)}, u32[]{:S(2)}) %collective-permute-start.2) | collective-permute-done | bytes 131104 | tf_op jit(solution)/shard_map/ppermute | solution.py:47
  77.0 0.9 collective-permute-done.3
  78.4 1.3 %collective-permute-start.4 = (f32[256,128]{1,0:T(8,128)S(1)}, f32[256,128]{1,0:T(8,128)S(1)}, u32[]{:S(2)}, u32[]{:S(2)}) collective-permute-start(f32[256,128]{1,0:T(8,128)S(1)} %convolution_add_fusion.4), channel_id=1, source_target_pairs={{0,16},{8,24},{16,0},{24,8},{32,48},{40,56},{48,32},{56,40},{64,80... | collective-permute-start | bytes 393224 | tf_op jit(solution)/shard_map/ppermute | solution.py:47
  80.0 4.0 %collective-permute-done.4 = f32[256,128]{1,0:T(8,128)S(1)} collective-permute-done((f32[256,128]{1,0:T(8,128)S(1)}, f32[256,128]{1,0:T(8,128)S(1)}, u32[]{:S(2)}, u32[]{:S(2)}) %collective-permute-start.4) | collective-permute-done | bytes 131104 | tf_op jit(solution)/shard_map/ppermute | solution.py:47
  84.4 1.6 %collective-permute-start.5 = (f32[256,128]{1,0:T(8,128)S(1)}, f32[256,128]{1,0:T(8,128)S(1)}, u32[]{:S(2)}, u32[]{:S(2)}) collective-permute-start(f32[256,128]{1,0:T(8,128)S(1)} %convolution_add_fusion.3), channel_id=1, source_target_pairs={{0,32},{8,40},{16,48},{24,56},{32,0},{40,8},{48,16},{56,24},{64,96... | collective-permute-start | bytes 393224 | tf_op jit(solution)/shard_map/ppermute | solution.py:47
  86.3 3.1 %collective-permute-done.5 = f32[256,128]{1,0:T(8,128)S(1)} collective-permute-done((f32[256,128]{1,0:T(8,128)S(1)}, f32[256,128]{1,0:T(8,128)S(1)}, u32[]{:S(2)}, u32[]{:S(2)}) %collective-permute-start.5) | collective-permute-done | bytes 131104 | tf_op jit(solution)/shard_map/ppermute | solution.py:47
  89.8 3.1 %collective-permute-start.6 = (f32[256,128]{1,0:T(8,128)S(1)}, f32[256,128]{1,0:T(8,128)S(1)}, u32[]{:S(2)}, u32[]{:S(2)}) collective-permute-start(f32[256,128]{1,0:T(8,128)S(1)} %convolution_add_fusion.2), channel_id=1, source_target_pairs={{0,64},{8,72},{16,80},{24,88},{32,96},{40,104},{48,112},{56,120},{... | collective-permute-start | bytes 393224 | tf_op jit(solution)/shard_map/ppermute | solution.py:47
  93.3 3.1 %collective-permute-done.6 = f32[256,128]{1,0:T(8,128)S(1)} collective-permute-done((f32[256,128]{1,0:T(8,128)S(1)}, f32[256,128]{1,0:T(8,128)S(1)}, u32[]{:S(2)}, u32[]{:S(2)}) %collective-permute-start.6) | collective-permute-done | bytes 131104 | tf_op jit(solution)/shard_map/ppermute | solution.py:47
  96.9 1.8 %fusion.8 = f32[64,2,8,256]{3,2,1,0:T(8,128)S(1)} fusion(f32[64,16,256]{2,1,0:T(8,128)} %fusion, f32[64,16,256]{2,1,0:T(8,128)S(1)} %fusion.2, bf16[32,64,16]{0,2,1:T(8,128)(2,1)S(1)} %bitcast.98, bf16[64,32,256]{2,1,0:T(8,128)(2,1)} %param.13), kind=kOutput, calls=%fused_computation.11 | convolution fusion | flops 17301504 | bytes 4259840 | tf_op jit(solution)/shard_map/lrp,rls->slp/dot_general | solution.py:115
  98.8 1.1 %copy.28 = f32[64,2,8,256]{3,2,0,1:T(8,128)} copy(f32[64,2,8,256]{3,2,1,0:T(8,128)S(1)} %fusion.8) | data formatting | bytes 2097152 | tf_op jit(solution)/shard_map/reshape | solution.py:126
  (57 shorter events, 7.3 us)
Async XLA Ops:
  0.0 41.9 %copy-start = (f32[1,7,8,2,32,32]{5,4,3,2,1,0:T(8,128)S(1)}, f32[1,7,8,2,32,32]{5,4,3,2,1,0:T(8,128)}, u32[]{:S(2)}) copy-start(f32[1,7,8,2,32,32]{5,4,3,2,1,0:T(8,128)} %param.12) | copy-start | bytes 1376260
  0.0 1.4 %copy-start.1 = (f32[16,16384]{1,0:T(8,128)S(1)}, f32[16,16384]{1,0:T(8,128)}, u32[]{:S(2)}) copy-start(f32[16,16384]{1,0:T(8,128)} %x_ref.1) | copy-start | bytes 3145732
  36.6 14.8 %collective-permute-start = (f32[256,128]{1,0:T(8,128)S(1)}, f32[256,128]{1,0:T(8,128)S(1)}, u32[]{:S(2)}, u32[]{:S(2)}) collective-permute-start(f32[256,128]{1,0:T(8,128)S(1)} %bitcast.113), channel_id=1, source_target_pairs={{0,1},{1,0},{2,3},{3,2},{4,5},{5,4},{6,7},{7,6},{8,9},{9,8},{10,11... | collective-permute-start | bytes 393224 | tf_op jit(solution)/shard_map/ppermute | solution.py:47
  38.4 18.8 %collective-permute-start.7 = (bf16[16,4096]{1,0:T(8,128)(2,1)S(1)}, bf16[16,4096]{1,0:T(8,128)(2,1)S(1)}, u32[]{:S(2)}, u32[]{:S(2)}) collective-permute-start(bf16[16,4096]{1,0:T(8,128)(2,1)S(1)} %get-tuple-element.21), channel_id=1, source_target_pairs={{0,1},{1,2},{2,3},{3,4},{4,5},{5,6},{6,7},{7,8},{8,9},{9,10},{10,1... | collective-permute-start | bytes 393224 | tf_op jit(solution)/shard_map/ppermute | solution.py:57
  40.6 16.5 %collective-permute-start.8 = (bf16[16,4096]{1,0:T(8,128)(2,1)S(1)}, bf16[16,4096]{1,0:T(8,128)(2,1)S(1)}, u32[]{:S(2)}, u32[]{:S(2)}) collective-permute-start(bf16[16,4096]{1,0:T(8,128)(2,1)S(1)} %get-tuple-element.22), channel_id=1, source_target_pairs={{1,0},{2,1},{3,2},{4,3},{5,4},{6,5},{7,6},{8,7},{9,8},{10,9},{11,1... | collective-permute-start | bytes 393224 | tf_op jit(solution)/shard_map/ppermute | solution.py:58
  45.7 5.7 %copy-start.15 = (s32[64]{0:T(128)S(1)}, s32[64]{0:T(128)}, u32[]{:S(2)}) copy-start(s32[64]{0:T(128)} %param.9) | copy-start | bytes 772
  51.8 15.3 %collective-permute-start.1 = (f32[256,128]{1,0:T(8,128)S(1)}, f32[256,128]{1,0:T(8,128)}, u32[]{:S(2)}, u32[]{:S(2)}) collective-permute-start(f32[256,128]{1,0:T(8,128)S(1)} %convolution_add_fusion.7), channel_id=1, source_target_pairs={{0,2},{1,3},{2,0},{3,1},{4,6},{5,7},{6,4},{7,5},{8,10},{9,11},{10,... | collective-permute-start | bytes 393224 | tf_op jit(solution)/shard_map/ppermute | solution.py:47
  59.9 6.9 %copy-start.14 = (f32[1,1,8,32,256]{4,3,1,0,2:T(8,128)S(1)}, f32[1,1,8,32,256]{4,3,1,0,2:T(8,128)}, u32[]{:S(2)}) copy-start(f32[1,1,8,32,256]{4,3,1,0,2:T(8,128)} %get-tuple-element.15) | copy-start | bytes 786436
  59.9 7.3 %copy-start.13 = (f32[1,1,8,32,256]{4,3,1,0,2:T(8,128)S(1)}, f32[1,1,8,32,256]{4,3,1,0,2:T(8,128)}, u32[]{:S(2)}) copy-start(f32[1,1,8,32,256]{4,3,1,0,2:T(8,128)} %get-tuple-element.12) | copy-start | bytes 786436
  59.9 13.3 %copy-start.12 = (f32[1,1,8,32,256]{4,3,1,0,2:T(8,128)S(1)}, f32[1,1,8,32,256]{4,3,1,0,2:T(8,128)}, u32[]{:S(2)}) copy-start(f32[1,1,8,32,256]{4,3,1,0,2:T(8,128)} %get-tuple-element.16) | copy-start | bytes 786436
  59.9 16.3 %copy-start.11 = (f32[1,1,8,32,256]{4,3,1,0,2:T(8,128)S(1)}, f32[1,1,8,32,256]{4,3,1,0,2:T(8,128)}, u32[]{:S(2)}) copy-start(f32[1,1,8,32,256]{4,3,1,0,2:T(8,128)} %get-tuple-element.11) | copy-start | bytes 786436
  59.9 16.8 %copy-start.10 = (f32[1,1,8,32,256]{4,3,1,0,2:T(8,128)S(1)}, f32[1,1,8,32,256]{4,3,1,0,2:T(8,128)}, u32[]{:S(2)}) copy-start(f32[1,1,8,32,256]{4,3,1,0,2:T(8,128)} %get-tuple-element.17) | copy-start | bytes 786436
  59.9 18.1 %copy-start.9 = (f32[1,1,8,32,256]{4,3,1,0,2:T(8,128)S(1)}, f32[1,1,8,32,256]{4,3,1,0,2:T(8,128)}, u32[]{:S(2)}) copy-start(f32[1,1,8,32,256]{4,3,1,0,2:T(8,128)} %get-tuple-element.10) | copy-start | bytes 786436
  66.7 13.0 %copy-start.8 = (f32[1,1,8,32,256]{4,3,1,0,2:T(8,128)S(1)}, f32[1,1,8,32,256]{4,3,1,0,2:T(8,128)}, u32[]{:S(2)}) copy-start(f32[1,1,8,32,256]{4,3,1,0,2:T(8,128)} %get-tuple-element.18) | copy-start | bytes 786436
  66.7 17.3 %copy-start.7 = (f32[1,1,8,32,256]{4,3,1,0,2:T(8,128)S(1)}, f32[1,1,8,32,256]{4,3,1,0,2:T(8,128)}, u32[]{:S(2)}) copy-start(f32[1,1,8,32,256]{4,3,1,0,2:T(8,128)} %get-tuple-element.9) | copy-start | bytes 786436
  66.7 19.3 %copy-start.6 = (f32[1,1,8,32,256]{4,3,1,0,2:T(8,128)S(1)}, f32[1,1,8,32,256]{4,3,1,0,2:T(8,128)}, u32[]{:S(2)}) copy-start(f32[1,1,8,32,256]{4,3,1,0,2:T(8,128)} %get-tuple-element.19) | copy-start | bytes 786436
  66.7 22.7 %copy-start.5 = (f32[1,1,8,32,256]{4,3,1,0,2:T(8,128)S(1)}, f32[1,1,8,32,256]{4,3,1,0,2:T(8,128)}, u32[]{:S(2)}) copy-start(f32[1,1,8,32,256]{4,3,1,0,2:T(8,128)} %get-tuple-element.8) | copy-start | bytes 786436
  66.7 26.2 %copy-start.4 = (f32[1,1,8,32,256]{4,3,1,0,2:T(8,128)S(1)}, f32[1,1,8,32,256]{4,3,1,0,2:T(8,128)}, u32[]{:S(2)}) copy-start(f32[1,1,8,32,256]{4,3,1,0,2:T(8,128)} %get-tuple-element.20) | copy-start | bytes 786436
  66.7 29.7 %copy-start.3 = (f32[1,1,8,32,256]{4,3,1,0,2:T(8,128)S(1)}, f32[1,1,8,32,256]{4,3,1,0,2:T(8,128)}, u32[]{:S(2)}) copy-start(f32[1,1,8,32,256]{4,3,1,0,2:T(8,128)} %get-tuple-element.7) | copy-start | bytes 786436
  68.5 7.7 %collective-permute-start.2 = (f32[256,128]{1,0:T(8,128)S(1)}, f32[256,128]{1,0:T(8,128)S(1)}, u32[]{:S(2)}, u32[]{:S(2)}) collective-permute-start(f32[256,128]{1,0:T(8,128)S(1)} %convolution_add_fusion.6), channel_id=1, source_target_pairs={{0,4},{1,5},{2,6},{3,7},{4,0},{5,1},{6,2},{7,3},{8,12},{9,13},{10,... | collective-permute-start | bytes 393224 | tf_op jit(solution)/shard_map/ppermute | solution.py:47
  76.5 1.4 %collective-permute-start.3 = (f32[256,128]{1,0:T(8,128)S(1)}, f32[256,128]{1,0:T(8,128)S(1)}, u32[]{:S(2)}, u32[]{:S(2)}) collective-permute-start(f32[256,128]{1,0:T(8,128)S(1)} %convolution_add_fusion.5), channel_id=1, source_target_pairs={{0,8},{8,0},{16,24},{24,16},{32,40},{40,32},{48,56},{56,48},{64,72... | collective-permute-start | bytes 393224 | tf_op jit(solution)/shard_map/ppermute | solution.py:47
  78.4 5.6 %collective-permute-start.4 = (f32[256,128]{1,0:T(8,128)S(1)}, f32[256,128]{1,0:T(8,128)S(1)}, u32[]{:S(2)}, u32[]{:S(2)}) collective-permute-start(f32[256,128]{1,0:T(8,128)S(1)} %convolution_add_fusion.4), channel_id=1, source_target_pairs={{0,16},{8,24},{16,0},{24,8},{32,48},{40,56},{48,32},{56,40},{64,80... | collective-permute-start | bytes 393224 | tf_op jit(solution)/shard_map/ppermute | solution.py:47
  84.4 5.0 %collective-permute-start.5 = (f32[256,128]{1,0:T(8,128)S(1)}, f32[256,128]{1,0:T(8,128)S(1)}, u32[]{:S(2)}, u32[]{:S(2)}) collective-permute-start(f32[256,128]{1,0:T(8,128)S(1)} %convolution_add_fusion.3), channel_id=1, source_target_pairs={{0,32},{8,40},{16,48},{24,56},{32,0},{40,8},{48,16},{56,24},{64,96... | collective-permute-start | bytes 393224 | tf_op jit(solution)/shard_map/ppermute | solution.py:47
  89.8 6.6 %collective-permute-start.6 = (f32[256,128]{1,0:T(8,128)S(1)}, f32[256,128]{1,0:T(8,128)S(1)}, u32[]{:S(2)}, u32[]{:S(2)}) collective-permute-start(f32[256,128]{1,0:T(8,128)S(1)} %convolution_add_fusion.2), channel_id=1, source_target_pairs={{0,64},{8,72},{16,80},{24,88},{32,96},{40,104},{48,112},{56,120},{... | collective-permute-start | bytes 393224 | tf_op jit(solution)/shard_map/ppermute | solution.py:47
  (1 other events, 0.8 us)

commit v8 on v7

--- a/solution.py
+++ b/solution.py
@@ -101,19 +101,22 @@
     weights = block_diagonals(translations[0])
     low_bits = lax.axis_size("gy").bit_length() - 1
     high_bits = lax.axis_size("gx").bit_length() - 1
+    levels = [("gy", bit) for bit in range(low_bits)] + [("gx", bit) for bit in range(high_bits)]
+    own_at, partner_at = min(2, len(levels) - 1), min(4, len(levels) - 1)
+    padded = extended(ordered, ((("gx", "gy"), 1),), HW * leaf_size)
     coeffs = coeffs.reshape(rank_size, group_total, group_width).transpose(1, 0, 2)
     coeffs = coeffs.reshape(group_total * rank_size, group_width)
-    for level_bit in range(low_bits):
-        partner = from_partner(coeffs, "gy", level_bit)
-        coeffs = translate(weights[level_bit], coeffs, partner)
-    for level_bit in range(high_bits):
-        partner = from_partner(coeffs, "gx", level_bit)
-        coeffs = translate(weights[low_bits + level_bit], coeffs, partner)
+    for level, (axis, bit) in enumerate(levels):
+        if level == own_at:
+            coeffs, leaves = lax.optimization_barrier((coeffs, leaves))
+        if level == partner_at:
+            coeffs, padded = lax.optimization_barrier((coeffs, padded))
+        partner = from_partner(coeffs, axis, bit)
+        coeffs = translate(weights[level], coeffs, partner)
     coeffs = coeffs.reshape(group_total, rank_size, group_width).transpose(1, 0, 2)
     coeffs = coeffs.reshape(rank_size, total_cols)
     coeff_bf = coeffs.astype(jnp.bfloat16).reshape(rank_size, leaf_count, rhs_count)
     far_term = jnp.einsum("lrp,rls->slp", out_basis, coeff_bf, preferred_element_type=jnp.float32)
-    padded = extended(ordered, ((("gx", "gy"), 1),), HW * leaf_size)
     blocks_all = padded.reshape(rhs_count, leaf_count + 2 * HW, leaf_size)
     block_index = jnp.arange(leaf_count, dtype=jnp.int32) + HW + band_offsets
     picked = jnp.take(blocks_all, block_index, axis=1)

time: 100 us -> 96.9 us (0.969)
  matrix products: 23.8 us -> 20.4 us
  starting transfers between devices: 21.3 us -> 24.3 us
  waiting for transfers between devices: 13.7 us -> 11.1 us
    dot_general x1, matrix products: 5.67 us -> 2.28 us  [local(): jnp.einsum('lpq,slq->slp', band_blocks[:, 0], leaves, preferred_element_t...]
    ppermute x7, starting transfers between devices: 17.8 us -> 20.8 us  [from_partner(): lax.ppermute(x, axis, [(i, i ^ 1 << distance) for i in range(lax.axis_siz...]
    ppermute x7, waiting for transfers between devices: 13.7 us -> 11.1 us  [from_partner(): lax.ppermute(x, axis, [(i, i ^ 1 << distance) for i in range(lax.axis_siz...]
    unnamed x32 -> x23, local copies, waits for them, and re-layouts: 2.26 us -> 2.35 us
  transfers between devices with their start and end apart: 9 -> 9, of which waited for: 5 -> 5; matrix products, arithmetic and copies ran while one was open for 22% -> 19% of each run, Pallas kernels for 0% -> 0%
where the time goes in v8:
time: 96.9 us; the launch traced here: 96.6 us
  Pallas kernels  32.6 us (34%)
  starting transfers between devices  24.3 us (25%)
  matrix products  20.4 us (21%)
  waiting for transfers between devices  11.1 us (11%)
  local copies, waits for them, and re-layouts  7.79 us (8%)
    pallas_call x1, Pallas kernels, gather_points(): pl.pallas_call(gather_kernel, out_shape=jax.ShapeDtypeStruct((width, coun...  32.6 us
    ppermute x7, starting transfers between devices, from_partner(): lax.ppermute(x, axis, [(i, i ^ 1 << distance) for i in range(lax.axis_siz...  20.8 us
    ppermute x7, waiting for transfers between devices, from_partner(): lax.ppermute(x, axis, [(i, i ^ 1 << distance) for i in range(lax.axis_siz...  11.1 us
    dot_general x1, matrix products, local(): jnp.einsum('lpq,slq->slp', band_blocks[:, 1], picked, preferred_element_t...  6.78 us
    dot_general x7, matrix products, translate(): jnp.dot(level_matrices[1], other_coeffs, precision=lax.Precision.HIGHEST,...  3.54 us
    dot_general x7, matrix products, translate(): jnp.dot(level_matrices[0], own_coeffs, precision=lax.Precision.HIGHEST, p...  2.65 us
    unnamed x23, local copies, waits for them, and re-layouts  2.35 us
    dot_general x1, matrix products, local(): jnp.einsum('lpq,slq->slp', band_blocks[:, 0], leaves, preferred_element_t...  2.28 us
  transfers between devices with their start and end apart: 9, of which 5 were waited for; matrix products, arithmetic and copies ran while one was open for 19% of the time, Pallas kernels for 0%

profile of v8, /device:TPU:0, one launch (start us, length us, event | category | flops | bytes accessed | tf_op | source)
XLA Modules:
  0.0 96.6 jit_solution(5960076301968124549)
XLA Ops:
  0.0 1.4 %copy-done.1 = f32[16,16384]{1,0:T(8,128)S(1)} copy-done((f32[16,16384]{1,0:T(8,128)S(1)}, f32[16,16384]{1,0:T(8,128)}, u32[]{:S(2)}) %copy-start.1) | copy-done | bytes 1048600
  2.2 32.6 %shard_map.73 = bf16[16,16384]{1,0:T(8,128)(2,1)S(1)} custom-call(s32[16384]{0:T(1024)S(1)} %copy-done.2, f32[16,16384]{1,0:T(8,128)S(1)} %copy-done.1), custom_call_target="tpu_custom_call" | custom-call | bytes 1572864 | tf_op jit(solution)/shard_map/pallas_call | solution.py:35
  34.8 1.6 %fusion.10 = f32[64,16,32]{2,1,0:T(8,128)S(1)} fusion(bf16[64,32,256]{2,1,0:T(8,128)(2,1)} %param.10, bf16[2,64,8,256]{3,2,1,0:T(8,128)(2,1)S(1)} %bitcast.93), kind=kOutput, calls=%fused_computation.22 | convolution fusion | flops 16777216 | bytes 1703936 | tf_op jit(solution)/shard_map/lrp,slp->rls/dot_general | solution.py:98
  36.6 1.8 %collective-permute-start = (f32[256,128]{1,0:T(8,128)S(1)}, f32[256,128]{1,0:T(8,128)S(1)}, u32[]{:S(2)}, u32[]{:S(2)}) collective-permute-start(f32[256,128]{1,0:T(8,128)S(1)} %bitcast.114), channel_id=1, source_target_pairs={{0,1},{1,0},{2,3},{3,2},{4,5},{5,4},{6,7},{7,6},{8,9},{9,8},{10,11... | collective-permute-start | bytes 393224 | tf_op jit(solution)/shard_map/ppermute | solution.py:47
  38.4 2.2 %collective-permute-start.4 = (bf16[16,4096]{1,0:T(8,128)(2,1)S(1)}, bf16[16,4096]{1,0:T(8,128)(2,1)S(1)}, u32[]{:S(2)}, u32[]{:S(2)}) collective-permute-start(bf16[16,4096]{1,0:T(8,128)(2,1)S(1)} %get-tuple-element.29), channel_id=1, source_target_pairs={{0,1},{1,2},{2,3},{3,4},{4,5},{5,6},{6,7},{7,8},{8,9},{9,10},{10,1... | collective-permute-start | bytes 393224 | tf_op jit(solution)/shard_map/ppermute | solution.py:57
  40.6 1.3 %collective-permute-start.5 = (bf16[16,4096]{1,0:T(8,128)(2,1)S(1)}, bf16[16,4096]{1,0:T(8,128)(2,1)S(1)}, u32[]{:S(2)}, u32[]{:S(2)}) collective-permute-start(bf16[16,4096]{1,0:T(8,128)(2,1)S(1)} %get-tuple-element.30), channel_id=1, source_target_pairs={{1,0},{2,1},{3,2},{4,3},{5,4},{6,5},{7,6},{8,7},{9,8},{10,9},{11,1... | collective-permute-start | bytes 393224 | tf_op jit(solution)/shard_map/ppermute | solution.py:58
  42.0 1.7 %convolution_bitcast_fusion = f32[7,2,8,32,256]{4,3,1,0,2:T(8,128)S(1)} fusion(s32[8]{0:T(128)S(1)} %iota_multiply_fusion, f32[1,7,8,2,32,32]{5,4,3,2,1,0:T(8,128)S(1)} %copy-done), kind=kOutput, calls=%fused_computation.7 | convolution fusion | flops 352452608 | bytes 4128800 | tf_op jit(solution)/shard_map/lgtab,gbc->ltgac/dot_general | solution.py:69
  43.7 1.4 %fusion.22 = (f32[1,1,8,32,256]{4,3,1,0,2:T(8,128)}, f32[1,1,8,32,256]{4,3,1,0,2:T(8,128)}, f32[1,1,8,32,256]{4,3,1,0,2:T(8,128)}, f32[1,1,8,32,256]{4,3,1,0,2:T...) fusion(f32[7,2,8,32,256]{4,3,1,0,2:T(8,128)S(1)} %convolution_b, ...), kind=kLoop, calls=%fused_computation.38 | loop fusion | bytes 7340032 | tf_op jit(solution)/shard_map/slice | solution.py:82
  46.0 5.3 %collective-permute-start.1 = (f32[256,128]{1,0:T(8,128)S(1)}, f32[256,128]{1,0:T(8,128)S(1)}, u32[]{:S(2)}, u32[]{:S(2)}) collective-permute-start(f32[256,128]{1,0:T(8,128)S(1)} %convolution_add_fusion.7), channel_id=1, source_target_pairs={{0,2},{1,3},{2,0},{3,1},{4,6},{5,7},{6,4},{7,5},{8,10},{9,11},{10,... | collective-permute-start | bytes 393224 | tf_op jit(solution)/shard_map/ppermute | solution.py:47
  51.7 3.4 %collective-permute-done.1 = f32[256,128]{1,0:T(8,128)S(1)} collective-permute-done((f32[256,128]{1,0:T(8,128)S(1)}, f32[256,128]{1,0:T(8,128)S(1)}, u32[]{:S(2)}, u32[]{:S(2)}) %collective-permute-start.1) | collective-permute-done | bytes 131104 | tf_op jit(solution)/shard_map/ppermute | solution.py:47
  55.5 7.3 %collective-permute-start.2 = (f32[256,128]{1,0:T(8,128)S(1)}, f32[256,128]{1,0:T(8,128)S(1)}, u32[]{:S(2)}, u32[]{:S(2)}) collective-permute-start(f32[256,128]{1,0:T(8,128)S(1)} %convolution_add_fusion.6), channel_id=1, source_target_pairs={{0,4},{1,5},{2,6},{3,7},{4,0},{5,1},{6,2},{7,3},{8,12},{9,13},{10,... | collective-permute-start | bytes 393224 | tf_op jit(solution)/shard_map/ppermute | solution.py:47
  62.8 2.3 %fusion.2 = f32[64,16,256]{2,1,0:T(8,128)S(1)} fusion(bf16[64,2,256,256]{3,2,1,0:T(8,128)(2,1)S(1)} %copy-done.3, bf16[16,64,256]{2,1,0:T(8,128)(2,1)S(1)} %bitcast.97), kind=kOutput, calls=%fused_computation.3 | convolution fusion | flops 134217728 | bytes 9961472 | tf_op jit(solution)/shard_map/lpq,slq->slp/dot_general | solution.py:123
  66.6 0.9 collective-permute-done.3
  67.9 1.7 %collective-permute-start.6 = (f32[256,128]{1,0:T(8,128)S(1)}, f32[256,128]{1,0:T(8,128)}, u32[]{:S(2)}, u32[]{:S(2)}) collective-permute-start(f32[256,128]{1,0:T(8,128)S(1)} %convolution_add_fusion.4), channel_id=1, source_target_pairs={{0,16},{8,24},{16,0},{24,8},{32,48},{40,56},{48,32},{56,40},{64,80... | collective-permute-start | bytes 393224 | tf_op jit(solution)/shard_map/ppermute | solution.py:47
  69.6 0.9 copy.39
  70.6 1.7 %gather_fusion = bf16[64,16,256]{2,1,0:T(8,128)(2,1)S(1)} fusion(bf16[16,96,256]{2,0,1:T(8,128)(2,1)} %bitcast.96, s32[1024]{0:T(1024)S(1)} %pad_clamp_fusion), kind=kCustom, calls=%fused_computation | custom fusion | bytes 1048832 | tf_op jit(solution)/shard_map/jit(_take)/gather | solution.py:122
  72.4 6.8 %fusion = f32[64,16,256]{2,1,0:T(8,128)} fusion(bf16[64,2,256,256]{3,2,1,0:T(8,128)(2,1)} %param.11, bf16[64,16,256]{2,1,0:T(8,128)(2,1)S(1)} %gather_fusion, pred[64]{0:T(512)(128)(4,1)S(1)} %get-tuple-element.13), kind=kOutput, calls=%fused_computation.1 | convolution fusion | flops 134479872 | bytes 9961536 | tf_op jit(solution)/shard_map/lpq,slq->slp/dot_general | solution.py:126
  79.5 1.3 %convolution_add_fusion.3 = f32[256,128]{1,0:T(8,128)S(1)} fusion(f32[256,128]{1,0:T(8,128)S(1)} %fusion.28, f32[256,256]{1,0:T(8,128)S(1)} %bitcast.104, f32[256,128]{1,0:T(8,128)} %collective-permute-done.6), kind=kOutput, calls=%fused_computation.14 | convolution fusion | flops 100696064 | bytes 655360 | tf_op jit(solution)/shard_map/dot_general | solution.py:81
  80.8 1.6 %collective-permute-start.7 = (f32[256,128]{1,0:T(8,128)S(1)}, f32[256,128]{1,0:T(8,128)S(1)}, u32[]{:S(2)}, u32[]{:S(2)}) collective-permute-start(f32[256,128]{1,0:T(8,128)S(1)} %convolution_add_fusion.3), channel_id=1, source_target_pairs={{0,32},{8,40},{16,48},{24,56},{32,0},{40,8},{48,16},{56,24},{64,96... | collective-permute-start | bytes 393224 | tf_op jit(solution)/shard_map/ppermute | solution.py:47
  82.8 3.4 %collective-permute-done.7 = f32[256,128]{1,0:T(8,128)S(1)} collective-permute-done((f32[256,128]{1,0:T(8,128)S(1)}, f32[256,128]{1,0:T(8,128)S(1)}, u32[]{:S(2)}, u32[]{:S(2)}) %collective-permute-start.7) | collective-permute-done | bytes 131104 | tf_op jit(solution)/shard_map/ppermute | solution.py:47
  86.6 3.1 %collective-permute-start.8 = (f32[256,128]{1,0:T(8,128)S(1)}, f32[256,128]{1,0:T(8,128)S(1)}, u32[]{:S(2)}, u32[]{:S(2)}) collective-permute-start(f32[256,128]{1,0:T(8,128)S(1)} %convolution_add_fusion.2), channel_id=1, source_target_pairs={{0,64},{8,72},{16,80},{24,88},{32,96},{40,104},{48,112},{56,120},{... | collective-permute-start | bytes 393224 | tf_op jit(solution)/shard_map/ppermute | solution.py:47
  90.1 3.0 %collective-permute-done.8 = f32[256,128]{1,0:T(8,128)S(1)} collective-permute-done((f32[256,128]{1,0:T(8,128)S(1)}, f32[256,128]{1,0:T(8,128)S(1)}, u32[]{:S(2)}, u32[]{:S(2)}) %collective-permute-start.8) | collective-permute-done | bytes 131104 | tf_op jit(solution)/shard_map/ppermute | solution.py:47
  93.7 1.8 %fusion.8 = f32[64,2,8,256]{3,2,1,0:T(8,128)S(1)} fusion(f32[64,16,256]{2,1,0:T(8,128)} %fusion, f32[64,16,256]{2,1,0:T(8,128)S(1)} %fusion.2, bf16[32,64,16]{0,2,1:T(8,128)(2,1)S(1)} %bitcast.99, bf16[64,32,256]{2,1,0:T(8,128)(2,1)} %param.13), kind=kOutput, calls=%fused_computation.11 | convolution fusion | flops 17301504 | bytes 4259840 | tf_op jit(solution)/shard_map/lrp,rls->slp/dot_general | solution.py:119
  95.5 1.1 %copy.28 = f32[64,2,8,256]{3,2,0,1:T(8,128)} copy(f32[64,2,8,256]{3,2,1,0:T(8,128)S(1)} %fusion.8) | data formatting | bytes 2097152 | tf_op jit(solution)/shard_map/reshape | solution.py:129
  (48 shorter events, 6.7 us)
Async XLA Ops:
  0.0 41.9 %copy-start = (f32[1,7,8,2,32,32]{5,4,3,2,1,0:T(8,128)S(1)}, f32[1,7,8,2,32,32]{5,4,3,2,1,0:T(8,128)}, u32[]{:S(2)}) copy-start(f32[1,7,8,2,32,32]{5,4,3,2,1,0:T(8,128)} %param.12) | copy-start | bytes 1376260
  0.0 1.4 %copy-start.1 = (f32[16,16384]{1,0:T(8,128)S(1)}, f32[16,16384]{1,0:T(8,128)}, u32[]{:S(2)}) copy-start(f32[16,16384]{1,0:T(8,128)} %x_ref.1) | copy-start | bytes 3145732
  1.4 0.8 copy-start.2
  36.6 9.0 %collective-permute-start = (f32[256,128]{1,0:T(8,128)S(1)}, f32[256,128]{1,0:T(8,128)S(1)}, u32[]{:S(2)}, u32[]{:S(2)}) collective-permute-start(f32[256,128]{1,0:T(8,128)S(1)} %bitcast.114), channel_id=1, source_target_pairs={{0,1},{1,0},{2,3},{3,2},{4,5},{5,4},{6,7},{7,6},{8,9},{9,8},{10,11... | collective-permute-start | bytes 393224 | tf_op jit(solution)/shard_map/ppermute | solution.py:47
  38.3 7.1 %copy-start.10 = (s32[64]{0:T(128)S(1)}, s32[64]{0:T(128)}, u32[]{:S(2)}) copy-start(s32[64]{0:T(128)} %param.9) | copy-start | bytes 772
  38.4 12.9 %collective-permute-start.4 = (bf16[16,4096]{1,0:T(8,128)(2,1)S(1)}, bf16[16,4096]{1,0:T(8,128)(2,1)S(1)}, u32[]{:S(2)}, u32[]{:S(2)}) collective-permute-start(bf16[16,4096]{1,0:T(8,128)(2,1)S(1)} %get-tuple-element.29), channel_id=1, source_target_pairs={{0,1},{1,2},{2,3},{3,4},{4,5},{5,6},{6,7},{7,8},{8,9},{9,10},{10,1... | collective-permute-start | bytes 393224 | tf_op jit(solution)/shard_map/ppermute | solution.py:57
  40.6 10.6 %collective-permute-start.5 = (bf16[16,4096]{1,0:T(8,128)(2,1)S(1)}, bf16[16,4096]{1,0:T(8,128)(2,1)S(1)}, u32[]{:S(2)}, u32[]{:S(2)}) collective-permute-start(bf16[16,4096]{1,0:T(8,128)(2,1)S(1)} %get-tuple-element.30), channel_id=1, source_target_pairs={{1,0},{2,1},{3,2},{4,3},{5,4},{6,5},{7,6},{8,7},{9,8},{10,9},{11,1... | collective-permute-start | bytes 393224 | tf_op jit(solution)/shard_map/ppermute | solution.py:58
  41.9 20.8 %copy-start.3 = (bf16[64,2,256,256]{3,2,1,0:T(8,128)(2,1)S(1)}, bf16[64,2,256,256]{3,2,1,0:T(8,128)(2,1)}, u32[]{:S(2)}) copy-start(bf16[64,2,256,256]{3,2,1,0:T(8,128)(2,1)} %param.11) | copy-start | bytes 50331652
  46.0 9.2 %collective-permute-start.1 = (f32[256,128]{1,0:T(8,128)S(1)}, f32[256,128]{1,0:T(8,128)S(1)}, u32[]{:S(2)}, u32[]{:S(2)}) collective-permute-start(f32[256,128]{1,0:T(8,128)S(1)} %convolution_add_fusion.7), channel_id=1, source_target_pairs={{0,2},{1,3},{2,0},{3,1},{4,6},{5,7},{6,4},{7,5},{8,10},{9,11},{10,... | collective-permute-start | bytes 393224 | tf_op jit(solution)/shard_map/ppermute | solution.py:47
  55.5 10.2 %collective-permute-start.2 = (f32[256,128]{1,0:T(8,128)S(1)}, f32[256,128]{1,0:T(8,128)S(1)}, u32[]{:S(2)}, u32[]{:S(2)}) collective-permute-start(f32[256,128]{1,0:T(8,128)S(1)} %convolution_add_fusion.6), channel_id=1, source_target_pairs={{0,4},{1,5},{2,6},{3,7},{4,0},{5,1},{6,2},{7,3},{8,12},{9,13},{10,... | collective-permute-start | bytes 393224 | tf_op jit(solution)/shard_map/ppermute | solution.py:47
  66.1 1.4 %collective-permute-start.3 = (f32[256,128]{1,0:T(8,128)S(1)}, f32[256,128]{1,0:T(8,128)S(1)}, u32[]{:S(2)}, u32[]{:S(2)}) collective-permute-start(f32[256,128]{1,0:T(8,128)S(1)} %convolution_add_fusion.5), channel_id=1, source_target_pairs={{0,8},{8,0},{16,24},{24,16},{32,40},{40,32},{48,56},{56,48},{64,72... | collective-permute-start | bytes 393224 | tf_op jit(solution)/shard_map/ppermute | solution.py:47
  67.9 11.6 %collective-permute-start.6 = (f32[256,128]{1,0:T(8,128)S(1)}, f32[256,128]{1,0:T(8,128)}, u32[]{:S(2)}, u32[]{:S(2)}) collective-permute-start(f32[256,128]{1,0:T(8,128)S(1)} %convolution_add_fusion.4), channel_id=1, source_target_pairs={{0,16},{8,24},{16,0},{24,8},{32,48},{40,56},{48,32},{56,40},{64,80... | collective-permute-start | bytes 393224 | tf_op jit(solution)/shard_map/ppermute | solution.py:47
  72.3 6.8 %copy-start.9 = (f32[1,1,8,32,256]{4,3,1,0,2:T(8,128)S(1)}, f32[1,1,8,32,256]{4,3,1,0,2:T(8,128)}, u32[]{:S(2)}) copy-start(f32[1,1,8,32,256]{4,3,1,0,2:T(8,128)} %get-tuple-element.26) | copy-start | bytes 786436
  72.3 7.2 %copy-start.8 = (f32[1,1,8,32,256]{4,3,1,0,2:T(8,128)S(1)}, f32[1,1,8,32,256]{4,3,1,0,2:T(8,128)}, u32[]{:S(2)}) copy-start(f32[1,1,8,32,256]{4,3,1,0,2:T(8,128)} %get-tuple-element.17) | copy-start | bytes 786436
  72.3 10.1 %copy-start.7 = (f32[1,1,8,32,256]{4,3,1,0,2:T(8,128)S(1)}, f32[1,1,8,32,256]{4,3,1,0,2:T(8,128)}, u32[]{:S(2)}) copy-start(f32[1,1,8,32,256]{4,3,1,0,2:T(8,128)} %get-tuple-element.27) | copy-start | bytes 786436
  72.3 13.9 %copy-start.6 = (f32[1,1,8,32,256]{4,3,1,0,2:T(8,128)S(1)}, f32[1,1,8,32,256]{4,3,1,0,2:T(8,128)}, u32[]{:S(2)}) copy-start(f32[1,1,8,32,256]{4,3,1,0,2:T(8,128)} %get-tuple-element.16) | copy-start | bytes 786436
  72.3 17.4 %copy-start.5 = (f32[1,1,8,32,256]{4,3,1,0,2:T(8,128)S(1)}, f32[1,1,8,32,256]{4,3,1,0,2:T(8,128)}, u32[]{:S(2)}) copy-start(f32[1,1,8,32,256]{4,3,1,0,2:T(8,128)} %get-tuple-element.28) | copy-start | bytes 786436
  72.4 20.8 %copy-start.4 = (f32[1,1,8,32,256]{4,3,1,0,2:T(8,128)S(1)}, f32[1,1,8,32,256]{4,3,1,0,2:T(8,128)}, u32[]{:S(2)}) copy-start(f32[1,1,8,32,256]{4,3,1,0,2:T(8,128)} %get-tuple-element.15) | copy-start | bytes 786436
  80.8 5.4 %collective-permute-start.7 = (f32[256,128]{1,0:T(8,128)S(1)}, f32[256,128]{1,0:T(8,128)S(1)}, u32[]{:S(2)}, u32[]{:S(2)}) collective-permute-start(f32[256,128]{1,0:T(8,128)S(1)} %convolution_add_fusion.3), channel_id=1, source_target_pairs={{0,32},{8,40},{16,48},{24,56},{32,0},{40,8},{48,16},{56,24},{64,96... | collective-permute-start | bytes 393224 | tf_op jit(solution)/shard_map/ppermute | solution.py:47
  86.6 6.6 %collective-permute-start.8 = (f32[256,128]{1,0:T(8,128)S(1)}, f32[256,128]{1,0:T(8,128)S(1)}, u32[]{:S(2)}, u32[]{:S(2)}) collective-permute-start(f32[256,128]{1,0:T(8,128)S(1)} %convolution_add_fusion.2), channel_id=1, source_target_pairs={{0,64},{8,72},{16,80},{24,88},{32,96},{40,104},{48,112},{56,120},{... | collective-permute-start | bytes 393224 | tf_op jit(solution)/shard_map/ppermute | solution.py:47

commit v9 on v8

--- a/solution.py
+++ b/solution.py
@@ -102,30 +102,41 @@
     low_bits = lax.axis_size("gy").bit_length() - 1
     high_bits = lax.axis_size("gx").bit_length() - 1
     levels = [("gy", bit) for bit in range(low_bits)] + [("gx", bit) for bit in range(high_bits)]
-    own_at, partner_at = min(2, len(levels) - 1), min(4, len(levels) - 1)
+    last = len(levels) - 1
+    take_at, own_at, first_at, second_at = (min(k, last) for k in (1, 2, 4, 5))
     padded = extended(ordered, ((("gx", "gy"), 1),), HW * leaf_size)
+    blocks_all = padded.reshape(rhs_count, leaf_count + 2 * HW, leaf_size)
+    block_index = jnp.arange(leaf_count, dtype=jnp.int32) + HW + band_offsets
+    half = leaf_count // 2
     coeffs = coeffs.reshape(rank_size, group_total, group_width).transpose(1, 0, 2)
     coeffs = coeffs.reshape(group_total * rank_size, group_width)
+    picked = None
     for level, (axis, bit) in enumerate(levels):
+        if level == take_at:
+            coeffs, blocks_all = lax.optimization_barrier((coeffs, blocks_all))
+            picked = jnp.take(blocks_all, block_index, axis=1)
         if level == own_at:
             coeffs, leaves = lax.optimization_barrier((coeffs, leaves))
-        if level == partner_at:
-            coeffs, padded = lax.optimization_barrier((coeffs, padded))
+        if level == first_at:
+            coeffs, picked_first = lax.optimization_barrier((coeffs, picked[:, :half]))
+        if level == second_at:
+            coeffs, picked_second = lax.optimization_barrier((coeffs, picked[:, half:]))
         partner = from_partner(coeffs, axis, bit)
         coeffs = translate(weights[level], coeffs, partner)
     coeffs = coeffs.reshape(group_total, rank_size, group_width).transpose(1, 0, 2)
     coeffs = coeffs.reshape(rank_size, total_cols)
     coeff_bf = coeffs.astype(jnp.bfloat16).reshape(rank_size, leaf_count, rhs_count)
     far_term = jnp.einsum("lrp,rls->slp", out_basis, coeff_bf, preferred_element_type=jnp.float32)
-    blocks_all = padded.reshape(rhs_count, leaf_count + 2 * HW, leaf_size)
-    block_index = jnp.arange(leaf_count, dtype=jnp.int32) + HW + band_offsets
-    picked = jnp.take(blocks_all, block_index, axis=1)
     own_term = jnp.einsum(
         "lpq,slq->slp", band_blocks[:, 0], leaves, preferred_element_type=jnp.float32
     )
-    partner_term = jnp.einsum(
-        "lpq,slq->slp", band_blocks[:, 1], picked, preferred_element_type=jnp.float32
+    partner_first = jnp.einsum(
+        "lpq,slq->slp", band_blocks[:half, 1], picked_first, preferred_element_type=jnp.float32
     )
+    partner_second = jnp.einsum(
+        "lpq,slq->slp", band_blocks[half:, 1], picked_second, preferred_element_type=jnp.float32
+    )
+    partner_term = jnp.concatenate([partner_first, partner_second], axis=1)
     return (far_term + own_term + partner_term).reshape(rhs_count, point_count)
 
 

time: 96.9 us -> 96.4 us (level)
  matrix products: 20.4 us -> 25.4 us
  waiting for transfers between devices: 11.1 us -> 7.22 us
  starting transfers between devices: 24.3 us -> 21 us
  other arithmetic: 0.07 us -> 1.25 us
    ppermute x7, waiting for transfers between devices: 11.1 us -> 5.04 us  [from_partner(): lax.ppermute(x, axis, [(i, i ^ 1 << distance) for i in range(lax.axis_siz...]
    dot_general x1, matrix products: 2.28 us -> 5.67 us  [local(): jnp.einsum('lpq,slq->slp', band_blocks[:, 0], leaves, preferred_element_t...]
    ppermute x7, starting transfers between devices: 20.8 us -> 17.5 us  [from_partner(): lax.ppermute(x, axis, [(i, i ^ 1 << distance) for i in range(lax.axis_siz...]
    ppermute x1, waiting for transfers between devices: 0.01 us -> 2.17 us  [extended(): after = lax.ppermute(initial, axis, down)]
    select_n x0 -> x1, other arithmetic: none -> 1.18 us  [local(): picked = jnp.take(blocks_all, block_index, axis=1)]
    dot_general x1 -> x2, matrix products: 6.78 us -> 7.57 us  [the longest x1 4.19 us: local(): jnp.einsum('lpq,slq->slp', band_blocks[half:, 1], picked_second, preferre...]
    unnamed x23 -> x30, local copies, waits for them, and re-layouts: 2.35 us -> 2.54 us
  transfers between devices with their start and end apart: 9 -> 9, of which waited for: 5 -> 4; matrix products, arithmetic and copies ran while one was open for 19% -> 25% of each run, Pallas kernels for 0% -> 0%
where the time goes in v9:
time: 96.4 us; the launch traced here: 95.9 us
  Pallas kernels  32.6 us (34%)
  matrix products  25.4 us (26%)
  starting transfers between devices  21 us (22%)
  local copies, waits for them, and re-layouts  8.08 us (8%)
  waiting for transfers between devices  7.22 us (7%)
  other arithmetic  1.25 us (1%)
    pallas_call x1, Pallas kernels, gather_points(): pl.pallas_call(gather_kernel, out_shape=jax.ShapeDtypeStruct((width, coun...  32.6 us
    ppermute x7, starting transfers between devices, from_partner(): lax.ppermute(x, axis, [(i, i ^ 1 << distance) for i in range(lax.axis_siz...  17.5 us
    dot_general x1, matrix products, local(): jnp.einsum('lpq,slq->slp', band_blocks[:, 0], leaves, preferred_element_t...  5.67 us
    ppermute x7, waiting for transfers between devices, from_partner(): lax.ppermute(x, axis, [(i, i ^ 1 << distance) for i in range(lax.axis_siz...  5.04 us
    dot_general x1, matrix products, local(): jnp.einsum('lpq,slq->slp', band_blocks[half:, 1], picked_second, preferre...  4.19 us
    dot_general x7, matrix products, translate(): jnp.dot(level_matrices[0], own_coeffs, precision=lax.Precision.HIGHEST, p...  3.6 us
    dot_general x7, matrix products, translate(): jnp.dot(level_matrices[1], other_coeffs, precision=lax.Precision.HIGHEST,...  3.54 us
    dot_general x1, matrix products, local(): jnp.einsum('lpq,slq->slp', band_blocks[:half, 1], picked_first, preferred...  3.38 us
  transfers between devices with their start and end apart: 9, of which 4 were waited for; matrix products, arithmetic and copies ran while one was open for 25% of the time, Pallas kernels for 0%

profile of v9, /device:TPU:0, one launch (start us, length us, event | category | flops | bytes accessed | tf_op | source)
XLA Modules:
  0.0 95.9 jit_solution(8246743520862935077)
XLA Ops:
  0.0 1.4 %copy-done.1 = f32[16,16384]{1,0:T(8,128)S(1)} copy-done((f32[16,16384]{1,0:T(8,128)S(1)}, f32[16,16384]{1,0:T(8,128)}, u32[]{:S(2)}) %copy-start.1) | copy-done | bytes 1048600
  2.2 32.6 %shard_map.73 = bf16[16,16384]{1,0:T(8,128)(2,1)S(1)} custom-call(s32[16384]{0:T(1024)S(1)} %copy-done.2, f32[16,16384]{1,0:T(8,128)S(1)} %copy-done.1), custom_call_target="tpu_custom_call" | custom-call | bytes 1572864 | tf_op jit(solution)/shard_map/pallas_call | solution.py:35
  34.8 1.6 %fusion.20 = f32[64,16,32]{2,1,0:T(8,128)S(1)} fusion(bf16[64,32,256]{2,1,0:T(8,128)(2,1)} %param.10, bf16[2,64,8,256]{3,2,1,0:T(8,128)(2,1)S(1)} %bitcast.110), kind=kOutput, calls=%fused_computation.27 | convolution fusion | flops 16777216 | bytes 1703936 | tf_op jit(solution)/shard_map/lrp,slp->rls/dot_general | solution.py:98
  36.6 1.8 %collective-permute-start = (f32[256,128]{1,0:T(8,128)S(1)}, f32[256,128]{1,0:T(8,128)S(1)}, u32[]{:S(2)}, u32[]{:S(2)}) collective-permute-start(f32[256,128]{1,0:T(8,128)S(1)} %bitcast.131), channel_id=1, source_target_pairs={{0,1},{1,0},{2,3},{3,2},{4,5},{5,4},{6,7},{7,6},{8,9},{9,8},{10,11... | collective-permute-start | bytes 393224 | tf_op jit(solution)/shard_map/ppermute | solution.py:47
  38.4 2.2 %collective-permute-start.1 = (bf16[16,4096]{1,0:T(8,128)(2,1)S(1)}, bf16[16,4096]{1,0:T(8,128)(2,1)S(1)}, u32[]{:S(2)}, u32[]{:S(2)}) collective-permute-start(bf16[16,4096]{1,0:T(8,128)(2,1)S(1)} %get-tuple-element.39), channel_id=1, source_target_pairs={{0,1},{1,2},{2,3},{3,4},{4,5},{5,6},{6,7},{7,8},{8,9},{9,10},{10,1... | collective-permute-start | bytes 393224 | tf_op jit(solution)/shard_map/ppermute | solution.py:57
  40.6 1.3 %collective-permute-start.2 = (bf16[16,4096]{1,0:T(8,128)(2,1)S(1)}, bf16[16,4096]{1,0:T(8,128)(2,1)S(1)}, u32[]{:S(2)}, u32[]{:S(2)}) collective-permute-start(bf16[16,4096]{1,0:T(8,128)(2,1)S(1)} %get-tuple-element.40), channel_id=1, source_target_pairs={{1,0},{2,1},{3,2},{4,3},{5,4},{6,5},{7,6},{8,7},{9,8},{10,9},{11,1... | collective-permute-start | bytes 393224 | tf_op jit(solution)/shard_map/ppermute | solution.py:58
  41.9 1.7 %convolution_bitcast_fusion = f32[7,2,8,32,256]{4,3,1,0,2:T(8,128)S(1)} fusion(s32[8]{0:T(128)S(1)} %iota_multiply_fusion, f32[1,7,8,2,32,32]{5,4,3,2,1,0:T(8,128)S(1)} %copy-done), kind=kOutput, calls=%fused_computation.10 | convolution fusion | flops 352452608 | bytes 4128800 | tf_op jit(solution)/shard_map/lgtab,gbc->ltgac/dot_general | solution.py:69
  43.7 1.6 %fusion.27 = (f32[1,1,8,32,256]{4,3,1,0,2:T(8,128)}, f32[1,1,8,32,256]{4,3,1,0,2:T(8,128)}, f32[1,1,8,32,256]{4,3,1,0,2:T(8,128)}, f32[1,1,8,32,256]{4,3,1,0,2:T...) fusion(f32[7,2,8,32,256]{4,3,1,0,2:T(8,128)S(1)} %convolution_b, ...), kind=kLoop, calls=%fused_computation.39 | loop fusion | bytes 7340032 | tf_op jit(solution)/shard_map/slice | solution.py:82
  45.8 2.2 %collective-permute-done.2 = bf16[16,4096]{1,0:T(8,128)(2,1)S(1)} collective-permute-done((bf16[16,4096]{1,0:T(8,128)(2,1)S(1)}, bf16[16,4096]{1,0:T(8,128)(2,1)S(1)}, u32[]{:S(2)}, u32[]{:S(2)}) %collective-permute-start.2) | collective-permute-done | bytes 131104 | tf_op jit(solution)/shard_map/ppermute | solution.py:58
  48.6 5.2 %collective-permute-start.3 = (f32[256,128]{1,0:T(8,128)S(1)}, f32[256,128]{1,0:T(8,128)}, u32[]{:S(2)}, u32[]{:S(2)}) collective-permute-start(f32[256,128]{1,0:T(8,128)S(1)} %convolution_add_fusion.7), channel_id=1, source_target_pairs={{0,2},{1,3},{2,0},{3,1},{4,6},{5,7},{6,4},{7,5},{8,10},{9,11},{10,... | collective-permute-start | bytes 393224 | tf_op jit(solution)/shard_map/ppermute | solution.py:47
  54.3 1.4 %gather_fusion = bf16[64,16,256]{2,1,0:T(8,128)(2,1)} fusion(bf16[16,96,256]{2,0,1:T(8,128)(2,1)S(1)} %copy.18, s32[1024]{0:T(1024)S(1)} %pad_clamp_fusion), kind=kCustom, calls=%fused_computation | custom fusion | bytes 1048832 | tf_op jit(solution)/shard_map/jit(_take)/gather | solution.py:117
  55.7 1.2 %select_bitcast_fusion = bf16[16,64,256]{2,0,1:T(8,128)(2,1)S(1)} fusion(bf16[64,16,256]{2,1,0:T(8,128)(2,1)} %gather_fusion, pred[64]{0:T(512)(128)(4,1)S(1)} %get-tuple-element.21), kind=kLoop, calls=%fused_computation.31 | loop fusion | flops 262144 | bytes 1048640 | tf_op jit(solution)/shard_map/jit(_take)/select_n | solution.py:117
  56.9 1.3 %fusion.31 = f32[256,128]{1,0:T(8,128)S(1)} fusion(f32[256,256]{1,0:T(8,128)} %bitcast.128, f32[256,128]{1,0:T(8,128)S(1)} %convolution_add_fusion.7), kind=kOutput, calls=%fused_computation.43 | convolution fusion | flops 100663296 | bytes 524288 | tf_op jit(solution)/shard_map/dot_general | solution.py:75
  58.2 1.3 %convolution_add_fusion.6 = f32[256,128]{1,0:T(8,128)S(1)} fusion(f32[256,128]{1,0:T(8,128)S(1)} %fusion.31, f32[256,256]{1,0:T(8,128)S(1)} %bitcast.127, f32[256,128]{1,0:T(8,128)} %collective-permute-done.3), kind=kOutput, calls=%fused_computation.23 | convolution fusion | flops 100696064 | bytes 655360 | tf_op jit(solution)/shard_map/dot_general | solution.py:81
  59.6 4.7 %collective-permute-start.4 = (f32[256,128]{1,0:T(8,128)S(1)}, f32[256,128]{1,0:T(8,128)S(1)}, u32[]{:S(2)}, u32[]{:S(2)}) collective-permute-start(f32[256,128]{1,0:T(8,128)S(1)} %convolution_add_fusion.6), channel_id=1, source_target_pairs={{0,4},{1,5},{2,6},{3,7},{4,0},{5,1},{6,2},{7,3},{8,12},{9,13},{10,... | collective-permute-start | bytes 393224 | tf_op jit(solution)/shard_map/ppermute | solution.py:47
  64.3 5.7 %fusion = f32[64,16,256]{2,1,0:T(8,128)S(1)} fusion(bf16[64,2,256,256]{3,2,1,0:T(8,128)(2,1)} %param.11, bf16[16,64,256]{2,1,0:T(8,128)(2,1)S(1)} %bitcast.114), kind=kOutput, calls=%fused_computation.1 | convolution fusion | flops 134217728 | bytes 9961472 | tf_op jit(solution)/shard_map/lpq,slq->slp/dot_general | solution.py:130
  72.6 1.1 %collective-permute-start.6 = (f32[256,128]{1,0:T(8,128)S(1)}, f32[256,128]{1,0:T(8,128)S(1)}, u32[]{:S(2)}, u32[]{:S(2)}) collective-permute-start(f32[256,128]{1,0:T(8,128)S(1)} %convolution_add_fusion.4), channel_id=1, source_target_pairs={{0,16},{8,24},{16,0},{24,8},{32,48},{40,56},{48,32},{56,40},{64,80... | collective-permute-start | bytes 393224 | tf_op jit(solution)/shard_map/ppermute | solution.py:47
  73.7 3.4 %fusion.13 = f32[16,32,256]{2,0,1:T(8,128)S(1)} fusion(bf16[16,32,256]{2,0,1:T(8,128)(2,1)S(1)} %get-tuple-element.19, bf16[64,2,256,256]{3,2,1,0:T(8,128)(2,1)} %param.11), kind=kOutput, calls=%fused_computation.16 | convolution fusion | flops 67108864 | bytes 4980736 | tf_op jit(solution)/shard_map/lpq,slq->slp/dot_general | solution.py:133
  78.6 1.8 %collective-permute-start.7 = (f32[256,128]{1,0:T(8,128)S(1)}, f32[256,128]{1,0:T(8,128)S(1)}, u32[]{:S(2)}, u32[]{:S(2)}) collective-permute-start(f32[256,128]{1,0:T(8,128)S(1)} %convolution_add_fusion.3), channel_id=1, source_target_pairs={{0,32},{8,40},{16,48},{24,56},{32,0},{40,8},{48,16},{56,24},{64,96... | collective-permute-start | bytes 393224 | tf_op jit(solution)/shard_map/ppermute | solution.py:47
  80.4 4.2 %fusion.16 = f32[16,32,256]{2,0,1:T(8,128)} fusion(bf16[16,32,256]{2,0,1:T(8,128)(2,1)S(1)} %get-tuple-element.20, bf16[64,2,256,256]{3,2,1,0:T(8,128)(2,1)} %param.11), kind=kOutput, calls=%fused_computation.17 | convolution fusion | flops 67108864 | bytes 4980736 | tf_op jit(solution)/shard_map/lpq,slq->slp/dot_general | solution.py:136
  85.4 2.8 %collective-permute-start.8 = (f32[256,128]{1,0:T(8,128)S(1)}, f32[256,128]{1,0:T(8,128)S(1)}, u32[]{:S(2)}, u32[]{:S(2)}) collective-permute-start(f32[256,128]{1,0:T(8,128)S(1)} %convolution_add_fusion.2), channel_id=1, source_target_pairs={{0,64},{8,72},{16,80},{24,88},{32,96},{40,104},{48,112},{56,120},{... | collective-permute-start | bytes 393224 | tf_op jit(solution)/shard_map/ppermute | solution.py:47
  88.6 3.4 %collective-permute-done.8 = f32[256,128]{1,0:T(8,128)S(1)} collective-permute-done((f32[256,128]{1,0:T(8,128)S(1)}, f32[256,128]{1,0:T(8,128)S(1)}, u32[]{:S(2)}, u32[]{:S(2)}) %collective-permute-start.8) | collective-permute-done | bytes 131104 | tf_op jit(solution)/shard_map/ppermute | solution.py:47
  93.1 1.7 %fusion.12 = f32[64,2,8,256]{3,2,1,0:T(8,128)S(1)} fusion(f32[64,16,256]{2,1,0:T(8,128)S(1)} %fusion, bf16[32,64,16]{0,2,1:T(8,128)(2,1)} %bitcast.116, bf16[64,32,256]{2,1,0:T(8,128)(2,1)} %param.13, f32[16,32,256]{2,0,1:T(8,128)} %fusion.16, f32[16,32,256]{2,0,1:T(8,128)S(1)} %fusion.13), kind=kOutput, calls=%fused_computation.15 | convolution fusion | flops 17563648 | bytes 4259840 | tf_op jit(solution)/shard_map/lrp,rls->slp/dot_general | solution.py:129
  94.9 1.1 %copy.30 = f32[64,2,8,256]{3,2,0,1:T(8,128)} copy(f32[64,2,8,256]{3,2,1,0:T(8,128)S(1)} %fusion.12) | data formatting | bytes 2097152 | tf_op jit(solution)/shard_map/reshape | solution.py:140
  (58 shorter events, 9.1 us)
Async XLA Ops:
  0.0 41.9 %copy-start = (f32[1,7,8,2,32,32]{5,4,3,2,1,0:T(8,128)S(1)}, f32[1,7,8,2,32,32]{5,4,3,2,1,0:T(8,128)}, u32[]{:S(2)}) copy-start(f32[1,7,8,2,32,32]{5,4,3,2,1,0:T(8,128)} %param.12) | copy-start | bytes 1376260
  0.0 1.4 %copy-start.1 = (f32[16,16384]{1,0:T(8,128)S(1)}, f32[16,16384]{1,0:T(8,128)}, u32[]{:S(2)}) copy-start(f32[16,16384]{1,0:T(8,128)} %x_ref.1) | copy-start | bytes 3145732
  1.4 0.8 copy-start.2
  36.6 11.6 %collective-permute-start = (f32[256,128]{1,0:T(8,128)S(1)}, f32[256,128]{1,0:T(8,128)S(1)}, u32[]{:S(2)}, u32[]{:S(2)}) collective-permute-start(f32[256,128]{1,0:T(8,128)S(1)} %bitcast.131), channel_id=1, source_target_pairs={{0,1},{1,0},{2,3},{3,2},{4,5},{5,4},{6,7},{7,6},{8,9},{9,8},{10,11... | collective-permute-start | bytes 393224 | tf_op jit(solution)/shard_map/ppermute | solution.py:47
  38.4 7.4 %collective-permute-start.1 = (bf16[16,4096]{1,0:T(8,128)(2,1)S(1)}, bf16[16,4096]{1,0:T(8,128)(2,1)S(1)}, u32[]{:S(2)}, u32[]{:S(2)}) collective-permute-start(bf16[16,4096]{1,0:T(8,128)(2,1)S(1)} %get-tuple-element.39), channel_id=1, source_target_pairs={{0,1},{1,2},{2,3},{3,4},{4,5},{5,6},{6,7},{7,8},{8,9},{9,10},{10,1... | collective-permute-start | bytes 393224 | tf_op jit(solution)/shard_map/ppermute | solution.py:57
  40.6 7.4 %collective-permute-start.2 = (bf16[16,4096]{1,0:T(8,128)(2,1)S(1)}, bf16[16,4096]{1,0:T(8,128)(2,1)S(1)}, u32[]{:S(2)}, u32[]{:S(2)}) collective-permute-start(bf16[16,4096]{1,0:T(8,128)(2,1)S(1)} %get-tuple-element.40), channel_id=1, source_target_pairs={{1,0},{2,1},{3,2},{4,3},{5,4},{6,5},{7,6},{8,7},{9,8},{10,9},{11,1... | collective-permute-start | bytes 393224 | tf_op jit(solution)/shard_map/ppermute | solution.py:58
  43.7 2.0 %copy-start.13 = (s32[64]{0:T(128)S(1)}, s32[64]{0:T(128)}, u32[]{:S(2)}) copy-start(s32[64]{0:T(128)} %param.9) | copy-start | bytes 772
  48.6 9.6 %collective-permute-start.3 = (f32[256,128]{1,0:T(8,128)S(1)}, f32[256,128]{1,0:T(8,128)}, u32[]{:S(2)}, u32[]{:S(2)}) collective-permute-start(f32[256,128]{1,0:T(8,128)S(1)} %convolution_add_fusion.7), channel_id=1, source_target_pairs={{0,2},{1,3},{2,0},{3,1},{4,6},{5,7},{6,4},{7,5},{8,10},{9,11},{10,... | collective-permute-start | bytes 393224 | tf_op jit(solution)/shard_map/ppermute | solution.py:47
  59.5 10.4 %copy-start.12 = (f32[1,1,8,32,256]{4,3,1,0,2:T(8,128)S(1)}, f32[1,1,8,32,256]{4,3,1,0,2:T(8,128)}, u32[]{:S(2)}) copy-start(f32[1,1,8,32,256]{4,3,1,0,2:T(8,128)} %get-tuple-element.32) | copy-start | bytes 786436
  59.5 10.8 %copy-start.11 = (f32[1,1,8,32,256]{4,3,1,0,2:T(8,128)S(1)}, f32[1,1,8,32,256]{4,3,1,0,2:T(8,128)}, u32[]{:S(2)}) copy-start(f32[1,1,8,32,256]{4,3,1,0,2:T(8,128)} %get-tuple-element.27) | copy-start | bytes 786436
  59.5 11.3 %copy-start.10 = (f32[1,1,8,32,256]{4,3,1,0,2:T(8,128)S(1)}, f32[1,1,8,32,256]{4,3,1,0,2:T(8,128)}, u32[]{:S(2)}) copy-start(f32[1,1,8,32,256]{4,3,1,0,2:T(8,128)} %get-tuple-element.33) | copy-start | bytes 786436
  59.6 12.7 %copy-start.9 = (f32[1,1,8,32,256]{4,3,1,0,2:T(8,128)S(1)}, f32[1,1,8,32,256]{4,3,1,0,2:T(8,128)}, u32[]{:S(2)}) copy-start(f32[1,1,8,32,256]{4,3,1,0,2:T(8,128)} %get-tuple-element.26) | copy-start | bytes 786436
  59.6 10.8 %collective-permute-start.4 = (f32[256,128]{1,0:T(8,128)S(1)}, f32[256,128]{1,0:T(8,128)S(1)}, u32[]{:S(2)}, u32[]{:S(2)}) collective-permute-start(f32[256,128]{1,0:T(8,128)S(1)} %convolution_add_fusion.6), channel_id=1, source_target_pairs={{0,4},{1,5},{2,6},{3,7},{4,0},{5,1},{6,2},{7,3},{8,12},{9,13},{10,... | collective-permute-start | bytes 393224 | tf_op jit(solution)/shard_map/ppermute | solution.py:47
  70.0 7.1 %copy-start.8 = (f32[1,1,8,32,256]{4,3,1,0,2:T(8,128)S(1)}, f32[1,1,8,32,256]{4,3,1,0,2:T(8,128)}, u32[]{:S(2)}) copy-start(f32[1,1,8,32,256]{4,3,1,0,2:T(8,128)} %get-tuple-element.34) | copy-start | bytes 786436
  70.4 7.8 %copy-start.7 = (f32[1,1,8,32,256]{4,3,1,0,2:T(8,128)S(1)}, f32[1,1,8,32,256]{4,3,1,0,2:T(8,128)}, u32[]{:S(2)}) copy-start(f32[1,1,8,32,256]{4,3,1,0,2:T(8,128)} %get-tuple-element.25) | copy-start | bytes 786436
  70.8 1.4 %collective-permute-start.5 = (f32[256,128]{1,0:T(8,128)S(1)}, f32[256,128]{1,0:T(8,128)S(1)}, u32[]{:S(2)}, u32[]{:S(2)}) collective-permute-start(f32[256,128]{1,0:T(8,128)S(1)} %convolution_add_fusion.5), channel_id=1, source_target_pairs={{0,8},{8,0},{16,24},{24,16},{32,40},{40,32},{48,56},{56,48},{64,72... | collective-permute-start | bytes 393224 | tf_op jit(solution)/shard_map/ppermute | solution.py:47
  72.6 5.6 %collective-permute-start.6 = (f32[256,128]{1,0:T(8,128)S(1)}, f32[256,128]{1,0:T(8,128)S(1)}, u32[]{:S(2)}, u32[]{:S(2)}) collective-permute-start(f32[256,128]{1,0:T(8,128)S(1)} %convolution_add_fusion.4), channel_id=1, source_target_pairs={{0,16},{8,24},{16,0},{24,8},{32,48},{40,56},{48,32},{56,40},{64,80... | collective-permute-start | bytes 393224 | tf_op jit(solution)/shard_map/ppermute | solution.py:47
  77.1 7.5 %copy-start.6 = (f32[1,1,8,32,256]{4,3,1,0,2:T(8,128)S(1)}, f32[1,1,8,32,256]{4,3,1,0,2:T(8,128)}, u32[]{:S(2)}) copy-start(f32[1,1,8,32,256]{4,3,1,0,2:T(8,128)} %get-tuple-element.35) | copy-start | bytes 786436
  77.1 7.9 %copy-start.5 = (f32[1,1,8,32,256]{4,3,1,0,2:T(8,128)S(1)}, f32[1,1,8,32,256]{4,3,1,0,2:T(8,128)}, u32[]{:S(2)}) copy-start(f32[1,1,8,32,256]{4,3,1,0,2:T(8,128)} %get-tuple-element.24) | copy-start | bytes 786436
  77.1 11.1 %copy-start.4 = (f32[1,1,8,32,256]{4,3,1,0,2:T(8,128)S(1)}, f32[1,1,8,32,256]{4,3,1,0,2:T(8,128)}, u32[]{:S(2)}) copy-start(f32[1,1,8,32,256]{4,3,1,0,2:T(8,128)} %get-tuple-element.36) | copy-start | bytes 786436
  78.2 13.7 %copy-start.3 = (f32[1,1,8,32,256]{4,3,1,0,2:T(8,128)S(1)}, f32[1,1,8,32,256]{4,3,1,0,2:T(8,128)}, u32[]{:S(2)}) copy-start(f32[1,1,8,32,256]{4,3,1,0,2:T(8,128)} %get-tuple-element.23) | copy-start | bytes 786436
  78.6 6.3 %collective-permute-start.7 = (f32[256,128]{1,0:T(8,128)S(1)}, f32[256,128]{1,0:T(8,128)S(1)}, u32[]{:S(2)}, u32[]{:S(2)}) collective-permute-start(f32[256,128]{1,0:T(8,128)S(1)} %convolution_add_fusion.3), channel_id=1, source_target_pairs={{0,32},{8,40},{16,48},{24,56},{32,0},{40,8},{48,16},{56,24},{64,96... | collective-permute-start | bytes 393224 | tf_op jit(solution)/shard_map/ppermute | solution.py:47
  85.4 6.6 %collective-permute-start.8 = (f32[256,128]{1,0:T(8,128)S(1)}, f32[256,128]{1,0:T(8,128)S(1)}, u32[]{:S(2)}, u32[]{:S(2)}) collective-permute-start(f32[256,128]{1,0:T(8,128)S(1)} %convolution_add_fusion.2), channel_id=1, source_target_pairs={{0,64},{8,72},{16,80},{24,88},{32,96},{40,104},{48,112},{56,120},{... | collective-permute-start | bytes 393224 | tf_op jit(solution)/shard_map/ppermute | solution.py:47

commit v10 on v9

--- a/solution.py
+++ b/solution.py
@@ -103,7 +103,7 @@
     high_bits = lax.axis_size("gx").bit_length() - 1
     levels = [("gy", bit) for bit in range(low_bits)] + [("gx", bit) for bit in range(high_bits)]
     last = len(levels) - 1
-    take_at, own_at, first_at, second_at = (min(k, last) for k in (1, 2, 4, 5))
+    take_at, own_at, first_at, second_at, own_late_at = (min(k, last) for k in (1, 2, 4, 5, 6))
     padded = extended(ordered, ((("gx", "gy"), 1),), HW * leaf_size)
     blocks_all = padded.reshape(rhs_count, leaf_count + 2 * HW, leaf_size)
     block_index = jnp.arange(leaf_count, dtype=jnp.int32) + HW + band_offsets
@@ -116,7 +116,9 @@
             coeffs, blocks_all = lax.optimization_barrier((coeffs, blocks_all))
             picked = jnp.take(blocks_all, block_index, axis=1)
         if level == own_at:
-            coeffs, leaves = lax.optimization_barrier((coeffs, leaves))
+            coeffs, own_first = lax.optimization_barrier((coeffs, leaves[:, :half]))
+        if level == own_late_at:
+            coeffs, own_second = lax.optimization_barrier((coeffs, leaves[:, half:]))
         if level == first_at:
             coeffs, picked_first = lax.optimization_barrier((coeffs, picked[:, :half]))
         if level == second_at:
@@ -127,8 +129,12 @@
     coeffs = coeffs.reshape(rank_size, total_cols)
     coeff_bf = coeffs.astype(jnp.bfloat16).reshape(rank_size, leaf_count, rhs_count)
     far_term = jnp.einsum("lrp,rls->slp", out_basis, coeff_bf, preferred_element_type=jnp.float32)
-    own_term = jnp.einsum(
-        "lpq,slq->slp", band_blocks[:, 0], leaves, preferred_element_type=jnp.float32
+    own_term = jnp.concatenate(
+        [
+            jnp.einsum("lpq,slq->slp", band_blocks[:half, 0], own_first, preferred_element_type=jnp.float32),
+            jnp.einsum("lpq,slq->slp", band_blocks[half:, 0], own_second, preferred_element_type=jnp.float32),
+        ],
+        axis=1,
     )
     partner_first = jnp.einsum(
         "lpq,slq->slp", band_blocks[:half, 1], picked_first, preferred_element_type=jnp.float32

time: 96.4 us -> 95.2 us (0.988)
  waiting for transfers between devices: 7.22 us -> 3.51 us
  starting transfers between devices: 21 us -> 22.9 us
  matrix products: 25.4 us -> 26.7 us
  other arithmetic: 1.25 us -> 0.21 us
    ppermute x7, waiting for transfers between devices: 5.04 us -> 2.08 us  [from_partner(): lax.ppermute(x, axis, [(i, i ^ 1 << distance) for i in range(lax.axis_siz...]
    dot_general x1 -> x2, matrix products: 5.67 us -> 7.66 us  [the longest x1 4.19 us: local(): jnp.einsum('lpq,slq->slp', band_blocks[half:, 0], own_second, preferred_e...]
    ppermute x7, starting transfers between devices: 17.5 us -> 19.4 us  [from_partner(): lax.ppermute(x, axis, [(i, i ^ 1 << distance) for i in range(lax.axis_siz...]
    select_n x1, other arithmetic: 1.18 us -> 0.14 us  [local(): picked = jnp.take(blocks_all, block_index, axis=1)]
    unnamed x30 -> x29, local copies, waits for them, and re-layouts: 2.54 us -> 2.44 us
where the time goes in v10:
time: 95.2 us; the launch traced here: 94.4 us
  Pallas kernels  32.6 us (34%)
  matrix products  26.7 us (28%)
  starting transfers between devices  22.9 us (24%)
  local copies, waits for them, and re-layouts  8.04 us (8%)
  waiting for transfers between devices  3.51 us (4%)
    pallas_call x1, Pallas kernels, gather_points(): pl.pallas_call(gather_kernel, out_shape=jax.ShapeDtypeStruct((width, coun...  32.6 us
    ppermute x7, starting transfers between devices, from_partner(): lax.ppermute(x, axis, [(i, i ^ 1 << distance) for i in range(lax.axis_siz...  19.4 us
    dot_general x1, matrix products, local(): jnp.einsum('lpq,slq->slp', band_blocks[half:, 0], own_second, preferred_e...  4.19 us
    dot_general x7, matrix products, translate(): jnp.dot(level_matrices[0], own_coeffs, precision=lax.Precision.HIGHEST, p...  3.65 us
    dot_general x7, matrix products, translate(): jnp.dot(level_matrices[1], other_coeffs, precision=lax.Precision.HIGHEST,...  3.62 us
    dot_general x1, matrix products, local(): jnp.einsum('lpq,slq->slp', band_blocks[:half, 0], own_first, preferred_el...  3.47 us
    dot_general x1, matrix products, local(): jnp.einsum('lpq,slq->slp', band_blocks[:half, 1], picked_first, preferred...  3.38 us
    dot_general x1, matrix products, local(): jnp.einsum('lpq,slq->slp', band_blocks[half:, 1], picked_second, preferre...  3.38 us
  transfers between devices with their start and end apart: 9, of which 4 were waited for; matrix products, arithmetic and copies ran while one was open for 25% of the time, Pallas kernels for 0%

profile of v10, /device:TPU:0, one launch (start us, length us, event | category | flops | bytes accessed | tf_op | source)
XLA Modules:
  0.0 94.4 jit_solution(208351743523587197)
XLA Ops:
  0.0 1.4 %copy-done.1 = f32[16,16384]{1,0:T(8,128)S(1)} copy-done((f32[16,16384]{1,0:T(8,128)S(1)}, f32[16,16384]{1,0:T(8,128)}, u32[]{:S(2)}) %copy-start.1) | copy-done | bytes 1048600
  2.2 32.6 %shard_map.73 = bf16[16,16384]{1,0:T(8,128)(2,1)S(1)} custom-call(s32[16384]{0:T(1024)S(1)} %copy-done.2, f32[16,16384]{1,0:T(8,128)S(1)} %copy-done.1), custom_call_target="tpu_custom_call" | custom-call | bytes 1572864 | tf_op jit(solution)/shard_map/pallas_call | solution.py:35
  34.8 1.6 %fusion.32 = f32[64,16,32]{2,1,0:T(8,128)S(1)} fusion(bf16[64,32,256]{2,1,0:T(8,128)(2,1)} %param.10, bf16[2,64,8,256]{3,2,1,0:T(8,128)(2,1)S(1)} %bitcast.126), kind=kOutput, calls=%fused_computation.41 | convolution fusion | flops 16777216 | bytes 1703936 | tf_op jit(solution)/shard_map/lrp,slp->rls/dot_general | solution.py:98
  36.6 1.8 %collective-permute-start = (f32[256,128]{1,0:T(8,128)S(1)}, f32[256,128]{1,0:T(8,128)S(1)}, u32[]{:S(2)}, u32[]{:S(2)}) collective-permute-start(f32[256,128]{1,0:T(8,128)S(1)} %bitcast.147), channel_id=1, source_target_pairs={{0,1},{1,0},{2,3},{3,2},{4,5},{5,4},{6,7},{7,6},{8,9},{9,8},{10,11... | collective-permute-start | bytes 393224 | tf_op jit(solution)/shard_map/ppermute | solution.py:47
  38.4 2.2 %collective-permute-start.1 = (bf16[16,4096]{1,0:T(8,128)(2,1)S(1)}, bf16[16,4096]{1,0:T(8,128)(2,1)S(1)}, u32[]{:S(2)}, u32[]{:S(2)}) collective-permute-start(bf16[16,4096]{1,0:T(8,128)(2,1)S(1)} %get-tuple-element.45), channel_id=1, source_target_pairs={{0,1},{1,2},{2,3},{3,4},{4,5},{5,6},{6,7},{7,8},{8,9},{9,10},{10,1... | collective-permute-start | bytes 393224 | tf_op jit(solution)/shard_map/ppermute | solution.py:57
  40.6 1.3 %collective-permute-start.2 = (bf16[16,4096]{1,0:T(8,128)(2,1)S(1)}, bf16[16,4096]{1,0:T(8,128)(2,1)S(1)}, u32[]{:S(2)}, u32[]{:S(2)}) collective-permute-start(bf16[16,4096]{1,0:T(8,128)(2,1)S(1)} %get-tuple-element.46), channel_id=1, source_target_pairs={{1,0},{2,1},{3,2},{4,3},{5,4},{6,5},{7,6},{8,7},{9,8},{10,9},{11,1... | collective-permute-start | bytes 393224 | tf_op jit(solution)/shard_map/ppermute | solution.py:58
  42.0 1.7 %convolution_bitcast_fusion = f32[7,2,8,32,256]{4,3,1,0,2:T(8,128)S(1)} fusion(s32[8]{0:T(128)S(1)} %iota_multiply_fusion, f32[1,7,8,2,32,32]{5,4,3,2,1,0:T(8,128)S(1)} %copy-done), kind=kOutput, calls=%fused_computation.13 | convolution fusion | flops 352452608 | bytes 4128800 | tf_op jit(solution)/shard_map/lgtab,gbc->ltgac/dot_general | solution.py:69
  43.7 1.6 %fusion.33 = (f32[1,1,8,32,256]{4,3,1,0,2:T(8,128)}, f32[1,1,8,32,256]{4,3,1,0,2:T(8,128)}, f32[1,1,8,32,256]{4,3,1,0,2:T(8,128)S(1)}, f32[1,1,8,32,256]{4,3,1,0...) fusion(f32[7,2,8,32,256]{4,3,1,0,2:T(8,128)S(1)} %convolution_b, ...), kind=kLoop, calls=%fused_computation.42 | loop fusion | bytes 7340032 | tf_op jit(solution)/shard_map/slice | solution.py:82
  46.6 1.4 %collective-permute-done.2 = bf16[16,4096]{1,0:T(8,128)(2,1)S(1)} collective-permute-done((bf16[16,4096]{1,0:T(8,128)(2,1)S(1)}, bf16[16,4096]{1,0:T(8,128)(2,1)S(1)}, u32[]{:S(2)}, u32[]{:S(2)}) %collective-permute-start.2) | collective-permute-done | bytes 131104 | tf_op jit(solution)/shard_map/ppermute | solution.py:58
  48.6 5.2 %collective-permute-start.3 = (f32[256,128]{1,0:T(8,128)S(1)}, f32[256,128]{1,0:T(8,128)}, u32[]{:S(2)}, u32[]{:S(2)}) collective-permute-start(f32[256,128]{1,0:T(8,128)S(1)} %convolution_add_fusion.6), channel_id=1, source_target_pairs={{0,2},{1,3},{2,0},{3,1},{4,6},{5,7},{6,4},{7,5},{8,10},{9,11},{10,... | collective-permute-start | bytes 393224 | tf_op jit(solution)/shard_map/ppermute | solution.py:47
  55.1 1.4 %fusion.38 = f32[256,128]{1,0:T(8,128)S(1)} fusion(f32[256,256]{1,0:T(8,128)} %bitcast.144, f32[256,128]{1,0:T(8,128)S(1)} %convolution_add_fusion.6), kind=kOutput, calls=%fused_computation.47 | convolution fusion | flops 100663296 | bytes 524288 | tf_op jit(solution)/shard_map/dot_general | solution.py:75
  56.9 1.4 %convolution_add_fusion.5 = f32[256,128]{1,0:T(8,128)S(1)} fusion(f32[256,128]{1,0:T(8,128)S(1)} %fusion.38, f32[256,256]{1,0:T(8,128)} %bitcast.143, f32[256,128]{1,0:T(8,128)} %collective-permute-done.3), kind=kOutput, calls=%fused_computation.28 | convolution fusion | flops 100696064 | bytes 655360 | tf_op jit(solution)/shard_map/dot_general | solution.py:81
  58.3 6.8 %collective-permute-start.4 = (f32[256,128]{1,0:T(8,128)S(1)}, f32[256,128]{1,0:T(8,128)S(1)}, u32[]{:S(2)}, u32[]{:S(2)}) collective-permute-start(f32[256,128]{1,0:T(8,128)S(1)} %convolution_add_fusion.5), channel_id=1, source_target_pairs={{0,4},{1,5},{2,6},{3,7},{4,0},{5,1},{6,2},{7,3},{8,12},{9,13},{10,... | collective-permute-start | bytes 393224 | tf_op jit(solution)/shard_map/ppermute | solution.py:47
  65.1 3.5 %fusion.16 = f32[16,32,256]{2,0,1:T(8,128)S(1)} fusion(bf16[16,32,256]{2,0,1:T(8,128)(2,1)} %get-tuple-element.21, bf16[64,2,256,256]{3,2,1,0:T(8,128)(2,1)} %param.11), kind=kOutput, calls=%fused_computation.19 | convolution fusion | flops 67108864 | bytes 4980736 | tf_op jit(solution)/shard_map/lpq,slq->slp/dot_general | solution.py:134
  69.9 0.9 collective-permute-done.5
  71.2 1.1 %collective-permute-start.6 = (f32[256,128]{1,0:T(8,128)S(1)}, f32[256,128]{1,0:T(8,128)S(1)}, u32[]{:S(2)}, u32[]{:S(2)}) collective-permute-start(f32[256,128]{1,0:T(8,128)S(1)} %convolution_add_fusion.3), channel_id=1, source_target_pairs={{0,16},{8,24},{16,0},{24,8},{32,48},{40,56},{48,32},{56,40},{64,80... | collective-permute-start | bytes 393224 | tf_op jit(solution)/shard_map/ppermute | solution.py:47
  72.3 3.4 %fusion.22 = f32[16,32,256]{2,0,1:T(8,128)S(1)} fusion(bf16[16,32,256]{2,0,1:T(8,128)(2,1)S(1)} %get-tuple-element.23, bf16[64,2,256,256]{3,2,1,0:T(8,128)(2,1)} %param.11), kind=kOutput, calls=%fused_computation.21 | convolution fusion | flops 67108864 | bytes 4980736 | tf_op jit(solution)/shard_map/lpq,slq->slp/dot_general | solution.py:139
  77.2 1.6 %collective-permute-start.7 = (f32[256,128]{1,0:T(8,128)S(1)}, f32[256,128]{1,0:T(8,128)S(1)}, u32[]{:S(2)}, u32[]{:S(2)}) collective-permute-start(f32[256,128]{1,0:T(8,128)S(1)} %convolution_add_fusion.2), channel_id=1, source_target_pairs={{0,32},{8,40},{16,48},{24,56},{32,0},{40,8},{48,16},{56,24},{64,96... | collective-permute-start | bytes 393224 | tf_op jit(solution)/shard_map/ppermute | solution.py:47
  78.8 3.4 %fusion.25 = f32[16,32,256]{2,0,1:T(8,128)S(1)} fusion(bf16[16,32,256]{2,0,1:T(8,128)(2,1)S(1)} %get-tuple-element.24, bf16[64,2,256,256]{3,2,1,0:T(8,128)(2,1)} %param.11), kind=kOutput, calls=%fused_computation.22 | convolution fusion | flops 67108864 | bytes 4980736 | tf_op jit(solution)/shard_map/lpq,slq->slp/dot_general | solution.py:142
  82.9 2.8 %collective-permute-start.8 = (f32[256,128]{1,0:T(8,128)S(1)}, f32[256,128]{1,0:T(8,128)S(1)}, u32[]{:S(2)}, u32[]{:S(2)}) collective-permute-start(f32[256,128]{1,0:T(8,128)S(1)} %convolution_add_fusion.1), channel_id=1, source_target_pairs={{0,64},{8,72},{16,80},{24,88},{32,96},{40,104},{48,112},{56,120},{... | collective-permute-start | bytes 393224 | tf_op jit(solution)/shard_map/ppermute | solution.py:47
  85.8 4.2 %fusion.19 = f32[16,32,256]{2,0,1:T(8,128)} fusion(bf16[16,32,256]{2,0,1:T(8,128)(2,1)S(1)} %copy-done.12, bf16[64,2,256,256]{3,2,1,0:T(8,128)(2,1)} %param.11), kind=kOutput, calls=%fused_computation.20 | convolution fusion | flops 67108864 | bytes 4980736 | tf_op jit(solution)/shard_map/lpq,slq->slp/dot_general | solution.py:135
  90.8 0.8 copy.23
  91.6 1.7 %fusion.15 = f32[64,2,8,256]{3,2,1,0:T(8,128)S(1)} fusion(bf16[32,64,16]{0,2,1:T(8,128)(2,1)} %bitcast.132, bf16[64,32,256]{2,1,0:T(8,128)(2,1)} %param.13, f32[16,32,256]{2,0,1:T(8,128)} %fusion.19, f32[16,32,256]{2,0,1:T(8,128)S(1)} %fusion.16, f32[16,32,256]{2,0,1:T(8,128)S(1)} %fusion.25, f32[16,32,256]{2,0,1:T(8,128)S(1)} %fusion.22), kind=kOutput, calls=%fused_computation.18 | convolution fusion | flops 17825792 | bytes 4259840 | tf_op jit(solution)/shard_map/lrp,rls->slp/dot_general | solution.py:131
  93.3 1.1 %copy.35 = f32[64,2,8,256]{3,2,0,1:T(8,128)} copy(f32[64,2,8,256]{3,2,1,0:T(8,128)S(1)} %fusion.15) | data formatting | bytes 2097152 | tf_op jit(solution)/shard_map/reshape | solution.py:146
  (60 shorter events, 9.2 us)
Async XLA Ops:
  0.0 42.0 %copy-start = (f32[1,7,8,2,32,32]{5,4,3,2,1,0:T(8,128)S(1)}, f32[1,7,8,2,32,32]{5,4,3,2,1,0:T(8,128)}, u32[]{:S(2)}) copy-start(f32[1,7,8,2,32,32]{5,4,3,2,1,0:T(8,128)} %param.12) | copy-start | bytes 1376260
  0.0 1.4 %copy-start.1 = (f32[16,16384]{1,0:T(8,128)S(1)}, f32[16,16384]{1,0:T(8,128)}, u32[]{:S(2)}) copy-start(f32[16,16384]{1,0:T(8,128)} %x_ref.1) | copy-start | bytes 3145732
  1.4 0.8 copy-start.2
  36.6 11.6 %collective-permute-start = (f32[256,128]{1,0:T(8,128)S(1)}, f32[256,128]{1,0:T(8,128)S(1)}, u32[]{:S(2)}, u32[]{:S(2)}) collective-permute-start(f32[256,128]{1,0:T(8,128)S(1)} %bitcast.147), channel_id=1, source_target_pairs={{0,1},{1,0},{2,3},{3,2},{4,5},{5,4},{6,7},{7,6},{8,9},{9,8},{10,11... | collective-permute-start | bytes 393224 | tf_op jit(solution)/shard_map/ppermute | solution.py:47
  38.4 8.2 %collective-permute-start.1 = (bf16[16,4096]{1,0:T(8,128)(2,1)S(1)}, bf16[16,4096]{1,0:T(8,128)(2,1)S(1)}, u32[]{:S(2)}, u32[]{:S(2)}) collective-permute-start(bf16[16,4096]{1,0:T(8,128)(2,1)S(1)} %get-tuple-element.45), channel_id=1, source_target_pairs={{0,1},{1,2},{2,3},{3,4},{4,5},{5,6},{6,7},{7,8},{8,9},{9,10},{10,1... | collective-permute-start | bytes 393224 | tf_op jit(solution)/shard_map/ppermute | solution.py:57
  40.6 7.4 %collective-permute-start.2 = (bf16[16,4096]{1,0:T(8,128)(2,1)S(1)}, bf16[16,4096]{1,0:T(8,128)(2,1)S(1)}, u32[]{:S(2)}, u32[]{:S(2)}) collective-permute-start(bf16[16,4096]{1,0:T(8,128)(2,1)S(1)} %get-tuple-element.46), channel_id=1, source_target_pairs={{1,0},{2,1},{3,2},{4,3},{5,4},{6,5},{7,6},{8,7},{9,8},{10,9},{11,1... | collective-permute-start | bytes 393224 | tf_op jit(solution)/shard_map/ppermute | solution.py:58
  43.7 2.8 %copy-start.13 = (s32[64]{0:T(128)S(1)}, s32[64]{0:T(128)}, u32[]{:S(2)}) copy-start(s32[64]{0:T(128)} %param.9) | copy-start | bytes 772
  48.6 8.3 %collective-permute-start.3 = (f32[256,128]{1,0:T(8,128)S(1)}, f32[256,128]{1,0:T(8,128)}, u32[]{:S(2)}, u32[]{:S(2)}) collective-permute-start(f32[256,128]{1,0:T(8,128)S(1)} %convolution_add_fusion.6), channel_id=1, source_target_pairs={{0,2},{1,3},{2,0},{3,1},{4,6},{5,7},{6,4},{7,5},{8,10},{9,11},{10,... | collective-permute-start | bytes 393224 | tf_op jit(solution)/shard_map/ppermute | solution.py:47
  54.9 13.7 %copy-start.11 = (f32[1,1,8,32,256]{4,3,1,0,2:T(8,128)S(1)}, f32[1,1,8,32,256]{4,3,1,0,2:T(8,128)}, u32[]{:S(2)}) copy-start(f32[1,1,8,32,256]{4,3,1,0,2:T(8,128)} %get-tuple-element.36) | copy-start | bytes 786436
  54.9 14.1 %copy-start.10 = (f32[1,1,8,32,256]{4,3,1,0,2:T(8,128)S(1)}, f32[1,1,8,32,256]{4,3,1,0,2:T(8,128)}, u32[]{:S(2)}) copy-start(f32[1,1,8,32,256]{4,3,1,0,2:T(8,128)} %get-tuple-element.31) | copy-start | bytes 786436
  55.1 14.4 %copy-start.9 = (f32[1,1,8,32,256]{4,3,1,0,2:T(8,128)S(1)}, f32[1,1,8,32,256]{4,3,1,0,2:T(8,128)}, u32[]{:S(2)}) copy-start(f32[1,1,8,32,256]{4,3,1,0,2:T(8,128)} %get-tuple-element.37) | copy-start | bytes 786436
  55.1 15.7 %copy-start.8 = (f32[1,1,8,32,256]{4,3,1,0,2:T(8,128)S(1)}, f32[1,1,8,32,256]{4,3,1,0,2:T(8,128)}, u32[]{:S(2)}) copy-start(f32[1,1,8,32,256]{4,3,1,0,2:T(8,128)} %get-tuple-element.30) | copy-start | bytes 786436
  58.3 10.7 %collective-permute-start.4 = (f32[256,128]{1,0:T(8,128)S(1)}, f32[256,128]{1,0:T(8,128)S(1)}, u32[]{:S(2)}, u32[]{:S(2)}) collective-permute-start(f32[256,128]{1,0:T(8,128)S(1)} %convolution_add_fusion.5), channel_id=1, source_target_pairs={{0,4},{1,5},{2,6},{3,7},{4,0},{5,1},{6,2},{7,3},{8,12},{9,13},{10,... | collective-permute-start | bytes 393224 | tf_op jit(solution)/shard_map/ppermute | solution.py:47
  68.6 7.1 %copy-start.7 = (f32[1,1,8,32,256]{4,3,1,0,2:T(8,128)S(1)}, f32[1,1,8,32,256]{4,3,1,0,2:T(8,128)}, u32[]{:S(2)}) copy-start(f32[1,1,8,32,256]{4,3,1,0,2:T(8,128)} %get-tuple-element.38) | copy-start | bytes 786436
  69.4 1.4 %collective-permute-start.5 = (f32[256,128]{1,0:T(8,128)S(1)}, f32[256,128]{1,0:T(8,128)S(1)}, u32[]{:S(2)}, u32[]{:S(2)}) collective-permute-start(f32[256,128]{1,0:T(8,128)S(1)} %convolution_add_fusion.4), channel_id=1, source_target_pairs={{0,8},{8,0},{16,24},{24,16},{32,40},{40,32},{48,56},{56,48},{64,72... | collective-permute-start | bytes 393224 | tf_op jit(solution)/shard_map/ppermute | solution.py:47
  71.2 5.6 %collective-permute-start.6 = (f32[256,128]{1,0:T(8,128)S(1)}, f32[256,128]{1,0:T(8,128)S(1)}, u32[]{:S(2)}, u32[]{:S(2)}) collective-permute-start(f32[256,128]{1,0:T(8,128)S(1)} %convolution_add_fusion.3), channel_id=1, source_target_pairs={{0,16},{8,24},{16,0},{24,8},{32,48},{40,56},{48,32},{56,40},{64,80... | collective-permute-start | bytes 393224 | tf_op jit(solution)/shard_map/ppermute | solution.py:47
  75.7 6.5 %copy-start.6 = (f32[1,1,8,32,256]{4,3,1,0,2:T(8,128)S(1)}, f32[1,1,8,32,256]{4,3,1,0,2:T(8,128)}, u32[]{:S(2)}) copy-start(f32[1,1,8,32,256]{4,3,1,0,2:T(8,128)} %get-tuple-element.39) | copy-start | bytes 786436
  75.7 6.9 %copy-start.5 = (f32[1,1,8,32,256]{4,3,1,0,2:T(8,128)S(1)}, f32[1,1,8,32,256]{4,3,1,0,2:T(8,128)}, u32[]{:S(2)}) copy-start(f32[1,1,8,32,256]{4,3,1,0,2:T(8,128)} %get-tuple-element.28) | copy-start | bytes 786436
  75.7 10.1 %copy-start.12 = (bf16[16,32,256]{2,0,1:T(8,128)(2,1)S(1)}, bf16[16,32,256]{2,0,1:T(8,128)(2,1)}, u32[]{:S(2)}) copy-start(bf16[16,32,256]{2,0,1:T(8,128)(2,1)} %get-tuple-element.22) | copy-start | bytes 786436
  77.2 5.4 %collective-permute-start.7 = (f32[256,128]{1,0:T(8,128)S(1)}, f32[256,128]{1,0:T(8,128)S(1)}, u32[]{:S(2)}, u32[]{:S(2)}) collective-permute-start(f32[256,128]{1,0:T(8,128)S(1)} %convolution_add_fusion.2), channel_id=1, source_target_pairs={{0,32},{8,40},{16,48},{24,56},{32,0},{40,8},{48,16},{56,24},{64,96... | collective-permute-start | bytes 393224 | tf_op jit(solution)/shard_map/ppermute | solution.py:47
  82.1 7.8 %copy-start.4 = (f32[1,1,8,32,256]{4,3,1,0,2:T(8,128)S(1)}, f32[1,1,8,32,256]{4,3,1,0,2:T(8,128)}, u32[]{:S(2)}) copy-start(f32[1,1,8,32,256]{4,3,1,0,2:T(8,128)} %get-tuple-element.40) | copy-start | bytes 786436
  82.1 8.2 %copy-start.3 = (f32[1,1,8,32,256]{4,3,1,0,2:T(8,128)S(1)}, f32[1,1,8,32,256]{4,3,1,0,2:T(8,128)}, u32[]{:S(2)}) copy-start(f32[1,1,8,32,256]{4,3,1,0,2:T(8,128)} %get-tuple-element.27) | copy-start | bytes 786436
  82.9 7.4 %collective-permute-start.8 = (f32[256,128]{1,0:T(8,128)S(1)}, f32[256,128]{1,0:T(8,128)S(1)}, u32[]{:S(2)}, u32[]{:S(2)}) collective-permute-start(f32[256,128]{1,0:T(8,128)S(1)} %convolution_add_fusion.1), channel_id=1, source_target_pairs={{0,64},{8,72},{16,80},{24,88},{32,96},{40,104},{48,112},{56,120},{... | collective-permute-start | bytes 393224 | tf_op jit(solution)/shard_map/ppermute | solution.py:47

commit v11 on v10

--- a/solution.py
+++ b/solution.py
@@ -75,13 +75,13 @@
     first = jnp.dot(
         level_matrices[0],
         own_coeffs,
-        precision=lax.Precision.HIGHEST,
+        precision=lax.Precision.HIGH,
         preferred_element_type=jnp.float32,
     )
     second = jnp.dot(
         level_matrices[1],
         other_coeffs,
-        precision=lax.Precision.HIGHEST,
+        precision=lax.Precision.HIGH,
         preferred_element_type=jnp.float32,
     )
     return first + second

time: 95.2 us -> 94.4 us (level)
  matrix products: 26.7 us -> 25.3 us
    dot_general x14, matrix products: 7.27 us -> 5.87 us  [the longest x7 2.94 us: translate(): jnp.dot(level_matrices[0], own_coeffs, precision=lax.Precision.HIGH, pref...]
where the time goes in v11:
time: 94.4 us; the launch traced here: 93.3 us
  Pallas kernels  32.6 us (35%)
  matrix products  25.3 us (27%)
  starting transfers between devices  22.8 us (24%)
  local copies, waits for them, and re-layouts  8.04 us (9%)
  waiting for transfers between devices  3.94 us (4%)
    pallas_call x1, Pallas kernels, gather_points(): pl.pallas_call(gather_kernel, out_shape=jax.ShapeDtypeStruct((width, coun...  32.6 us
    ppermute x7, starting transfers between devices, from_partner(): lax.ppermute(x, axis, [(i, i ^ 1 << distance) for i in range(lax.axis_siz...  19.3 us
    dot_general x1, matrix products, local(): jnp.einsum('lpq,slq->slp', band_blocks[half:, 0], own_second, preferred_e...  4.19 us
    dot_general x1, matrix products, local(): jnp.einsum('lpq,slq->slp', band_blocks[:half, 0], own_first, preferred_el...  3.47 us
    dot_general x1, matrix products, local(): jnp.einsum('lpq,slq->slp', band_blocks[:half, 1], picked_first, preferred...  3.38 us
    dot_general x1, matrix products, local(): jnp.einsum('lpq,slq->slp', band_blocks[half:, 1], picked_second, preferre...  3.38 us
    dot_general x7, matrix products, translate(): jnp.dot(level_matrices[0], own_coeffs, precision=lax.Precision.HIGH, pref...  2.94 us
    dot_general x7, matrix products, translate(): jnp.dot(level_matrices[1], other_coeffs, precision=lax.Precision.HIGH, pr...  2.93 us
  transfers between devices with their start and end apart: 9, of which 4 were waited for; matrix products, arithmetic and copies ran while one was open for 25% of the time, Pallas kernels for 0%

profile of v11, /device:TPU:0, one launch (start us, length us, event | category | flops | bytes accessed | tf_op | source)
XLA Modules:
  0.0 93.3 jit_solution(14603445304343371394)
XLA Ops:
  0.0 1.4 %copy-done.1 = f32[16,16384]{1,0:T(8,128)S(1)} copy-done((f32[16,16384]{1,0:T(8,128)S(1)}, f32[16,16384]{1,0:T(8,128)}, u32[]{:S(2)}) %copy-start.1) | copy-done | bytes 1048600
  2.2 32.6 %shard_map.73 = bf16[16,16384]{1,0:T(8,128)(2,1)S(1)} custom-call(s32[16384]{0:T(1024)S(1)} %copy-done.2, f32[16,16384]{1,0:T(8,128)S(1)} %copy-done.1), custom_call_target="tpu_custom_call" | custom-call | bytes 1572864 | tf_op jit(solution)/shard_map/pallas_call | solution.py:35
  34.8 1.6 %fusion.32 = f32[64,16,32]{2,1,0:T(8,128)S(1)} fusion(bf16[64,32,256]{2,1,0:T(8,128)(2,1)} %param.10, bf16[2,64,8,256]{3,2,1,0:T(8,128)(2,1)S(1)} %bitcast.126), kind=kOutput, calls=%fused_computation.41 | convolution fusion | flops 16777216 | bytes 1703936 | tf_op jit(solution)/shard_map/lrp,slp->rls/dot_general | solution.py:98
  36.6 1.8 %collective-permute-start = (f32[256,128]{1,0:T(8,128)S(1)}, f32[256,128]{1,0:T(8,128)S(1)}, u32[]{:S(2)}, u32[]{:S(2)}) collective-permute-start(f32[256,128]{1,0:T(8,128)S(1)} %bitcast.147), channel_id=1, source_target_pairs={{0,1},{1,0},{2,3},{3,2},{4,5},{5,4},{6,7},{7,6},{8,9},{9,8},{10,11... | collective-permute-start | bytes 393224 | tf_op jit(solution)/shard_map/ppermute | solution.py:47
  38.4 2.2 %collective-permute-start.1 = (bf16[16,4096]{1,0:T(8,128)(2,1)S(1)}, bf16[16,4096]{1,0:T(8,128)(2,1)S(1)}, u32[]{:S(2)}, u32[]{:S(2)}) collective-permute-start(bf16[16,4096]{1,0:T(8,128)(2,1)S(1)} %get-tuple-element.45), channel_id=1, source_target_pairs={{0,1},{1,2},{2,3},{3,4},{4,5},{5,6},{6,7},{7,8},{8,9},{9,10},{10,1... | collective-permute-start | bytes 393224 | tf_op jit(solution)/shard_map/ppermute | solution.py:57
  40.6 1.3 %collective-permute-start.2 = (bf16[16,4096]{1,0:T(8,128)(2,1)S(1)}, bf16[16,4096]{1,0:T(8,128)(2,1)S(1)}, u32[]{:S(2)}, u32[]{:S(2)}) collective-permute-start(bf16[16,4096]{1,0:T(8,128)(2,1)S(1)} %get-tuple-element.46), channel_id=1, source_target_pairs={{1,0},{2,1},{3,2},{4,3},{5,4},{6,5},{7,6},{8,7},{9,8},{10,9},{11,1... | collective-permute-start | bytes 393224 | tf_op jit(solution)/shard_map/ppermute | solution.py:58
  42.0 1.7 %convolution_bitcast_fusion = f32[7,2,8,32,256]{4,3,1,0,2:T(8,128)S(1)} fusion(s32[8]{0:T(128)S(1)} %iota_multiply_fusion, f32[1,7,8,2,32,32]{5,4,3,2,1,0:T(8,128)S(1)} %copy-done), kind=kOutput, calls=%fused_computation.13 | convolution fusion | flops 352452608 | bytes 4128800 | tf_op jit(solution)/shard_map/lgtab,gbc->ltgac/dot_general | solution.py:69
  43.7 1.6 %fusion.33 = (f32[1,1,8,32,256]{4,3,1,0,2:T(8,128)}, f32[1,1,8,32,256]{4,3,1,0,2:T(8,128)}, f32[1,1,8,32,256]{4,3,1,0,2:T(8,128)S(1)}, f32[1,1,8,32,256]{4,3,1,0...) fusion(f32[7,2,8,32,256]{4,3,1,0,2:T(8,128)S(1)} %convolution_b, ...), kind=kLoop, calls=%fused_computation.42 | loop fusion | bytes 7340032 | tf_op jit(solution)/shard_map/slice | solution.py:82
  46.5 1.5 %collective-permute-done.2 = bf16[16,4096]{1,0:T(8,128)(2,1)S(1)} collective-permute-done((bf16[16,4096]{1,0:T(8,128)(2,1)S(1)}, bf16[16,4096]{1,0:T(8,128)(2,1)S(1)}, u32[]{:S(2)}, u32[]{:S(2)}) %collective-permute-start.2) | collective-permute-done | bytes 131104 | tf_op jit(solution)/shard_map/ppermute | solution.py:58
  48.5 5.2 %collective-permute-start.3 = (f32[256,128]{1,0:T(8,128)S(1)}, f32[256,128]{1,0:T(8,128)}, u32[]{:S(2)}, u32[]{:S(2)}) collective-permute-start(f32[256,128]{1,0:T(8,128)S(1)} %convolution_add_fusion.6), channel_id=1, source_target_pairs={{0,2},{1,3},{2,0},{3,1},{4,6},{5,7},{6,4},{7,5},{8,10},{9,11},{10,... | collective-permute-start | bytes 393224 | tf_op jit(solution)/shard_map/ppermute | solution.py:47
  55.0 1.3 %fusion.38 = f32[256,128]{1,0:T(8,128)S(1)} fusion(f32[256,256]{1,0:T(8,128)} %bitcast.144, f32[256,128]{1,0:T(8,128)S(1)} %convolution_add_fusion.6), kind=kOutput, calls=%fused_computation.47 | convolution fusion | flops 50331648 | bytes 524288 | tf_op jit(solution)/shard_map/dot_general | solution.py:75
  56.8 1.3 %convolution_add_fusion.5 = f32[256,128]{1,0:T(8,128)S(1)} fusion(f32[256,128]{1,0:T(8,128)S(1)} %fusion.38, f32[256,256]{1,0:T(8,128)} %bitcast.143, f32[256,128]{1,0:T(8,128)} %collective-permute-done.3), kind=kOutput, calls=%fused_computation.28 | convolution fusion | flops 50364416 | bytes 655360 | tf_op jit(solution)/shard_map/dot_general | solution.py:81
  58.1 6.7 %collective-permute-start.4 = (f32[256,128]{1,0:T(8,128)S(1)}, f32[256,128]{1,0:T(8,128)S(1)}, u32[]{:S(2)}, u32[]{:S(2)}) collective-permute-start(f32[256,128]{1,0:T(8,128)S(1)} %convolution_add_fusion.5), channel_id=1, source_target_pairs={{0,4},{1,5},{2,6},{3,7},{4,0},{5,1},{6,2},{7,3},{8,12},{9,13},{10,... | collective-permute-start | bytes 393224 | tf_op jit(solution)/shard_map/ppermute | solution.py:47
  64.8 3.5 %fusion.16 = f32[16,32,256]{2,0,1:T(8,128)S(1)} fusion(bf16[16,32,256]{2,0,1:T(8,128)(2,1)} %get-tuple-element.21, bf16[64,2,256,256]{3,2,1,0:T(8,128)(2,1)} %param.11), kind=kOutput, calls=%fused_computation.19 | convolution fusion | flops 67108864 | bytes 4980736 | tf_op jit(solution)/shard_map/lpq,slq->slp/dot_general | solution.py:134
  69.3 1.0 %collective-permute-done.5 = f32[256,128]{1,0:T(8,128)S(1)} collective-permute-done((f32[256,128]{1,0:T(8,128)S(1)}, f32[256,128]{1,0:T(8,128)S(1)}, u32[]{:S(2)}, u32[]{:S(2)}) %collective-permute-start.5) | collective-permute-done | bytes 131104 | tf_op jit(solution)/shard_map/ppermute | solution.py:47
  70.6 1.1 %collective-permute-start.6 = (f32[256,128]{1,0:T(8,128)S(1)}, f32[256,128]{1,0:T(8,128)S(1)}, u32[]{:S(2)}, u32[]{:S(2)}) collective-permute-start(f32[256,128]{1,0:T(8,128)S(1)} %convolution_add_fusion.3), channel_id=1, source_target_pairs={{0,16},{8,24},{16,0},{24,8},{32,48},{40,56},{48,32},{56,40},{64,80... | collective-permute-start | bytes 393224 | tf_op jit(solution)/shard_map/ppermute | solution.py:47
  71.7 3.4 %fusion.22 = f32[16,32,256]{2,0,1:T(8,128)S(1)} fusion(bf16[16,32,256]{2,0,1:T(8,128)(2,1)S(1)} %get-tuple-element.23, bf16[64,2,256,256]{3,2,1,0:T(8,128)(2,1)} %param.11), kind=kOutput, calls=%fused_computation.21 | convolution fusion | flops 67108864 | bytes 4980736 | tf_op jit(solution)/shard_map/lpq,slq->slp/dot_general | solution.py:139
  75.4 0.8 collective-permute-done.6
  76.5 1.6 %collective-permute-start.7 = (f32[256,128]{1,0:T(8,128)S(1)}, f32[256,128]{1,0:T(8,128)S(1)}, u32[]{:S(2)}, u32[]{:S(2)}) collective-permute-start(f32[256,128]{1,0:T(8,128)S(1)} %convolution_add_fusion.2), channel_id=1, source_target_pairs={{0,32},{8,40},{16,48},{24,56},{32,0},{40,8},{48,16},{56,24},{64,96... | collective-permute-start | bytes 393224 | tf_op jit(solution)/shard_map/ppermute | solution.py:47
  78.1 3.4 %fusion.25 = f32[16,32,256]{2,0,1:T(8,128)S(1)} fusion(bf16[16,32,256]{2,0,1:T(8,128)(2,1)S(1)} %get-tuple-element.24, bf16[64,2,256,256]{3,2,1,0:T(8,128)(2,1)} %param.11), kind=kOutput, calls=%fused_computation.22 | convolution fusion | flops 67108864 | bytes 4980736 | tf_op jit(solution)/shard_map/lpq,slq->slp/dot_general | solution.py:142
  82.1 2.9 %collective-permute-start.8 = (f32[256,128]{1,0:T(8,128)S(1)}, f32[256,128]{1,0:T(8,128)S(1)}, u32[]{:S(2)}, u32[]{:S(2)}) collective-permute-start(f32[256,128]{1,0:T(8,128)S(1)} %convolution_add_fusion.1), channel_id=1, source_target_pairs={{0,64},{8,72},{16,80},{24,88},{32,96},{40,104},{48,112},{56,120},{... | collective-permute-start | bytes 393224 | tf_op jit(solution)/shard_map/ppermute | solution.py:47
  84.9 4.2 %fusion.19 = f32[16,32,256]{2,0,1:T(8,128)} fusion(bf16[16,32,256]{2,0,1:T(8,128)(2,1)S(1)} %copy-done.12, bf16[64,2,256,256]{3,2,1,0:T(8,128)(2,1)} %param.11), kind=kOutput, calls=%fused_computation.20 | convolution fusion | flops 67108864 | bytes 4980736 | tf_op jit(solution)/shard_map/lpq,slq->slp/dot_general | solution.py:135
  90.6 1.7 %fusion.15 = f32[64,2,8,256]{3,2,1,0:T(8,128)S(1)} fusion(bf16[32,64,16]{0,2,1:T(8,128)(2,1)} %bitcast.132, bf16[64,32,256]{2,1,0:T(8,128)(2,1)} %param.13, f32[16,32,256]{2,0,1:T(8,128)} %fusion.19, f32[16,32,256]{2,0,1:T(8,128)S(1)} %fusion.16, f32[16,32,256]{2,0,1:T(8,128)S(1)} %fusion.25, f32[16,32,256]{2,0,1:T(8,128)S(1)} %fusion.22), kind=kOutput, calls=%fused_computation.18 | convolution fusion | flops 17825792 | bytes 4259840 | tf_op jit(solution)/shard_map/lrp,rls->slp/dot_general | solution.py:131
  92.3 1.1 %copy.35 = f32[64,2,8,256]{3,2,0,1:T(8,128)} copy(f32[64,2,8,256]{3,2,1,0:T(8,128)S(1)} %fusion.15) | data formatting | bytes 2097152 | tf_op jit(solution)/shard_map/reshape | solution.py:146
  (60 shorter events, 8.2 us)
Async XLA Ops:
  0.0 42.0 %copy-start = (f32[1,7,8,2,32,32]{5,4,3,2,1,0:T(8,128)S(1)}, f32[1,7,8,2,32,32]{5,4,3,2,1,0:T(8,128)}, u32[]{:S(2)}) copy-start(f32[1,7,8,2,32,32]{5,4,3,2,1,0:T(8,128)} %param.12) | copy-start | bytes 1376260
  0.0 1.4 %copy-start.1 = (f32[16,16384]{1,0:T(8,128)S(1)}, f32[16,16384]{1,0:T(8,128)}, u32[]{:S(2)}) copy-start(f32[16,16384]{1,0:T(8,128)} %x_ref.1) | copy-start | bytes 3145732
  1.4 0.8 copy-start.2
  36.6 11.6 %collective-permute-start = (f32[256,128]{1,0:T(8,128)S(1)}, f32[256,128]{1,0:T(8,128)S(1)}, u32[]{:S(2)}, u32[]{:S(2)}) collective-permute-start(f32[256,128]{1,0:T(8,128)S(1)} %bitcast.147), channel_id=1, source_target_pairs={{0,1},{1,0},{2,3},{3,2},{4,5},{5,4},{6,7},{7,6},{8,9},{9,8},{10,11... | collective-permute-start | bytes 393224 | tf_op jit(solution)/shard_map/ppermute | solution.py:47
  38.4 8.1 %collective-permute-start.1 = (bf16[16,4096]{1,0:T(8,128)(2,1)S(1)}, bf16[16,4096]{1,0:T(8,128)(2,1)S(1)}, u32[]{:S(2)}, u32[]{:S(2)}) collective-permute-start(bf16[16,4096]{1,0:T(8,128)(2,1)S(1)} %get-tuple-element.45), channel_id=1, source_target_pairs={{0,1},{1,2},{2,3},{3,4},{4,5},{5,6},{6,7},{7,8},{8,9},{9,10},{10,1... | collective-permute-start | bytes 393224 | tf_op jit(solution)/shard_map/ppermute | solution.py:57
  40.6 7.4 %collective-permute-start.2 = (bf16[16,4096]{1,0:T(8,128)(2,1)S(1)}, bf16[16,4096]{1,0:T(8,128)(2,1)S(1)}, u32[]{:S(2)}, u32[]{:S(2)}) collective-permute-start(bf16[16,4096]{1,0:T(8,128)(2,1)S(1)} %get-tuple-element.46), channel_id=1, source_target_pairs={{1,0},{2,1},{3,2},{4,3},{5,4},{6,5},{7,6},{8,7},{9,8},{10,9},{11,1... | collective-permute-start | bytes 393224 | tf_op jit(solution)/shard_map/ppermute | solution.py:58
  43.7 2.7 %copy-start.13 = (s32[64]{0:T(128)S(1)}, s32[64]{0:T(128)}, u32[]{:S(2)}) copy-start(s32[64]{0:T(128)} %param.9) | copy-start | bytes 772
  48.5 8.3 %collective-permute-start.3 = (f32[256,128]{1,0:T(8,128)S(1)}, f32[256,128]{1,0:T(8,128)}, u32[]{:S(2)}, u32[]{:S(2)}) collective-permute-start(f32[256,128]{1,0:T(8,128)S(1)} %convolution_add_fusion.6), channel_id=1, source_target_pairs={{0,2},{1,3},{2,0},{3,1},{4,6},{5,7},{6,4},{7,5},{8,10},{9,11},{10,... | collective-permute-start | bytes 393224 | tf_op jit(solution)/shard_map/ppermute | solution.py:47
  54.8 13.5 %copy-start.11 = (f32[1,1,8,32,256]{4,3,1,0,2:T(8,128)S(1)}, f32[1,1,8,32,256]{4,3,1,0,2:T(8,128)}, u32[]{:S(2)}) copy-start(f32[1,1,8,32,256]{4,3,1,0,2:T(8,128)} %get-tuple-element.36) | copy-start | bytes 786436
  54.8 13.8 %copy-start.10 = (f32[1,1,8,32,256]{4,3,1,0,2:T(8,128)S(1)}, f32[1,1,8,32,256]{4,3,1,0,2:T(8,128)}, u32[]{:S(2)}) copy-start(f32[1,1,8,32,256]{4,3,1,0,2:T(8,128)} %get-tuple-element.31) | copy-start | bytes 786436
  55.0 14.0 %copy-start.9 = (f32[1,1,8,32,256]{4,3,1,0,2:T(8,128)S(1)}, f32[1,1,8,32,256]{4,3,1,0,2:T(8,128)}, u32[]{:S(2)}) copy-start(f32[1,1,8,32,256]{4,3,1,0,2:T(8,128)} %get-tuple-element.37) | copy-start | bytes 786436
  55.0 15.3 %copy-start.8 = (f32[1,1,8,32,256]{4,3,1,0,2:T(8,128)S(1)}, f32[1,1,8,32,256]{4,3,1,0,2:T(8,128)}, u32[]{:S(2)}) copy-start(f32[1,1,8,32,256]{4,3,1,0,2:T(8,128)} %get-tuple-element.30) | copy-start | bytes 786436
  58.1 10.5 %collective-permute-start.4 = (f32[256,128]{1,0:T(8,128)S(1)}, f32[256,128]{1,0:T(8,128)S(1)}, u32[]{:S(2)}, u32[]{:S(2)}) collective-permute-start(f32[256,128]{1,0:T(8,128)S(1)} %convolution_add_fusion.5), channel_id=1, source_target_pairs={{0,4},{1,5},{2,6},{3,7},{4,0},{5,1},{6,2},{7,3},{8,12},{9,13},{10,... | collective-permute-start | bytes 393224 | tf_op jit(solution)/shard_map/ppermute | solution.py:47
  68.3 6.8 %copy-start.7 = (f32[1,1,8,32,256]{4,3,1,0,2:T(8,128)S(1)}, f32[1,1,8,32,256]{4,3,1,0,2:T(8,128)}, u32[]{:S(2)}) copy-start(f32[1,1,8,32,256]{4,3,1,0,2:T(8,128)} %get-tuple-element.38) | copy-start | bytes 786436
  68.9 1.4 %collective-permute-start.5 = (f32[256,128]{1,0:T(8,128)S(1)}, f32[256,128]{1,0:T(8,128)S(1)}, u32[]{:S(2)}, u32[]{:S(2)}) collective-permute-start(f32[256,128]{1,0:T(8,128)S(1)} %convolution_add_fusion.4), channel_id=1, source_target_pairs={{0,8},{8,0},{16,24},{24,16},{32,40},{40,32},{48,56},{56,48},{64,72... | collective-permute-start | bytes 393224 | tf_op jit(solution)/shard_map/ppermute | solution.py:47
  70.6 5.6 %collective-permute-start.6 = (f32[256,128]{1,0:T(8,128)S(1)}, f32[256,128]{1,0:T(8,128)S(1)}, u32[]{:S(2)}, u32[]{:S(2)}) collective-permute-start(f32[256,128]{1,0:T(8,128)S(1)} %convolution_add_fusion.3), channel_id=1, source_target_pairs={{0,16},{8,24},{16,0},{24,8},{32,48},{40,56},{48,32},{56,40},{64,80... | collective-permute-start | bytes 393224 | tf_op jit(solution)/shard_map/ppermute | solution.py:47
  75.1 6.4 %copy-start.6 = (f32[1,1,8,32,256]{4,3,1,0,2:T(8,128)S(1)}, f32[1,1,8,32,256]{4,3,1,0,2:T(8,128)}, u32[]{:S(2)}) copy-start(f32[1,1,8,32,256]{4,3,1,0,2:T(8,128)} %get-tuple-element.39) | copy-start | bytes 786436
  75.1 6.7 %copy-start.5 = (f32[1,1,8,32,256]{4,3,1,0,2:T(8,128)S(1)}, f32[1,1,8,32,256]{4,3,1,0,2:T(8,128)}, u32[]{:S(2)}) copy-start(f32[1,1,8,32,256]{4,3,1,0,2:T(8,128)} %get-tuple-element.28) | copy-start | bytes 786436
  75.1 9.9 %copy-start.12 = (bf16[16,32,256]{2,0,1:T(8,128)(2,1)S(1)}, bf16[16,32,256]{2,0,1:T(8,128)(2,1)}, u32[]{:S(2)}) copy-start(bf16[16,32,256]{2,0,1:T(8,128)(2,1)} %get-tuple-element.22) | copy-start | bytes 786436
  76.5 5.3 %collective-permute-start.7 = (f32[256,128]{1,0:T(8,128)S(1)}, f32[256,128]{1,0:T(8,128)S(1)}, u32[]{:S(2)}, u32[]{:S(2)}) collective-permute-start(f32[256,128]{1,0:T(8,128)S(1)} %convolution_add_fusion.2), channel_id=1, source_target_pairs={{0,32},{8,40},{16,48},{24,56},{32,0},{40,8},{48,16},{56,24},{64,96... | collective-permute-start | bytes 393224 | tf_op jit(solution)/shard_map/ppermute | solution.py:47
  81.4 7.7 %copy-start.4 = (f32[1,1,8,32,256]{4,3,1,0,2:T(8,128)S(1)}, f32[1,1,8,32,256]{4,3,1,0,2:T(8,128)}, u32[]{:S(2)}) copy-start(f32[1,1,8,32,256]{4,3,1,0,2:T(8,128)} %get-tuple-element.40) | copy-start | bytes 786436
  81.4 8.0 %copy-start.3 = (f32[1,1,8,32,256]{4,3,1,0,2:T(8,128)S(1)}, f32[1,1,8,32,256]{4,3,1,0,2:T(8,128)}, u32[]{:S(2)}) copy-start(f32[1,1,8,32,256]{4,3,1,0,2:T(8,128)} %get-tuple-element.27) | copy-start | bytes 786436
  82.1 7.3 %collective-permute-start.8 = (f32[256,128]{1,0:T(8,128)S(1)}, f32[256,128]{1,0:T(8,128)S(1)}, u32[]{:S(2)}, u32[]{:S(2)}) collective-permute-start(f32[256,128]{1,0:T(8,128)S(1)} %convolution_add_fusion.1), channel_id=1, source_target_pairs={{0,64},{8,72},{16,80},{24,88},{32,96},{40,104},{48,112},{56,120},{... | collective-permute-start | bytes 393224 | tf_op jit(solution)/shard_map/ppermute | solution.py:47

commit v12 on v11

--- a/solution.py
+++ b/solution.py
@@ -9,17 +9,27 @@
 
 
 CHUNK = 128
+PARTS = 4
 
 
-def gather_kernel(idx_ref, x_ref, o_ref, xt_ref):
+def gather_kernel(idx_ref, x_hbm, o_ref, x_ref, xt_ref, sems):
     count = o_ref.shape[1]
+    span = count // PARTS
+    fetches = [
+        pltpu.make_async_copy(x_hbm.at[:, pl.ds(q * span, span)], x_ref.at[:, pl.ds(q * span, span)], sems.at[q])
+        for q in range(PARTS)
+    ]
+    for fetch in fetches:
+        fetch.start()
+    for q, fetch in enumerate(fetches):
+        fetch.wait()
 
-    def spread(c, carry):
-        col = pl.multiple_of(c * CHUNK, CHUNK)
-        xt_ref[pl.ds(col, CHUNK), :] = x_ref[:, pl.ds(col, CHUNK)].T
-        return carry
+        def spread(c, carry, q=q):
+            col = pl.multiple_of(q * span + c * CHUNK, CHUNK)
+            xt_ref[pl.ds(col, CHUNK), :] = x_ref[:, pl.ds(col, CHUNK)].T
+            return carry
 
-    lax.fori_loop(0, count // CHUNK, spread, 0)
+        lax.fori_loop(0, span // CHUNK, spread, 0)
 
     def body(c, carry):
         col = pl.multiple_of(c * CHUNK, CHUNK)
@@ -35,10 +45,14 @@
     return pl.pallas_call(
         gather_kernel,
         out_shape=jax.ShapeDtypeStruct((width, count), jnp.bfloat16),
-        in_specs=[pl.BlockSpec(memory_space=pltpu.SMEM), pl.BlockSpec(memory_space=pltpu.VMEM)],
+        in_specs=[pl.BlockSpec(memory_space=pltpu.SMEM), pl.BlockSpec(memory_space=pl.ANY)],
         out_specs=pl.BlockSpec(memory_space=pltpu.VMEM),
-        scratch_shapes=[pltpu.VMEM((count, width), jnp.float32)],
-        compiler_params=pltpu.CompilerParams(vmem_limit_bytes=40 * 1024 * 1024),
+        scratch_shapes=[
+            pltpu.VMEM((width, count), jnp.float32),
+            pltpu.VMEM((count, width), jnp.float32),
+            pltpu.SemaphoreType.DMA((PARTS,)),
+        ],
+        compiler_params=pltpu.CompilerParams(vmem_limit_bytes=67043328),
         cost_estimate=pl.CostEstimate(flops=0, transcendentals=0, bytes_accessed=count * width * 6),
     )(index, points)
 

time: 94.4 us -> 92.5 us (0.980)
  matrix products: 25.3 us -> 23.4 us
  Pallas kernels: 32.6 us -> 34.5 us
  local copies, waits for them, and re-layouts: 8.04 us -> 6.78 us
    unnamed x29 -> x15, local copies, waits for them, and re-layouts: 2.44 us -> 0.2 us
    pallas_call x1, Pallas kernels: 32.6 us -> 34.5 us  [gather_points(): pl.pallas_call(gather_kernel, out_shape=jax.ShapeDtypeStruct((width, coun...]
    dot_general x1, matrix products: 1.72 us -> 0.29 us  [local(): jnp.einsum('lrp,rls->slp', out_basis, coeff_bf, preferred_element_type=jn...]
    reshape x1, local copies, waits for them, and re-layouts: 0.04 us -> 1.08 us  [local(): leaves = ordered.reshape(rhs_count, leaf_count, leaf_size)]
    slice x1, local copies, waits for them, and re-layouts: 0.02 us -> 0.98 us  [extended(): last = lax.slice_in_dim(x, length - width, length, axis=dim)]
  transfers between devices with their start and end apart: 9 -> 9, of which waited for: 4 -> 4; matrix products, arithmetic and copies ran while one was open for 25% -> 26% of each run, Pallas kernels for 0% -> 0%
where the time goes in v12:
time: 92.5 us; the launch traced here: 92.1 us
  Pallas kernels  34.5 us (37%)
  starting transfers between devices  23.5 us (25%)
  matrix products  23.4 us (25%)
  local copies, waits for them, and re-layouts  6.78 us (7%)
  waiting for transfers between devices  3.4 us (4%)
    pallas_call x1, Pallas kernels, gather_points(): pl.pallas_call(gather_kernel, out_shape=jax.ShapeDtypeStruct((width, coun...  34.5 us
    ppermute x7, starting transfers between devices, from_partner(): lax.ppermute(x, axis, [(i, i ^ 1 << distance) for i in range(lax.axis_siz...  20 us
    dot_general x1, matrix products, local(): jnp.einsum('lpq,slq->slp', band_blocks[:half, 0], own_first, preferred_el...  3.47 us
    dot_general x1, matrix products, local(): jnp.einsum('lpq,slq->slp', band_blocks[half:, 0], own_second, preferred_e...  3.38 us
    dot_general x1, matrix products, local(): jnp.einsum('lpq,slq->slp', band_blocks[:half, 1], picked_first, preferred...  3.38 us
    dot_general x1, matrix products, local(): jnp.einsum('lpq,slq->slp', band_blocks[half:, 1], picked_second, preferre...  3.38 us
    dot_general x7, matrix products, translate(): jnp.dot(level_matrices[0], own_coeffs, precision=lax.Precision.HIGH, pref...  2.95 us
    dot_general x7, matrix products, translate(): jnp.dot(level_matrices[1], other_coeffs, precision=lax.Precision.HIGH, pr...  2.92 us
  transfers between devices with their start and end apart: 9, of which 4 were waited for; matrix products, arithmetic and copies ran while one was open for 26% of the time, Pallas kernels for 0%

profile of v12, /device:TPU:0, one launch (start us, length us, event | category | flops | bytes accessed | tf_op | source)
XLA Modules:
  0.0 92.1 jit_solution(3684325409680496036)
XLA Ops:
  0.0 34.5 %shard_map.73 = bf16[16,16384]{1,0:T(8,128)(2,1)} custom-call(s32[16384]{0:T(1024)} %idx_ref.1, f32[16,16384]{1,0:T(8,128)} %x_hbm.1), custom_call_target="tpu_custom_call" | custom-call | bytes 1572864 | tf_op jit(solution)/shard_map/pallas_call | solution.py:45
  34.5 1.9 %fusion.32 = f32[64,16,32]{2,1,0:T(8,128)S(1)} fusion(bf16[64,32,256]{2,1,0:T(8,128)(2,1)} %param.10, bf16[2,64,8,256]{3,2,1,0:T(8,128)(2,1)} %bitcast.126), kind=kOutput, calls=%fused_computation.41 | convolution fusion | flops 16777216 | bytes 1703936 | tf_op jit(solution)/shard_map/lrp,slp->rls/dot_general | solution.py:112
  36.6 1.8 %collective-permute-start = (f32[256,128]{1,0:T(8,128)S(1)}, f32[256,128]{1,0:T(8,128)S(1)}, u32[]{:S(2)}, u32[]{:S(2)}) collective-permute-start(f32[256,128]{1,0:T(8,128)S(1)} %bitcast.147), channel_id=1, source_target_pairs={{0,1},{1,0},{2,3},{3,2},{4,5},{5,4},{6,7},{7,6},{8,9},{9,8},{10,11... | collective-permute-start | bytes 393224 | tf_op jit(solution)/shard_map/ppermute | solution.py:61
  38.3 1.0 %fusion.36 = (bf16[16,4096]{1,0:T(8,128)(2,1)S(1)}, bf16[16,4096]{1,0:T(8,128)(2,1)S(1)}) fusion(bf16[16,16384]{1,0:T(8,128)(2,1)} %shard_map.73), kind=kLoop, calls=%fused_computation.45 | loop fusion | bytes 524288 | tf_op jit(solution)/shard_map/slice | solution.py:69
  39.3 2.2 %collective-permute-start.1 = (bf16[16,4096]{1,0:T(8,128)(2,1)S(1)}, bf16[16,4096]{1,0:T(8,128)(2,1)S(1)}, u32[]{:S(2)}, u32[]{:S(2)}) collective-permute-start(bf16[16,4096]{1,0:T(8,128)(2,1)S(1)} %get-tuple-element.45), channel_id=1, source_target_pairs={{0,1},{1,2},{2,3},{3,4},{4,5},{5,6},{6,7},{7,8},{8,9},{9,10},{10,1... | collective-permute-start | bytes 393224 | tf_op jit(solution)/shard_map/ppermute | solution.py:71
  41.6 1.3 %collective-permute-start.2 = (bf16[16,4096]{1,0:T(8,128)(2,1)S(1)}, bf16[16,4096]{1,0:T(8,128)(2,1)S(1)}, u32[]{:S(2)}, u32[]{:S(2)}) collective-permute-start(bf16[16,4096]{1,0:T(8,128)(2,1)S(1)} %get-tuple-element.46), channel_id=1, source_target_pairs={{1,0},{2,1},{3,2},{4,3},{5,4},{6,5},{7,6},{8,7},{9,8},{10,9},{11,1... | collective-permute-start | bytes 393224 | tf_op jit(solution)/shard_map/ppermute | solution.py:72
  42.9 1.1 %copy.41 = bf16[2,64,8,256]{3,2,0,1:T(8,128)(2,1)S(1)} copy(bf16[2,64,8,256]{3,2,1,0:T(8,128)(2,1)} %bitcast.127) | data formatting | bytes 1048576 | tf_op jit(solution)/shard_map/reshape | solution.py:111
  44.0 1.7 %convolution_bitcast_fusion = f32[7,2,8,32,256]{4,3,1,0,2:T(8,128)S(1)} fusion(s32[8]{0:T(128)S(1)} %iota_multiply_fusion, f32[1,7,8,2,32,32]{5,4,3,2,1,0:T(8,128)S(1)} %copy-done.1), kind=kOutput, calls=%fused_computation.13 | convolution fusion | flops 352452608 | bytes 4128800 | tf_op jit(solution)/shard_map/lgtab,gbc->ltgac/dot_general | solution.py:83
  45.7 1.2 %fusion.33 = (f32[1,1,8,32,256]{4,3,1,0,2:T(8,128)S(1)}, f32[1,1,8,32,256]{4,3,1,0,2:T(8,128)S(1)}, f32[1,1,8,32,256]{4,3,1,0,2:T(8,128)S(1)}, f32[1,1,8,32,256]...) fusion(f32[7,2,8,32,256]{4,3,1,0,2:T(8,128)S(1)} %convolution_b, ...), kind=kLoop, calls=%fused_computation.42 | loop fusion | bytes 7340032 | tf_op jit(solution)/shard_map/slice | solution.py:96
  47.2 0.8 fusion.34
  49.4 5.2 %collective-permute-start.3 = (f32[256,128]{1,0:T(8,128)S(1)}, f32[256,128]{1,0:T(8,128)}, u32[]{:S(2)}, u32[]{:S(2)}) collective-permute-start(f32[256,128]{1,0:T(8,128)S(1)} %convolution_add_fusion.6), channel_id=1, source_target_pairs={{0,2},{1,3},{2,0},{3,1},{4,6},{5,7},{6,4},{7,5},{8,10},{9,11},{10,... | collective-permute-start | bytes 393224 | tf_op jit(solution)/shard_map/ppermute | solution.py:61
  55.9 1.2 %fusion.38 = f32[256,128]{1,0:T(8,128)S(1)} fusion(f32[256,256]{1,0:T(8,128)} %bitcast.144, f32[256,128]{1,0:T(8,128)S(1)} %convolution_add_fusion.6), kind=kOutput, calls=%fused_computation.47 | convolution fusion | flops 50331648 | bytes 524288 | tf_op jit(solution)/shard_map/dot_general | solution.py:89
  57.8 1.3 %convolution_add_fusion.5 = f32[256,128]{1,0:T(8,128)S(1)} fusion(f32[256,128]{1,0:T(8,128)S(1)} %fusion.38, f32[256,256]{1,0:T(8,128)} %bitcast.143, f32[256,128]{1,0:T(8,128)} %collective-permute-done.3), kind=kOutput, calls=%fused_computation.28 | convolution fusion | flops 50364416 | bytes 655360 | tf_op jit(solution)/shard_map/dot_general | solution.py:95
  59.1 7.4 %collective-permute-start.4 = (f32[256,128]{1,0:T(8,128)S(1)}, f32[256,128]{1,0:T(8,128)S(1)}, u32[]{:S(2)}, u32[]{:S(2)}) collective-permute-start(f32[256,128]{1,0:T(8,128)S(1)} %convolution_add_fusion.5), channel_id=1, source_target_pairs={{0,4},{1,5},{2,6},{3,7},{4,0},{5,1},{6,2},{7,3},{8,12},{9,13},{10,... | collective-permute-start | bytes 393224 | tf_op jit(solution)/shard_map/ppermute | solution.py:61
  66.4 3.5 %fusion.16 = f32[16,32,256]{2,0,1:T(8,128)S(1)} fusion(bf16[16,32,256]{2,0,1:T(8,128)(2,1)} %get-tuple-element.21, bf16[64,2,256,256]{3,2,1,0:T(8,128)(2,1)} %param.11), kind=kOutput, calls=%fused_computation.19 | convolution fusion | flops 67108864 | bytes 4980736 | tf_op jit(solution)/shard_map/lpq,slq->slp/dot_general | solution.py:148
  70.9 1.0 %collective-permute-done.5 = f32[256,128]{1,0:T(8,128)S(1)} collective-permute-done((f32[256,128]{1,0:T(8,128)S(1)}, f32[256,128]{1,0:T(8,128)S(1)}, u32[]{:S(2)}, u32[]{:S(2)}) %collective-permute-start.5) | collective-permute-done | bytes 131104 | tf_op jit(solution)/shard_map/ppermute | solution.py:61
  72.2 1.1 %collective-permute-start.6 = (f32[256,128]{1,0:T(8,128)S(1)}, f32[256,128]{1,0:T(8,128)S(1)}, u32[]{:S(2)}, u32[]{:S(2)}) collective-permute-start(f32[256,128]{1,0:T(8,128)S(1)} %convolution_add_fusion.3), channel_id=1, source_target_pairs={{0,16},{8,24},{16,0},{24,8},{32,48},{40,56},{48,32},{56,40},{64,80... | collective-permute-start | bytes 393224 | tf_op jit(solution)/shard_map/ppermute | solution.py:61
  73.3 3.4 %fusion.22 = f32[16,32,256]{2,0,1:T(8,128)S(1)} fusion(bf16[16,32,256]{2,0,1:T(8,128)(2,1)S(1)} %get-tuple-element.23, bf16[64,2,256,256]{3,2,1,0:T(8,128)(2,1)} %param.11), kind=kOutput, calls=%fused_computation.21 | convolution fusion | flops 67108864 | bytes 4980736 | tf_op jit(solution)/shard_map/lpq,slq->slp/dot_general | solution.py:153
  77.0 0.9 collective-permute-done.6
  78.1 1.6 %collective-permute-start.7 = (f32[256,128]{1,0:T(8,128)S(1)}, f32[256,128]{1,0:T(8,128)S(1)}, u32[]{:S(2)}, u32[]{:S(2)}) collective-permute-start(f32[256,128]{1,0:T(8,128)S(1)} %convolution_add_fusion.2), channel_id=1, source_target_pairs={{0,32},{8,40},{16,48},{24,56},{32,0},{40,8},{48,16},{56,24},{64,96... | collective-permute-start | bytes 393224 | tf_op jit(solution)/shard_map/ppermute | solution.py:61
  79.7 3.4 %fusion.25 = f32[16,32,256]{2,0,1:T(8,128)S(1)} fusion(bf16[16,32,256]{2,0,1:T(8,128)(2,1)S(1)} %get-tuple-element.24, bf16[64,2,256,256]{3,2,1,0:T(8,128)(2,1)} %param.11), kind=kOutput, calls=%fused_computation.22 | convolution fusion | flops 67108864 | bytes 4980736 | tf_op jit(solution)/shard_map/lpq,slq->slp/dot_general | solution.py:156
  83.6 2.9 %collective-permute-start.8 = (f32[256,128]{1,0:T(8,128)S(1)}, f32[256,128]{1,0:T(8,128)S(1)}, u32[]{:S(2)}, u32[]{:S(2)}) collective-permute-start(f32[256,128]{1,0:T(8,128)S(1)} %convolution_add_fusion.1), channel_id=1, source_target_pairs={{0,64},{8,72},{16,80},{24,88},{32,96},{40,104},{48,112},{56,120},{... | collective-permute-start | bytes 393224 | tf_op jit(solution)/shard_map/ppermute | solution.py:61
  86.5 3.4 %fusion.19 = f32[16,32,256]{2,0,1:T(8,128)S(1)} fusion(bf16[16,32,256]{2,0,1:T(8,128)(2,1)S(1)} %copy-done.5, bf16[64,2,256,256]{3,2,1,0:T(8,128)(2,1)} %param.11), kind=kOutput, calls=%fused_computation.20 | convolution fusion | flops 67108864 | bytes 4980736 | tf_op jit(solution)/shard_map/lpq,slq->slp/dot_general | solution.py:149
  91.0 1.1 %copy.35 = f32[64,2,8,256]{3,2,0,1:T(8,128)} copy(f32[64,2,8,256]{3,2,1,0:T(8,128)S(1)} %fusion.15) | data formatting | bytes 2097152 | tf_op jit(solution)/shard_map/reshape | solution.py:160
  (46 shorter events, 7.1 us)
Async XLA Ops:
  34.5 9.5 %copy-start.1 = (f32[1,7,8,2,32,32]{5,4,3,2,1,0:T(8,128)S(1)}, f32[1,7,8,2,32,32]{5,4,3,2,1,0:T(8,128)}, u32[]{:S(2)}) copy-start(f32[1,7,8,2,32,32]{5,4,3,2,1,0:T(8,128)} %param.12) | copy-start | bytes 1376260
  36.6 12.6 %collective-permute-start = (f32[256,128]{1,0:T(8,128)S(1)}, f32[256,128]{1,0:T(8,128)S(1)}, u32[]{:S(2)}, u32[]{:S(2)}) collective-permute-start(f32[256,128]{1,0:T(8,128)S(1)} %bitcast.147), channel_id=1, source_target_pairs={{0,1},{1,0},{2,3},{3,2},{4,5},{5,4},{6,7},{7,6},{8,9},{9,8},{10,11... | collective-permute-start | bytes 393224 | tf_op jit(solution)/shard_map/ppermute | solution.py:61
  39.3 8.8 %collective-permute-start.1 = (bf16[16,4096]{1,0:T(8,128)(2,1)S(1)}, bf16[16,4096]{1,0:T(8,128)(2,1)S(1)}, u32[]{:S(2)}, u32[]{:S(2)}) collective-permute-start(bf16[16,4096]{1,0:T(8,128)(2,1)S(1)} %get-tuple-element.45), channel_id=1, source_target_pairs={{0,1},{1,2},{2,3},{3,4},{4,5},{5,6},{6,7},{7,8},{8,9},{9,10},{10,1... | collective-permute-start | bytes 393224 | tf_op jit(solution)/shard_map/ppermute | solution.py:71
  41.6 7.4 %collective-permute-start.2 = (bf16[16,4096]{1,0:T(8,128)(2,1)S(1)}, bf16[16,4096]{1,0:T(8,128)(2,1)S(1)}, u32[]{:S(2)}, u32[]{:S(2)}) collective-permute-start(bf16[16,4096]{1,0:T(8,128)(2,1)S(1)} %get-tuple-element.46), channel_id=1, source_target_pairs={{1,0},{2,1},{3,2},{4,3},{5,4},{6,5},{7,6},{8,7},{9,8},{10,9},{11,1... | collective-permute-start | bytes 393224 | tf_op jit(solution)/shard_map/ppermute | solution.py:72
  45.7 2.4 %copy-start.6 = (s32[64]{0:T(128)S(1)}, s32[64]{0:T(128)}, u32[]{:S(2)}) copy-start(s32[64]{0:T(128)} %param.9) | copy-start | bytes 772
  45.7 3.2 %copy-start = (bf16[16,16384]{1,0:T(8,128)(2,1)S(1)}, bf16[16,16384]{1,0:T(8,128)(2,1)}, u32[]{:S(2)}) copy-start(bf16[16,16384]{1,0:T(8,128)(2,1)} %shard_map.73) | copy-start | bytes 1572868
  49.4 8.4 %collective-permute-start.3 = (f32[256,128]{1,0:T(8,128)S(1)}, f32[256,128]{1,0:T(8,128)}, u32[]{:S(2)}, u32[]{:S(2)}) collective-permute-start(f32[256,128]{1,0:T(8,128)S(1)} %convolution_add_fusion.6), channel_id=1, source_target_pairs={{0,2},{1,3},{2,0},{3,1},{4,6},{5,7},{6,4},{7,5},{8,10},{9,11},{10,... | collective-permute-start | bytes 393224 | tf_op jit(solution)/shard_map/ppermute | solution.py:61
  55.7 14.2 %copy-start.4 = (f32[1,1,8,32,256]{4,3,1,0,2:T(8,128)S(1)}, f32[1,1,8,32,256]{4,3,1,0,2:T(8,128)}, u32[]{:S(2)}) copy-start(f32[1,1,8,32,256]{4,3,1,0,2:T(8,128)} %get-tuple-element.36) | copy-start | bytes 786436
  59.1 11.1 %collective-permute-start.4 = (f32[256,128]{1,0:T(8,128)S(1)}, f32[256,128]{1,0:T(8,128)S(1)}, u32[]{:S(2)}, u32[]{:S(2)}) collective-permute-start(f32[256,128]{1,0:T(8,128)S(1)} %convolution_add_fusion.5), channel_id=1, source_target_pairs={{0,4},{1,5},{2,6},{3,7},{4,0},{5,1},{6,2},{7,3},{8,12},{9,13},{10,... | collective-permute-start | bytes 393224 | tf_op jit(solution)/shard_map/ppermute | solution.py:61
  70.5 1.4 %collective-permute-start.5 = (f32[256,128]{1,0:T(8,128)S(1)}, f32[256,128]{1,0:T(8,128)S(1)}, u32[]{:S(2)}, u32[]{:S(2)}) collective-permute-start(f32[256,128]{1,0:T(8,128)S(1)} %convolution_add_fusion.4), channel_id=1, source_target_pairs={{0,8},{8,0},{16,24},{24,16},{32,40},{40,32},{48,56},{56,48},{64,72... | collective-permute-start | bytes 393224 | tf_op jit(solution)/shard_map/ppermute | solution.py:61
  72.2 5.6 %collective-permute-start.6 = (f32[256,128]{1,0:T(8,128)S(1)}, f32[256,128]{1,0:T(8,128)S(1)}, u32[]{:S(2)}, u32[]{:S(2)}) collective-permute-start(f32[256,128]{1,0:T(8,128)S(1)} %convolution_add_fusion.3), channel_id=1, source_target_pairs={{0,16},{8,24},{16,0},{24,8},{32,48},{40,56},{48,32},{56,40},{64,80... | collective-permute-start | bytes 393224 | tf_op jit(solution)/shard_map/ppermute | solution.py:61
  76.7 9.9 %copy-start.5 = (bf16[16,32,256]{2,0,1:T(8,128)(2,1)S(1)}, bf16[16,32,256]{2,0,1:T(8,128)(2,1)}, u32[]{:S(2)}) copy-start(bf16[16,32,256]{2,0,1:T(8,128)(2,1)} %get-tuple-element.22) | copy-start | bytes 786436
  78.1 5.2 %collective-permute-start.7 = (f32[256,128]{1,0:T(8,128)S(1)}, f32[256,128]{1,0:T(8,128)S(1)}, u32[]{:S(2)}, u32[]{:S(2)}) collective-permute-start(f32[256,128]{1,0:T(8,128)S(1)} %convolution_add_fusion.2), channel_id=1, source_target_pairs={{0,32},{8,40},{16,48},{24,56},{32,0},{40,8},{48,16},{56,24},{64,96... | collective-permute-start | bytes 393224 | tf_op jit(solution)/shard_map/ppermute | solution.py:61
  83.0 6.9 %copy-start.3 = (f32[1,1,8,32,256]{4,3,1,0,2:T(8,128)S(1)}, f32[1,1,8,32,256]{4,3,1,0,2:T(8,128)}, u32[]{:S(2)}) copy-start(f32[1,1,8,32,256]{4,3,1,0,2:T(8,128)} %get-tuple-element.40) | copy-start | bytes 786436
  83.0 7.6 %copy-start.2 = (bf16[64,32,256]{2,1,0:T(8,128)(2,1)S(1)}, bf16[64,32,256]{2,1,0:T(8,128)(2,1)}, u32[]{:S(2)}) copy-start(bf16[64,32,256]{2,1,0:T(8,128)(2,1)} %param.13) | copy-start | bytes 3145732
  83.6 6.6 %collective-permute-start.8 = (f32[256,128]{1,0:T(8,128)S(1)}, f32[256,128]{1,0:T(8,128)S(1)}, u32[]{:S(2)}, u32[]{:S(2)}) collective-permute-start(f32[256,128]{1,0:T(8,128)S(1)} %convolution_add_fusion.1), channel_id=1, source_target_pairs={{0,64},{8,72},{16,80},{24,88},{32,96},{40,104},{48,112},{56,120},{... | collective-permute-start | bytes 393224 | tf_op jit(solution)/shard_map/ppermute | solution.py:61

commit v13 on v12

--- a/solution.py
+++ b/solution.py
@@ -78,10 +78,10 @@
     levels, groups, terms, rank, _ = weights.shape
     width = groups * rank
     shape = (groups, rank, width)
-    target = lax.broadcasted_iota(jnp.int32, shape, 0) * rank + lax.broadcasted_iota(jnp.int32, shape, 1)
+    target = lax.broadcasted_iota(jnp.int32, shape, 1) * groups + lax.broadcasted_iota(jnp.int32, shape, 0)
     spread = (lax.broadcasted_iota(jnp.int32, shape, 2) == target).astype(weights.dtype)
     return jnp.einsum(
-        "lgtab,gbc->ltgac", weights, spread, precision=lax.Precision.HIGHEST, preferred_element_type=jnp.float32
+        "lgtab,gbc->ltagc", weights, spread, precision=lax.Precision.HIGHEST, preferred_element_type=jnp.float32
     ).reshape(levels, terms, width, width)
 
 
@@ -122,8 +122,7 @@
     blocks_all = padded.reshape(rhs_count, leaf_count + 2 * HW, leaf_size)
     block_index = jnp.arange(leaf_count, dtype=jnp.int32) + HW + band_offsets
     half = leaf_count // 2
-    coeffs = coeffs.reshape(rank_size, group_total, group_width).transpose(1, 0, 2)
-    coeffs = coeffs.reshape(group_total * rank_size, group_width)
+    coeffs = coeffs.reshape(rank_size * group_total, group_width)
     picked = None
     for level, (axis, bit) in enumerate(levels):
         if level == take_at:
@@ -139,7 +138,6 @@
             coeffs, picked_second = lax.optimization_barrier((coeffs, picked[:, half:]))
         partner = from_partner(coeffs, axis, bit)
         coeffs = translate(weights[level], coeffs, partner)
-    coeffs = coeffs.reshape(group_total, rank_size, group_width).transpose(1, 0, 2)
     coeffs = coeffs.reshape(rank_size, total_cols)
     coeff_bf = coeffs.astype(jnp.bfloat16).reshape(rank_size, leaf_count, rhs_count)
     far_term = jnp.einsum("lrp,rls->slp", out_basis, coeff_bf, preferred_element_type=jnp.float32)

time: 92.5 us -> 95.4 us (1.031)
  matrix products: 23.4 us -> 27.4 us
    dot_general x1, matrix products: 1.71 us -> 3.23 us  [block_diagonals(): jnp.einsum('lgtab,gbc->ltagc', weights, spread, precision=lax.Precision.H...]
    dot_general x1, matrix products: 0.29 us -> 1.74 us  [local(): jnp.einsum('lrp,rls->slp', out_basis, coeff_bf, preferred_element_type=jn...]
    reshape x1, local copies, waits for them, and re-layouts: 1.08 us -> 0.04 us  [local(): leaves = ordered.reshape(rhs_count, leaf_count, leaf_size)]
    slice x1, local copies, waits for them, and re-layouts: 0.98 us -> 0.02 us  [extended(): last = lax.slice_in_dim(x, length - width, length, axis=dim)]
  transfers between devices with their start and end apart: 9 -> 9, of which waited for: 4 -> 4; matrix products, arithmetic and copies ran while one was open for 26% -> 25% of each run, Pallas kernels for 0% -> 0%
where the time goes in v13:
time: 95.4 us; the launch traced here: 94.9 us
  Pallas kernels  34.5 us (36%)
  matrix products  27.4 us (29%)
  starting transfers between devices  23.4 us (25%)
  local copies, waits for them, and re-layouts  5.95 us (6%)
  waiting for transfers between devices  3.16 us (3%)
    pallas_call x1, Pallas kernels, gather_points(): pl.pallas_call(gather_kernel, out_shape=jax.ShapeDtypeStruct((width, coun...  34.5 us
    ppermute x7, starting transfers between devices, from_partner(): lax.ppermute(x, axis, [(i, i ^ 1 << distance) for i in range(lax.axis_siz...  19.9 us
    dot_general x7, matrix products, translate(): jnp.dot(level_matrices[0], own_coeffs, precision=lax.Precision.HIGH, pref...  3.52 us
    dot_general x7, matrix products, translate(): jnp.dot(level_matrices[1], other_coeffs, precision=lax.Precision.HIGH, pr...  3.5 us
    dot_general x1, matrix products, local(): jnp.einsum('lpq,slq->slp', band_blocks[:half, 0], own_first, preferred_el...  3.47 us
    dot_general x1, matrix products, local(): jnp.einsum('lpq,slq->slp', band_blocks[half:, 0], own_second, preferred_e...  3.38 us
    dot_general x1, matrix products, local(): jnp.einsum('lpq,slq->slp', band_blocks[:half, 1], picked_first, preferred...  3.38 us
    dot_general x1, matrix products, local(): jnp.einsum('lpq,slq->slp', band_blocks[half:, 1], picked_second, preferre...  3.38 us
  transfers between devices with their start and end apart: 9, of which 4 were waited for; matrix products, arithmetic and copies ran while one was open for 25% of the time, Pallas kernels for 0%

profile of v13, /device:TPU:0, one launch (start us, length us, event | category | flops | bytes accessed | tf_op | source)
XLA Modules:
  0.0 94.9 jit_solution(1596232498313177211)
XLA Ops:
  0.0 34.5 %shard_map.73 = bf16[16,16384]{1,0:T(8,128)(2,1)} custom-call(s32[16384]{0:T(1024)} %idx_ref.1, f32[16,16384]{1,0:T(8,128)} %x_hbm.1), custom_call_target="tpu_custom_call" | custom-call | bytes 1572864 | tf_op jit(solution)/shard_map/pallas_call | solution.py:45
  34.5 1.8 %convolution_bitcast_fusion.2 = f32[32,64,16]{0,2,1:T(8,128)S(1)} fusion(bf16[64,32,256]{2,1,0:T(8,128)(2,1)} %param.10, bf16[2,64,8,256]{3,2,1,0:T(8,128)(2,1)} %bitcast.131), kind=kOutput, calls=%fused_computation.23 | convolution fusion | flops 16777216 | bytes 1703936 | tf_op jit(solution)/shard_map/lrp,slp->rls/dot_general | solution.py:112
  36.3 0.9 copy.26
  37.5 1.8 %collective-permute-start = (f32[256,128]{1,0:T(8,128)S(1)}, f32[256,128]{1,0:T(8,128)S(1)}, u32[]{:S(2)}, u32[]{:S(2)}) collective-permute-start(f32[256,128]{1,0:T(8,128)S(1)} %reshape_reshape.3), channel_id=1, source_target_pairs={{0,1},{1,0},{2,3},{3,2},{4,5},{5,4},{6,7},{7,6},{8,9},{9,8},{10,11... | collective-permute-start | bytes 393224 | tf_op jit(solution)/shard_map/ppermute | solution.py:61
  39.3 2.2 %collective-permute-start.1 = (bf16[16,4096]{1,0:T(8,128)(2,1)S(1)}, bf16[16,4096]{1,0:T(8,128)(2,1)S(1)}, u32[]{:S(2)}, u32[]{:S(2)}) collective-permute-start(bf16[16,4096]{1,0:T(8,128)(2,1)S(1)} %get-tuple-element.45), channel_id=1, source_target_pairs={{0,1},{1,2},{2,3},{3,4},{4,5},{5,6},{6,7},{7,8},{8,9},{9,10},{10,1... | collective-permute-start | bytes 393224 | tf_op jit(solution)/shard_map/ppermute | solution.py:71
  41.6 1.3 %collective-permute-start.2 = (bf16[16,4096]{1,0:T(8,128)(2,1)S(1)}, bf16[16,4096]{1,0:T(8,128)(2,1)S(1)}, u32[]{:S(2)}, u32[]{:S(2)}) collective-permute-start(bf16[16,4096]{1,0:T(8,128)(2,1)S(1)} %get-tuple-element.46), channel_id=1, source_target_pairs={{1,0},{2,1},{3,2},{4,3},{5,4},{6,5},{7,6},{8,7},{9,8},{10,9},{11,1... | collective-permute-start | bytes 393224 | tf_op jit(solution)/shard_map/ppermute | solution.py:72
  42.9 3.2 %convolution_bitcast_fusion = f32[7,2,32,8,256]{4,2,1,0,3:T(8,128)S(1)} fusion(s32[32]{0:T(128)S(1)} %iota_multiply_fusion, f32[1,7,8,2,32,32]{5,4,3,2,1,0:T(8,128)} %param.12), kind=kOutput, calls=%fused_computation.13 | convolution fusion | flops 352452608 | bytes 4128896 | tf_op jit(solution)/shard_map/lgtab,gbc->ltagc/dot_general | solution.py:83
  46.2 1.2 %fusion.68 = (f32[1,1,32,8,256]{4,2,1,0,3:T(8,128)S(1)}, f32[1,1,32,8,256]{4,2,1,0,3:T(8,128)S(1)}, f32[1,1,32,8,256]{4,2,1,0,3:T(8,128)S(1)}, f32[1,1,32,8,256]...) fusion(f32[7,2,32,8,256]{4,2,1,0,3:T(8,128)S(1)} %convolution_b, ...), kind=kLoop, calls=%fused_computation.78 | loop fusion | bytes 7340032 | tf_op jit(solution)/shard_map/slice | solution.py:96
  47.7 0.8 fusion.69
  49.6 5.2 %collective-permute-start.3 = (f32[256,128]{1,0:T(8,128)S(1)}, f32[256,128]{1,0:T(8,128)}, u32[]{:S(2)}, u32[]{:S(2)}) collective-permute-start(f32[256,128]{1,0:T(8,128)S(1)} %convolution_add_fusion.6), channel_id=1, source_target_pairs={{0,2},{1,3},{2,0},{3,1},{4,6},{5,7},{6,4},{7,5},{8,10},{9,11},{10,... | collective-permute-start | bytes 393224 | tf_op jit(solution)/shard_map/ppermute | solution.py:61
  56.0 1.3 %fusion.39 = f32[256,128]{1,0:T(8,128)S(1)} fusion(f32[256,128]{1,0:T(8,128)S(1)} %convolution_add_fusion.6, f32[1,1,32,8,256]{4,2,1,0,3:T(8,128)} %get-tuple-element.35), kind=kOutput, calls=%fused_computation.45 | convolution fusion | flops 50331648 | bytes 524288 | tf_op jit(solution)/shard_map/dot_general | solution.py:89
  57.4 1.1 %collective-permute-done.3 = f32[256,128]{1,0:T(8,128)} collective-permute-done((f32[256,128]{1,0:T(8,128)S(1)}, f32[256,128]{1,0:T(8,128)}, u32[]{:S(2)}, u32[]{:S(2)}) %collective-permute-start.3) | collective-permute-done | bytes 131104 | tf_op jit(solution)/shard_map/ppermute | solution.py:61
  58.4 1.3 %convolution_add_fusion.5 = f32[256,128]{1,0:T(8,128)S(1)} fusion(f32[256,128]{1,0:T(8,128)S(1)} %fusion.39, f32[256,128]{1,0:T(8,128)} %collective-permute-done.3, f32[1,1,32,8,256]{4,2,1,0,3:T(8,128)} %get-tuple-element.32), kind=kOutput, calls=%fused_computation.29 | convolution fusion | flops 50364416 | bytes 655360 | tf_op jit(solution)/shard_map/dot_general | solution.py:95
  59.8 7.3 %collective-permute-start.4 = (f32[256,128]{1,0:T(8,128)S(1)}, f32[256,128]{1,0:T(8,128)S(1)}, u32[]{:S(2)}, u32[]{:S(2)}) collective-permute-start(f32[256,128]{1,0:T(8,128)S(1)} %convolution_add_fusion.5), channel_id=1, source_target_pairs={{0,4},{1,5},{2,6},{3,7},{4,0},{5,1},{6,2},{7,3},{8,12},{9,13},{10,... | collective-permute-start | bytes 393224 | tf_op jit(solution)/shard_map/ppermute | solution.py:61
  67.1 3.5 %fusion.16 = f32[16,32,256]{2,0,1:T(8,128)S(1)} fusion(bf16[16,32,256]{2,0,1:T(8,128)(2,1)} %get-tuple-element.21, bf16[64,2,256,256]{3,2,1,0:T(8,128)(2,1)} %param.11), kind=kOutput, calls=%fused_computation.19 | convolution fusion | flops 67108864 | bytes 4980736 | tf_op jit(solution)/shard_map/lpq,slq->slp/dot_general | solution.py:146
  71.8 1.0 %collective-permute-done.5 = f32[256,128]{1,0:T(8,128)S(1)} collective-permute-done((f32[256,128]{1,0:T(8,128)S(1)}, f32[256,128]{1,0:T(8,128)S(1)}, u32[]{:S(2)}, u32[]{:S(2)}) %collective-permute-start.5) | collective-permute-done | bytes 131104 | tf_op jit(solution)/shard_map/ppermute | solution.py:61
  73.1 1.1 %collective-permute-start.6 = (f32[256,128]{1,0:T(8,128)S(1)}, f32[256,128]{1,0:T(8,128)S(1)}, u32[]{:S(2)}, u32[]{:S(2)}) collective-permute-start(f32[256,128]{1,0:T(8,128)S(1)} %convolution_add_fusion.3), channel_id=1, source_target_pairs={{0,16},{8,24},{16,0},{24,8},{32,48},{40,56},{48,32},{56,40},{64,80... | collective-permute-start | bytes 393224 | tf_op jit(solution)/shard_map/ppermute | solution.py:61
  74.2 3.4 %fusion.22 = f32[16,32,256]{2,0,1:T(8,128)S(1)} fusion(bf16[16,32,256]{2,0,1:T(8,128)(2,1)S(1)} %get-tuple-element.23, bf16[64,2,256,256]{3,2,1,0:T(8,128)(2,1)} %param.11), kind=kOutput, calls=%fused_computation.21 | convolution fusion | flops 67108864 | bytes 4980736 | tf_op jit(solution)/shard_map/lpq,slq->slp/dot_general | solution.py:151
  79.1 1.6 %collective-permute-start.7 = (f32[256,128]{1,0:T(8,128)S(1)}, f32[256,128]{1,0:T(8,128)S(1)}, u32[]{:S(2)}, u32[]{:S(2)}) collective-permute-start(f32[256,128]{1,0:T(8,128)S(1)} %convolution_add_fusion.2), channel_id=1, source_target_pairs={{0,32},{8,40},{16,48},{24,56},{32,0},{40,8},{48,16},{56,24},{64,96... | collective-permute-start | bytes 393224 | tf_op jit(solution)/shard_map/ppermute | solution.py:61
  80.7 3.4 %fusion.25 = f32[16,32,256]{2,0,1:T(8,128)S(1)} fusion(bf16[16,32,256]{2,0,1:T(8,128)(2,1)S(1)} %get-tuple-element.24, bf16[64,2,256,256]{3,2,1,0:T(8,128)(2,1)} %param.11), kind=kOutput, calls=%fused_computation.22 | convolution fusion | flops 67108864 | bytes 4980736 | tf_op jit(solution)/shard_map/lpq,slq->slp/dot_general | solution.py:154
  84.8 2.8 %collective-permute-start.8 = (f32[256,128]{1,0:T(8,128)S(1)}, f32[256,128]{1,0:T(8,128)S(1)}, u32[]{:S(2)}, u32[]{:S(2)}) collective-permute-start(f32[256,128]{1,0:T(8,128)S(1)} %convolution_add_fusion.1), channel_id=1, source_target_pairs={{0,64},{8,72},{16,80},{24,88},{32,96},{40,104},{48,112},{56,120},{... | collective-permute-start | bytes 393224 | tf_op jit(solution)/shard_map/ppermute | solution.py:61
  87.6 3.4 %fusion.19 = f32[16,32,256]{2,0,1:T(8,128)S(1)} fusion(bf16[16,32,256]{2,0,1:T(8,128)(2,1)S(1)} %copy-done.3, bf16[64,2,256,256]{3,2,1,0:T(8,128)(2,1)} %param.11), kind=kOutput, calls=%fused_computation.20 | convolution fusion | flops 67108864 | bytes 4980736 | tf_op jit(solution)/shard_map/lpq,slq->slp/dot_general | solution.py:147
  92.1 1.7 %fusion.15 = f32[64,2,8,256]{3,2,1,0:T(8,128)S(1)} fusion(bf16[64,32,256]{2,1,0:T(8,128)(2,1)} %param.13, f32[16,32,256]{2,0,1:T(8,128)S(1)} %fusion.19, f32[16,32,256]{2,0,1:T(8,128)S(1)} %fusion.16, f32[16,32,256]{2,0,1:T(8,128)S(1)} %fusion.25, f32[16,32,256]{2,0,1:T(8,128)S(1)} %fusion.22, bf16[32,64,16]{2,1,0:T(8,128)(2,1)S(1)} %convert_element_type.9), kind=kOutput, calls=%fused_computation.18 | convolution fusion | flops 17825792 | bytes 4259840 | tf_op jit(solution)/shard_map/lrp,rls->slp/dot_general | solution.py:143
  93.9 1.0 %copy.49 = f32[64,2,8,256]{3,2,0,1:T(8,128)} copy(f32[64,2,8,256]{3,2,1,0:T(8,128)S(1)} %fusion.15) | data formatting | bytes 2097152 | tf_op jit(solution)/shard_map/reshape | solution.py:158
  (43 shorter events, 7.8 us)
Async XLA Ops:
  34.5 4.9 %copy-start = (bf16[16,16384]{1,0:T(8,128)(2,1)S(1)}, bf16[16,16384]{1,0:T(8,128)(2,1)}, u32[]{:S(2)}) copy-start(bf16[16,16384]{1,0:T(8,128)(2,1)} %shard_map.73) | copy-start | bytes 1572868
  37.5 11.6 %collective-permute-start = (f32[256,128]{1,0:T(8,128)S(1)}, f32[256,128]{1,0:T(8,128)S(1)}, u32[]{:S(2)}, u32[]{:S(2)}) collective-permute-start(f32[256,128]{1,0:T(8,128)S(1)} %reshape_reshape.3), channel_id=1, source_target_pairs={{0,1},{1,0},{2,3},{3,2},{4,5},{5,4},{6,7},{7,6},{8,9},{9,8},{10,11... | collective-permute-start | bytes 393224 | tf_op jit(solution)/shard_map/ppermute | solution.py:61
  39.3 9.3 %collective-permute-start.1 = (bf16[16,4096]{1,0:T(8,128)(2,1)S(1)}, bf16[16,4096]{1,0:T(8,128)(2,1)S(1)}, u32[]{:S(2)}, u32[]{:S(2)}) collective-permute-start(bf16[16,4096]{1,0:T(8,128)(2,1)S(1)} %get-tuple-element.45), channel_id=1, source_target_pairs={{0,1},{1,2},{2,3},{3,4},{4,5},{5,6},{6,7},{7,8},{8,9},{9,10},{10,1... | collective-permute-start | bytes 393224 | tf_op jit(solution)/shard_map/ppermute | solution.py:71
  41.6 7.4 %collective-permute-start.2 = (bf16[16,4096]{1,0:T(8,128)(2,1)S(1)}, bf16[16,4096]{1,0:T(8,128)(2,1)S(1)}, u32[]{:S(2)}, u32[]{:S(2)}) collective-permute-start(bf16[16,4096]{1,0:T(8,128)(2,1)S(1)} %get-tuple-element.46), channel_id=1, source_target_pairs={{1,0},{2,1},{3,2},{4,3},{5,4},{6,5},{7,6},{8,7},{9,8},{10,9},{11,1... | collective-permute-start | bytes 393224 | tf_op jit(solution)/shard_map/ppermute | solution.py:72
  46.2 2.4 %copy-start.4 = (s32[64]{0:T(128)S(1)}, s32[64]{0:T(128)}, u32[]{:S(2)}) copy-start(s32[64]{0:T(128)} %param.9) | copy-start | bytes 772
  49.6 8.8 %collective-permute-start.3 = (f32[256,128]{1,0:T(8,128)S(1)}, f32[256,128]{1,0:T(8,128)}, u32[]{:S(2)}, u32[]{:S(2)}) collective-permute-start(f32[256,128]{1,0:T(8,128)S(1)} %convolution_add_fusion.6), channel_id=1, source_target_pairs={{0,2},{1,3},{2,0},{3,1},{4,6},{5,7},{6,4},{7,5},{8,10},{9,11},{10,... | collective-permute-start | bytes 393224 | tf_op jit(solution)/shard_map/ppermute | solution.py:61
  55.8 14.7 %copy-start.2 = (f32[1,1,32,8,256]{4,2,1,0,3:T(8,128)S(1)}, f32[1,1,32,8,256]{4,2,1,0,3:T(8,128)}, u32[]{:S(2)}) copy-start(f32[1,1,32,8,256]{4,2,1,0,3:T(8,128)} %get-tuple-element.36) | copy-start | bytes 786436
  55.8 15.1 %copy-start.1 = (f32[1,1,32,8,256]{4,2,1,0,3:T(8,128)S(1)}, f32[1,1,32,8,256]{4,2,1,0,3:T(8,128)}, u32[]{:S(2)}) copy-start(f32[1,1,32,8,256]{4,2,1,0,3:T(8,128)} %get-tuple-element.31) | copy-start | bytes 786436
  59.8 11.2 %collective-permute-start.4 = (f32[256,128]{1,0:T(8,128)S(1)}, f32[256,128]{1,0:T(8,128)S(1)}, u32[]{:S(2)}, u32[]{:S(2)}) collective-permute-start(f32[256,128]{1,0:T(8,128)S(1)} %convolution_add_fusion.5), channel_id=1, source_target_pairs={{0,4},{1,5},{2,6},{3,7},{4,0},{5,1},{6,2},{7,3},{8,12},{9,13},{10,... | collective-permute-start | bytes 393224 | tf_op jit(solution)/shard_map/ppermute | solution.py:61
  71.3 1.4 %collective-permute-start.5 = (f32[256,128]{1,0:T(8,128)S(1)}, f32[256,128]{1,0:T(8,128)S(1)}, u32[]{:S(2)}, u32[]{:S(2)}) collective-permute-start(f32[256,128]{1,0:T(8,128)S(1)} %convolution_add_fusion.4), channel_id=1, source_target_pairs={{0,8},{8,0},{16,24},{24,16},{32,40},{40,32},{48,56},{56,48},{64,72... | collective-permute-start | bytes 393224 | tf_op jit(solution)/shard_map/ppermute | solution.py:61
  73.1 5.6 %collective-permute-start.6 = (f32[256,128]{1,0:T(8,128)S(1)}, f32[256,128]{1,0:T(8,128)S(1)}, u32[]{:S(2)}, u32[]{:S(2)}) collective-permute-start(f32[256,128]{1,0:T(8,128)S(1)} %convolution_add_fusion.3), channel_id=1, source_target_pairs={{0,16},{8,24},{16,0},{24,8},{32,48},{40,56},{48,32},{56,40},{64,80... | collective-permute-start | bytes 393224 | tf_op jit(solution)/shard_map/ppermute | solution.py:61
  77.6 10.0 %copy-start.3 = (bf16[16,32,256]{2,0,1:T(8,128)(2,1)S(1)}, bf16[16,32,256]{2,0,1:T(8,128)(2,1)}, u32[]{:S(2)}) copy-start(bf16[16,32,256]{2,0,1:T(8,128)(2,1)} %get-tuple-element.22) | copy-start | bytes 786436
  79.1 5.3 %collective-permute-start.7 = (f32[256,128]{1,0:T(8,128)S(1)}, f32[256,128]{1,0:T(8,128)S(1)}, u32[]{:S(2)}, u32[]{:S(2)}) collective-permute-start(f32[256,128]{1,0:T(8,128)S(1)} %convolution_add_fusion.2), channel_id=1, source_target_pairs={{0,32},{8,40},{16,48},{24,56},{32,0},{40,8},{48,16},{56,24},{64,96... | collective-permute-start | bytes 393224 | tf_op jit(solution)/shard_map/ppermute | solution.py:61
  84.8 6.6 %collective-permute-start.8 = (f32[256,128]{1,0:T(8,128)S(1)}, f32[256,128]{1,0:T(8,128)S(1)}, u32[]{:S(2)}, u32[]{:S(2)}) collective-permute-start(f32[256,128]{1,0:T(8,128)S(1)} %convolution_add_fusion.1), channel_id=1, source_target_pairs={{0,64},{8,72},{16,80},{24,88},{32,96},{40,104},{48,112},{56,120},{... | collective-permute-start | bytes 393224 | tf_op jit(solution)/shard_map/ppermute | solution.py:61

commit v14 on v12

--- a/solution.py
+++ b/solution.py
@@ -37,7 +37,7 @@
         o_ref[:, pl.ds(col, CHUNK)] = jnp.concatenate(rows, axis=0).T.astype(o_ref.dtype)
         return carry
 
-    lax.fori_loop(0, count // CHUNK, body, 0)
+    lax.fori_loop(0, count // CHUNK, body, 0, unroll=2)
 
 
 def gather_points(points, index):

time: 92.5 us -> 90.1 us (0.974)
  Pallas kernels: 34.5 us -> 32 us
    pallas_call x1, Pallas kernels: 34.5 us -> 32 us  [gather_points(): pl.pallas_call(gather_kernel, out_shape=jax.ShapeDtypeStruct((width, coun...]
  transfers between devices with their start and end apart: 9 -> 9, of which waited for: 4 -> 4; matrix products, arithmetic and copies ran while one was open for 26% -> 27% of each run, Pallas kernels for 0% -> 0%
where the time goes in v14:
time: 90.1 us; the launch traced here: 89.6 us
  Pallas kernels  32 us (36%)
  starting transfers between devices  23.5 us (26%)
  matrix products  23.4 us (26%)
  local copies, waits for them, and re-layouts  6.78 us (8%)
  waiting for transfers between devices  3.4 us (4%)
    pallas_call x1, Pallas kernels, gather_points(): pl.pallas_call(gather_kernel, out_shape=jax.ShapeDtypeStruct((width, coun...  32 us
    ppermute x7, starting transfers between devices, from_partner(): lax.ppermute(x, axis, [(i, i ^ 1 << distance) for i in range(lax.axis_siz...  20 us
    dot_general x1, matrix products, local(): jnp.einsum('lpq,slq->slp', band_blocks[:half, 0], own_first, preferred_el...  3.47 us
    dot_general x1, matrix products, local(): jnp.einsum('lpq,slq->slp', band_blocks[half:, 0], own_second, preferred_e...  3.38 us
    dot_general x1, matrix products, local(): jnp.einsum('lpq,slq->slp', band_blocks[:half, 1], picked_first, preferred...  3.38 us
    dot_general x1, matrix products, local(): jnp.einsum('lpq,slq->slp', band_blocks[half:, 1], picked_second, preferre...  3.38 us
    dot_general x7, matrix products, translate(): jnp.dot(level_matrices[0], own_coeffs, precision=lax.Precision.HIGH, pref...  2.95 us
    dot_general x7, matrix products, translate(): jnp.dot(level_matrices[1], other_coeffs, precision=lax.Precision.HIGH, pr...  2.92 us
  transfers between devices with their start and end apart: 9, of which 4 were waited for; matrix products, arithmetic and copies ran while one was open for 27% of the time, Pallas kernels for 0%

profile of v14, /device:TPU:0, one launch (start us, length us, event | category | flops | bytes accessed | tf_op | source)
XLA Modules:
  0.0 89.6 jit_solution(13002428153836218707)
XLA Ops:
  0.0 32.0 %shard_map.73 = bf16[16,16384]{1,0:T(8,128)(2,1)} custom-call(s32[16384]{0:T(1024)} %idx_ref.1, f32[16,16384]{1,0:T(8,128)} %x_hbm.1), custom_call_target="tpu_custom_call" | custom-call | bytes 1572864 | tf_op jit(solution)/shard_map/pallas_call | solution.py:45
  32.0 1.9 %fusion.32 = f32[64,16,32]{2,1,0:T(8,128)S(1)} fusion(bf16[64,32,256]{2,1,0:T(8,128)(2,1)} %param.10, bf16[2,64,8,256]{3,2,1,0:T(8,128)(2,1)} %bitcast.126), kind=kOutput, calls=%fused_computation.41 | convolution fusion | flops 16777216 | bytes 1703936 | tf_op jit(solution)/shard_map/lrp,slp->rls/dot_general | solution.py:112
  34.1 1.8 %collective-permute-start = (f32[256,128]{1,0:T(8,128)S(1)}, f32[256,128]{1,0:T(8,128)S(1)}, u32[]{:S(2)}, u32[]{:S(2)}) collective-permute-start(f32[256,128]{1,0:T(8,128)S(1)} %bitcast.147), channel_id=1, source_target_pairs={{0,1},{1,0},{2,3},{3,2},{4,5},{5,4},{6,7},{7,6},{8,9},{9,8},{10,11... | collective-permute-start | bytes 393224 | tf_op jit(solution)/shard_map/ppermute | solution.py:61
  35.8 1.0 %fusion.36 = (bf16[16,4096]{1,0:T(8,128)(2,1)S(1)}, bf16[16,4096]{1,0:T(8,128)(2,1)S(1)}) fusion(bf16[16,16384]{1,0:T(8,128)(2,1)} %shard_map.73), kind=kLoop, calls=%fused_computation.45 | loop fusion | bytes 524288 | tf_op jit(solution)/shard_map/slice | solution.py:69
  36.8 2.2 %collective-permute-start.1 = (bf16[16,4096]{1,0:T(8,128)(2,1)S(1)}, bf16[16,4096]{1,0:T(8,128)(2,1)S(1)}, u32[]{:S(2)}, u32[]{:S(2)}) collective-permute-start(bf16[16,4096]{1,0:T(8,128)(2,1)S(1)} %get-tuple-element.45), channel_id=1, source_target_pairs={{0,1},{1,2},{2,3},{3,4},{4,5},{5,6},{6,7},{7,8},{8,9},{9,10},{10,1... | collective-permute-start | bytes 393224 | tf_op jit(solution)/shard_map/ppermute | solution.py:71
  39.1 1.3 %collective-permute-start.2 = (bf16[16,4096]{1,0:T(8,128)(2,1)S(1)}, bf16[16,4096]{1,0:T(8,128)(2,1)S(1)}, u32[]{:S(2)}, u32[]{:S(2)}) collective-permute-start(bf16[16,4096]{1,0:T(8,128)(2,1)S(1)} %get-tuple-element.46), channel_id=1, source_target_pairs={{1,0},{2,1},{3,2},{4,3},{5,4},{6,5},{7,6},{8,7},{9,8},{10,9},{11,1... | collective-permute-start | bytes 393224 | tf_op jit(solution)/shard_map/ppermute | solution.py:72
  40.4 1.1 %copy.41 = bf16[2,64,8,256]{3,2,0,1:T(8,128)(2,1)S(1)} copy(bf16[2,64,8,256]{3,2,1,0:T(8,128)(2,1)} %bitcast.127) | data formatting | bytes 1048576 | tf_op jit(solution)/shard_map/reshape | solution.py:111
  41.5 1.7 %convolution_bitcast_fusion = f32[7,2,8,32,256]{4,3,1,0,2:T(8,128)S(1)} fusion(s32[8]{0:T(128)S(1)} %iota_multiply_fusion, f32[1,7,8,2,32,32]{5,4,3,2,1,0:T(8,128)S(1)} %copy-done.1), kind=kOutput, calls=%fused_computation.13 | convolution fusion | flops 352452608 | bytes 4128800 | tf_op jit(solution)/shard_map/lgtab,gbc->ltgac/dot_general | solution.py:83
  43.2 1.2 %fusion.33 = (f32[1,1,8,32,256]{4,3,1,0,2:T(8,128)S(1)}, f32[1,1,8,32,256]{4,3,1,0,2:T(8,128)S(1)}, f32[1,1,8,32,256]{4,3,1,0,2:T(8,128)S(1)}, f32[1,1,8,32,256]...) fusion(f32[7,2,8,32,256]{4,3,1,0,2:T(8,128)S(1)} %convolution_b, ...), kind=kLoop, calls=%fused_computation.42 | loop fusion | bytes 7340032 | tf_op jit(solution)/shard_map/slice | solution.py:96
  44.7 0.8 fusion.34
  47.0 5.2 %collective-permute-start.3 = (f32[256,128]{1,0:T(8,128)S(1)}, f32[256,128]{1,0:T(8,128)}, u32[]{:S(2)}, u32[]{:S(2)}) collective-permute-start(f32[256,128]{1,0:T(8,128)S(1)} %convolution_add_fusion.6), channel_id=1, source_target_pairs={{0,2},{1,3},{2,0},{3,1},{4,6},{5,7},{6,4},{7,5},{8,10},{9,11},{10,... | collective-permute-start | bytes 393224 | tf_op jit(solution)/shard_map/ppermute | solution.py:61
  53.5 1.2 %fusion.38 = f32[256,128]{1,0:T(8,128)S(1)} fusion(f32[256,256]{1,0:T(8,128)} %bitcast.144, f32[256,128]{1,0:T(8,128)S(1)} %convolution_add_fusion.6), kind=kOutput, calls=%fused_computation.47 | convolution fusion | flops 50331648 | bytes 524288 | tf_op jit(solution)/shard_map/dot_general | solution.py:89
  55.3 1.3 %convolution_add_fusion.5 = f32[256,128]{1,0:T(8,128)S(1)} fusion(f32[256,128]{1,0:T(8,128)S(1)} %fusion.38, f32[256,256]{1,0:T(8,128)} %bitcast.143, f32[256,128]{1,0:T(8,128)} %collective-permute-done.3), kind=kOutput, calls=%fused_computation.28 | convolution fusion | flops 50364416 | bytes 655360 | tf_op jit(solution)/shard_map/dot_general | solution.py:95
  56.6 7.4 %collective-permute-start.4 = (f32[256,128]{1,0:T(8,128)S(1)}, f32[256,128]{1,0:T(8,128)S(1)}, u32[]{:S(2)}, u32[]{:S(2)}) collective-permute-start(f32[256,128]{1,0:T(8,128)S(1)} %convolution_add_fusion.5), channel_id=1, source_target_pairs={{0,4},{1,5},{2,6},{3,7},{4,0},{5,1},{6,2},{7,3},{8,12},{9,13},{10,... | collective-permute-start | bytes 393224 | tf_op jit(solution)/shard_map/ppermute | solution.py:61
  64.0 3.5 %fusion.16 = f32[16,32,256]{2,0,1:T(8,128)S(1)} fusion(bf16[16,32,256]{2,0,1:T(8,128)(2,1)} %get-tuple-element.21, bf16[64,2,256,256]{3,2,1,0:T(8,128)(2,1)} %param.11), kind=kOutput, calls=%fused_computation.19 | convolution fusion | flops 67108864 | bytes 4980736 | tf_op jit(solution)/shard_map/lpq,slq->slp/dot_general | solution.py:148
  68.4 1.0 %collective-permute-done.5 = f32[256,128]{1,0:T(8,128)S(1)} collective-permute-done((f32[256,128]{1,0:T(8,128)S(1)}, f32[256,128]{1,0:T(8,128)S(1)}, u32[]{:S(2)}, u32[]{:S(2)}) %collective-permute-start.5) | collective-permute-done | bytes 131104 | tf_op jit(solution)/shard_map/ppermute | solution.py:61
  69.7 1.1 %collective-permute-start.6 = (f32[256,128]{1,0:T(8,128)S(1)}, f32[256,128]{1,0:T(8,128)S(1)}, u32[]{:S(2)}, u32[]{:S(2)}) collective-permute-start(f32[256,128]{1,0:T(8,128)S(1)} %convolution_add_fusion.3), channel_id=1, source_target_pairs={{0,16},{8,24},{16,0},{24,8},{32,48},{40,56},{48,32},{56,40},{64,80... | collective-permute-start | bytes 393224 | tf_op jit(solution)/shard_map/ppermute | solution.py:61
  70.8 3.4 %fusion.22 = f32[16,32,256]{2,0,1:T(8,128)S(1)} fusion(bf16[16,32,256]{2,0,1:T(8,128)(2,1)S(1)} %get-tuple-element.23, bf16[64,2,256,256]{3,2,1,0:T(8,128)(2,1)} %param.11), kind=kOutput, calls=%fused_computation.21 | convolution fusion | flops 67108864 | bytes 4980736 | tf_op jit(solution)/shard_map/lpq,slq->slp/dot_general | solution.py:153
  74.5 0.9 collective-permute-done.6
  75.6 1.6 %collective-permute-start.7 = (f32[256,128]{1,0:T(8,128)S(1)}, f32[256,128]{1,0:T(8,128)S(1)}, u32[]{:S(2)}, u32[]{:S(2)}) collective-permute-start(f32[256,128]{1,0:T(8,128)S(1)} %convolution_add_fusion.2), channel_id=1, source_target_pairs={{0,32},{8,40},{16,48},{24,56},{32,0},{40,8},{48,16},{56,24},{64,96... | collective-permute-start | bytes 393224 | tf_op jit(solution)/shard_map/ppermute | solution.py:61
  77.2 3.4 %fusion.25 = f32[16,32,256]{2,0,1:T(8,128)S(1)} fusion(bf16[16,32,256]{2,0,1:T(8,128)(2,1)S(1)} %get-tuple-element.24, bf16[64,2,256,256]{3,2,1,0:T(8,128)(2,1)} %param.11), kind=kOutput, calls=%fused_computation.22 | convolution fusion | flops 67108864 | bytes 4980736 | tf_op jit(solution)/shard_map/lpq,slq->slp/dot_general | solution.py:156
  81.2 2.9 %collective-permute-start.8 = (f32[256,128]{1,0:T(8,128)S(1)}, f32[256,128]{1,0:T(8,128)S(1)}, u32[]{:S(2)}, u32[]{:S(2)}) collective-permute-start(f32[256,128]{1,0:T(8,128)S(1)} %convolution_add_fusion.1), channel_id=1, source_target_pairs={{0,64},{8,72},{16,80},{24,88},{32,96},{40,104},{48,112},{56,120},{... | collective-permute-start | bytes 393224 | tf_op jit(solution)/shard_map/ppermute | solution.py:61
  84.1 3.4 %fusion.19 = f32[16,32,256]{2,0,1:T(8,128)S(1)} fusion(bf16[16,32,256]{2,0,1:T(8,128)(2,1)S(1)} %copy-done.5, bf16[64,2,256,256]{3,2,1,0:T(8,128)(2,1)} %param.11), kind=kOutput, calls=%fused_computation.20 | convolution fusion | flops 67108864 | bytes 4980736 | tf_op jit(solution)/shard_map/lpq,slq->slp/dot_general | solution.py:149
  88.5 1.1 %copy.35 = f32[64,2,8,256]{3,2,0,1:T(8,128)} copy(f32[64,2,8,256]{3,2,1,0:T(8,128)S(1)} %fusion.15) | data formatting | bytes 2097152 | tf_op jit(solution)/shard_map/reshape | solution.py:160
  (46 shorter events, 7.1 us)
Async XLA Ops:
  32.0 9.5 %copy-start.1 = (f32[1,7,8,2,32,32]{5,4,3,2,1,0:T(8,128)S(1)}, f32[1,7,8,2,32,32]{5,4,3,2,1,0:T(8,128)}, u32[]{:S(2)}) copy-start(f32[1,7,8,2,32,32]{5,4,3,2,1,0:T(8,128)} %param.12) | copy-start | bytes 1376260
  34.1 12.6 %collective-permute-start = (f32[256,128]{1,0:T(8,128)S(1)}, f32[256,128]{1,0:T(8,128)S(1)}, u32[]{:S(2)}, u32[]{:S(2)}) collective-permute-start(f32[256,128]{1,0:T(8,128)S(1)} %bitcast.147), channel_id=1, source_target_pairs={{0,1},{1,0},{2,3},{3,2},{4,5},{5,4},{6,7},{7,6},{8,9},{9,8},{10,11... | collective-permute-start | bytes 393224 | tf_op jit(solution)/shard_map/ppermute | solution.py:61
  36.8 8.8 %collective-permute-start.1 = (bf16[16,4096]{1,0:T(8,128)(2,1)S(1)}, bf16[16,4096]{1,0:T(8,128)(2,1)S(1)}, u32[]{:S(2)}, u32[]{:S(2)}) collective-permute-start(bf16[16,4096]{1,0:T(8,128)(2,1)S(1)} %get-tuple-element.45), channel_id=1, source_target_pairs={{0,1},{1,2},{2,3},{3,4},{4,5},{5,6},{6,7},{7,8},{8,9},{9,10},{10,1... | collective-permute-start | bytes 393224 | tf_op jit(solution)/shard_map/ppermute | solution.py:71
  39.1 7.4 %collective-permute-start.2 = (bf16[16,4096]{1,0:T(8,128)(2,1)S(1)}, bf16[16,4096]{1,0:T(8,128)(2,1)S(1)}, u32[]{:S(2)}, u32[]{:S(2)}) collective-permute-start(bf16[16,4096]{1,0:T(8,128)(2,1)S(1)} %get-tuple-element.46), channel_id=1, source_target_pairs={{1,0},{2,1},{3,2},{4,3},{5,4},{6,5},{7,6},{8,7},{9,8},{10,9},{11,1... | collective-permute-start | bytes 393224 | tf_op jit(solution)/shard_map/ppermute | solution.py:72
  43.2 2.4 %copy-start.6 = (s32[64]{0:T(128)S(1)}, s32[64]{0:T(128)}, u32[]{:S(2)}) copy-start(s32[64]{0:T(128)} %param.9) | copy-start | bytes 772
  43.2 3.2 %copy-start = (bf16[16,16384]{1,0:T(8,128)(2,1)S(1)}, bf16[16,16384]{1,0:T(8,128)(2,1)}, u32[]{:S(2)}) copy-start(bf16[16,16384]{1,0:T(8,128)(2,1)} %shard_map.73) | copy-start | bytes 1572868
  47.0 8.4 %collective-permute-start.3 = (f32[256,128]{1,0:T(8,128)S(1)}, f32[256,128]{1,0:T(8,128)}, u32[]{:S(2)}, u32[]{:S(2)}) collective-permute-start(f32[256,128]{1,0:T(8,128)S(1)} %convolution_add_fusion.6), channel_id=1, source_target_pairs={{0,2},{1,3},{2,0},{3,1},{4,6},{5,7},{6,4},{7,5},{8,10},{9,11},{10,... | collective-permute-start | bytes 393224 | tf_op jit(solution)/shard_map/ppermute | solution.py:61
  53.3 14.2 %copy-start.4 = (f32[1,1,8,32,256]{4,3,1,0,2:T(8,128)S(1)}, f32[1,1,8,32,256]{4,3,1,0,2:T(8,128)}, u32[]{:S(2)}) copy-start(f32[1,1,8,32,256]{4,3,1,0,2:T(8,128)} %get-tuple-element.36) | copy-start | bytes 786436
  56.6 11.1 %collective-permute-start.4 = (f32[256,128]{1,0:T(8,128)S(1)}, f32[256,128]{1,0:T(8,128)S(1)}, u32[]{:S(2)}, u32[]{:S(2)}) collective-permute-start(f32[256,128]{1,0:T(8,128)S(1)} %convolution_add_fusion.5), channel_id=1, source_target_pairs={{0,4},{1,5},{2,6},{3,7},{4,0},{5,1},{6,2},{7,3},{8,12},{9,13},{10,... | collective-permute-start | bytes 393224 | tf_op jit(solution)/shard_map/ppermute | solution.py:61
  68.0 1.4 %collective-permute-start.5 = (f32[256,128]{1,0:T(8,128)S(1)}, f32[256,128]{1,0:T(8,128)S(1)}, u32[]{:S(2)}, u32[]{:S(2)}) collective-permute-start(f32[256,128]{1,0:T(8,128)S(1)} %convolution_add_fusion.4), channel_id=1, source_target_pairs={{0,8},{8,0},{16,24},{24,16},{32,40},{40,32},{48,56},{56,48},{64,72... | collective-permute-start | bytes 393224 | tf_op jit(solution)/shard_map/ppermute | solution.py:61
  69.7 5.6 %collective-permute-start.6 = (f32[256,128]{1,0:T(8,128)S(1)}, f32[256,128]{1,0:T(8,128)S(1)}, u32[]{:S(2)}, u32[]{:S(2)}) collective-permute-start(f32[256,128]{1,0:T(8,128)S(1)} %convolution_add_fusion.3), channel_id=1, source_target_pairs={{0,16},{8,24},{16,0},{24,8},{32,48},{40,56},{48,32},{56,40},{64,80... | collective-permute-start | bytes 393224 | tf_op jit(solution)/shard_map/ppermute | solution.py:61
  74.2 9.9 %copy-start.5 = (bf16[16,32,256]{2,0,1:T(8,128)(2,1)S(1)}, bf16[16,32,256]{2,0,1:T(8,128)(2,1)}, u32[]{:S(2)}) copy-start(bf16[16,32,256]{2,0,1:T(8,128)(2,1)} %get-tuple-element.22) | copy-start | bytes 786436
  75.6 5.2 %collective-permute-start.7 = (f32[256,128]{1,0:T(8,128)S(1)}, f32[256,128]{1,0:T(8,128)S(1)}, u32[]{:S(2)}, u32[]{:S(2)}) collective-permute-start(f32[256,128]{1,0:T(8,128)S(1)} %convolution_add_fusion.2), channel_id=1, source_target_pairs={{0,32},{8,40},{16,48},{24,56},{32,0},{40,8},{48,16},{56,24},{64,96... | collective-permute-start | bytes 393224 | tf_op jit(solution)/shard_map/ppermute | solution.py:61
  80.6 6.9 %copy-start.3 = (f32[1,1,8,32,256]{4,3,1,0,2:T(8,128)S(1)}, f32[1,1,8,32,256]{4,3,1,0,2:T(8,128)}, u32[]{:S(2)}) copy-start(f32[1,1,8,32,256]{4,3,1,0,2:T(8,128)} %get-tuple-element.40) | copy-start | bytes 786436
  80.6 7.6 %copy-start.2 = (bf16[64,32,256]{2,1,0:T(8,128)(2,1)S(1)}, bf16[64,32,256]{2,1,0:T(8,128)(2,1)}, u32[]{:S(2)}) copy-start(bf16[64,32,256]{2,1,0:T(8,128)(2,1)} %param.13) | copy-start | bytes 3145732
  81.2 6.6 %collective-permute-start.8 = (f32[256,128]{1,0:T(8,128)S(1)}, f32[256,128]{1,0:T(8,128)S(1)}, u32[]{:S(2)}, u32[]{:S(2)}) collective-permute-start(f32[256,128]{1,0:T(8,128)S(1)} %convolution_add_fusion.1), channel_id=1, source_target_pairs={{0,64},{8,72},{16,80},{24,88},{32,96},{40,104},{48,112},{56,120},{... | collective-permute-start | bytes 393224 | tf_op jit(solution)/shard_map/ppermute | solution.py:61

commit v15 on v14

--- a/solution.py
+++ b/solution.py
@@ -29,7 +29,7 @@
             xt_ref[pl.ds(col, CHUNK), :] = x_ref[:, pl.ds(col, CHUNK)].T
             return carry
 
-        lax.fori_loop(0, span // CHUNK, spread, 0)
+        lax.fori_loop(0, span // CHUNK, spread, 0, unroll=2)
 
     def body(c, carry):
         col = pl.multiple_of(c * CHUNK, CHUNK)
@@ -37,7 +37,7 @@
         o_ref[:, pl.ds(col, CHUNK)] = jnp.concatenate(rows, axis=0).T.astype(o_ref.dtype)
         return carry
 
-    lax.fori_loop(0, count // CHUNK, body, 0, unroll=2)
+    lax.fori_loop(0, count // CHUNK, body, 0, unroll=4)
 
 
 def gather_points(points, index):

time: 90.1 us -> 82.3 us (0.913)
  Pallas kernels: 32 us -> 24.3 us
    pallas_call x1, Pallas kernels: 32 us -> 24.3 us  [gather_points(): pl.pallas_call(gather_kernel, out_shape=jax.ShapeDtypeStruct((width, coun...]
  transfers between devices with their start and end apart: 9 -> 9, of which waited for: 4 -> 4; matrix products, arithmetic and copies ran while one was open for 27% -> 29% of each run, Pallas kernels for 0% -> 0%
where the time goes in v15:
time: 82.3 us; the launch traced here: 81.9 us
  Pallas kernels  24.3 us (30%)
  starting transfers between devices  23.5 us (29%)
  matrix products  23.4 us (28%)
  local copies, waits for them, and re-layouts  6.78 us (8%)
  waiting for transfers between devices  3.4 us (4%)
    pallas_call x1, Pallas kernels, gather_points(): pl.pallas_call(gather_kernel, out_shape=jax.ShapeDtypeStruct((width, coun...  24.3 us
    ppermute x7, starting transfers between devices, from_partner(): lax.ppermute(x, axis, [(i, i ^ 1 << distance) for i in range(lax.axis_siz...  20 us
    dot_general x1, matrix products, local(): jnp.einsum('lpq,slq->slp', band_blocks[:half, 0], own_first, preferred_el...  3.47 us
    dot_general x1, matrix products, local(): jnp.einsum('lpq,slq->slp', band_blocks[half:, 0], own_second, preferred_e...  3.38 us
    dot_general x1, matrix products, local(): jnp.einsum('lpq,slq->slp', band_blocks[:half, 1], picked_first, preferred...  3.38 us
    dot_general x1, matrix products, local(): jnp.einsum('lpq,slq->slp', band_blocks[half:, 1], picked_second, preferre...  3.38 us
    dot_general x7, matrix products, translate(): jnp.dot(level_matrices[0], own_coeffs, precision=lax.Precision.HIGH, pref...  2.95 us
    dot_general x7, matrix products, translate(): jnp.dot(level_matrices[1], other_coeffs, precision=lax.Precision.HIGH, pr...  2.92 us
  transfers between devices with their start and end apart: 9, of which 4 were waited for; matrix products, arithmetic and copies ran while one was open for 29% of the time, Pallas kernels for 0%

profile of v15, /device:TPU:0, one launch (start us, length us, event | category | flops | bytes accessed | tf_op | source)
XLA Modules:
  0.0 81.9 jit_solution(1738200047192820224)
XLA Ops:
  0.0 24.3 %shard_map.73 = bf16[16,16384]{1,0:T(8,128)(2,1)} custom-call(s32[16384]{0:T(1024)} %idx_ref.1, f32[16,16384]{1,0:T(8,128)} %x_hbm.1), custom_call_target="tpu_custom_call" | custom-call | bytes 1572864 | tf_op jit(solution)/shard_map/pallas_call | solution.py:45
  24.3 1.9 %fusion.32 = f32[64,16,32]{2,1,0:T(8,128)S(1)} fusion(bf16[64,32,256]{2,1,0:T(8,128)(2,1)} %param.10, bf16[2,64,8,256]{3,2,1,0:T(8,128)(2,1)} %bitcast.126), kind=kOutput, calls=%fused_computation.41 | convolution fusion | flops 16777216 | bytes 1703936 | tf_op jit(solution)/shard_map/lrp,slp->rls/dot_general | solution.py:112
  26.4 1.8 %collective-permute-start = (f32[256,128]{1,0:T(8,128)S(1)}, f32[256,128]{1,0:T(8,128)S(1)}, u32[]{:S(2)}, u32[]{:S(2)}) collective-permute-start(f32[256,128]{1,0:T(8,128)S(1)} %bitcast.147), channel_id=1, source_target_pairs={{0,1},{1,0},{2,3},{3,2},{4,5},{5,4},{6,7},{7,6},{8,9},{9,8},{10,11... | collective-permute-start | bytes 393224 | tf_op jit(solution)/shard_map/ppermute | solution.py:61
  28.1 1.0 %fusion.36 = (bf16[16,4096]{1,0:T(8,128)(2,1)S(1)}, bf16[16,4096]{1,0:T(8,128)(2,1)S(1)}) fusion(bf16[16,16384]{1,0:T(8,128)(2,1)} %shard_map.73), kind=kLoop, calls=%fused_computation.45 | loop fusion | bytes 524288 | tf_op jit(solution)/shard_map/slice | solution.py:69
  29.1 2.2 %collective-permute-start.1 = (bf16[16,4096]{1,0:T(8,128)(2,1)S(1)}, bf16[16,4096]{1,0:T(8,128)(2,1)S(1)}, u32[]{:S(2)}, u32[]{:S(2)}) collective-permute-start(bf16[16,4096]{1,0:T(8,128)(2,1)S(1)} %get-tuple-element.45), channel_id=1, source_target_pairs={{0,1},{1,2},{2,3},{3,4},{4,5},{5,6},{6,7},{7,8},{8,9},{9,10},{10,1... | collective-permute-start | bytes 393224 | tf_op jit(solution)/shard_map/ppermute | solution.py:71
  31.4 1.3 %collective-permute-start.2 = (bf16[16,4096]{1,0:T(8,128)(2,1)S(1)}, bf16[16,4096]{1,0:T(8,128)(2,1)S(1)}, u32[]{:S(2)}, u32[]{:S(2)}) collective-permute-start(bf16[16,4096]{1,0:T(8,128)(2,1)S(1)} %get-tuple-element.46), channel_id=1, source_target_pairs={{1,0},{2,1},{3,2},{4,3},{5,4},{6,5},{7,6},{8,7},{9,8},{10,9},{11,1... | collective-permute-start | bytes 393224 | tf_op jit(solution)/shard_map/ppermute | solution.py:72
  32.7 1.1 %copy.41 = bf16[2,64,8,256]{3,2,0,1:T(8,128)(2,1)S(1)} copy(bf16[2,64,8,256]{3,2,1,0:T(8,128)(2,1)} %bitcast.127) | data formatting | bytes 1048576 | tf_op jit(solution)/shard_map/reshape | solution.py:111
  33.8 1.7 %convolution_bitcast_fusion = f32[7,2,8,32,256]{4,3,1,0,2:T(8,128)S(1)} fusion(s32[8]{0:T(128)S(1)} %iota_multiply_fusion, f32[1,7,8,2,32,32]{5,4,3,2,1,0:T(8,128)S(1)} %copy-done.1), kind=kOutput, calls=%fused_computation.13 | convolution fusion | flops 352452608 | bytes 4128800 | tf_op jit(solution)/shard_map/lgtab,gbc->ltgac/dot_general | solution.py:83
  35.5 1.2 %fusion.33 = (f32[1,1,8,32,256]{4,3,1,0,2:T(8,128)S(1)}, f32[1,1,8,32,256]{4,3,1,0,2:T(8,128)S(1)}, f32[1,1,8,32,256]{4,3,1,0,2:T(8,128)S(1)}, f32[1,1,8,32,256]...) fusion(f32[7,2,8,32,256]{4,3,1,0,2:T(8,128)S(1)} %convolution_b, ...), kind=kLoop, calls=%fused_computation.42 | loop fusion | bytes 7340032 | tf_op jit(solution)/shard_map/slice | solution.py:96
  37.0 0.8 %fusion.34 = (bf16[16,32,256]{2,0,1:T(8,128)(2,1)}, bf16[16,32,256]{2,0,1:T(8,128)(2,1)}) fusion(bf16[16,64,256]{2,0,1:T(8,128)(2,1)S(1)} %bitcast.130), kind=kLoop, calls=%fused_computation.43 | loop fusion | bytes 1048576 | tf_op jit(solution)/shard_map/slice | solution.py:135
  39.2 5.2 %collective-permute-start.3 = (f32[256,128]{1,0:T(8,128)S(1)}, f32[256,128]{1,0:T(8,128)}, u32[]{:S(2)}, u32[]{:S(2)}) collective-permute-start(f32[256,128]{1,0:T(8,128)S(1)} %convolution_add_fusion.6), channel_id=1, source_target_pairs={{0,2},{1,3},{2,0},{3,1},{4,6},{5,7},{6,4},{7,5},{8,10},{9,11},{10,... | collective-permute-start | bytes 393224 | tf_op jit(solution)/shard_map/ppermute | solution.py:61
  45.7 1.2 %fusion.38 = f32[256,128]{1,0:T(8,128)S(1)} fusion(f32[256,256]{1,0:T(8,128)} %bitcast.144, f32[256,128]{1,0:T(8,128)S(1)} %convolution_add_fusion.6), kind=kOutput, calls=%fused_computation.47 | convolution fusion | flops 50331648 | bytes 524288 | tf_op jit(solution)/shard_map/dot_general | solution.py:89
  47.6 1.3 %convolution_add_fusion.5 = f32[256,128]{1,0:T(8,128)S(1)} fusion(f32[256,128]{1,0:T(8,128)S(1)} %fusion.38, f32[256,256]{1,0:T(8,128)} %bitcast.143, f32[256,128]{1,0:T(8,128)} %collective-permute-done.3), kind=kOutput, calls=%fused_computation.28 | convolution fusion | flops 50364416 | bytes 655360 | tf_op jit(solution)/shard_map/dot_general | solution.py:95
  48.9 7.4 %collective-permute-start.4 = (f32[256,128]{1,0:T(8,128)S(1)}, f32[256,128]{1,0:T(8,128)S(1)}, u32[]{:S(2)}, u32[]{:S(2)}) collective-permute-start(f32[256,128]{1,0:T(8,128)S(1)} %convolution_add_fusion.5), channel_id=1, source_target_pairs={{0,4},{1,5},{2,6},{3,7},{4,0},{5,1},{6,2},{7,3},{8,12},{9,13},{10,... | collective-permute-start | bytes 393224 | tf_op jit(solution)/shard_map/ppermute | solution.py:61
  56.2 3.5 %fusion.16 = f32[16,32,256]{2,0,1:T(8,128)S(1)} fusion(bf16[16,32,256]{2,0,1:T(8,128)(2,1)} %get-tuple-element.21, bf16[64,2,256,256]{3,2,1,0:T(8,128)(2,1)} %param.11), kind=kOutput, calls=%fused_computation.19 | convolution fusion | flops 67108864 | bytes 4980736 | tf_op jit(solution)/shard_map/lpq,slq->slp/dot_general | solution.py:148
  60.7 1.0 %collective-permute-done.5 = f32[256,128]{1,0:T(8,128)S(1)} collective-permute-done((f32[256,128]{1,0:T(8,128)S(1)}, f32[256,128]{1,0:T(8,128)S(1)}, u32[]{:S(2)}, u32[]{:S(2)}) %collective-permute-start.5) | collective-permute-done | bytes 131104 | tf_op jit(solution)/shard_map/ppermute | solution.py:61
  62.0 1.1 %collective-permute-start.6 = (f32[256,128]{1,0:T(8,128)S(1)}, f32[256,128]{1,0:T(8,128)S(1)}, u32[]{:S(2)}, u32[]{:S(2)}) collective-permute-start(f32[256,128]{1,0:T(8,128)S(1)} %convolution_add_fusion.3), channel_id=1, source_target_pairs={{0,16},{8,24},{16,0},{24,8},{32,48},{40,56},{48,32},{56,40},{64,80... | collective-permute-start | bytes 393224 | tf_op jit(solution)/shard_map/ppermute | solution.py:61
  63.1 3.4 %fusion.22 = f32[16,32,256]{2,0,1:T(8,128)S(1)} fusion(bf16[16,32,256]{2,0,1:T(8,128)(2,1)S(1)} %get-tuple-element.23, bf16[64,2,256,256]{3,2,1,0:T(8,128)(2,1)} %param.11), kind=kOutput, calls=%fused_computation.21 | convolution fusion | flops 67108864 | bytes 4980736 | tf_op jit(solution)/shard_map/lpq,slq->slp/dot_general | solution.py:153
  66.8 0.9 %collective-permute-done.6 = f32[256,128]{1,0:T(8,128)S(1)} collective-permute-done((f32[256,128]{1,0:T(8,128)S(1)}, f32[256,128]{1,0:T(8,128)S(1)}, u32[]{:S(2)}, u32[]{:S(2)}) %collective-permute-start.6) | collective-permute-done | bytes 131104 | tf_op jit(solution)/shard_map/ppermute | solution.py:61
  67.9 1.6 %collective-permute-start.7 = (f32[256,128]{1,0:T(8,128)S(1)}, f32[256,128]{1,0:T(8,128)S(1)}, u32[]{:S(2)}, u32[]{:S(2)}) collective-permute-start(f32[256,128]{1,0:T(8,128)S(1)} %convolution_add_fusion.2), channel_id=1, source_target_pairs={{0,32},{8,40},{16,48},{24,56},{32,0},{40,8},{48,16},{56,24},{64,96... | collective-permute-start | bytes 393224 | tf_op jit(solution)/shard_map/ppermute | solution.py:61
  69.5 3.4 %fusion.25 = f32[16,32,256]{2,0,1:T(8,128)S(1)} fusion(bf16[16,32,256]{2,0,1:T(8,128)(2,1)S(1)} %get-tuple-element.24, bf16[64,2,256,256]{3,2,1,0:T(8,128)(2,1)} %param.11), kind=kOutput, calls=%fused_computation.22 | convolution fusion | flops 67108864 | bytes 4980736 | tf_op jit(solution)/shard_map/lpq,slq->slp/dot_general | solution.py:156
  73.4 2.9 %collective-permute-start.8 = (f32[256,128]{1,0:T(8,128)S(1)}, f32[256,128]{1,0:T(8,128)S(1)}, u32[]{:S(2)}, u32[]{:S(2)}) collective-permute-start(f32[256,128]{1,0:T(8,128)S(1)} %convolution_add_fusion.1), channel_id=1, source_target_pairs={{0,64},{8,72},{16,80},{24,88},{32,96},{40,104},{48,112},{56,120},{... | collective-permute-start | bytes 393224 | tf_op jit(solution)/shard_map/ppermute | solution.py:61
  76.3 3.4 %fusion.19 = f32[16,32,256]{2,0,1:T(8,128)S(1)} fusion(bf16[16,32,256]{2,0,1:T(8,128)(2,1)S(1)} %copy-done.5, bf16[64,2,256,256]{3,2,1,0:T(8,128)(2,1)} %param.11), kind=kOutput, calls=%fused_computation.20 | convolution fusion | flops 67108864 | bytes 4980736 | tf_op jit(solution)/shard_map/lpq,slq->slp/dot_general | solution.py:149
  80.8 1.1 %copy.35 = f32[64,2,8,256]{3,2,0,1:T(8,128)} copy(f32[64,2,8,256]{3,2,1,0:T(8,128)S(1)} %fusion.15) | data formatting | bytes 2097152 | tf_op jit(solution)/shard_map/reshape | solution.py:160
  (46 shorter events, 7.1 us)
Async XLA Ops:
  24.3 9.5 %copy-start.1 = (f32[1,7,8,2,32,32]{5,4,3,2,1,0:T(8,128)S(1)}, f32[1,7,8,2,32,32]{5,4,3,2,1,0:T(8,128)}, u32[]{:S(2)}) copy-start(f32[1,7,8,2,32,32]{5,4,3,2,1,0:T(8,128)} %param.12) | copy-start | bytes 1376260
  26.4 12.6 %collective-permute-start = (f32[256,128]{1,0:T(8,128)S(1)}, f32[256,128]{1,0:T(8,128)S(1)}, u32[]{:S(2)}, u32[]{:S(2)}) collective-permute-start(f32[256,128]{1,0:T(8,128)S(1)} %bitcast.147), channel_id=1, source_target_pairs={{0,1},{1,0},{2,3},{3,2},{4,5},{5,4},{6,7},{7,6},{8,9},{9,8},{10,11... | collective-permute-start | bytes 393224 | tf_op jit(solution)/shard_map/ppermute | solution.py:61
  29.1 8.8 %collective-permute-start.1 = (bf16[16,4096]{1,0:T(8,128)(2,1)S(1)}, bf16[16,4096]{1,0:T(8,128)(2,1)S(1)}, u32[]{:S(2)}, u32[]{:S(2)}) collective-permute-start(bf16[16,4096]{1,0:T(8,128)(2,1)S(1)} %get-tuple-element.45), channel_id=1, source_target_pairs={{0,1},{1,2},{2,3},{3,4},{4,5},{5,6},{6,7},{7,8},{8,9},{9,10},{10,1... | collective-permute-start | bytes 393224 | tf_op jit(solution)/shard_map/ppermute | solution.py:71
  31.4 7.4 %collective-permute-start.2 = (bf16[16,4096]{1,0:T(8,128)(2,1)S(1)}, bf16[16,4096]{1,0:T(8,128)(2,1)S(1)}, u32[]{:S(2)}, u32[]{:S(2)}) collective-permute-start(bf16[16,4096]{1,0:T(8,128)(2,1)S(1)} %get-tuple-element.46), channel_id=1, source_target_pairs={{1,0},{2,1},{3,2},{4,3},{5,4},{6,5},{7,6},{8,7},{9,8},{10,9},{11,1... | collective-permute-start | bytes 393224 | tf_op jit(solution)/shard_map/ppermute | solution.py:72
  35.5 2.4 %copy-start.6 = (s32[64]{0:T(128)S(1)}, s32[64]{0:T(128)}, u32[]{:S(2)}) copy-start(s32[64]{0:T(128)} %param.9) | copy-start | bytes 772
  35.5 3.2 %copy-start = (bf16[16,16384]{1,0:T(8,128)(2,1)S(1)}, bf16[16,16384]{1,0:T(8,128)(2,1)}, u32[]{:S(2)}) copy-start(bf16[16,16384]{1,0:T(8,128)(2,1)} %shard_map.73) | copy-start | bytes 1572868
  39.2 8.4 %collective-permute-start.3 = (f32[256,128]{1,0:T(8,128)S(1)}, f32[256,128]{1,0:T(8,128)}, u32[]{:S(2)}, u32[]{:S(2)}) collective-permute-start(f32[256,128]{1,0:T(8,128)S(1)} %convolution_add_fusion.6), channel_id=1, source_target_pairs={{0,2},{1,3},{2,0},{3,1},{4,6},{5,7},{6,4},{7,5},{8,10},{9,11},{10,... | collective-permute-start | bytes 393224 | tf_op jit(solution)/shard_map/ppermute | solution.py:61
  45.5 14.2 %copy-start.4 = (f32[1,1,8,32,256]{4,3,1,0,2:T(8,128)S(1)}, f32[1,1,8,32,256]{4,3,1,0,2:T(8,128)}, u32[]{:S(2)}) copy-start(f32[1,1,8,32,256]{4,3,1,0,2:T(8,128)} %get-tuple-element.36) | copy-start | bytes 786436
  48.9 11.1 %collective-permute-start.4 = (f32[256,128]{1,0:T(8,128)S(1)}, f32[256,128]{1,0:T(8,128)S(1)}, u32[]{:S(2)}, u32[]{:S(2)}) collective-permute-start(f32[256,128]{1,0:T(8,128)S(1)} %convolution_add_fusion.5), channel_id=1, source_target_pairs={{0,4},{1,5},{2,6},{3,7},{4,0},{5,1},{6,2},{7,3},{8,12},{9,13},{10,... | collective-permute-start | bytes 393224 | tf_op jit(solution)/shard_map/ppermute | solution.py:61
  60.3 1.4 %collective-permute-start.5 = (f32[256,128]{1,0:T(8,128)S(1)}, f32[256,128]{1,0:T(8,128)S(1)}, u32[]{:S(2)}, u32[]{:S(2)}) collective-permute-start(f32[256,128]{1,0:T(8,128)S(1)} %convolution_add_fusion.4), channel_id=1, source_target_pairs={{0,8},{8,0},{16,24},{24,16},{32,40},{40,32},{48,56},{56,48},{64,72... | collective-permute-start | bytes 393224 | tf_op jit(solution)/shard_map/ppermute | solution.py:61
  62.0 5.6 %collective-permute-start.6 = (f32[256,128]{1,0:T(8,128)S(1)}, f32[256,128]{1,0:T(8,128)S(1)}, u32[]{:S(2)}, u32[]{:S(2)}) collective-permute-start(f32[256,128]{1,0:T(8,128)S(1)} %convolution_add_fusion.3), channel_id=1, source_target_pairs={{0,16},{8,24},{16,0},{24,8},{32,48},{40,56},{48,32},{56,40},{64,80... | collective-permute-start | bytes 393224 | tf_op jit(solution)/shard_map/ppermute | solution.py:61
  66.5 9.9 %copy-start.5 = (bf16[16,32,256]{2,0,1:T(8,128)(2,1)S(1)}, bf16[16,32,256]{2,0,1:T(8,128)(2,1)}, u32[]{:S(2)}) copy-start(bf16[16,32,256]{2,0,1:T(8,128)(2,1)} %get-tuple-element.22) | copy-start | bytes 786436
  67.9 5.2 %collective-permute-start.7 = (f32[256,128]{1,0:T(8,128)S(1)}, f32[256,128]{1,0:T(8,128)S(1)}, u32[]{:S(2)}, u32[]{:S(2)}) collective-permute-start(f32[256,128]{1,0:T(8,128)S(1)} %convolution_add_fusion.2), channel_id=1, source_target_pairs={{0,32},{8,40},{16,48},{24,56},{32,0},{40,8},{48,16},{56,24},{64,96... | collective-permute-start | bytes 393224 | tf_op jit(solution)/shard_map/ppermute | solution.py:61
  72.8 6.9 %copy-start.3 = (f32[1,1,8,32,256]{4,3,1,0,2:T(8,128)S(1)}, f32[1,1,8,32,256]{4,3,1,0,2:T(8,128)}, u32[]{:S(2)}) copy-start(f32[1,1,8,32,256]{4,3,1,0,2:T(8,128)} %get-tuple-element.40) | copy-start | bytes 786436
  72.9 7.6 %copy-start.2 = (bf16[64,32,256]{2,1,0:T(8,128)(2,1)S(1)}, bf16[64,32,256]{2,1,0:T(8,128)(2,1)}, u32[]{:S(2)}) copy-start(bf16[64,32,256]{2,1,0:T(8,128)(2,1)} %param.13) | copy-start | bytes 3145732
  73.4 6.6 %collective-permute-start.8 = (f32[256,128]{1,0:T(8,128)S(1)}, f32[256,128]{1,0:T(8,128)S(1)}, u32[]{:S(2)}, u32[]{:S(2)}) collective-permute-start(f32[256,128]{1,0:T(8,128)S(1)} %convolution_add_fusion.1), channel_id=1, source_target_pairs={{0,64},{8,72},{16,80},{24,88},{32,96},{40,104},{48,112},{56,120},{... | collective-permute-start | bytes 393224 | tf_op jit(solution)/shard_map/ppermute | solution.py:61

commit v16 on v15

--- a/solution.py
+++ b/solution.py
@@ -29,7 +29,7 @@
             xt_ref[pl.ds(col, CHUNK), :] = x_ref[:, pl.ds(col, CHUNK)].T
             return carry
 
-        lax.fori_loop(0, span // CHUNK, spread, 0, unroll=2)
+        lax.fori_loop(0, span // CHUNK, spread, 0, unroll=4)
 
     def body(c, carry):
         col = pl.multiple_of(c * CHUNK, CHUNK)
@@ -37,7 +37,7 @@
         o_ref[:, pl.ds(col, CHUNK)] = jnp.concatenate(rows, axis=0).T.astype(o_ref.dtype)
         return carry
 
-    lax.fori_loop(0, count // CHUNK, body, 0, unroll=4)
+    lax.fori_loop(0, count // CHUNK, body, 0, unroll=8)
 
 
 def gather_points(points, index):

time: 82.3 us -> 79.5 us (0.966)
  Pallas kernels: 24.3 us -> 21.4 us
    pallas_call x1, Pallas kernels: 24.3 us -> 21.4 us  [gather_points(): pl.pallas_call(gather_kernel, out_shape=jax.ShapeDtypeStruct((width, coun...]
  transfers between devices with their start and end apart: 9 -> 9, of which waited for: 4 -> 4; matrix products, arithmetic and copies ran while one was open for 29% -> 30% of each run, Pallas kernels for 0% -> 0%
where the time goes in v16:
time: 79.5 us; the launch traced here: 79 us
  starting transfers between devices  23.5 us (30%)
  matrix products  23.4 us (29%)
  Pallas kernels  21.4 us (27%)
  local copies, waits for them, and re-layouts  6.78 us (9%)
  waiting for transfers between devices  3.41 us (4%)
    pallas_call x1, Pallas kernels, gather_points(): pl.pallas_call(gather_kernel, out_shape=jax.ShapeDtypeStruct((width, coun...  21.4 us
    ppermute x7, starting transfers between devices, from_partner(): lax.ppermute(x, axis, [(i, i ^ 1 << distance) for i in range(lax.axis_siz...  20 us
    dot_general x1, matrix products, local(): jnp.einsum('lpq,slq->slp', band_blocks[:half, 0], own_first, preferred_el...  3.47 us
    dot_general x1, matrix products, local(): jnp.einsum('lpq,slq->slp', band_blocks[half:, 0], own_second, preferred_e...  3.38 us
    dot_general x1, matrix products, local(): jnp.einsum('lpq,slq->slp', band_blocks[:half, 1], picked_first, preferred...  3.38 us
    dot_general x1, matrix products, local(): jnp.einsum('lpq,slq->slp', band_blocks[half:, 1], picked_second, preferre...  3.38 us
    dot_general x7, matrix products, translate(): jnp.dot(level_matrices[0], own_coeffs, precision=lax.Precision.HIGH, pref...  2.95 us
    dot_general x7, matrix products, translate(): jnp.dot(level_matrices[1], other_coeffs, precision=lax.Precision.HIGH, pr...  2.92 us
  transfers between devices with their start and end apart: 9, of which 4 were waited for; matrix products, arithmetic and copies ran while one was open for 30% of the time, Pallas kernels for 0%

profile of v16, /device:TPU:0, one launch (start us, length us, event | category | flops | bytes accessed | tf_op | source)
XLA Modules:
  0.0 79.0 jit_solution(12731229289915244425)
XLA Ops:
  0.0 21.4 %shard_map.73 = bf16[16,16384]{1,0:T(8,128)(2,1)} custom-call(s32[16384]{0:T(1024)} %idx_ref.1, f32[16,16384]{1,0:T(8,128)} %x_hbm.1), custom_call_target="tpu_custom_call" | custom-call | bytes 1572864 | tf_op jit(solution)/shard_map/pallas_call | solution.py:45
  21.4 1.9 %fusion.32 = f32[64,16,32]{2,1,0:T(8,128)S(1)} fusion(bf16[64,32,256]{2,1,0:T(8,128)(2,1)} %param.10, bf16[2,64,8,256]{3,2,1,0:T(8,128)(2,1)} %bitcast.126), kind=kOutput, calls=%fused_computation.41 | convolution fusion | flops 16777216 | bytes 1703936 | tf_op jit(solution)/shard_map/lrp,slp->rls/dot_general | solution.py:112
  23.5 1.8 %collective-permute-start = (f32[256,128]{1,0:T(8,128)S(1)}, f32[256,128]{1,0:T(8,128)S(1)}, u32[]{:S(2)}, u32[]{:S(2)}) collective-permute-start(f32[256,128]{1,0:T(8,128)S(1)} %bitcast.147), channel_id=1, source_target_pairs={{0,1},{1,0},{2,3},{3,2},{4,5},{5,4},{6,7},{7,6},{8,9},{9,8},{10,11... | collective-permute-start | bytes 393224 | tf_op jit(solution)/shard_map/ppermute | solution.py:61
  25.3 1.0 %fusion.36 = (bf16[16,4096]{1,0:T(8,128)(2,1)S(1)}, bf16[16,4096]{1,0:T(8,128)(2,1)S(1)}) fusion(bf16[16,16384]{1,0:T(8,128)(2,1)} %shard_map.73), kind=kLoop, calls=%fused_computation.45 | loop fusion | bytes 524288 | tf_op jit(solution)/shard_map/slice | solution.py:69
  26.3 2.2 %collective-permute-start.1 = (bf16[16,4096]{1,0:T(8,128)(2,1)S(1)}, bf16[16,4096]{1,0:T(8,128)(2,1)S(1)}, u32[]{:S(2)}, u32[]{:S(2)}) collective-permute-start(bf16[16,4096]{1,0:T(8,128)(2,1)S(1)} %get-tuple-element.45), channel_id=1, source_target_pairs={{0,1},{1,2},{2,3},{3,4},{4,5},{5,6},{6,7},{7,8},{8,9},{9,10},{10,1... | collective-permute-start | bytes 393224 | tf_op jit(solution)/shard_map/ppermute | solution.py:71
  28.5 1.3 %collective-permute-start.2 = (bf16[16,4096]{1,0:T(8,128)(2,1)S(1)}, bf16[16,4096]{1,0:T(8,128)(2,1)S(1)}, u32[]{:S(2)}, u32[]{:S(2)}) collective-permute-start(bf16[16,4096]{1,0:T(8,128)(2,1)S(1)} %get-tuple-element.46), channel_id=1, source_target_pairs={{1,0},{2,1},{3,2},{4,3},{5,4},{6,5},{7,6},{8,7},{9,8},{10,9},{11,1... | collective-permute-start | bytes 393224 | tf_op jit(solution)/shard_map/ppermute | solution.py:72
  29.8 1.1 %copy.41 = bf16[2,64,8,256]{3,2,0,1:T(8,128)(2,1)S(1)} copy(bf16[2,64,8,256]{3,2,1,0:T(8,128)(2,1)} %bitcast.127) | data formatting | bytes 1048576 | tf_op jit(solution)/shard_map/reshape | solution.py:111
  30.9 1.7 %convolution_bitcast_fusion = f32[7,2,8,32,256]{4,3,1,0,2:T(8,128)S(1)} fusion(s32[8]{0:T(128)S(1)} %iota_multiply_fusion, f32[1,7,8,2,32,32]{5,4,3,2,1,0:T(8,128)S(1)} %copy-done.1), kind=kOutput, calls=%fused_computation.13 | convolution fusion | flops 352452608 | bytes 4128800 | tf_op jit(solution)/shard_map/lgtab,gbc->ltgac/dot_general | solution.py:83
  32.7 1.2 %fusion.33 = (f32[1,1,8,32,256]{4,3,1,0,2:T(8,128)S(1)}, f32[1,1,8,32,256]{4,3,1,0,2:T(8,128)S(1)}, f32[1,1,8,32,256]{4,3,1,0,2:T(8,128)S(1)}, f32[1,1,8,32,256]...) fusion(f32[7,2,8,32,256]{4,3,1,0,2:T(8,128)S(1)} %convolution_b, ...), kind=kLoop, calls=%fused_computation.42 | loop fusion | bytes 7340032 | tf_op jit(solution)/shard_map/slice | solution.py:96
  34.1 0.8 %fusion.34 = (bf16[16,32,256]{2,0,1:T(8,128)(2,1)}, bf16[16,32,256]{2,0,1:T(8,128)(2,1)}) fusion(bf16[16,64,256]{2,0,1:T(8,128)(2,1)S(1)} %bitcast.130), kind=kLoop, calls=%fused_computation.43 | loop fusion | bytes 1048576 | tf_op jit(solution)/shard_map/slice | solution.py:135
  35.0 0.9 %collective-permute-done.2 = bf16[16,4096]{1,0:T(8,128)(2,1)S(1)} collective-permute-done((bf16[16,4096]{1,0:T(8,128)(2,1)S(1)}, bf16[16,4096]{1,0:T(8,128)(2,1)S(1)}, u32[]{:S(2)}, u32[]{:S(2)}) %collective-permute-start.2) | collective-permute-done | bytes 131104 | tf_op jit(solution)/shard_map/ppermute | solution.py:72
  36.4 5.2 %collective-permute-start.3 = (f32[256,128]{1,0:T(8,128)S(1)}, f32[256,128]{1,0:T(8,128)}, u32[]{:S(2)}, u32[]{:S(2)}) collective-permute-start(f32[256,128]{1,0:T(8,128)S(1)} %convolution_add_fusion.6), channel_id=1, source_target_pairs={{0,2},{1,3},{2,0},{3,1},{4,6},{5,7},{6,4},{7,5},{8,10},{9,11},{10,... | collective-permute-start | bytes 393224 | tf_op jit(solution)/shard_map/ppermute | solution.py:61
  42.9 1.2 %fusion.38 = f32[256,128]{1,0:T(8,128)S(1)} fusion(f32[256,256]{1,0:T(8,128)} %bitcast.144, f32[256,128]{1,0:T(8,128)S(1)} %convolution_add_fusion.6), kind=kOutput, calls=%fused_computation.47 | convolution fusion | flops 50331648 | bytes 524288 | tf_op jit(solution)/shard_map/dot_general | solution.py:89
  44.8 1.3 %convolution_add_fusion.5 = f32[256,128]{1,0:T(8,128)S(1)} fusion(f32[256,128]{1,0:T(8,128)S(1)} %fusion.38, f32[256,256]{1,0:T(8,128)} %bitcast.143, f32[256,128]{1,0:T(8,128)} %collective-permute-done.3), kind=kOutput, calls=%fused_computation.28 | convolution fusion | flops 50364416 | bytes 655360 | tf_op jit(solution)/shard_map/dot_general | solution.py:95
  46.1 7.3 %collective-permute-start.4 = (f32[256,128]{1,0:T(8,128)S(1)}, f32[256,128]{1,0:T(8,128)S(1)}, u32[]{:S(2)}, u32[]{:S(2)}) collective-permute-start(f32[256,128]{1,0:T(8,128)S(1)} %convolution_add_fusion.5), channel_id=1, source_target_pairs={{0,4},{1,5},{2,6},{3,7},{4,0},{5,1},{6,2},{7,3},{8,12},{9,13},{10,... | collective-permute-start | bytes 393224 | tf_op jit(solution)/shard_map/ppermute | solution.py:61
  53.4 3.5 %fusion.16 = f32[16,32,256]{2,0,1:T(8,128)S(1)} fusion(bf16[16,32,256]{2,0,1:T(8,128)(2,1)} %get-tuple-element.21, bf16[64,2,256,256]{3,2,1,0:T(8,128)(2,1)} %param.11), kind=kOutput, calls=%fused_computation.19 | convolution fusion | flops 67108864 | bytes 4980736 | tf_op jit(solution)/shard_map/lpq,slq->slp/dot_general | solution.py:148
  57.8 1.0 %collective-permute-done.5 = f32[256,128]{1,0:T(8,128)S(1)} collective-permute-done((f32[256,128]{1,0:T(8,128)S(1)}, f32[256,128]{1,0:T(8,128)S(1)}, u32[]{:S(2)}, u32[]{:S(2)}) %collective-permute-start.5) | collective-permute-done | bytes 131104 | tf_op jit(solution)/shard_map/ppermute | solution.py:61
  59.2 1.1 %collective-permute-start.6 = (f32[256,128]{1,0:T(8,128)S(1)}, f32[256,128]{1,0:T(8,128)S(1)}, u32[]{:S(2)}, u32[]{:S(2)}) collective-permute-start(f32[256,128]{1,0:T(8,128)S(1)} %convolution_add_fusion.3), channel_id=1, source_target_pairs={{0,16},{8,24},{16,0},{24,8},{32,48},{40,56},{48,32},{56,40},{64,80... | collective-permute-start | bytes 393224 | tf_op jit(solution)/shard_map/ppermute | solution.py:61
  60.3 3.4 %fusion.22 = f32[16,32,256]{2,0,1:T(8,128)S(1)} fusion(bf16[16,32,256]{2,0,1:T(8,128)(2,1)S(1)} %get-tuple-element.23, bf16[64,2,256,256]{3,2,1,0:T(8,128)(2,1)} %param.11), kind=kOutput, calls=%fused_computation.21 | convolution fusion | flops 67108864 | bytes 4980736 | tf_op jit(solution)/shard_map/lpq,slq->slp/dot_general | solution.py:153
  65.1 1.6 %collective-permute-start.7 = (f32[256,128]{1,0:T(8,128)S(1)}, f32[256,128]{1,0:T(8,128)S(1)}, u32[]{:S(2)}, u32[]{:S(2)}) collective-permute-start(f32[256,128]{1,0:T(8,128)S(1)} %convolution_add_fusion.2), channel_id=1, source_target_pairs={{0,32},{8,40},{16,48},{24,56},{32,0},{40,8},{48,16},{56,24},{64,96... | collective-permute-start | bytes 393224 | tf_op jit(solution)/shard_map/ppermute | solution.py:61
  66.6 3.4 %fusion.25 = f32[16,32,256]{2,0,1:T(8,128)S(1)} fusion(bf16[16,32,256]{2,0,1:T(8,128)(2,1)S(1)} %get-tuple-element.24, bf16[64,2,256,256]{3,2,1,0:T(8,128)(2,1)} %param.11), kind=kOutput, calls=%fused_computation.22 | convolution fusion | flops 67108864 | bytes 4980736 | tf_op jit(solution)/shard_map/lpq,slq->slp/dot_general | solution.py:156
  70.6 2.9 %collective-permute-start.8 = (f32[256,128]{1,0:T(8,128)S(1)}, f32[256,128]{1,0:T(8,128)S(1)}, u32[]{:S(2)}, u32[]{:S(2)}) collective-permute-start(f32[256,128]{1,0:T(8,128)S(1)} %convolution_add_fusion.1), channel_id=1, source_target_pairs={{0,64},{8,72},{16,80},{24,88},{32,96},{40,104},{48,112},{56,120},{... | collective-permute-start | bytes 393224 | tf_op jit(solution)/shard_map/ppermute | solution.py:61
  73.5 3.4 %fusion.19 = f32[16,32,256]{2,0,1:T(8,128)S(1)} fusion(bf16[16,32,256]{2,0,1:T(8,128)(2,1)S(1)} %copy-done.5, bf16[64,2,256,256]{3,2,1,0:T(8,128)(2,1)} %param.11), kind=kOutput, calls=%fused_computation.20 | convolution fusion | flops 67108864 | bytes 4980736 | tf_op jit(solution)/shard_map/lpq,slq->slp/dot_general | solution.py:149
  78.0 1.1 %copy.35 = f32[64,2,8,256]{3,2,0,1:T(8,128)} copy(f32[64,2,8,256]{3,2,1,0:T(8,128)S(1)} %fusion.15) | data formatting | bytes 2097152 | tf_op jit(solution)/shard_map/reshape | solution.py:160
  (46 shorter events, 7.1 us)
Async XLA Ops:
  21.4 9.5 %copy-start.1 = (f32[1,7,8,2,32,32]{5,4,3,2,1,0:T(8,128)S(1)}, f32[1,7,8,2,32,32]{5,4,3,2,1,0:T(8,128)}, u32[]{:S(2)}) copy-start(f32[1,7,8,2,32,32]{5,4,3,2,1,0:T(8,128)} %param.12) | copy-start | bytes 1376260
  23.5 12.6 %collective-permute-start = (f32[256,128]{1,0:T(8,128)S(1)}, f32[256,128]{1,0:T(8,128)S(1)}, u32[]{:S(2)}, u32[]{:S(2)}) collective-permute-start(f32[256,128]{1,0:T(8,128)S(1)} %bitcast.147), channel_id=1, source_target_pairs={{0,1},{1,0},{2,3},{3,2},{4,5},{5,4},{6,7},{7,6},{8,9},{9,8},{10,11... | collective-permute-start | bytes 393224 | tf_op jit(solution)/shard_map/ppermute | solution.py:61
  26.3 8.8 %collective-permute-start.1 = (bf16[16,4096]{1,0:T(8,128)(2,1)S(1)}, bf16[16,4096]{1,0:T(8,128)(2,1)S(1)}, u32[]{:S(2)}, u32[]{:S(2)}) collective-permute-start(bf16[16,4096]{1,0:T(8,128)(2,1)S(1)} %get-tuple-element.45), channel_id=1, source_target_pairs={{0,1},{1,2},{2,3},{3,4},{4,5},{5,6},{6,7},{7,8},{8,9},{9,10},{10,1... | collective-permute-start | bytes 393224 | tf_op jit(solution)/shard_map/ppermute | solution.py:71
  28.5 7.4 %collective-permute-start.2 = (bf16[16,4096]{1,0:T(8,128)(2,1)S(1)}, bf16[16,4096]{1,0:T(8,128)(2,1)S(1)}, u32[]{:S(2)}, u32[]{:S(2)}) collective-permute-start(bf16[16,4096]{1,0:T(8,128)(2,1)S(1)} %get-tuple-element.46), channel_id=1, source_target_pairs={{1,0},{2,1},{3,2},{4,3},{5,4},{6,5},{7,6},{8,7},{9,8},{10,9},{11,1... | collective-permute-start | bytes 393224 | tf_op jit(solution)/shard_map/ppermute | solution.py:72
  32.6 2.4 %copy-start.6 = (s32[64]{0:T(128)S(1)}, s32[64]{0:T(128)}, u32[]{:S(2)}) copy-start(s32[64]{0:T(128)} %param.9) | copy-start | bytes 772
  32.7 3.2 %copy-start = (bf16[16,16384]{1,0:T(8,128)(2,1)S(1)}, bf16[16,16384]{1,0:T(8,128)(2,1)}, u32[]{:S(2)}) copy-start(bf16[16,16384]{1,0:T(8,128)(2,1)} %shard_map.73) | copy-start | bytes 1572868
  36.4 8.4 %collective-permute-start.3 = (f32[256,128]{1,0:T(8,128)S(1)}, f32[256,128]{1,0:T(8,128)}, u32[]{:S(2)}, u32[]{:S(2)}) collective-permute-start(f32[256,128]{1,0:T(8,128)S(1)} %convolution_add_fusion.6), channel_id=1, source_target_pairs={{0,2},{1,3},{2,0},{3,1},{4,6},{5,7},{6,4},{7,5},{8,10},{9,11},{10,... | collective-permute-start | bytes 393224 | tf_op jit(solution)/shard_map/ppermute | solution.py:61
  42.7 14.2 %copy-start.4 = (f32[1,1,8,32,256]{4,3,1,0,2:T(8,128)S(1)}, f32[1,1,8,32,256]{4,3,1,0,2:T(8,128)}, u32[]{:S(2)}) copy-start(f32[1,1,8,32,256]{4,3,1,0,2:T(8,128)} %get-tuple-element.36) | copy-start | bytes 786436
  46.1 11.1 %collective-permute-start.4 = (f32[256,128]{1,0:T(8,128)S(1)}, f32[256,128]{1,0:T(8,128)S(1)}, u32[]{:S(2)}, u32[]{:S(2)}) collective-permute-start(f32[256,128]{1,0:T(8,128)S(1)} %convolution_add_fusion.5), channel_id=1, source_target_pairs={{0,4},{1,5},{2,6},{3,7},{4,0},{5,1},{6,2},{7,3},{8,12},{9,13},{10,... | collective-permute-start | bytes 393224 | tf_op jit(solution)/shard_map/ppermute | solution.py:61
  57.4 1.4 %collective-permute-start.5 = (f32[256,128]{1,0:T(8,128)S(1)}, f32[256,128]{1,0:T(8,128)S(1)}, u32[]{:S(2)}, u32[]{:S(2)}) collective-permute-start(f32[256,128]{1,0:T(8,128)S(1)} %convolution_add_fusion.4), channel_id=1, source_target_pairs={{0,8},{8,0},{16,24},{24,16},{32,40},{40,32},{48,56},{56,48},{64,72... | collective-permute-start | bytes 393224 | tf_op jit(solution)/shard_map/ppermute | solution.py:61
  59.2 5.6 %collective-permute-start.6 = (f32[256,128]{1,0:T(8,128)S(1)}, f32[256,128]{1,0:T(8,128)S(1)}, u32[]{:S(2)}, u32[]{:S(2)}) collective-permute-start(f32[256,128]{1,0:T(8,128)S(1)} %convolution_add_fusion.3), channel_id=1, source_target_pairs={{0,16},{8,24},{16,0},{24,8},{32,48},{40,56},{48,32},{56,40},{64,80... | collective-permute-start | bytes 393224 | tf_op jit(solution)/shard_map/ppermute | solution.py:61
  63.6 9.9 %copy-start.5 = (bf16[16,32,256]{2,0,1:T(8,128)(2,1)S(1)}, bf16[16,32,256]{2,0,1:T(8,128)(2,1)}, u32[]{:S(2)}) copy-start(bf16[16,32,256]{2,0,1:T(8,128)(2,1)} %get-tuple-element.22) | copy-start | bytes 786436
  65.1 5.3 %collective-permute-start.7 = (f32[256,128]{1,0:T(8,128)S(1)}, f32[256,128]{1,0:T(8,128)S(1)}, u32[]{:S(2)}, u32[]{:S(2)}) collective-permute-start(f32[256,128]{1,0:T(8,128)S(1)} %convolution_add_fusion.2), channel_id=1, source_target_pairs={{0,32},{8,40},{16,48},{24,56},{32,0},{40,8},{48,16},{56,24},{64,96... | collective-permute-start | bytes 393224 | tf_op jit(solution)/shard_map/ppermute | solution.py:61
  70.0 6.9 %copy-start.3 = (f32[1,1,8,32,256]{4,3,1,0,2:T(8,128)S(1)}, f32[1,1,8,32,256]{4,3,1,0,2:T(8,128)}, u32[]{:S(2)}) copy-start(f32[1,1,8,32,256]{4,3,1,0,2:T(8,128)} %get-tuple-element.40) | copy-start | bytes 786436
  70.0 7.7 %copy-start.2 = (bf16[64,32,256]{2,1,0:T(8,128)(2,1)S(1)}, bf16[64,32,256]{2,1,0:T(8,128)(2,1)}, u32[]{:S(2)}) copy-start(bf16[64,32,256]{2,1,0:T(8,128)(2,1)} %param.13) | copy-start | bytes 3145732
  70.6 6.6 %collective-permute-start.8 = (f32[256,128]{1,0:T(8,128)S(1)}, f32[256,128]{1,0:T(8,128)S(1)}, u32[]{:S(2)}, u32[]{:S(2)}) collective-permute-start(f32[256,128]{1,0:T(8,128)S(1)} %convolution_add_fusion.1), channel_id=1, source_target_pairs={{0,64},{8,72},{16,80},{24,88},{32,96},{40,104},{48,112},{56,120},{... | collective-permute-start | bytes 393224 | tf_op jit(solution)/shard_map/ppermute | solution.py:61

commit v17 on v16

--- a/solution.py
+++ b/solution.py
@@ -37,7 +37,7 @@
         o_ref[:, pl.ds(col, CHUNK)] = jnp.concatenate(rows, axis=0).T.astype(o_ref.dtype)
         return carry
 
-    lax.fori_loop(0, count // CHUNK, body, 0, unroll=8)
+    lax.fori_loop(0, count // CHUNK, body, 0, unroll=16)
 
 
 def gather_points(points, index):

time: 79.5 us -> 79.2 us (level)
  no operation moved by 1% of the time
where the time goes in v17:
time: 79.2 us; the launch traced here: 78.7 us
  starting transfers between devices  23.5 us (30%)
  matrix products  23.4 us (30%)
  Pallas kernels  21.1 us (27%)
  local copies, waits for them, and re-layouts  6.78 us (9%)
  waiting for transfers between devices  3.4 us (4%)
    pallas_call x1, Pallas kernels, gather_points(): pl.pallas_call(gather_kernel, out_shape=jax.ShapeDtypeStruct((width, coun...  21.1 us
    ppermute x7, starting transfers between devices, from_partner(): lax.ppermute(x, axis, [(i, i ^ 1 << distance) for i in range(lax.axis_siz...  20 us
    dot_general x1, matrix products, local(): jnp.einsum('lpq,slq->slp', band_blocks[:half, 0], own_first, preferred_el...  3.47 us
    dot_general x1, matrix products, local(): jnp.einsum('lpq,slq->slp', band_blocks[half:, 0], own_second, preferred_e...  3.38 us
    dot_general x1, matrix products, local(): jnp.einsum('lpq,slq->slp', band_blocks[half:, 1], picked_second, preferre...  3.38 us
    dot_general x1, matrix products, local(): jnp.einsum('lpq,slq->slp', band_blocks[:half, 1], picked_first, preferred...  3.38 us
    dot_general x7, matrix products, translate(): jnp.dot(level_matrices[0], own_coeffs, precision=lax.Precision.HIGH, pref...  2.95 us
    dot_general x7, matrix products, translate(): jnp.dot(level_matrices[1], other_coeffs, precision=lax.Precision.HIGH, pr...  2.92 us
  transfers between devices with their start and end apart: 9, of which 4 were waited for; matrix products, arithmetic and copies ran while one was open for 30% of the time, Pallas kernels for 0%

profile of v17, /device:TPU:0, one launch (start us, length us, event | category | flops | bytes accessed | tf_op | source)
XLA Modules:
  0.0 78.7 jit_solution(7140739835525562638)
XLA Ops:
  0.0 21.1 %shard_map.73 = bf16[16,16384]{1,0:T(8,128)(2,1)} custom-call(s32[16384]{0:T(1024)} %idx_ref.1, f32[16,16384]{1,0:T(8,128)} %x_hbm.1), custom_call_target="tpu_custom_call" | custom-call | bytes 1572864 | tf_op jit(solution)/shard_map/pallas_call | solution.py:45
  21.1 1.9 %fusion.32 = f32[64,16,32]{2,1,0:T(8,128)S(1)} fusion(bf16[64,32,256]{2,1,0:T(8,128)(2,1)} %param.10, bf16[2,64,8,256]{3,2,1,0:T(8,128)(2,1)} %bitcast.126), kind=kOutput, calls=%fused_computation.41 | convolution fusion | flops 16777216 | bytes 1703936 | tf_op jit(solution)/shard_map/lrp,slp->rls/dot_general | solution.py:112
  23.2 1.8 %collective-permute-start = (f32[256,128]{1,0:T(8,128)S(1)}, f32[256,128]{1,0:T(8,128)S(1)}, u32[]{:S(2)}, u32[]{:S(2)}) collective-permute-start(f32[256,128]{1,0:T(8,128)S(1)} %bitcast.147), channel_id=1, source_target_pairs={{0,1},{1,0},{2,3},{3,2},{4,5},{5,4},{6,7},{7,6},{8,9},{9,8},{10,11... | collective-permute-start | bytes 393224 | tf_op jit(solution)/shard_map/ppermute | solution.py:61
  24.9 1.0 %fusion.36 = (bf16[16,4096]{1,0:T(8,128)(2,1)S(1)}, bf16[16,4096]{1,0:T(8,128)(2,1)S(1)}) fusion(bf16[16,16384]{1,0:T(8,128)(2,1)} %shard_map.73), kind=kLoop, calls=%fused_computation.45 | loop fusion | bytes 524288 | tf_op jit(solution)/shard_map/slice | solution.py:69
  25.9 2.2 %collective-permute-start.1 = (bf16[16,4096]{1,0:T(8,128)(2,1)S(1)}, bf16[16,4096]{1,0:T(8,128)(2,1)S(1)}, u32[]{:S(2)}, u32[]{:S(2)}) collective-permute-start(bf16[16,4096]{1,0:T(8,128)(2,1)S(1)} %get-tuple-element.45), channel_id=1, source_target_pairs={{0,1},{1,2},{2,3},{3,4},{4,5},{5,6},{6,7},{7,8},{8,9},{9,10},{10,1... | collective-permute-start | bytes 393224 | tf_op jit(solution)/shard_map/ppermute | solution.py:71
  28.2 1.3 %collective-permute-start.2 = (bf16[16,4096]{1,0:T(8,128)(2,1)S(1)}, bf16[16,4096]{1,0:T(8,128)(2,1)S(1)}, u32[]{:S(2)}, u32[]{:S(2)}) collective-permute-start(bf16[16,4096]{1,0:T(8,128)(2,1)S(1)} %get-tuple-element.46), channel_id=1, source_target_pairs={{1,0},{2,1},{3,2},{4,3},{5,4},{6,5},{7,6},{8,7},{9,8},{10,9},{11,1... | collective-permute-start | bytes 393224 | tf_op jit(solution)/shard_map/ppermute | solution.py:72
  29.5 1.1 %copy.41 = bf16[2,64,8,256]{3,2,0,1:T(8,128)(2,1)S(1)} copy(bf16[2,64,8,256]{3,2,1,0:T(8,128)(2,1)} %bitcast.127) | data formatting | bytes 1048576 | tf_op jit(solution)/shard_map/reshape | solution.py:111
  30.6 1.7 %convolution_bitcast_fusion = f32[7,2,8,32,256]{4,3,1,0,2:T(8,128)S(1)} fusion(s32[8]{0:T(128)S(1)} %iota_multiply_fusion, f32[1,7,8,2,32,32]{5,4,3,2,1,0:T(8,128)S(1)} %copy-done.1), kind=kOutput, calls=%fused_computation.13 | convolution fusion | flops 352452608 | bytes 4128800 | tf_op jit(solution)/shard_map/lgtab,gbc->ltgac/dot_general | solution.py:83
  32.3 1.2 %fusion.33 = (f32[1,1,8,32,256]{4,3,1,0,2:T(8,128)S(1)}, f32[1,1,8,32,256]{4,3,1,0,2:T(8,128)S(1)}, f32[1,1,8,32,256]{4,3,1,0,2:T(8,128)S(1)}, f32[1,1,8,32,256]...) fusion(f32[7,2,8,32,256]{4,3,1,0,2:T(8,128)S(1)} %convolution_b, ...), kind=kLoop, calls=%fused_computation.42 | loop fusion | bytes 7340032 | tf_op jit(solution)/shard_map/slice | solution.py:96
  33.8 0.8 %fusion.34 = (bf16[16,32,256]{2,0,1:T(8,128)(2,1)}, bf16[16,32,256]{2,0,1:T(8,128)(2,1)}) fusion(bf16[16,64,256]{2,0,1:T(8,128)(2,1)S(1)} %bitcast.130), kind=kLoop, calls=%fused_computation.43 | loop fusion | bytes 1048576 | tf_op jit(solution)/shard_map/slice | solution.py:135
  36.1 5.2 %collective-permute-start.3 = (f32[256,128]{1,0:T(8,128)S(1)}, f32[256,128]{1,0:T(8,128)}, u32[]{:S(2)}, u32[]{:S(2)}) collective-permute-start(f32[256,128]{1,0:T(8,128)S(1)} %convolution_add_fusion.6), channel_id=1, source_target_pairs={{0,2},{1,3},{2,0},{3,1},{4,6},{5,7},{6,4},{7,5},{8,10},{9,11},{10,... | collective-permute-start | bytes 393224 | tf_op jit(solution)/shard_map/ppermute | solution.py:61
  42.6 1.2 %fusion.38 = f32[256,128]{1,0:T(8,128)S(1)} fusion(f32[256,256]{1,0:T(8,128)} %bitcast.144, f32[256,128]{1,0:T(8,128)S(1)} %convolution_add_fusion.6), kind=kOutput, calls=%fused_computation.47 | convolution fusion | flops 50331648 | bytes 524288 | tf_op jit(solution)/shard_map/dot_general | solution.py:89
  44.4 1.3 %convolution_add_fusion.5 = f32[256,128]{1,0:T(8,128)S(1)} fusion(f32[256,128]{1,0:T(8,128)S(1)} %fusion.38, f32[256,256]{1,0:T(8,128)} %bitcast.143, f32[256,128]{1,0:T(8,128)} %collective-permute-done.3), kind=kOutput, calls=%fused_computation.28 | convolution fusion | flops 50364416 | bytes 655360 | tf_op jit(solution)/shard_map/dot_general | solution.py:95
  45.7 7.4 %collective-permute-start.4 = (f32[256,128]{1,0:T(8,128)S(1)}, f32[256,128]{1,0:T(8,128)S(1)}, u32[]{:S(2)}, u32[]{:S(2)}) collective-permute-start(f32[256,128]{1,0:T(8,128)S(1)} %convolution_add_fusion.5), channel_id=1, source_target_pairs={{0,4},{1,5},{2,6},{3,7},{4,0},{5,1},{6,2},{7,3},{8,12},{9,13},{10,... | collective-permute-start | bytes 393224 | tf_op jit(solution)/shard_map/ppermute | solution.py:61
  53.1 3.5 %fusion.16 = f32[16,32,256]{2,0,1:T(8,128)S(1)} fusion(bf16[16,32,256]{2,0,1:T(8,128)(2,1)} %get-tuple-element.21, bf16[64,2,256,256]{3,2,1,0:T(8,128)(2,1)} %param.11), kind=kOutput, calls=%fused_computation.19 | convolution fusion | flops 67108864 | bytes 4980736 | tf_op jit(solution)/shard_map/lpq,slq->slp/dot_general | solution.py:148
  57.5 1.0 %collective-permute-done.5 = f32[256,128]{1,0:T(8,128)S(1)} collective-permute-done((f32[256,128]{1,0:T(8,128)S(1)}, f32[256,128]{1,0:T(8,128)S(1)}, u32[]{:S(2)}, u32[]{:S(2)}) %collective-permute-start.5) | collective-permute-done | bytes 131104 | tf_op jit(solution)/shard_map/ppermute | solution.py:61
  58.8 1.1 %collective-permute-start.6 = (f32[256,128]{1,0:T(8,128)S(1)}, f32[256,128]{1,0:T(8,128)S(1)}, u32[]{:S(2)}, u32[]{:S(2)}) collective-permute-start(f32[256,128]{1,0:T(8,128)S(1)} %convolution_add_fusion.3), channel_id=1, source_target_pairs={{0,16},{8,24},{16,0},{24,8},{32,48},{40,56},{48,32},{56,40},{64,80... | collective-permute-start | bytes 393224 | tf_op jit(solution)/shard_map/ppermute | solution.py:61
  59.9 3.4 %fusion.22 = f32[16,32,256]{2,0,1:T(8,128)S(1)} fusion(bf16[16,32,256]{2,0,1:T(8,128)(2,1)S(1)} %get-tuple-element.23, bf16[64,2,256,256]{3,2,1,0:T(8,128)(2,1)} %param.11), kind=kOutput, calls=%fused_computation.21 | convolution fusion | flops 67108864 | bytes 4980736 | tf_op jit(solution)/shard_map/lpq,slq->slp/dot_general | solution.py:153
  63.6 0.9 %collective-permute-done.6 = f32[256,128]{1,0:T(8,128)S(1)} collective-permute-done((f32[256,128]{1,0:T(8,128)S(1)}, f32[256,128]{1,0:T(8,128)S(1)}, u32[]{:S(2)}, u32[]{:S(2)}) %collective-permute-start.6) | collective-permute-done | bytes 131104 | tf_op jit(solution)/shard_map/ppermute | solution.py:61
  64.8 1.6 %collective-permute-start.7 = (f32[256,128]{1,0:T(8,128)S(1)}, f32[256,128]{1,0:T(8,128)S(1)}, u32[]{:S(2)}, u32[]{:S(2)}) collective-permute-start(f32[256,128]{1,0:T(8,128)S(1)} %convolution_add_fusion.2), channel_id=1, source_target_pairs={{0,32},{8,40},{16,48},{24,56},{32,0},{40,8},{48,16},{56,24},{64,96... | collective-permute-start | bytes 393224 | tf_op jit(solution)/shard_map/ppermute | solution.py:61
  66.3 3.4 %fusion.25 = f32[16,32,256]{2,0,1:T(8,128)S(1)} fusion(bf16[16,32,256]{2,0,1:T(8,128)(2,1)S(1)} %get-tuple-element.24, bf16[64,2,256,256]{3,2,1,0:T(8,128)(2,1)} %param.11), kind=kOutput, calls=%fused_computation.22 | convolution fusion | flops 67108864 | bytes 4980736 | tf_op jit(solution)/shard_map/lpq,slq->slp/dot_general | solution.py:156
  70.3 2.9 %collective-permute-start.8 = (f32[256,128]{1,0:T(8,128)S(1)}, f32[256,128]{1,0:T(8,128)S(1)}, u32[]{:S(2)}, u32[]{:S(2)}) collective-permute-start(f32[256,128]{1,0:T(8,128)S(1)} %convolution_add_fusion.1), channel_id=1, source_target_pairs={{0,64},{8,72},{16,80},{24,88},{32,96},{40,104},{48,112},{56,120},{... | collective-permute-start | bytes 393224 | tf_op jit(solution)/shard_map/ppermute | solution.py:61
  73.2 3.4 %fusion.19 = f32[16,32,256]{2,0,1:T(8,128)S(1)} fusion(bf16[16,32,256]{2,0,1:T(8,128)(2,1)S(1)} %copy-done.5, bf16[64,2,256,256]{3,2,1,0:T(8,128)(2,1)} %param.11), kind=kOutput, calls=%fused_computation.20 | convolution fusion | flops 67108864 | bytes 4980736 | tf_op jit(solution)/shard_map/lpq,slq->slp/dot_general | solution.py:149
  77.6 1.1 %copy.35 = f32[64,2,8,256]{3,2,0,1:T(8,128)} copy(f32[64,2,8,256]{3,2,1,0:T(8,128)S(1)} %fusion.15) | data formatting | bytes 2097152 | tf_op jit(solution)/shard_map/reshape | solution.py:160
  (46 shorter events, 7.1 us)
Async XLA Ops:
  21.1 9.5 %copy-start.1 = (f32[1,7,8,2,32,32]{5,4,3,2,1,0:T(8,128)S(1)}, f32[1,7,8,2,32,32]{5,4,3,2,1,0:T(8,128)}, u32[]{:S(2)}) copy-start(f32[1,7,8,2,32,32]{5,4,3,2,1,0:T(8,128)} %param.12) | copy-start | bytes 1376260
  23.2 12.6 %collective-permute-start = (f32[256,128]{1,0:T(8,128)S(1)}, f32[256,128]{1,0:T(8,128)S(1)}, u32[]{:S(2)}, u32[]{:S(2)}) collective-permute-start(f32[256,128]{1,0:T(8,128)S(1)} %bitcast.147), channel_id=1, source_target_pairs={{0,1},{1,0},{2,3},{3,2},{4,5},{5,4},{6,7},{7,6},{8,9},{9,8},{10,11... | collective-permute-start | bytes 393224 | tf_op jit(solution)/shard_map/ppermute | solution.py:61
  25.9 8.8 %collective-permute-start.1 = (bf16[16,4096]{1,0:T(8,128)(2,1)S(1)}, bf16[16,4096]{1,0:T(8,128)(2,1)S(1)}, u32[]{:S(2)}, u32[]{:S(2)}) collective-permute-start(bf16[16,4096]{1,0:T(8,128)(2,1)S(1)} %get-tuple-element.45), channel_id=1, source_target_pairs={{0,1},{1,2},{2,3},{3,4},{4,5},{5,6},{6,7},{7,8},{8,9},{9,10},{10,1... | collective-permute-start | bytes 393224 | tf_op jit(solution)/shard_map/ppermute | solution.py:71
  28.2 7.4 %collective-permute-start.2 = (bf16[16,4096]{1,0:T(8,128)(2,1)S(1)}, bf16[16,4096]{1,0:T(8,128)(2,1)S(1)}, u32[]{:S(2)}, u32[]{:S(2)}) collective-permute-start(bf16[16,4096]{1,0:T(8,128)(2,1)S(1)} %get-tuple-element.46), channel_id=1, source_target_pairs={{1,0},{2,1},{3,2},{4,3},{5,4},{6,5},{7,6},{8,7},{9,8},{10,9},{11,1... | collective-permute-start | bytes 393224 | tf_op jit(solution)/shard_map/ppermute | solution.py:72
  32.3 2.4 %copy-start.6 = (s32[64]{0:T(128)S(1)}, s32[64]{0:T(128)}, u32[]{:S(2)}) copy-start(s32[64]{0:T(128)} %param.9) | copy-start | bytes 772
  32.3 3.2 %copy-start = (bf16[16,16384]{1,0:T(8,128)(2,1)S(1)}, bf16[16,16384]{1,0:T(8,128)(2,1)}, u32[]{:S(2)}) copy-start(bf16[16,16384]{1,0:T(8,128)(2,1)} %shard_map.73) | copy-start | bytes 1572868
  36.1 8.4 %collective-permute-start.3 = (f32[256,128]{1,0:T(8,128)S(1)}, f32[256,128]{1,0:T(8,128)}, u32[]{:S(2)}, u32[]{:S(2)}) collective-permute-start(f32[256,128]{1,0:T(8,128)S(1)} %convolution_add_fusion.6), channel_id=1, source_target_pairs={{0,2},{1,3},{2,0},{3,1},{4,6},{5,7},{6,4},{7,5},{8,10},{9,11},{10,... | collective-permute-start | bytes 393224 | tf_op jit(solution)/shard_map/ppermute | solution.py:61
  42.4 14.2 %copy-start.4 = (f32[1,1,8,32,256]{4,3,1,0,2:T(8,128)S(1)}, f32[1,1,8,32,256]{4,3,1,0,2:T(8,128)}, u32[]{:S(2)}) copy-start(f32[1,1,8,32,256]{4,3,1,0,2:T(8,128)} %get-tuple-element.36) | copy-start | bytes 786436
  45.7 11.1 %collective-permute-start.4 = (f32[256,128]{1,0:T(8,128)S(1)}, f32[256,128]{1,0:T(8,128)S(1)}, u32[]{:S(2)}, u32[]{:S(2)}) collective-permute-start(f32[256,128]{1,0:T(8,128)S(1)} %convolution_add_fusion.5), channel_id=1, source_target_pairs={{0,4},{1,5},{2,6},{3,7},{4,0},{5,1},{6,2},{7,3},{8,12},{9,13},{10,... | collective-permute-start | bytes 393224 | tf_op jit(solution)/shard_map/ppermute | solution.py:61
  57.1 1.4 %collective-permute-start.5 = (f32[256,128]{1,0:T(8,128)S(1)}, f32[256,128]{1,0:T(8,128)S(1)}, u32[]{:S(2)}, u32[]{:S(2)}) collective-permute-start(f32[256,128]{1,0:T(8,128)S(1)} %convolution_add_fusion.4), channel_id=1, source_target_pairs={{0,8},{8,0},{16,24},{24,16},{32,40},{40,32},{48,56},{56,48},{64,72... | collective-permute-start | bytes 393224 | tf_op jit(solution)/shard_map/ppermute | solution.py:61
  58.8 5.6 %collective-permute-start.6 = (f32[256,128]{1,0:T(8,128)S(1)}, f32[256,128]{1,0:T(8,128)S(1)}, u32[]{:S(2)}, u32[]{:S(2)}) collective-permute-start(f32[256,128]{1,0:T(8,128)S(1)} %convolution_add_fusion.3), channel_id=1, source_target_pairs={{0,16},{8,24},{16,0},{24,8},{32,48},{40,56},{48,32},{56,40},{64,80... | collective-permute-start | bytes 393224 | tf_op jit(solution)/shard_map/ppermute | solution.py:61
  63.3 9.9 %copy-start.5 = (bf16[16,32,256]{2,0,1:T(8,128)(2,1)S(1)}, bf16[16,32,256]{2,0,1:T(8,128)(2,1)}, u32[]{:S(2)}) copy-start(bf16[16,32,256]{2,0,1:T(8,128)(2,1)} %get-tuple-element.22) | copy-start | bytes 786436
  64.8 5.2 %collective-permute-start.7 = (f32[256,128]{1,0:T(8,128)S(1)}, f32[256,128]{1,0:T(8,128)S(1)}, u32[]{:S(2)}, u32[]{:S(2)}) collective-permute-start(f32[256,128]{1,0:T(8,128)S(1)} %convolution_add_fusion.2), channel_id=1, source_target_pairs={{0,32},{8,40},{16,48},{24,56},{32,0},{40,8},{48,16},{56,24},{64,96... | collective-permute-start | bytes 393224 | tf_op jit(solution)/shard_map/ppermute | solution.py:61
  69.7 6.9 %copy-start.3 = (f32[1,1,8,32,256]{4,3,1,0,2:T(8,128)S(1)}, f32[1,1,8,32,256]{4,3,1,0,2:T(8,128)}, u32[]{:S(2)}) copy-start(f32[1,1,8,32,256]{4,3,1,0,2:T(8,128)} %get-tuple-element.40) | copy-start | bytes 786436
  69.7 7.6 %copy-start.2 = (bf16[64,32,256]{2,1,0:T(8,128)(2,1)S(1)}, bf16[64,32,256]{2,1,0:T(8,128)(2,1)}, u32[]{:S(2)}) copy-start(bf16[64,32,256]{2,1,0:T(8,128)(2,1)} %param.13) | copy-start | bytes 3145732
  70.3 6.6 %collective-permute-start.8 = (f32[256,128]{1,0:T(8,128)S(1)}, f32[256,128]{1,0:T(8,128)S(1)}, u32[]{:S(2)}, u32[]{:S(2)}) collective-permute-start(f32[256,128]{1,0:T(8,128)S(1)} %convolution_add_fusion.1), channel_id=1, source_target_pairs={{0,64},{8,72},{16,80},{24,88},{32,96},{40,104},{48,112},{56,120},{... | collective-permute-start | bytes 393224 | tf_op jit(solution)/shard_map/ppermute | solution.py:61

commit v18 on v17

--- a/solution.py
+++ b/solution.py
@@ -37,7 +37,7 @@
         o_ref[:, pl.ds(col, CHUNK)] = jnp.concatenate(rows, axis=0).T.astype(o_ref.dtype)
         return carry
 
-    lax.fori_loop(0, count // CHUNK, body, 0, unroll=16)
+    lax.fori_loop(0, count // CHUNK, body, 0, unroll=32)
 
 
 def gather_points(points, index):

time: 79.2 us -> 79.2 us (level)
  no operation moved by 1% of the time
where the time goes in v18:
time: 79.2 us; the launch traced here: 78.7 us
  starting transfers between devices  23.7 us (30%)
  matrix products  23.4 us (30%)
  Pallas kernels  20.9 us (26%)
  local copies, waits for them, and re-layouts  6.78 us (9%)
  waiting for transfers between devices  3.43 us (4%)
    pallas_call x1, Pallas kernels, gather_points(): pl.pallas_call(gather_kernel, out_shape=jax.ShapeDtypeStruct((width, coun...  20.9 us
    ppermute x7, starting transfers between devices, from_partner(): lax.ppermute(x, axis, [(i, i ^ 1 << distance) for i in range(lax.axis_siz...  20.1 us
    dot_general x1, matrix products, local(): jnp.einsum('lpq,slq->slp', band_blocks[:half, 0], own_first, preferred_el...  3.47 us
    dot_general x1, matrix products, local(): jnp.einsum('lpq,slq->slp', band_blocks[half:, 0], own_second, preferred_e...  3.38 us
    dot_general x1, matrix products, local(): jnp.einsum('lpq,slq->slp', band_blocks[:half, 1], picked_first, preferred...  3.38 us
    dot_general x1, matrix products, local(): jnp.einsum('lpq,slq->slp', band_blocks[half:, 1], picked_second, preferre...  3.38 us
    dot_general x7, matrix products, translate(): jnp.dot(level_matrices[0], own_coeffs, precision=lax.Precision.HIGH, pref...  2.93 us
    dot_general x7, matrix products, translate(): jnp.dot(level_matrices[1], other_coeffs, precision=lax.Precision.HIGH, pr...  2.92 us
  transfers between devices with their start and end apart: 9, of which 4 were waited for; matrix products, arithmetic and copies ran while one was open for 30% of the time, Pallas kernels for 0%

profile of v18, /device:TPU:0, one launch (start us, length us, event | category | flops | bytes accessed | tf_op | source)
XLA Modules:
  0.0 78.7 jit_solution(12658013248707576408)
XLA Ops:
  0.0 20.9 %shard_map.73 = bf16[16,16384]{1,0:T(8,128)(2,1)} custom-call(s32[16384]{0:T(1024)} %idx_ref.1, f32[16,16384]{1,0:T(8,128)} %x_hbm.1), custom_call_target="tpu_custom_call" | custom-call | bytes 1572864 | tf_op jit(solution)/shard_map/pallas_call | solution.py:45
  21.0 1.9 %fusion.32 = f32[64,16,32]{2,1,0:T(8,128)S(1)} fusion(bf16[64,32,256]{2,1,0:T(8,128)(2,1)} %param.10, bf16[2,64,8,256]{3,2,1,0:T(8,128)(2,1)} %bitcast.126), kind=kOutput, calls=%fused_computation.41 | convolution fusion | flops 16777216 | bytes 1703936 | tf_op jit(solution)/shard_map/lrp,slp->rls/dot_general | solution.py:112
  23.0 1.8 %collective-permute-start = (f32[256,128]{1,0:T(8,128)S(1)}, f32[256,128]{1,0:T(8,128)S(1)}, u32[]{:S(2)}, u32[]{:S(2)}) collective-permute-start(f32[256,128]{1,0:T(8,128)S(1)} %bitcast.147), channel_id=1, source_target_pairs={{0,1},{1,0},{2,3},{3,2},{4,5},{5,4},{6,7},{7,6},{8,9},{9,8},{10,11... | collective-permute-start | bytes 393224 | tf_op jit(solution)/shard_map/ppermute | solution.py:61
  24.8 1.0 %fusion.36 = (bf16[16,4096]{1,0:T(8,128)(2,1)S(1)}, bf16[16,4096]{1,0:T(8,128)(2,1)S(1)}) fusion(bf16[16,16384]{1,0:T(8,128)(2,1)} %shard_map.73), kind=kLoop, calls=%fused_computation.45 | loop fusion | bytes 524288 | tf_op jit(solution)/shard_map/slice | solution.py:69
  25.8 2.2 %collective-permute-start.1 = (bf16[16,4096]{1,0:T(8,128)(2,1)S(1)}, bf16[16,4096]{1,0:T(8,128)(2,1)S(1)}, u32[]{:S(2)}, u32[]{:S(2)}) collective-permute-start(bf16[16,4096]{1,0:T(8,128)(2,1)S(1)} %get-tuple-element.45), channel_id=1, source_target_pairs={{0,1},{1,2},{2,3},{3,4},{4,5},{5,6},{6,7},{7,8},{8,9},{9,10},{10,1... | collective-permute-start | bytes 393224 | tf_op jit(solution)/shard_map/ppermute | solution.py:71
  28.0 1.3 %collective-permute-start.2 = (bf16[16,4096]{1,0:T(8,128)(2,1)S(1)}, bf16[16,4096]{1,0:T(8,128)(2,1)S(1)}, u32[]{:S(2)}, u32[]{:S(2)}) collective-permute-start(bf16[16,4096]{1,0:T(8,128)(2,1)S(1)} %get-tuple-element.46), channel_id=1, source_target_pairs={{1,0},{2,1},{3,2},{4,3},{5,4},{6,5},{7,6},{8,7},{9,8},{10,9},{11,1... | collective-permute-start | bytes 393224 | tf_op jit(solution)/shard_map/ppermute | solution.py:72
  29.3 1.1 %copy.41 = bf16[2,64,8,256]{3,2,0,1:T(8,128)(2,1)S(1)} copy(bf16[2,64,8,256]{3,2,1,0:T(8,128)(2,1)} %bitcast.127) | data formatting | bytes 1048576 | tf_op jit(solution)/shard_map/reshape | solution.py:111
  30.4 1.7 %convolution_bitcast_fusion = f32[7,2,8,32,256]{4,3,1,0,2:T(8,128)S(1)} fusion(s32[8]{0:T(128)S(1)} %iota_multiply_fusion, f32[1,7,8,2,32,32]{5,4,3,2,1,0:T(8,128)S(1)} %copy-done.1), kind=kOutput, calls=%fused_computation.13 | convolution fusion | flops 352452608 | bytes 4128800 | tf_op jit(solution)/shard_map/lgtab,gbc->ltgac/dot_general | solution.py:83
  32.2 1.2 %fusion.33 = (f32[1,1,8,32,256]{4,3,1,0,2:T(8,128)S(1)}, f32[1,1,8,32,256]{4,3,1,0,2:T(8,128)S(1)}, f32[1,1,8,32,256]{4,3,1,0,2:T(8,128)S(1)}, f32[1,1,8,32,256]...) fusion(f32[7,2,8,32,256]{4,3,1,0,2:T(8,128)S(1)} %convolution_b, ...), kind=kLoop, calls=%fused_computation.42 | loop fusion | bytes 7340032 | tf_op jit(solution)/shard_map/slice | solution.py:96
  33.7 0.8 %fusion.34 = (bf16[16,32,256]{2,0,1:T(8,128)(2,1)}, bf16[16,32,256]{2,0,1:T(8,128)(2,1)}) fusion(bf16[16,64,256]{2,0,1:T(8,128)(2,1)S(1)} %bitcast.130), kind=kLoop, calls=%fused_computation.43 | loop fusion | bytes 1048576 | tf_op jit(solution)/shard_map/slice | solution.py:135
  34.5 0.9 %collective-permute-done.2 = bf16[16,4096]{1,0:T(8,128)(2,1)S(1)} collective-permute-done((bf16[16,4096]{1,0:T(8,128)(2,1)S(1)}, bf16[16,4096]{1,0:T(8,128)(2,1)S(1)}, u32[]{:S(2)}, u32[]{:S(2)}) %collective-permute-start.2) | collective-permute-done | bytes 131104 | tf_op jit(solution)/shard_map/ppermute | solution.py:72
  35.9 5.2 %collective-permute-start.3 = (f32[256,128]{1,0:T(8,128)S(1)}, f32[256,128]{1,0:T(8,128)}, u32[]{:S(2)}, u32[]{:S(2)}) collective-permute-start(f32[256,128]{1,0:T(8,128)S(1)} %convolution_add_fusion.6), channel_id=1, source_target_pairs={{0,2},{1,3},{2,0},{3,1},{4,6},{5,7},{6,4},{7,5},{8,10},{9,11},{10,... | collective-permute-start | bytes 393224 | tf_op jit(solution)/shard_map/ppermute | solution.py:61
  42.4 1.2 %fusion.38 = f32[256,128]{1,0:T(8,128)S(1)} fusion(f32[256,256]{1,0:T(8,128)} %bitcast.144, f32[256,128]{1,0:T(8,128)S(1)} %convolution_add_fusion.6), kind=kOutput, calls=%fused_computation.47 | convolution fusion | flops 50331648 | bytes 524288 | tf_op jit(solution)/shard_map/dot_general | solution.py:89
  44.3 1.3 %convolution_add_fusion.5 = f32[256,128]{1,0:T(8,128)S(1)} fusion(f32[256,128]{1,0:T(8,128)S(1)} %fusion.38, f32[256,256]{1,0:T(8,128)} %bitcast.143, f32[256,128]{1,0:T(8,128)} %collective-permute-done.3), kind=kOutput, calls=%fused_computation.28 | convolution fusion | flops 50364416 | bytes 655360 | tf_op jit(solution)/shard_map/dot_general | solution.py:95
  45.6 7.3 %collective-permute-start.4 = (f32[256,128]{1,0:T(8,128)S(1)}, f32[256,128]{1,0:T(8,128)S(1)}, u32[]{:S(2)}, u32[]{:S(2)}) collective-permute-start(f32[256,128]{1,0:T(8,128)S(1)} %convolution_add_fusion.5), channel_id=1, source_target_pairs={{0,4},{1,5},{2,6},{3,7},{4,0},{5,1},{6,2},{7,3},{8,12},{9,13},{10,... | collective-permute-start | bytes 393224 | tf_op jit(solution)/shard_map/ppermute | solution.py:61
  52.9 3.5 %fusion.16 = f32[16,32,256]{2,0,1:T(8,128)S(1)} fusion(bf16[16,32,256]{2,0,1:T(8,128)(2,1)} %get-tuple-element.21, bf16[64,2,256,256]{3,2,1,0:T(8,128)(2,1)} %param.11), kind=kOutput, calls=%fused_computation.19 | convolution fusion | flops 67108864 | bytes 4980736 | tf_op jit(solution)/shard_map/lpq,slq->slp/dot_general | solution.py:148
  57.3 1.0 %collective-permute-done.5 = f32[256,128]{1,0:T(8,128)S(1)} collective-permute-done((f32[256,128]{1,0:T(8,128)S(1)}, f32[256,128]{1,0:T(8,128)S(1)}, u32[]{:S(2)}, u32[]{:S(2)}) %collective-permute-start.5) | collective-permute-done | bytes 131104 | tf_op jit(solution)/shard_map/ppermute | solution.py:61
  58.7 1.1 %collective-permute-start.6 = (f32[256,128]{1,0:T(8,128)S(1)}, f32[256,128]{1,0:T(8,128)S(1)}, u32[]{:S(2)}, u32[]{:S(2)}) collective-permute-start(f32[256,128]{1,0:T(8,128)S(1)} %convolution_add_fusion.3), channel_id=1, source_target_pairs={{0,16},{8,24},{16,0},{24,8},{32,48},{40,56},{48,32},{56,40},{64,80... | collective-permute-start | bytes 393224 | tf_op jit(solution)/shard_map/ppermute | solution.py:61
  59.8 3.4 %fusion.22 = f32[16,32,256]{2,0,1:T(8,128)S(1)} fusion(bf16[16,32,256]{2,0,1:T(8,128)(2,1)S(1)} %get-tuple-element.23, bf16[64,2,256,256]{3,2,1,0:T(8,128)(2,1)} %param.11), kind=kOutput, calls=%fused_computation.21 | convolution fusion | flops 67108864 | bytes 4980736 | tf_op jit(solution)/shard_map/lpq,slq->slp/dot_general | solution.py:153
  64.6 1.8 %collective-permute-start.7 = (f32[256,128]{1,0:T(8,128)S(1)}, f32[256,128]{1,0:T(8,128)S(1)}, u32[]{:S(2)}, u32[]{:S(2)}) collective-permute-start(f32[256,128]{1,0:T(8,128)S(1)} %convolution_add_fusion.2), channel_id=1, source_target_pairs={{0,32},{8,40},{16,48},{24,56},{32,0},{40,8},{48,16},{56,24},{64,96... | collective-permute-start | bytes 393224 | tf_op jit(solution)/shard_map/ppermute | solution.py:61
  66.3 3.4 %fusion.25 = f32[16,32,256]{2,0,1:T(8,128)S(1)} fusion(bf16[16,32,256]{2,0,1:T(8,128)(2,1)S(1)} %get-tuple-element.24, bf16[64,2,256,256]{3,2,1,0:T(8,128)(2,1)} %param.11), kind=kOutput, calls=%fused_computation.22 | convolution fusion | flops 67108864 | bytes 4980736 | tf_op jit(solution)/shard_map/lpq,slq->slp/dot_general | solution.py:156
  70.3 2.9 %collective-permute-start.8 = (f32[256,128]{1,0:T(8,128)S(1)}, f32[256,128]{1,0:T(8,128)S(1)}, u32[]{:S(2)}, u32[]{:S(2)}) collective-permute-start(f32[256,128]{1,0:T(8,128)S(1)} %convolution_add_fusion.1), channel_id=1, source_target_pairs={{0,64},{8,72},{16,80},{24,88},{32,96},{40,104},{48,112},{56,120},{... | collective-permute-start | bytes 393224 | tf_op jit(solution)/shard_map/ppermute | solution.py:61
  73.2 3.4 %fusion.19 = f32[16,32,256]{2,0,1:T(8,128)S(1)} fusion(bf16[16,32,256]{2,0,1:T(8,128)(2,1)S(1)} %copy-done.5, bf16[64,2,256,256]{3,2,1,0:T(8,128)(2,1)} %param.11), kind=kOutput, calls=%fused_computation.20 | convolution fusion | flops 67108864 | bytes 4980736 | tf_op jit(solution)/shard_map/lpq,slq->slp/dot_general | solution.py:149
  77.7 1.1 %copy.35 = f32[64,2,8,256]{3,2,0,1:T(8,128)} copy(f32[64,2,8,256]{3,2,1,0:T(8,128)S(1)} %fusion.15) | data formatting | bytes 2097152 | tf_op jit(solution)/shard_map/reshape | solution.py:160
  (46 shorter events, 7.1 us)
Async XLA Ops:
  20.9 9.5 %copy-start.1 = (f32[1,7,8,2,32,32]{5,4,3,2,1,0:T(8,128)S(1)}, f32[1,7,8,2,32,32]{5,4,3,2,1,0:T(8,128)}, u32[]{:S(2)}) copy-start(f32[1,7,8,2,32,32]{5,4,3,2,1,0:T(8,128)} %param.12) | copy-start | bytes 1376260
  23.0 12.6 %collective-permute-start = (f32[256,128]{1,0:T(8,128)S(1)}, f32[256,128]{1,0:T(8,128)S(1)}, u32[]{:S(2)}, u32[]{:S(2)}) collective-permute-start(f32[256,128]{1,0:T(8,128)S(1)} %bitcast.147), channel_id=1, source_target_pairs={{0,1},{1,0},{2,3},{3,2},{4,5},{5,4},{6,7},{7,6},{8,9},{9,8},{10,11... | collective-permute-start | bytes 393224 | tf_op jit(solution)/shard_map/ppermute | solution.py:61
  25.8 8.8 %collective-permute-start.1 = (bf16[16,4096]{1,0:T(8,128)(2,1)S(1)}, bf16[16,4096]{1,0:T(8,128)(2,1)S(1)}, u32[]{:S(2)}, u32[]{:S(2)}) collective-permute-start(bf16[16,4096]{1,0:T(8,128)(2,1)S(1)} %get-tuple-element.45), channel_id=1, source_target_pairs={{0,1},{1,2},{2,3},{3,4},{4,5},{5,6},{6,7},{7,8},{8,9},{9,10},{10,1... | collective-permute-start | bytes 393224 | tf_op jit(solution)/shard_map/ppermute | solution.py:71
  28.0 7.4 %collective-permute-start.2 = (bf16[16,4096]{1,0:T(8,128)(2,1)S(1)}, bf16[16,4096]{1,0:T(8,128)(2,1)S(1)}, u32[]{:S(2)}, u32[]{:S(2)}) collective-permute-start(bf16[16,4096]{1,0:T(8,128)(2,1)S(1)} %get-tuple-element.46), channel_id=1, source_target_pairs={{1,0},{2,1},{3,2},{4,3},{5,4},{6,5},{7,6},{8,7},{9,8},{10,9},{11,1... | collective-permute-start | bytes 393224 | tf_op jit(solution)/shard_map/ppermute | solution.py:72
  32.2 2.4 %copy-start.6 = (s32[64]{0:T(128)S(1)}, s32[64]{0:T(128)}, u32[]{:S(2)}) copy-start(s32[64]{0:T(128)} %param.9) | copy-start | bytes 772
  32.2 3.2 %copy-start = (bf16[16,16384]{1,0:T(8,128)(2,1)S(1)}, bf16[16,16384]{1,0:T(8,128)(2,1)}, u32[]{:S(2)}) copy-start(bf16[16,16384]{1,0:T(8,128)(2,1)} %shard_map.73) | copy-start | bytes 1572868
  35.9 8.4 %collective-permute-start.3 = (f32[256,128]{1,0:T(8,128)S(1)}, f32[256,128]{1,0:T(8,128)}, u32[]{:S(2)}, u32[]{:S(2)}) collective-permute-start(f32[256,128]{1,0:T(8,128)S(1)} %convolution_add_fusion.6), channel_id=1, source_target_pairs={{0,2},{1,3},{2,0},{3,1},{4,6},{5,7},{6,4},{7,5},{8,10},{9,11},{10,... | collective-permute-start | bytes 393224 | tf_op jit(solution)/shard_map/ppermute | solution.py:61
  42.2 14.2 %copy-start.4 = (f32[1,1,8,32,256]{4,3,1,0,2:T(8,128)S(1)}, f32[1,1,8,32,256]{4,3,1,0,2:T(8,128)}, u32[]{:S(2)}) copy-start(f32[1,1,8,32,256]{4,3,1,0,2:T(8,128)} %get-tuple-element.36) | copy-start | bytes 786436
  45.6 11.1 %collective-permute-start.4 = (f32[256,128]{1,0:T(8,128)S(1)}, f32[256,128]{1,0:T(8,128)S(1)}, u32[]{:S(2)}, u32[]{:S(2)}) collective-permute-start(f32[256,128]{1,0:T(8,128)S(1)} %convolution_add_fusion.5), channel_id=1, source_target_pairs={{0,4},{1,5},{2,6},{3,7},{4,0},{5,1},{6,2},{7,3},{8,12},{9,13},{10,... | collective-permute-start | bytes 393224 | tf_op jit(solution)/shard_map/ppermute | solution.py:61
  57.0 1.4 %collective-permute-start.5 = (f32[256,128]{1,0:T(8,128)S(1)}, f32[256,128]{1,0:T(8,128)S(1)}, u32[]{:S(2)}, u32[]{:S(2)}) collective-permute-start(f32[256,128]{1,0:T(8,128)S(1)} %convolution_add_fusion.4), channel_id=1, source_target_pairs={{0,8},{8,0},{16,24},{24,16},{32,40},{40,32},{48,56},{56,48},{64,72... | collective-permute-start | bytes 393224 | tf_op jit(solution)/shard_map/ppermute | solution.py:61
  58.7 5.6 %collective-permute-start.6 = (f32[256,128]{1,0:T(8,128)S(1)}, f32[256,128]{1,0:T(8,128)S(1)}, u32[]{:S(2)}, u32[]{:S(2)}) collective-permute-start(f32[256,128]{1,0:T(8,128)S(1)} %convolution_add_fusion.3), channel_id=1, source_target_pairs={{0,16},{8,24},{16,0},{24,8},{32,48},{40,56},{48,32},{56,40},{64,80... | collective-permute-start | bytes 393224 | tf_op jit(solution)/shard_map/ppermute | solution.py:61
  63.2 10.0 %copy-start.5 = (bf16[16,32,256]{2,0,1:T(8,128)(2,1)S(1)}, bf16[16,32,256]{2,0,1:T(8,128)(2,1)}, u32[]{:S(2)}) copy-start(bf16[16,32,256]{2,0,1:T(8,128)(2,1)} %get-tuple-element.22) | copy-start | bytes 786436
  64.6 5.4 %collective-permute-start.7 = (f32[256,128]{1,0:T(8,128)S(1)}, f32[256,128]{1,0:T(8,128)S(1)}, u32[]{:S(2)}, u32[]{:S(2)}) collective-permute-start(f32[256,128]{1,0:T(8,128)S(1)} %convolution_add_fusion.2), channel_id=1, source_target_pairs={{0,32},{8,40},{16,48},{24,56},{32,0},{40,8},{48,16},{56,24},{64,96... | collective-permute-start | bytes 393224 | tf_op jit(solution)/shard_map/ppermute | solution.py:61
  69.7 6.9 %copy-start.3 = (f32[1,1,8,32,256]{4,3,1,0,2:T(8,128)S(1)}, f32[1,1,8,32,256]{4,3,1,0,2:T(8,128)}, u32[]{:S(2)}) copy-start(f32[1,1,8,32,256]{4,3,1,0,2:T(8,128)} %get-tuple-element.40) | copy-start | bytes 786436
  69.7 7.6 %copy-start.2 = (bf16[64,32,256]{2,1,0:T(8,128)(2,1)S(1)}, bf16[64,32,256]{2,1,0:T(8,128)(2,1)}, u32[]{:S(2)}) copy-start(bf16[64,32,256]{2,1,0:T(8,128)(2,1)} %param.13) | copy-start | bytes 3145732
  70.3 6.6 %collective-permute-start.8 = (f32[256,128]{1,0:T(8,128)S(1)}, f32[256,128]{1,0:T(8,128)S(1)}, u32[]{:S(2)}, u32[]{:S(2)}) collective-permute-start(f32[256,128]{1,0:T(8,128)S(1)} %convolution_add_fusion.1), channel_id=1, source_target_pairs={{0,64},{8,72},{16,80},{24,88},{32,96},{40,104},{48,112},{56,120},{... | collective-permute-start | bytes 393224 | tf_op jit(solution)/shard_map/ppermute | solution.py:61
